TPU v7x, 256 devices: a whole 4x4x8 slice. The times are simulated.
256 devices in a mesh: blk: 32 (over y, z), tp: 8 (over x, core).
Axes of the slice: x: 4, y: 4, z: 8, core: 2. Of those that a mesh axis runs over, the one named last changes fastest.
Arguments:
- queries: bfloat16 [32768, 1664], P(('blk', 'tp')), may hold values from -120 to 120
- keys: bfloat16 [32768, 1664], P(('blk', 'tp')), may hold values from -6 to 6
- values: bfloat16 [32768, 1664], P(('blk', 'tp')), may hold values from -6 to 6
- segment_ids: int32 [32768], replicated, may hold values from -1 to 31, as said below
- proj_weight: bfloat16 [6656, 3072], P(None, 'tp'), may hold values from -0.078125 to 0.078125
Outputs:
- normed: bfloat16 [8192, 3072], P('blk', 'tp')
- seg_peaks: float32 [32], replicated
Inputs may be any that keep to these rules, and one draw needn't show every extreme that they name: `segment_ids`: ids other than -1 never fall along the pack; every image 0 to 31 occurs as one run of tokens that starts at a multiple of 4 and has a multiple of 4 tokens, at most 1024; some image has exactly 1024; -1 marks padding tokens, which may stand between images.
All inputs are finite; a program needn't handle non-finite values.
Results may differ from a plain program's by a relative error of at most 0.0056.
Values may be sent and summed in bfloat16 or wider, within the bound.
No kernel may reach another device: no remote copies, remote signals or barrier semaphores. Data moves between devices by JAX's collectives and lax.ppermute only.
A program may use at most 128 MiB of HBM per device.

v0:
```python
import jax
import jax.numpy as jnp
from jax import lax
from jax.sharding import PartitionSpec as P

HEAD = 128


masked_score = -1e30
epsilon = 1e-06


def from_behind(x, axis, by):
    devices = lax.axis_size(axis)
    pairs = [(i, i + by) for i in range(devices) if 0 <= i + by < devices]
    return lax.ppermute(x, axis, pairs)


def key_scores(query_heads, key_heads):
    return jnp.einsum(
        "rhd,khd->hrk", query_heads, key_heads, preferred_element_type=jnp.float32
    ) * HEAD ** (-0.5)


def finish(scores, allowed, value_heads):
    scores = jnp.where(allowed[None], scores, masked_score)
    row_top = jnp.max(scores, axis=2, keepdims=True)
    exp_terms = jnp.where(allowed[None], jnp.exp(scores - row_top), 0.0)
    row_total = jnp.maximum(jnp.sum(exp_terms, axis=2), 1.0)
    weights = exp_terms.astype(jnp.bfloat16)
    mixed_out = jnp.einsum("hrk,khd->rhd", weights, value_heads, preferred_element_type=jnp.float32)
    return mixed_out / row_total.T[:, :, None]


def per_device(queries, keys, values, segment_ids, proj_weight):
    group_count = lax.axis_size("blk")
    group_index = lax.axis_index("blk")
    part_index = lax.axis_index("tp")
    row_count = queries.shape[0]
    width = queries.shape[1]
    heads_count = width // HEAD
    block_len = segment_ids.shape[0] // group_count
    own_begin = group_index * block_len
    query_segs = lax.dynamic_slice_in_dim(
        segment_ids, own_begin + part_index * row_count, row_count
    )
    own_keys, own_values = (
        lax.all_gather(keys, "tp", axis=0, tiled=True),
        lax.all_gather(values, "tp", axis=0, tiled=True),
    )
    before_keys, before_values = from_behind((own_keys, own_values), "blk", 1)
    after_keys, after_values = from_behind((own_keys, own_values), "blk", -1)

    def neighbor_segs(offset):
        target = group_index + offset
        inside = (target >= 0) & (target < group_count)
        begin_at = jnp.clip(target, 0, group_count - 1) * block_len
        return jnp.where(inside, lax.dynamic_slice_in_dim(segment_ids, begin_at, block_len), -2)

    seg_sets = (neighbor_segs(-1), neighbor_segs(0), neighbor_segs(1))
    key_sets = (before_keys, own_keys, after_keys)
    masks = [
        (query_segs[:, None] == key_segs[None, :]) & (query_segs[:, None] >= 0)
        for key_segs in seg_sets
    ]
    query_heads = queries.reshape(row_count, heads_count, HEAD)
    all_keys = jnp.concatenate(key_sets, axis=0).reshape(3 * block_len, heads_count, HEAD)
    scores = key_scores(query_heads, all_keys)
    full_mask = jnp.concatenate(masks, axis=1)
    value_heads = jnp.concatenate((before_values, own_values, after_values), axis=0).reshape(
        3 * block_len, heads_count, HEAD
    )
    attended = finish(scores, full_mask, value_heads).reshape(row_count, width).astype(jnp.bfloat16)
    merged = attended.reshape(row_count // 4, 4 * width)
    projected = jnp.dot(
        lax.all_gather(merged, "tp", axis=0, tiled=True),
        proj_weight,
        preferred_element_type=jnp.float32,
    )
    row_segs = lax.dynamic_slice_in_dim(segment_ids, own_begin, block_len)[::4]
    member = row_segs[:, None] == jnp.arange(group_count, dtype=jnp.int32)[None, :]
    squares = jnp.sum(projected * projected, axis=1)
    seg_sums = jnp.sum(jnp.where(member, squares[:, None], 0.0), axis=0)
    seg_counts = jnp.sum(member.astype(jnp.float32), axis=0) * projected.shape[1]
    row_peak = jnp.max(jnp.where(member, jnp.max(projected, axis=1)[:, None], masked_score), axis=0)
    seg_sums, seg_counts = lax.psum((seg_sums, seg_counts), ("blk", "tp"))
    row_peak = lax.pmax(row_peak, ("blk", "tp"))
    seg_scale = lax.rsqrt(seg_sums / seg_counts + epsilon)
    row_scale = jnp.sum(jnp.where(member, seg_scale[None, :], 0.0), axis=1)
    normed = (projected * row_scale[:, None]).astype(jnp.bfloat16)
    return (normed, row_peak * seg_scale)


def solution(mesh):
    in_specs = (
        P(("blk", "tp"), None),
        P(("blk", "tp"), None),
        P(("blk", "tp"), None),
        P(),
        P(None, "tp"),
    )
    out_specs = (P("blk", "tp"), P())
    return jax.shard_map(
        per_device, mesh=mesh, in_specs=in_specs, out_specs=out_specs, check_vma=False
    )
```

profile of v0, /device:TPU:8, one launch (start us, length us, event | category | flops | bytes accessed | tf_op | source)
XLA Modules:
  0.0 440.0 jit_solution(14741535118343284138)
XLA Ops:
  7.2 2.0 copy.18
  9.3 0.7 all-gather.4.cloned.1.call-update
  10.0 38.0 %all-gather.6.cloned.1.call-done = bf16[1024,1664]{0,1:T(8,128)(2,1)} async-done(((bf16[128,1664]{0,1:T(8,128)(2,1)}), bf16[1024,1664]{0,1:T(8,128)(2,1)}) %all-gather.6.cloned.1.call-update) | async-done | bytes 3407888 | tf_op jit(solution)/shard_map/all_gather | solution.py:48
  48.0 5.2 %collective-permute-start.3 = (bf16[1024,1664]{0,1:T(8,128)(2,1)}, bf16[1024,1664]{0,1:T(8,128)(2,1)S(1)}, u32[]{:S(2)}, u32[]{:S(2)}) collective-permute-start(bf16[1024,1664]{0,1:T(8,128)(2,1)} %all-gather.6.cloned.1.call-done), channel_id=1, source_target_pairs={{8,0},{16,8},{24,16},{32,24},{40,32},{48,40},{56,48},{64,56},{72,6... | collective-permute-start | bytes 10223624 | tf_op jit(solution)/shard_map/ppermute | solution.py:16
  53.2 1.9 collective-permute-start.2
  55.2 2.0 copy.19
  57.1 0.8 broadcast_compare_fusion
  57.9 0.8 fusion.21
  58.7 23.6 %all-gather.4.cloned.1.call-done = bf16[1024,1664]{1,0:T(8,128)(2,1)} async-done(((bf16[128,1664]{1,0:T(8,128)(2,1)}), bf16[1024,1664]{1,0:T(8,128)(2,1)}) %all-gather.4.cloned.1.call-update) | async-done | bytes 3407888 | tf_op jit(solution)/shard_map/all_gather | solution.py:49
  82.3 5.2 %collective-permute-start.1 = (bf16[1024,1664]{1,0:T(8,128)(2,1)}, bf16[1024,1664]{1,0:T(8,128)(2,1)}, u32[]{:S(2)}, u32[]{:S(2)}) collective-permute-start(bf16[1024,1664]{1,0:T(8,128)(2,1)} %all-gather.4.cloned.1.call-done), channel_id=1, source_target_pairs={{8,0},{16,8},{24,16},{32,24},{40,32},{48,40},{56,48},{64,56},{72,6... | collective-permute-start | bytes 10223624 | tf_op jit(solution)/shard_map/ppermute | solution.py:16
  87.5 1.9 collective-permute-start
  89.4 0.7 compare_and_fusion.2
  90.1 0.8 pad_add_fusion
  90.9 36.6 %collective-permute-done.3 = bf16[1024,1664]{0,1:T(8,128)(2,1)S(1)} collective-permute-done((bf16[1024,1664]{0,1:T(8,128)(2,1)}, bf16[1024,1664]{0,1:T(8,128)(2,1)S(1)}, u32[]{:S(2)}, u32[]{:S(2)}) %collective-permute-start.3) | collective-permute-done | bytes 3407904 | tf_op jit(solution)/shard_map/ppermute | solution.py:16
  127.6 6.5 %collective-permute-done.2 = bf16[1024,1664]{0,1:T(8,128)(2,1)} collective-permute-done((bf16[1024,1664]{0,1:T(8,128)(2,1)}, bf16[1024,1664]{0,1:T(8,128)(2,1)}, u32[]{:S(2)}, u32[]{:S(2)}) %collective-permute-start.2) | collective-permute-done | bytes 3407904 | tf_op jit(solution)/shard_map/ppermute | solution.py:16
  134.1 7.9 %pad_maximum_fusion.1 = bf16[3072,1664]{0,1:T(8,128)(2,1)} fusion(bf16[1024,1664]{0,1:T(8,128)(2,1)S(1)} %collective-permute-done.3, bf16[1024,1664]{0,1:T(8,128)(2,1)} %all-gather.6.cloned.1.call-done, bf16[1024,1664]{0,1:T(8,128)(2,1)} %collective-permute-done.2), kind=kLoop, calls=%fused_computation.5 | loop fusion | flops 30670848 | bytes 20447232 | tf_op jit(solution)/shard_map/concatenate | solution.py:67
  142.0 17.8 %fusion.22 = (f32[13,128]{1,0:T(8,128)S(1)}, bf16[13,128,3072]{1,2,0:T(8,128)(2,1)}) fusion(pred[128,3072]{0,1:T(8,128)(4,1)} %pad_add_fusion, bf16[3072,13,128]{0,2,1:T(8,128)(2,1)} %bitcast.30, bf16[128,13,128]{0,2,1:T(8,128)(2,1)} %bitcast.32), kind=kOutput, calls=%fused_computation.37 | convolution fusion | flops 1339296768 | bytes 21273088 | tf_op jit(solution)/shard_map/sub | solution.py:28
  159.8 40.1 %collective-permute-done.1 = bf16[1024,1664]{1,0:T(8,128)(2,1)} collective-permute-done((bf16[1024,1664]{1,0:T(8,128)(2,1)}, bf16[1024,1664]{1,0:T(8,128)(2,1)}, u32[]{:S(2)}, u32[]{:S(2)}) %collective-permute-start.1) | collective-permute-done | bytes 3407904 | tf_op jit(solution)/shard_map/ppermute | solution.py:16
  199.9 6.2 %collective-permute-done = bf16[1024,1664]{1,0:T(8,128)(2,1)} collective-permute-done((bf16[1024,1664]{1,0:T(8,128)(2,1)}, bf16[1024,1664]{1,0:T(8,128)(2,1)}, u32[]{:S(2)}, u32[]{:S(2)}) %collective-permute-start) | collective-permute-done | bytes 3407904 | tf_op jit(solution)/shard_map/ppermute | solution.py:16
  206.2 15.7 %pad_maximum_fusion = bf16[3072,1664]{1,0:T(8,128)(2,1)} fusion(bf16[1024,1664]{1,0:T(8,128)(2,1)} %collective-permute-done.1, bf16[1024,1664]{1,0:T(8,128)(2,1)S(1)} %copy-done, bf16[1024,1664]{1,0:T(8,128)(2,1)} %collective-permute-done), kind=kLoop, calls=%fused_computation.4 | loop fusion | flops 30670848 | bytes 20447232 | tf_op jit(solution)/shard_map/concatenate | solution.py:70
  221.9 14.3 %copy.17 = bf16[3072,1664]{0,1:T(8,128)(2,1)} copy(bf16[3072,1664]{1,0:T(8,128)(2,1)} %pad_maximum_fusion) | data formatting | bytes 20447232 | tf_op jit(solution)/shard_map/concatenate | solution.py:70
  236.2 9.6 %fusion.15 = bf16[128,13,128]{0,2,1:T(8,128)(2,1)S(1)} fusion(bf16[3072,13,128]{0,2,1:T(8,128)(2,1)} %bitcast.31, bf16[13,128,3072]{1,2,0:T(8,128)(2,1)} %get-tuple-element.20, f32[128,13]{0,1:T(8,128)S(1)} %maximum_bitcast_fusion), kind=kOutput, calls=%fused_computation.15 | convolution fusion | flops 1309048832 | bytes 20879872 | tf_op jit(solution)/shard_map/hrk,khd->rhd/dot_general | solution.py:31
  245.8 0.4 copy.23
  246.3 1.1 convert_element_type.18
  247.4 0.2 slice.3
  247.6 28.6 %all-gather.8.cloned.1.call-done = bf16[256,6656]{1,0:T(8,128)(2,1)} async-done(((bf16[32,6656]{1,0:T(8,128)(2,1)}), bf16[256,6656]{1,0:T(8,128)(2,1)}) %all-gather.8.cloned.1.call-update) | async-done | bytes 3407888 | tf_op jit(solution)/shard_map/all_gather | solution.py:76
  276.2 5.5 %fusion.20 = (f32[256]{0:T(256)S(1)}, f32[256]{0:T(256)S(1)}, f32[256,384]{1,0:T(8,128)S(1)}) fusion(bf16[256,6656]{1,0:T(8,128)(2,1)} %all-gather.8.cloned.1.call-done, bf16[6656,384]{1,0:T(8,128)(2,1)} %param.9), kind=kOutput, calls=%fused_computation.35 | convolution fusion | flops 1308917248 | bytes 8914944 | tf_op jit(solution)/shard_map/dot_general | solution.py:75
  281.9 75.9 %all-reduce = (f32[32]{0:T(128)S(1)}, f32[32]{0:T(128)S(1)}) all-reduce(f32[32]{0:T(128)S(1)} %get-tuple-element.7, f32[32]{0:T(128)S(1)} %broadcast_multiply_fusion), channel_id=1, replica_groups=mesh['blk'=32,'tp'=8] {'blk','tp'}, use_global_device_ids=true, to_apply=%region_4.5 | all-reduce | flops 64 | bytes 512 | tf_op jit(solution)/shard_map/psum | solution.py:86
  357.8 0.1 select_reduce_fusion
  357.9 74.3 %pmax.7 = f32[32]{0:T(128)S(1)} all-reduce(f32[32]{0:T(128)S(1)} %get-tuple-element.4), channel_id=1, replica_groups=mesh['blk'=32,'tp'=8] {'blk','tp'}, use_global_device_ids=true, to_apply=%region_10.11 | all-reduce | flops 32 | bytes 256 | tf_op jit(solution)/shard_map/pmax | solution.py:87
  432.2 0.5 mul.57
  432.7 0.8 multiply_convert_fusion
  (11 shorter events, 0.3 us)
Async XLA Ops:
  7.2 40.8 %all-gather.6.cloned.1.call-start = ((), (), s32[]{:S(2)}) async-start(), calls=%async_computation.1 | async-start | bytes 3833856 | tf_op jit(solution)/shard_map/all_gather | solution.py:48
  9.2 73.1 %all-gather.4.cloned.1.call-start = ((), (), s32[]{:S(2)}) async-start(), calls=%async_computation | async-start | bytes 3833856 | tf_op jit(solution)/shard_map/all_gather | solution.py:49
  10.0 266.2 %all-gather.8.cloned.1.call-start = ((), (), s32[]{:S(2)}) async-start(), calls=%async_computation.2 | async-start | bytes 3833856 | tf_op jit(solution)/shard_map/all_gather | solution.py:76
  48.0 79.6 %collective-permute-start.3 = (bf16[1024,1664]{0,1:T(8,128)(2,1)}, bf16[1024,1664]{0,1:T(8,128)(2,1)S(1)}, u32[]{:S(2)}, u32[]{:S(2)}) collective-permute-start(bf16[1024,1664]{0,1:T(8,128)(2,1)} %all-gather.6.cloned.1.call-done), channel_id=1, source_target_pairs={{8,0},{16,8},{24,16},{32,24},{40,32},{48,40},{56,48},{64,56},{72,6... | collective-permute-start | bytes 10223624 | tf_op jit(solution)/shard_map/ppermute | solution.py:16
  53.2 80.9 %collective-permute-start.2 = (bf16[1024,1664]{0,1:T(8,128)(2,1)}, bf16[1024,1664]{0,1:T(8,128)(2,1)}, u32[]{:S(2)}, u32[]{:S(2)}) collective-permute-start(bf16[1024,1664]{0,1:T(8,128)(2,1)} %all-gather.6.cloned.1.call-done), channel_id=1, source_target_pairs={{0,8},{8,16},{16,24},{24,32},{32,40},{40,48},{48,56},{56,64},{64,7... | collective-permute-start | bytes 10223624 | tf_op jit(solution)/shard_map/ppermute | solution.py:16
  82.3 117.7 %collective-permute-start.1 = (bf16[1024,1664]{1,0:T(8,128)(2,1)}, bf16[1024,1664]{1,0:T(8,128)(2,1)}, u32[]{:S(2)}, u32[]{:S(2)}) collective-permute-start(bf16[1024,1664]{1,0:T(8,128)(2,1)} %all-gather.4.cloned.1.call-done), channel_id=1, source_target_pairs={{8,0},{16,8},{24,16},{32,24},{40,32},{48,40},{56,48},{64,56},{72,6... | collective-permute-start | bytes 10223624 | tf_op jit(solution)/shard_map/ppermute | solution.py:16
  87.5 118.7 %collective-permute-start = (bf16[1024,1664]{1,0:T(8,128)(2,1)}, bf16[1024,1664]{1,0:T(8,128)(2,1)}, u32[]{:S(2)}, u32[]{:S(2)}) collective-permute-start(bf16[1024,1664]{1,0:T(8,128)(2,1)} %all-gather.4.cloned.1.call-done), channel_id=1, source_target_pairs={{0,8},{8,16},{16,24},{24,32},{32,40},{40,48},{48,56},{56,64},{64,7... | collective-permute-start | bytes 10223624 | tf_op jit(solution)/shard_map/ppermute | solution.py:16
  142.0 64.1 %copy-start = (bf16[1024,1664]{1,0:T(8,128)(2,1)S(1)}, bf16[1024,1664]{1,0:T(8,128)(2,1)}, u32[]{:S(2)}) copy-start(bf16[1024,1664]{1,0:T(8,128)(2,1)} %all-gather.4.cloned.1.call-done) | copy-start | bytes 10223620
Sparse Core Ops, SparseCore 0:
  9.8 38.1 all-gather.5
  49.8 32.3 all-gather.3
  247.5 28.6 all-gather.7
where the time goes:
time: 442 us; the launch traced here: 440 us
  waiting for transfers between devices  180 us (41%)
  blocking collectives  150 us (34%)
  matrix products  32.9 us (7%)
  other arithmetic  28.2 us (6%)
  local copies, waits for them, and re-layouts  20 us (5%)
  starting transfers between devices  14.3 us (3%)
  between operations  13.8 us (3%)
    ppermute x4, waiting for transfers between devices, from_behind(): return lax.ppermute(x, axis, pairs)  89.5 us
    psum x1, blocking collectives, per_device(): seg_sums, seg_counts = lax.psum((seg_sums, seg_counts), ('blk', 'tp'))  75.9 us
    pmax x1, blocking collectives, per_device(): row_peak = lax.pmax(row_peak, ('blk', 'tp'))  74.3 us
    all_gather x1, waiting for transfers between devices, per_device(): lax.all_gather(keys, 'tp', axis=0, tiled=True)  38 us
    all_gather x1, waiting for transfers between devices, per_device(): lax.all_gather(merged, 'tp', axis=0, tiled=True)  28.6 us
    all_gather x1, waiting for transfers between devices, per_device(): lax.all_gather(values, 'tp', axis=0, tiled=True)  23.6 us
    sub x1, matrix products, finish(): exp_terms = jnp.where(allowed[None], jnp.exp(scores - row_top), 0.0)  17.8 us
    concatenate x1, other arithmetic, per_device(): jnp.concatenate((before_values, own_values, after_values), axis=0)  15.7 us
  transfers between devices with their start and end apart: 7, of which 7 were waited for; matrix products, arithmetic and copies ran while one was open for 7% of the time, Pallas kernels for 0%

commit v1 on v0

--- a/solution.py
+++ b/solution.py
@@ -81,10 +81,15 @@
     member = row_segs[:, None] == jnp.arange(group_count, dtype=jnp.int32)[None, :]
     squares = jnp.sum(projected * projected, axis=1)
     seg_sums = jnp.sum(jnp.where(member, squares[:, None], 0.0), axis=0)
-    seg_counts = jnp.sum(member.astype(jnp.float32), axis=0) * projected.shape[1]
     row_peak = jnp.max(jnp.where(member, jnp.max(projected, axis=1)[:, None], masked_score), axis=0)
-    seg_sums, seg_counts = lax.psum((seg_sums, seg_counts), ("blk", "tp"))
-    row_peak = lax.pmax(row_peak, ("blk", "tp"))
+    all_segs = segment_ids[::4]
+    all_member = all_segs[:, None] == jnp.arange(group_count, dtype=jnp.int32)[None, :]
+    seg_counts = jnp.sum(all_member.astype(jnp.float32), axis=0) * (
+        projected.shape[1] * lax.axis_size("tp")
+    )
+    stats = lax.all_gather(jnp.stack([seg_sums, row_peak]), ("blk", "tp"), axis=0)
+    seg_sums = jnp.sum(stats[:, 0], axis=0)
+    row_peak = jnp.max(stats[:, 1], axis=0)
     seg_scale = lax.rsqrt(seg_sums / seg_counts + epsilon)
     row_scale = jnp.sum(jnp.where(member, seg_scale[None, :], 0.0), axis=1)
     normed = (projected * row_scale[:, None]).astype(jnp.bfloat16)

time: 442 us -> 355 us (0.80)
  blocking collectives: 150 us -> 60.9 us
    psum x1 -> x0, blocking collectives: 75.9 us -> none  [per_device(): seg_sums, seg_counts = lax.psum((seg_sums, seg_counts), ('blk', 'tp'))]
    pmax x1 -> x0, blocking collectives: 74.3 us -> none  [per_device(): row_peak = lax.pmax(row_peak, ('blk', 'tp'))]
    all_gather x0 -> x1, blocking collectives: none -> 60.9 us  [per_device(): lax.all_gather(jnp.stack([seg_sums, row_peak]), ('blk', 'tp'), axis=0)]
  transfers between devices with their start and end apart: 7 -> 7, of which waited for: 7 -> 7; matrix products, arithmetic and copies ran while one was open for 7% -> 9% of each run, Pallas kernels for 0% -> 0%
where the time goes in v1:
time: 355 us; the launch traced here: 351 us
  waiting for transfers between devices  178 us (50%)
  blocking collectives  60.9 us (17%)
  matrix products  32.9 us (9%)
  other arithmetic  28.8 us (8%)
  local copies, waits for them, and re-layouts  22.1 us (6%)
  starting transfers between devices  14.3 us (4%)
  between operations  13.8 us (4%)
    ppermute x4, waiting for transfers between devices, from_behind(): return lax.ppermute(x, axis, pairs)  89.5 us
    all_gather x1, blocking collectives, per_device(): lax.all_gather(jnp.stack([seg_sums, row_peak]), ('blk', 'tp'), axis=0)  60.9 us
    all_gather x1, waiting for transfers between devices, per_device(): lax.all_gather(keys, 'tp', axis=0, tiled=True)  38 us
    all_gather x1, waiting for transfers between devices, per_device(): lax.all_gather(merged, 'tp', axis=0, tiled=True)  26.3 us
    all_gather x1, waiting for transfers between devices, per_device(): lax.all_gather(values, 'tp', axis=0, tiled=True)  23.6 us
    sub x1, matrix products, finish(): exp_terms = jnp.where(allowed[None], jnp.exp(scores - row_top), 0.0)  17.8 us
    concatenate x1, other arithmetic, per_device(): jnp.concatenate((before_values, own_values, after_values), axis=0)  15.7 us
    concatenate x1, local copies, waits for them, and re-layouts, per_device(): jnp.concatenate((before_values, own_values, after_values), axis=0)  14.3 us
  transfers between devices with their start and end apart: 7, of which 7 were waited for; matrix products, arithmetic and copies ran while one was open for 9% of the time, Pallas kernels for 0%

profile of v1, /device:TPU:8, one launch (start us, length us, event | category | flops | bytes accessed | tf_op | source)
XLA Modules:
  0.0 351.0 jit_solution(16058946123086117243)
XLA Ops:
  7.2 2.0 copy.25
  9.3 0.7 all-gather.6.cloned.1.call-update
  10.0 38.0 %all-gather.8.cloned.1.call-done = bf16[1024,1664]{0,1:T(8,128)(2,1)} async-done(((bf16[128,1664]{0,1:T(8,128)(2,1)}), bf16[1024,1664]{0,1:T(8,128)(2,1)}) %all-gather.8.cloned.1.call-update) | async-done | bytes 3407888 | tf_op jit(solution)/shard_map/all_gather | solution.py:48
  48.0 5.2 %collective-permute-start.3 = (bf16[1024,1664]{0,1:T(8,128)(2,1)}, bf16[1024,1664]{0,1:T(8,128)(2,1)S(1)}, u32[]{:S(2)}, u32[]{:S(2)}) collective-permute-start(bf16[1024,1664]{0,1:T(8,128)(2,1)} %all-gather.8.cloned.1.call-done), channel_id=1, source_target_pairs={{8,0},{16,8},{24,16},{32,24},{40,32},{48,40},{56,48},{64,56},{72,6... | collective-permute-start | bytes 10223624 | tf_op jit(solution)/shard_map/ppermute | solution.py:16
  53.2 1.9 collective-permute-start.2
  55.2 2.0 copy.26
  57.1 0.8 broadcast_compare_fusion
  57.9 0.8 fusion.21
  58.7 23.6 %all-gather.6.cloned.1.call-done = bf16[1024,1664]{1,0:T(8,128)(2,1)} async-done(((bf16[128,1664]{1,0:T(8,128)(2,1)}), bf16[1024,1664]{1,0:T(8,128)(2,1)}) %all-gather.6.cloned.1.call-update) | async-done | bytes 3407888 | tf_op jit(solution)/shard_map/all_gather | solution.py:49
  82.3 5.2 %collective-permute-start.1 = (bf16[1024,1664]{1,0:T(8,128)(2,1)}, bf16[1024,1664]{1,0:T(8,128)(2,1)}, u32[]{:S(2)}, u32[]{:S(2)}) collective-permute-start(bf16[1024,1664]{1,0:T(8,128)(2,1)} %all-gather.6.cloned.1.call-done), channel_id=1, source_target_pairs={{8,0},{16,8},{24,16},{32,24},{40,32},{48,40},{56,48},{64,56},{72,6... | collective-permute-start | bytes 10223624 | tf_op jit(solution)/shard_map/ppermute | solution.py:16
  87.5 1.9 collective-permute-start
  89.4 0.7 compare_and_fusion.2
  90.1 0.8 pad_add_fusion
  90.9 36.6 %collective-permute-done.3 = bf16[1024,1664]{0,1:T(8,128)(2,1)S(1)} collective-permute-done((bf16[1024,1664]{0,1:T(8,128)(2,1)}, bf16[1024,1664]{0,1:T(8,128)(2,1)S(1)}, u32[]{:S(2)}, u32[]{:S(2)}) %collective-permute-start.3) | collective-permute-done | bytes 3407904 | tf_op jit(solution)/shard_map/ppermute | solution.py:16
  127.6 6.5 %collective-permute-done.2 = bf16[1024,1664]{0,1:T(8,128)(2,1)} collective-permute-done((bf16[1024,1664]{0,1:T(8,128)(2,1)}, bf16[1024,1664]{0,1:T(8,128)(2,1)}, u32[]{:S(2)}, u32[]{:S(2)}) %collective-permute-start.2) | collective-permute-done | bytes 3407904 | tf_op jit(solution)/shard_map/ppermute | solution.py:16
  134.1 7.9 %pad_maximum_fusion.1 = bf16[3072,1664]{0,1:T(8,128)(2,1)} fusion(bf16[1024,1664]{0,1:T(8,128)(2,1)S(1)} %collective-permute-done.3, bf16[1024,1664]{0,1:T(8,128)(2,1)} %all-gather.8.cloned.1.call-done, bf16[1024,1664]{0,1:T(8,128)(2,1)} %collective-permute-done.2), kind=kLoop, calls=%fused_computation.5 | loop fusion | flops 30670848 | bytes 20447232 | tf_op jit(solution)/shard_map/concatenate | solution.py:67
  142.0 17.8 %fusion.22 = (f32[13,128]{1,0:T(8,128)S(1)}, bf16[13,128,3072]{1,2,0:T(8,128)(2,1)}) fusion(pred[128,3072]{0,1:T(8,128)(4,1)} %pad_add_fusion, bf16[3072,13,128]{0,2,1:T(8,128)(2,1)} %bitcast.34, bf16[128,13,128]{0,2,1:T(8,128)(2,1)} %bitcast.36), kind=kOutput, calls=%fused_computation.41 | convolution fusion | flops 1339296768 | bytes 21273088 | tf_op jit(solution)/shard_map/sub | solution.py:28
  159.8 40.1 %collective-permute-done.1 = bf16[1024,1664]{1,0:T(8,128)(2,1)} collective-permute-done((bf16[1024,1664]{1,0:T(8,128)(2,1)}, bf16[1024,1664]{1,0:T(8,128)(2,1)}, u32[]{:S(2)}, u32[]{:S(2)}) %collective-permute-start.1) | collective-permute-done | bytes 3407904 | tf_op jit(solution)/shard_map/ppermute | solution.py:16
  199.9 6.2 %collective-permute-done = bf16[1024,1664]{1,0:T(8,128)(2,1)} collective-permute-done((bf16[1024,1664]{1,0:T(8,128)(2,1)}, bf16[1024,1664]{1,0:T(8,128)(2,1)}, u32[]{:S(2)}, u32[]{:S(2)}) %collective-permute-start) | collective-permute-done | bytes 3407904 | tf_op jit(solution)/shard_map/ppermute | solution.py:16
  206.2 15.7 %pad_maximum_fusion = bf16[3072,1664]{1,0:T(8,128)(2,1)} fusion(bf16[1024,1664]{1,0:T(8,128)(2,1)} %collective-permute-done.1, bf16[1024,1664]{1,0:T(8,128)(2,1)S(1)} %copy-done, bf16[1024,1664]{1,0:T(8,128)(2,1)} %collective-permute-done), kind=kLoop, calls=%fused_computation.4 | loop fusion | flops 30670848 | bytes 20447232 | tf_op jit(solution)/shard_map/concatenate | solution.py:70
  221.9 14.3 %copy.24 = bf16[3072,1664]{0,1:T(8,128)(2,1)} copy(bf16[3072,1664]{1,0:T(8,128)(2,1)} %pad_maximum_fusion) | data formatting | bytes 20447232 | tf_op jit(solution)/shard_map/concatenate | solution.py:70
  236.2 9.6 %fusion.15 = bf16[128,13,128]{0,2,1:T(8,128)(2,1)S(1)} fusion(bf16[3072,13,128]{0,2,1:T(8,128)(2,1)} %bitcast.35, bf16[13,128,3072]{1,2,0:T(8,128)(2,1)} %get-tuple-element.20, f32[128,13]{0,1:T(8,128)S(1)} %maximum_bitcast_fusion), kind=kOutput, calls=%fused_computation.17 | convolution fusion | flops 1309048832 | bytes 20879872 | tf_op jit(solution)/shard_map/hrk,khd->rhd/dot_general | solution.py:31
  245.8 0.4 copy.30
  246.3 1.1 convert_element_type.18
  247.4 2.1 slice.14
  249.7 0.3 convert_reduce_fusion
  249.9 26.3 %all-gather.10.cloned.1.call-done = bf16[256,6656]{1,0:T(8,128)(2,1)} async-done(((bf16[32,6656]{1,0:T(8,128)(2,1)}), bf16[256,6656]{1,0:T(8,128)(2,1)}) %all-gather.10.cloned.1.call-update) | async-done | bytes 3407888 | tf_op jit(solution)/shard_map/all_gather | solution.py:76
  276.2 5.5 %multiply_reduce_fusion = (f32[256]{0:T(256)S(1)}, f32[256]{0:T(256)S(1)}, f32[256,384]{1,0:T(8,128)S(1)}) fusion(bf16[256,6656]{1,0:T(8,128)(2,1)} %all-gather.10.cloned.1.call-done, bf16[6656,384]{1,0:T(8,128)(2,1)} %param.9), kind=kOutput, calls=%fused_computation.22 | convolution fusion | flops 1308917248 | bytes 8914944 | tf_op jit(solution)/shard_map/dot_general | solution.py:75
  281.9 60.9 %all-gather.1 = f32[256,2,32]{2,1,0:T(2,128)S(1)} all-gather(f32[1,2,32]{2,1,0:T(2,128)S(1)} %maximum_bitcast_fusion.1), channel_id=2, replica_groups=mesh['blk'=32,'tp'=8] {'blk','tp'}, dimensions={0}, use_global_device_ids=true | all-gather | bytes 65792 | tf_op jit(solution)/shard_map/all_gather | solution.py:90
  342.8 0.3 slice_reduce_fusion
  343.1 0.5 fusion.20
  343.7 0.8 multiply_convert_fusion
  (12 shorter events, 0.6 us)
Async XLA Ops:
  7.2 40.8 %all-gather.8.cloned.1.call-start = ((), (), s32[]{:S(2)}) async-start(), calls=%async_computation.1 | async-start | bytes 3833856 | tf_op jit(solution)/shard_map/all_gather | solution.py:48
  9.2 73.1 %all-gather.6.cloned.1.call-start = ((), (), s32[]{:S(2)}) async-start(), calls=%async_computation | async-start | bytes 3833856 | tf_op jit(solution)/shard_map/all_gather | solution.py:49
  10.0 266.2 %all-gather.10.cloned.1.call-start = ((), (), s32[]{:S(2)}) async-start(), calls=%async_computation.2 | async-start | bytes 3833856 | tf_op jit(solution)/shard_map/all_gather | solution.py:76
  48.0 79.6 %collective-permute-start.3 = (bf16[1024,1664]{0,1:T(8,128)(2,1)}, bf16[1024,1664]{0,1:T(8,128)(2,1)S(1)}, u32[]{:S(2)}, u32[]{:S(2)}) collective-permute-start(bf16[1024,1664]{0,1:T(8,128)(2,1)} %all-gather.8.cloned.1.call-done), channel_id=1, source_target_pairs={{8,0},{16,8},{24,16},{32,24},{40,32},{48,40},{56,48},{64,56},{72,6... | collective-permute-start | bytes 10223624 | tf_op jit(solution)/shard_map/ppermute | solution.py:16
  53.2 80.9 %collective-permute-start.2 = (bf16[1024,1664]{0,1:T(8,128)(2,1)}, bf16[1024,1664]{0,1:T(8,128)(2,1)}, u32[]{:S(2)}, u32[]{:S(2)}) collective-permute-start(bf16[1024,1664]{0,1:T(8,128)(2,1)} %all-gather.8.cloned.1.call-done), channel_id=1, source_target_pairs={{0,8},{8,16},{16,24},{24,32},{32,40},{40,48},{48,56},{56,64},{64,7... | collective-permute-start | bytes 10223624 | tf_op jit(solution)/shard_map/ppermute | solution.py:16
  82.3 117.7 %collective-permute-start.1 = (bf16[1024,1664]{1,0:T(8,128)(2,1)}, bf16[1024,1664]{1,0:T(8,128)(2,1)}, u32[]{:S(2)}, u32[]{:S(2)}) collective-permute-start(bf16[1024,1664]{1,0:T(8,128)(2,1)} %all-gather.6.cloned.1.call-done), channel_id=1, source_target_pairs={{8,0},{16,8},{24,16},{32,24},{40,32},{48,40},{56,48},{64,56},{72,6... | collective-permute-start | bytes 10223624 | tf_op jit(solution)/shard_map/ppermute | solution.py:16
  87.5 118.7 %collective-permute-start = (bf16[1024,1664]{1,0:T(8,128)(2,1)}, bf16[1024,1664]{1,0:T(8,128)(2,1)}, u32[]{:S(2)}, u32[]{:S(2)}) collective-permute-start(bf16[1024,1664]{1,0:T(8,128)(2,1)} %all-gather.6.cloned.1.call-done), channel_id=1, source_target_pairs={{0,8},{8,16},{16,24},{24,32},{32,40},{40,48},{48,56},{56,64},{64,7... | collective-permute-start | bytes 10223624 | tf_op jit(solution)/shard_map/ppermute | solution.py:16
  142.0 64.1 %copy-start = (bf16[1024,1664]{1,0:T(8,128)(2,1)S(1)}, bf16[1024,1664]{1,0:T(8,128)(2,1)}, u32[]{:S(2)}) copy-start(bf16[1024,1664]{1,0:T(8,128)(2,1)} %all-gather.6.cloned.1.call-done) | copy-start | bytes 10223620
Sparse Core Ops, SparseCore 0:
  9.8 38.1 all-gather.7
  49.8 32.3 all-gather.5
  247.5 28.6 all-gather.9

commit v2 on v1

v2 whole, which is shorter than its diff:
```python
import jax
import jax.numpy as jnp
from jax import lax
from jax.sharding import Mesh
from jax.sharding import PartitionSpec as P

HEAD = 128


masked_score = -1e30
epsilon = 1e-06

ALL = ("blk", "x", "core")


def key_scores(query_heads, key_heads):
    return jnp.einsum(
        "rhd,khd->hrk", query_heads, key_heads, preferred_element_type=jnp.float32
    ) * HEAD ** (-0.5)


def finish(scores, allowed, value_heads):
    scores = jnp.where(allowed[None], scores, masked_score)
    row_top = jnp.max(scores, axis=2, keepdims=True)
    exp_terms = jnp.where(allowed[None], jnp.exp(scores - row_top), 0.0)
    row_total = jnp.maximum(jnp.sum(exp_terms, axis=2), 1.0)
    weights = exp_terms.astype(jnp.bfloat16)
    mixed_out = jnp.einsum("hrk,khd->rhd", weights, value_heads, preferred_element_type=jnp.float32)
    return mixed_out / row_total.T[:, :, None]


def shifted(x, axis, by):
    n = lax.axis_size(axis)
    return lax.ppermute(x, axis, [(i, i + by) for i in range(n) if 0 <= i + by < n])


def cyclic(x, axis, by):
    n = lax.axis_size(axis)
    return lax.ppermute(x, axis, [(i, (i + by) % n) for i in range(n)])


def butterfly(sums, peaks):
    n = 1
    for name in ALL:
        n *= lax.axis_size(name)
    bit = 1
    while bit < n:
        perm = [(i, i ^ bit) for i in range(n)]
        other_sums, other_peaks = lax.ppermute((sums, peaks), ALL, perm)
        sums = sums + other_sums
        peaks = jnp.maximum(peaks, other_peaks)
        bit *= 2
    return sums, peaks


def per_device(queries, keys, values, segment_ids, proj_weight):
    group_count = lax.axis_size("blk")
    chips = lax.axis_size("x")
    cores = lax.axis_size("core")
    b = lax.axis_index("blk")
    xi = lax.axis_index("x")
    c = lax.axis_index("core")
    row_count, width = queries.shape
    heads_count = width // HEAD
    slot_heads = -(-heads_count // cores)
    slot = slot_heads * HEAD
    block_len = segment_ids.shape[0] // group_count
    chunk = row_count * cores
    chip_begin = b * block_len + xi * chunk

    my_col = c * (width - slot)
    sib_col = (1 - c) * (width - slot)

    def cols(a, at):
        return lax.dynamic_slice_in_dim(a, at, slot, axis=1)

    own = jnp.concatenate([cols(queries, my_col), cols(keys, my_col), cols(values, my_col)], axis=1)
    give = jnp.concatenate([cols(queries, sib_col), cols(keys, sib_col), cols(values, sib_col)], axis=1)
    got = cyclic(give, "core", 1)
    first = c == 0
    chip_rows = jnp.concatenate(
        [jnp.where(first, own, got), jnp.where(first, got, own)], axis=0
    )
    q_chip = chip_rows[:, :slot]
    kv_chip = chip_rows[:, slot:]

    kv_block = lax.all_gather(kv_chip, "x", axis=0, tiled=True)
    kv_prev = shifted(kv_chip, "blk", 1)
    kv_next = shifted(kv_chip, "blk", -1)

    padded_segs = jnp.concatenate(
        [jnp.full((block_len,), -2, jnp.int32), segment_ids, jnp.full((block_len,), -2, jnp.int32)]
    )

    def segs_at(begin, length):
        return lax.dynamic_slice_in_dim(padded_segs, begin + block_len, length)

    kv_sets = [kv_block, kv_prev, kv_next]
    seg_sets = [
        segs_at(b * block_len, block_len),
        segs_at((b - 1) * block_len + xi * chunk, chunk),
        segs_at((b + 1) * block_len + xi * chunk, chunk),
    ]
    for s in range(1, chips):
        send = jnp.where(xi >= s, kv_prev, kv_next)
        kv_sets.append(cyclic(send, "x", -s))
        src = xi + s
        begin = jnp.where(
            src < chips,
            (b - 1) * block_len + src * chunk,
            (b + 1) * block_len + (src - chips) * chunk,
        )
        seg_sets.append(segs_at(begin, chunk))

    query_segs = lax.dynamic_slice_in_dim(segment_ids, chip_begin, chunk)
    key_segs = jnp.concatenate(seg_sets)
    all_kv = jnp.concatenate(kv_sets, axis=0)
    key_total = all_kv.shape[0]
    allowed = (query_segs[:, None] == key_segs[None, :]) & (query_segs[:, None] >= 0)
    query_heads = q_chip.reshape(chunk, slot_heads, HEAD)
    key_heads = all_kv[:, :slot].reshape(key_total, slot_heads, HEAD)
    value_heads = all_kv[:, slot:].reshape(key_total, slot_heads, HEAD)
    scores = key_scores(query_heads, key_heads)
    mixed = finish(scores, allowed, value_heads).reshape(chunk, slot).astype(jnp.bfloat16)

    mine = lax.dynamic_slice_in_dim(mixed, c * row_count, row_count)
    theirs = lax.dynamic_slice_in_dim(mixed, (1 - c) * row_count, row_count)
    back = cyclic(theirs, "core", 1)
    overlap = 2 * slot - width
    attended = jnp.where(
        first,
        jnp.concatenate([mine, back[:, overlap:]], axis=1),
        jnp.concatenate([back[:, : width - slot], mine], axis=1),
    )

    merged = attended.reshape(row_count // 4, 4 * width)
    projected = jnp.dot(
        lax.all_gather(merged, ("x", "core"), axis=0, tiled=True),
        proj_weight,
        preferred_element_type=jnp.float32,
    )
    own_begin = b * block_len
    row_segs = lax.dynamic_slice_in_dim(segment_ids, own_begin, block_len)[::4]
    member = row_segs[:, None] == jnp.arange(group_count, dtype=jnp.int32)[None, :]
    squares = jnp.sum(projected * projected, axis=1)
    seg_sums = jnp.sum(jnp.where(member, squares[:, None], 0.0), axis=0)
    row_peak = jnp.max(jnp.where(member, jnp.max(projected, axis=1)[:, None], masked_score), axis=0)
    all_segs = segment_ids[::4]
    all_member = all_segs[:, None] == jnp.arange(group_count, dtype=jnp.int32)[None, :]
    seg_counts = jnp.sum(all_member.astype(jnp.float32), axis=0) * (
        projected.shape[1] * chips * cores
    )
    seg_sums, row_peak = butterfly(seg_sums, row_peak)
    seg_scale = lax.rsqrt(seg_sums / seg_counts + epsilon)
    row_scale = jnp.sum(jnp.where(member, seg_scale[None, :], 0.0), axis=1)
    normed = (projected * row_scale[:, None]).astype(jnp.bfloat16)
    return (normed, row_peak * seg_scale)


def solution(mesh):
    blk, tp = mesh.devices.shape
    cores = 2
    chip_mesh = Mesh(mesh.devices.reshape(blk, tp // cores, cores), ALL)
    rows = P(ALL, None)
    in_specs = (rows, rows, rows, P(), P(None, ("x", "core")))
    out_specs = (P("blk", ("x", "core")), P())
    return jax.shard_map(
        per_device, mesh=chip_mesh, in_specs=in_specs, out_specs=out_specs, check_vma=False
    )
```

time: 355 us -> 266 us (0.75)
  blocking collectives: 60.9 us -> 0 us
  starting transfers between devices: 14.3 us -> 44.2 us
  waiting for transfers between devices: 178 us -> 149 us
  other arithmetic: 28.8 us -> 8.87 us
  matrix products: 32.9 us -> 25.5 us
    all_gather x1 -> x0, blocking collectives: 60.9 us -> none  [per_device(): lax.all_gather(jnp.stack([seg_sums, row_peak]), ('blk', 'tp'), axis=0)]
    ppermute x4 -> x23, starting transfers between devices: 14.2 us -> 44.1 us  [the longest x16 29.4 us: butterfly(): other_sums, other_peaks = lax.ppermute((sums, peaks), ALL, perm)]
    concatenate x3 -> x4, other arithmetic: 24.4 us -> 1.93 us  [the longest x2 1.87 us: per_device(): jnp.concatenate([jnp.where(first, own, got), jnp.where(first, got, own)],...]
    ppermute x4 -> x23, waiting for transfers between devices: 89.5 us -> 73.3 us  [the longest x5 37.4 us: cyclic(): return lax.ppermute(x, axis, [(i, (i + by) % n) for i in range(n)])]
    concatenate x1 -> x2, local copies, waits for them, and re-layouts: 14.3 us -> 1.14 us  [the longest x1 1.07 us: per_device(): all_kv = jnp.concatenate(kv_sets, axis=0)]
    all_gather x3 -> x2, waiting for transfers between devices: 87.9 us -> 75.6 us  [the longest x1 43 us: per_device(): kv_block = lax.all_gather(kv_chip, 'x', axis=0, tiled=True)]
    unnamed x4 -> x23, local copies, waits for them, and re-layouts: 3.96 us -> 11.5 us
    slice x0 -> x2, local copies, waits for them, and re-layouts: none -> 5.74 us  [the longest x1 5.71 us: per_device(): key_heads = all_kv[:, :slot].reshape(key_total, slot_heads, HEAD)]
  transfers between devices with their start and end apart: 7 -> 25, of which waited for: 7 -> 22; matrix products, arithmetic and copies ran while one was open for 9% -> 6% of each run, Pallas kernels for 0% -> 0%
where the time goes in v2:
time: 266 us; the launch traced here: 265 us
  waiting for transfers between devices  149 us (56%)
  starting transfers between devices  44.2 us (17%)
  matrix products  25.5 us (10%)
  local copies, waits for them, and re-layouts  23.4 us (9%)
  between operations  14.4 us (5%)
  other arithmetic  8.87 us (3%)
    all_gather x1, waiting for transfers between devices, per_device(): kv_block = lax.all_gather(kv_chip, 'x', axis=0, tiled=True)  43 us
    ppermute x5, waiting for transfers between devices, cyclic(): return lax.ppermute(x, axis, [(i, (i + by) % n) for i in range(n)])  37.4 us
    ppermute x16, waiting for transfers between devices, butterfly(): other_sums, other_peaks = lax.ppermute((sums, peaks), ALL, perm)  35.9 us
    all_gather x1, waiting for transfers between devices, per_device(): lax.all_gather(merged, ('x', 'core'), axis=0, tiled=True)  32.7 us
    ppermute x16, starting transfers between devices, butterfly(): other_sums, other_peaks = lax.ppermute((sums, peaks), ALL, perm)  29.4 us
    sub x1, matrix products, finish(): exp_terms = jnp.where(allowed[None], jnp.exp(scores - row_top), 0.0)  12.6 us
    unnamed x23, local copies, waits for them, and re-layouts  11.5 us
    ppermute x2, starting transfers between devices, shifted(): lax.ppermute(x, axis, [(i, i + by) for i in range(n) if 0 <= i + by < n])  9.56 us
  transfers between devices with their start and end apart: 25, of which 22 were waited for; matrix products, arithmetic and copies ran while one was open for 6% of the time, Pallas kernels for 0%

profile of v2, /device:TPU:8, one launch (start us, length us, event | category | flops | bytes accessed | tf_op | source)
XLA Modules:
  0.0 265.3 jit_solution(1071546361594159836)
XLA Ops:
  14.0 3.8 %collective-permute-start.1 = (bf16[256,1792]{0,1:T(8,128)(2,1)}, bf16[256,1792]{0,1:T(8,128)(2,1)S(1)}, u32[]{:S(2)}, u32[]{:S(2)}) collective-permute-start(bf16[256,1792]{0,1:T(8,128)(2,1)} %fusion.16), channel_id=1, source_target_pairs={{0,8},{8,16},{16,24},{24,32},{32,40},{40,48},{48,56},{56,64},{64,7... | collective-permute-start | bytes 2752520 | tf_op jit(solution)/shard_map/ppermute | solution.py:34
  18.0 5.7 %collective-permute-start.2 = (bf16[256,1792]{0,1:T(8,128)(2,1)}, bf16[256,1792]{0,1:T(8,128)(2,1)}, u32[]{:S(2)}, u32[]{:S(2)}) collective-permute-start(bf16[256,1792]{0,1:T(8,128)(2,1)} %fusion.16), channel_id=1, source_target_pairs={{8,0},{16,8},{24,16},{32,24},{40,32},{48,40},{56,48},{64,56},{72,6... | collective-permute-start | bytes 2752520 | tf_op jit(solution)/shard_map/ppermute | solution.py:34
  24.0 43.0 %all-gather.3.cloned.1.call-done = bf16[1024,1792]{0,1:T(8,128)(2,1)} async-done(((bf16[256,1792]{0,1:T(8,128)(2,1)}), bf16[1024,1792]{0,1:T(8,128)(2,1)}) %all-gather.3.cloned.1.call-update) | async-done | bytes 3670032 | tf_op jit(solution)/shard_map/all_gather | solution.py:87
  67.0 4.3 %constant_dynamic-update-slice_fusion.5 = bf16[2304,1792]{0,1:T(8,128)(2,1)} fusion(bf16[1024,1792]{0,1:T(8,128)(2,1)} %all-gather.3.cloned.1.call-done), kind=kLoop, calls=%fused_computation.39 | loop fusion | bytes 7340032
  72.4 3.4 %broadcast_select_fusion = (bf16[256,1792]{0,1:T(8,128)(2,1)S(1)}, bf16[256,1792]{0,1:T(8,128)(2,1)}, bf16[256,1792]{0,1:T(8,128)(2,1)}, bf16[2304,1792]{0,1:T(8,128)(2,1)}) fusion(bf16[256,1792]{0,1:T(8,128)(2,1)S(1)} %collective-permute-done.1, bf16[256,1792]{0,1:T(8,128)(2,1)} %collective-permute-done.2, pred[]{:T(512)S(6)} %ge.18, pred[]{:T(512)S(6)} %ge.17, ...), kind=kLoop, calls=%fused_computation.18 | loop fusion | flops 1376256 | bytes 5505027 | tf_op jit(solution)/shard_map/jit(_where)/select_n | solution.py:105
  75.7 2.1 collective-permute-start.3
  77.9 2.7 %collective-permute-start.4 = (bf16[256,1792]{0,1:T(8,128)(2,1)}, bf16[256,1792]{0,1:T(8,128)(2,1)}, u32[]{:S(2)}, u32[]{:S(2)}) collective-permute-start(bf16[256,1792]{0,1:T(8,128)(2,1)} %get-tuple-element.11), channel_id=1, source_target_pairs={{0,4},{2,6},{4,0},{6,2},{1,5},{3,7},{5,1},{7,3},{8,12},{10,14},{12... | collective-permute-start | bytes 2752520 | tf_op jit(solution)/shard_map/ppermute | solution.py:39
  82.7 33.9 %collective-permute-done.3 = bf16[256,1792]{0,1:T(8,128)(2,1)} collective-permute-done((bf16[256,1792]{0,1:T(8,128)(2,1)}, bf16[256,1792]{0,1:T(8,128)(2,1)}, u32[]{:S(2)}, u32[]{:S(2)}) %collective-permute-start.3) | collective-permute-done | bytes 917536 | tf_op jit(solution)/shard_map/ppermute | solution.py:39
  116.5 2.2 constant_dynamic-update-slice_fusion.2
  119.3 2.3 constant_dynamic-update-slice_fusion.1
  122.7 5.7 %fusion.22 = (bf16[2304,896]{0,1:T(8,128)(2,1)}, bf16[2304,896]{0,1:T(8,128)(2,1)}) fusion(bf16[2304,1792]{0,1:T(8,128)(2,1)} %constant_dynamic-update-slice_fusion), kind=kLoop, calls=%fused_computation.63 | loop fusion | bytes 16515072 | tf_op jit(solution)/shard_map/slice | solution.py:121
  128.4 12.6 %fusion.24 = (f32[7,256]{1,0:T(8,128)S(1)}, bf16[7,256,2304]{2,1,0:T(8,128)(2,1)}) fusion(pred[256,2304]{1,0:T(8,128)(4,1)S(1)} %copy-done, bf16[256,7,128]{0,2,1:T(8,128)(2,1)S(1)} %bitcast.22, bf16[2304,7,128]{0,2,1:T(8,128)(2,1)} %bitcast.21), kind=kOutput, calls=%fused_computation.65 | convolution fusion | flops 1081739520 | bytes 13442048 | tf_op jit(solution)/shard_map/sub | solution.py:25
  141.0 7.4 %fusion.13 = bf16[256,7,128]{0,2,1:T(8,128)(2,1)S(1)} fusion(bf16[2304,7,128]{0,2,1:T(8,128)(2,1)} %bitcast.20, bf16[7,256,2304]{2,1,0:T(8,128)(2,1)} %get-tuple-element.27, f32[256,7]{0,1:T(8,128)S(1)} %maximum_bitcast_fusion), kind=kOutput, calls=%fused_computation.14 | convolution fusion | flops 1057423360 | bytes 12852224 | tf_op jit(solution)/shard_map/hrk,khd->rhd/dot_general | solution.py:28
  151.8 32.7 %all-gather.5.cloned.1.call-done = bf16[256,6656]{1,0:T(8,128)(2,1)} async-done(((bf16[32,6656]{1,0:T(8,128)(2,1)}), bf16[256,6656]{1,0:T(8,128)(2,1)}) %all-gather.5.cloned.1.call-update) | async-done | bytes 3407888 | tf_op jit(solution)/shard_map/all_gather | solution.py:138
  184.5 5.5 %fusion.21 = (f32[256]{0:T(256)S(1)}, f32[256]{0:T(256)S(1)}, f32[256,384]{1,0:T(8,128)S(1)}) fusion(bf16[256,6656]{1,0:T(8,128)(2,1)} %all-gather.5.cloned.1.call-done, bf16[6656,384]{1,0:T(8,128)(2,1)} %param.9), kind=kOutput, calls=%fused_computation.62 | convolution fusion | flops 1308917248 | bytes 8914944 | tf_op jit(solution)/shard_map/dot_general | solution.py:137
  191.8 3.1 %collective-permute-done.8 = f32[32]{0:T(128)S(1)} collective-permute-done((f32[32]{0:T(128)S(1)}, f32[32]{0:T(128)S(1)}, u32[]{:S(2)}, u32[]{:S(2)}) %collective-permute-start.8) | collective-permute-done | bytes 160 | tf_op jit(solution)/shard_map/ppermute | solution.py:49
  196.5 3.4 %collective-permute-done.9 = f32[32]{0:T(128)S(1)} collective-permute-done((f32[32]{0:T(128)S(1)}, f32[32]{0:T(128)S(1)}, u32[]{:S(2)}, u32[]{:S(2)}) %collective-permute-start.9) | collective-permute-done | bytes 160 | tf_op jit(solution)/shard_map/ppermute | solution.py:49
  201.5 2.0 collective-permute-done.10
  203.5 2.5 collective-permute-start.11
  206.0 1.9 collective-permute-done.11
  207.9 5.7 %collective-permute-start.12 = (f32[32]{0:T(128)S(1)}, f32[32]{0:T(128)S(1)}, u32[]{:S(2)}, u32[]{:S(2)}) collective-permute-start(f32[32]{0:T(128)S(1)} %add.187), channel_id=1, source_target_pairs={{0,32},{1,33},{2,34},{3,35},{4,36},{5,37},{6,38},{7,39},{8,40},{9,... | collective-permute-start | bytes 392 | tf_op jit(solution)/shard_map/ppermute | solution.py:49
  218.9 2.1 collective-permute-start.14
  221.3 2.7 %collective-permute-done.14 = f32[32]{0:T(128)S(1)} collective-permute-done((f32[32]{0:T(128)S(1)}, f32[32]{0:T(128)S(1)}, u32[]{:S(2)}, u32[]{:S(2)}) %collective-permute-start.14) | collective-permute-done | bytes 160 | tf_op jit(solution)/shard_map/ppermute | solution.py:49
  225.7 3.1 %collective-permute-done.16 = f32[32]{0:T(128)S(1)} collective-permute-done((f32[32]{0:T(128)S(1)}, f32[32]{0:T(128)S(1)}, u32[]{:S(2)}, u32[]{:S(2)}) %collective-permute-start.16) | collective-permute-done | bytes 160 | tf_op jit(solution)/shard_map/ppermute | solution.py:49
  230.5 3.4 %collective-permute-done.17 = f32[32]{0:T(128)S(1)} collective-permute-done((f32[32]{0:T(128)S(1)}, f32[32]{0:T(128)S(1)}, u32[]{:S(2)}, u32[]{:S(2)}) %collective-permute-start.17) | collective-permute-done | bytes 160 | tf_op jit(solution)/shard_map/ppermute | solution.py:49
  235.5 2.0 collective-permute-done.18
  237.5 2.5 collective-permute-start.19
  240.0 1.9 collective-permute-done.19
  241.9 5.7 %collective-permute-start.20 = (f32[32]{0:T(128)S(1)}, f32[32]{0:T(128)S(1)}, u32[]{:S(2)}, u32[]{:S(2)}) collective-permute-start(f32[32]{0:T(128)S(1)} %max.41), channel_id=1, source_target_pairs={{0,32},{1,33},{2,34},{3,35},{4,36},{5,37},{6,38},{7,39},{8,40},{9,... | collective-permute-start | bytes 392 | tf_op jit(solution)/shard_map/ppermute | solution.py:49
  249.9 3.0 %collective-permute-done.21 = f32[32]{0:T(128)S(1)} collective-permute-done((f32[32]{0:T(128)S(1)}, f32[32]{0:T(128)S(1)}, u32[]{:S(2)}, u32[]{:S(2)}) %collective-permute-start.21) | collective-permute-done | bytes 160 | tf_op jit(solution)/shard_map/ppermute | solution.py:49
  252.9 2.1 collective-permute-start.22
  255.8 2.2 collective-permute-done.22
  (88 shorter events, 34.3 us)
Async XLA Ops:
  7.2 59.8 %all-gather.3.cloned.1.call-start = ((), (), s32[]{:S(2)}) async-start(), calls=%async_computation | async-start | bytes 4587520 | tf_op jit(solution)/shard_map/all_gather | solution.py:87
  9.9 4.1 %copy-start.2 = (s32[32768]{0:T(1024)S(1)}, s32[32768]{0:T(1024)}, u32[]{:S(2)}) copy-start(s32[32768]{0:T(1024)} %param.8) | copy-start | bytes 393220
  10.3 2.2 collective-permute-start
  13.9 170.6 %all-gather.5.cloned.1.call-start = ((), (), s32[]{:S(2)}) async-start(), calls=%async_computation.1 | async-start | bytes 3833856 | tf_op jit(solution)/shard_map/all_gather | solution.py:138
  14.0 57.4 %collective-permute-start.1 = (bf16[256,1792]{0,1:T(8,128)(2,1)}, bf16[256,1792]{0,1:T(8,128)(2,1)S(1)}, u32[]{:S(2)}, u32[]{:S(2)}) collective-permute-start(bf16[256,1792]{0,1:T(8,128)(2,1)} %fusion.16), channel_id=1, source_target_pairs={{0,8},{8,16},{16,24},{24,32},{32,40},{40,48},{48,56},{56,64},{64,7... | collective-permute-start | bytes 2752520 | tf_op jit(solution)/shard_map/ppermute | solution.py:34
  18.0 54.3 %collective-permute-start.2 = (bf16[256,1792]{0,1:T(8,128)(2,1)}, bf16[256,1792]{0,1:T(8,128)(2,1)}, u32[]{:S(2)}, u32[]{:S(2)}) collective-permute-start(bf16[256,1792]{0,1:T(8,128)(2,1)} %fusion.16), channel_id=1, source_target_pairs={{8,0},{16,8},{24,16},{32,24},{40,32},{48,40},{56,48},{64,56},{72,6... | collective-permute-start | bytes 2752520 | tf_op jit(solution)/shard_map/ppermute | solution.py:34
  75.7 40.8 %collective-permute-start.3 = (bf16[256,1792]{0,1:T(8,128)(2,1)}, bf16[256,1792]{0,1:T(8,128)(2,1)}, u32[]{:S(2)}, u32[]{:S(2)}) collective-permute-start(bf16[256,1792]{0,1:T(8,128)(2,1)} %get-tuple-element.12), channel_id=1, source_target_pairs={{0,6},{2,0},{4,2},{6,4},{1,7},{3,1},{5,3},{7,5},{8,14},{10,8},{12,... | collective-permute-start | bytes 2752520 | tf_op jit(solution)/shard_map/ppermute | solution.py:39
  77.9 43.7 %collective-permute-start.5 = (bf16[256,1792]{0,1:T(8,128)(2,1)S(1)}, bf16[256,1792]{0,1:T(8,128)(2,1)S(1)}, u32[]{:S(2)}, u32[]{:S(2)}) collective-permute-start(bf16[256,1792]{0,1:T(8,128)(2,1)S(1)} %get-tuple-element.10), channel_id=1, source_target_pairs={{0,2},{2,4},{4,6},{6,0},{1,3},{3,5},{5,7},{7,1},{8,10},{10,12},{12... | collective-permute-start | bytes 2752520 | tf_op jit(solution)/shard_map/ppermute | solution.py:39
  77.9 41.5 %collective-permute-start.4 = (bf16[256,1792]{0,1:T(8,128)(2,1)}, bf16[256,1792]{0,1:T(8,128)(2,1)}, u32[]{:S(2)}, u32[]{:S(2)}) collective-permute-start(bf16[256,1792]{0,1:T(8,128)(2,1)} %get-tuple-element.11), channel_id=1, source_target_pairs={{0,4},{2,6},{4,0},{6,2},{1,5},{3,7},{5,1},{7,3},{8,12},{10,14},{12... | collective-permute-start | bytes 2752520 | tf_op jit(solution)/shard_map/ppermute | solution.py:39
  122.7 5.7 %copy-start = (pred[256,2304]{1,0:T(8,128)(4,1)S(1)}, pred[256,2304]{1,0:T(8,128)(4,1)}, u32[]{:S(2)}) copy-start(pred[256,2304]{1,0:T(8,128)(4,1)} %compare_and_fusion) | copy-start | bytes 1769476
  122.7 5.7 %copy-start.1 = (bf16[256,896]{0,1:T(8,128)(2,1)S(1)}, bf16[256,896]{0,1:T(8,128)(2,1)}, u32[]{:S(2)}) copy-start(bf16[256,896]{0,1:T(8,128)(2,1)} %pad_maximum_fusion.2) | copy-start | bytes 1376260
  148.6 1.8 collective-permute-start.6
  190.1 1.2 collective-permute-start.7
  191.4 3.5 %collective-permute-start.8 = (f32[32]{0:T(128)S(1)}, f32[32]{0:T(128)S(1)}, u32[]{:S(2)}, u32[]{:S(2)}) collective-permute-start(f32[32]{0:T(128)S(1)} %add.183), channel_id=1, source_target_pairs={{0,2},{1,3},{2,0},{3,1},{4,6},{5,7},{6,4},{7,5},{8,10},{9,11},{10,... | collective-permute-start | bytes 392 | tf_op jit(solution)/shard_map/ppermute | solution.py:49
  194.9 5.0 %collective-permute-start.9 = (f32[32]{0:T(128)S(1)}, f32[32]{0:T(128)S(1)}, u32[]{:S(2)}, u32[]{:S(2)}) collective-permute-start(f32[32]{0:T(128)S(1)} %add.184), channel_id=1, source_target_pairs={{0,4},{1,5},{2,6},{3,7},{4,0},{5,1},{6,2},{7,3},{8,12},{9,13},{10,... | collective-permute-start | bytes 392 | tf_op jit(solution)/shard_map/ppermute | solution.py:49
  199.9 3.5 %collective-permute-start.10 = (f32[32]{0:T(128)S(1)}, f32[32]{0:T(128)S(1)}, u32[]{:S(2)}, u32[]{:S(2)}) collective-permute-start(f32[32]{0:T(128)S(1)} %add.185), channel_id=1, source_target_pairs={{0,8},{1,9},{2,10},{3,11},{4,12},{5,13},{6,14},{7,15},{8,0},{9,1},... | collective-permute-start | bytes 392 | tf_op jit(solution)/shard_map/ppermute | solution.py:49
  203.5 4.4 %collective-permute-start.11 = (f32[32]{0:T(128)S(1)}, f32[32]{0:T(128)S(1)}, u32[]{:S(2)}, u32[]{:S(2)}) collective-permute-start(f32[32]{0:T(128)S(1)} %add.186), channel_id=1, source_target_pairs={{0,16},{1,17},{2,18},{3,19},{4,20},{5,21},{6,22},{7,23},{8,24},{9,... | collective-permute-start | bytes 392 | tf_op jit(solution)/shard_map/ppermute | solution.py:49
  207.9 7.4 %collective-permute-start.12 = (f32[32]{0:T(128)S(1)}, f32[32]{0:T(128)S(1)}, u32[]{:S(2)}, u32[]{:S(2)}) collective-permute-start(f32[32]{0:T(128)S(1)} %add.187), channel_id=1, source_target_pairs={{0,32},{1,33},{2,34},{3,35},{4,36},{5,37},{6,38},{7,39},{8,40},{9,... | collective-permute-start | bytes 392 | tf_op jit(solution)/shard_map/ppermute | solution.py:49
  215.4 3.5 %collective-permute-start.13 = (f32[32]{0:T(128)S(1)}, f32[32]{0:T(128)S(1)}, u32[]{:S(2)}, u32[]{:S(2)}) collective-permute-start(f32[32]{0:T(128)S(1)} %add.188), channel_id=1, source_target_pairs={{0,64},{1,65},{2,66},{3,67},{4,68},{5,69},{6,70},{7,71},{8,72},{9,... | collective-permute-start | bytes 392 | tf_op jit(solution)/shard_map/ppermute | solution.py:49
  218.9 5.0 %collective-permute-start.14 = (f32[32]{0:T(128)S(1)}, f32[32]{0:T(128)S(1)}, u32[]{:S(2)}, u32[]{:S(2)}) collective-permute-start(f32[32]{0:T(128)S(1)} %add.189), channel_id=1, source_target_pairs={{0,128},{1,129},{2,130},{3,131},{4,132},{5,133},{6,134},{7,135},{8... | collective-permute-start | bytes 392 | tf_op jit(solution)/shard_map/ppermute | solution.py:49
  224.1 1.2 collective-permute-start.15
  225.3 3.5 %collective-permute-start.16 = (f32[32]{0:T(128)S(1)}, f32[32]{0:T(128)S(1)}, u32[]{:S(2)}, u32[]{:S(2)}) collective-permute-start(f32[32]{0:T(128)S(1)} %max.37), channel_id=1, source_target_pairs={{0,2},{1,3},{2,0},{3,1},{4,6},{5,7},{6,4},{7,5},{8,10},{9,11},{10,... | collective-permute-start | bytes 392 | tf_op jit(solution)/shard_map/ppermute | solution.py:49
  228.9 5.0 %collective-permute-start.17 = (f32[32]{0:T(128)S(1)}, f32[32]{0:T(128)S(1)}, u32[]{:S(2)}, u32[]{:S(2)}) collective-permute-start(f32[32]{0:T(128)S(1)} %max.38), channel_id=1, source_target_pairs={{0,4},{1,5},{2,6},{3,7},{4,0},{5,1},{6,2},{7,3},{8,12},{9,13},{10,... | collective-permute-start | bytes 392 | tf_op jit(solution)/shard_map/ppermute | solution.py:49
  233.9 3.5 %collective-permute-start.18 = (f32[32]{0:T(128)S(1)}, f32[32]{0:T(128)S(1)}, u32[]{:S(2)}, u32[]{:S(2)}) collective-permute-start(f32[32]{0:T(128)S(1)} %max.39), channel_id=1, source_target_pairs={{0,8},{1,9},{2,10},{3,11},{4,12},{5,13},{6,14},{7,15},{8,0},{9,1},... | collective-permute-start | bytes 392 | tf_op jit(solution)/shard_map/ppermute | solution.py:49
  237.5 4.4 %collective-permute-start.19 = (f32[32]{0:T(128)S(1)}, f32[32]{0:T(128)S(1)}, u32[]{:S(2)}, u32[]{:S(2)}) collective-permute-start(f32[32]{0:T(128)S(1)} %max.40), channel_id=1, source_target_pairs={{0,16},{1,17},{2,18},{3,19},{4,20},{5,21},{6,22},{7,23},{8,24},{9,... | collective-permute-start | bytes 392 | tf_op jit(solution)/shard_map/ppermute | solution.py:49
  241.9 7.4 %collective-permute-start.20 = (f32[32]{0:T(128)S(1)}, f32[32]{0:T(128)S(1)}, u32[]{:S(2)}, u32[]{:S(2)}) collective-permute-start(f32[32]{0:T(128)S(1)} %max.41), channel_id=1, source_target_pairs={{0,32},{1,33},{2,34},{3,35},{4,36},{5,37},{6,38},{7,39},{8,40},{9,... | collective-permute-start | bytes 392 | tf_op jit(solution)/shard_map/ppermute | solution.py:49
  249.4 3.5 %collective-permute-start.21 = (f32[32]{0:T(128)S(1)}, f32[32]{0:T(128)S(1)}, u32[]{:S(2)}, u32[]{:S(2)}) collective-permute-start(f32[32]{0:T(128)S(1)} %max.42), channel_id=1, source_target_pairs={{0,64},{1,65},{2,66},{3,67},{4,68},{5,69},{6,70},{7,71},{8,72},{9,... | collective-permute-start | bytes 392 | tf_op jit(solution)/shard_map/ppermute | solution.py:49
  252.9 5.0 %collective-permute-start.22 = (f32[32]{0:T(128)S(1)}, f32[32]{0:T(128)S(1)}, u32[]{:S(2)}, u32[]{:S(2)}) collective-permute-start(f32[32]{0:T(128)S(1)} %max.43), channel_id=1, source_target_pairs={{0,128},{1,129},{2,130},{3,131},{4,132},{5,133},{6,134},{7,135},{8... | collective-permute-start | bytes 392 | tf_op jit(solution)/shard_map/ppermute | solution.py:49
Sparse Core Ops, SparseCore 0:
  14.0 52.9 all-gather.2
  151.7 32.7 all-gather.4

commit v3 on v2

--- a/solution.py
+++ b/solution.py
@@ -46,9 +46,9 @@
     bit = 1
     while bit < n:
         perm = [(i, i ^ bit) for i in range(n)]
-        other_sums, other_peaks = lax.ppermute((sums, peaks), ALL, perm)
-        sums = sums + other_sums
-        peaks = jnp.maximum(peaks, other_peaks)
+        other = lax.ppermute(jnp.stack([sums, peaks]), ALL, perm)
+        sums = sums + other[0]
+        peaks = jnp.maximum(peaks, other[1])
         bit *= 2
     return sums, peaks
 
@@ -101,7 +101,27 @@
         segs_at((b - 1) * block_len + xi * chunk, chunk),
         segs_at((b + 1) * block_len + xi * chunk, chunk),
     ]
-    for s in range(1, chips):
+    half = chips // 2
+    far = lax.dynamic_slice_in_dim(kv_block, ((xi + half) % chips) * chunk, chunk)
+    pairs = []
+    for bb in range(group_count):
+        for xx in range(chips):
+            for cc in range(cores):
+                to = bb + 1 if xx < half else bb - 1
+                if 0 <= to < group_count:
+                    pairs.append(((bb * chips + xx) * cores + cc, (to * chips + xx) * cores + cc))
+    kv_sets.append(lax.ppermute(far, ALL, pairs))
+    seg_sets.append(
+        segs_at(
+            jnp.where(
+                xi < half,
+                (b - 1) * block_len + (xi + half) * chunk,
+                (b + 1) * block_len + (xi - half) * chunk,
+            ),
+            chunk,
+        )
+    )
+    for s in (1, chips - 1):
         send = jnp.where(xi >= s, kv_prev, kv_next)
         kv_sets.append(cyclic(send, "x", -s))
         src = xi + s

time: 266 us -> 217 us (0.82)
  waiting for transfers between devices: 149 us -> 109 us
  starting transfers between devices: 44.2 us -> 32.7 us
    ppermute x5 -> x4, waiting for transfers between devices: 37.4 us -> 10.5 us  [cyclic(): return lax.ppermute(x, axis, [(i, (i + by) % n) for i in range(n)])]
    ppermute x16 -> x9, starting transfers between devices: 29.4 us -> 18.9 us  [the longest x8 15.4 us: butterfly(): other = lax.ppermute(jnp.stack([sums, peaks]), ALL, perm)]
    ppermute x16 -> x9, waiting for transfers between devices: 35.9 us -> 25.6 us  [the longest x8 17.7 us: butterfly(): other = lax.ppermute(jnp.stack([sums, peaks]), ALL, perm)]
  transfers between devices with their start and end apart: 25 -> 17, of which waited for: 22 -> 14; matrix products, arithmetic and copies ran while one was open for 6% -> 9% of each run, Pallas kernels for 0% -> 0%
where the time goes in v3:
time: 217 us; the launch traced here: 216 us
  waiting for transfers between devices  109 us (50%)
  starting transfers between devices  32.7 us (15%)
  local copies, waits for them, and re-layouts  25.7 us (12%)
  matrix products  25.5 us (12%)
  between operations  14.4 us (7%)
  other arithmetic  8.42 us (4%)
    all_gather x1, waiting for transfers between devices, per_device(): kv_block = lax.all_gather(kv_chip, 'x', axis=0, tiled=True)  42.9 us
    all_gather x1, waiting for transfers between devices, per_device(): lax.all_gather(merged, ('x', 'core'), axis=0, tiled=True)  30.5 us
    ppermute x8, waiting for transfers between devices, butterfly(): other = lax.ppermute(jnp.stack([sums, peaks]), ALL, perm)  17.7 us
    ppermute x8, starting transfers between devices, butterfly(): other = lax.ppermute(jnp.stack([sums, peaks]), ALL, perm)  15.4 us
    sub x1, matrix products, finish(): exp_terms = jnp.where(allowed[None], jnp.exp(scores - row_top), 0.0)  12.6 us
    unnamed x23, local copies, waits for them, and re-layouts  11.6 us
    ppermute x4, waiting for transfers between devices, cyclic(): return lax.ppermute(x, axis, [(i, (i + by) % n) for i in range(n)])  10.5 us
    ppermute x2, starting transfers between devices, shifted(): lax.ppermute(x, axis, [(i, i + by) for i in range(n) if 0 <= i + by < n])  9.55 us
  transfers between devices with their start and end apart: 17, of which 14 were waited for; matrix products, arithmetic and copies ran while one was open for 9% of the time, Pallas kernels for 0%

profile of v3, /device:TPU:8, one launch (start us, length us, event | category | flops | bytes accessed | tf_op | source)
XLA Modules:
  0.0 216.1 jit_solution(14549143388012764471)
XLA Ops:
  8.5 1.4 constant_dynamic-slice_fusion.6
  10.9 1.6 collective-permute-done
  14.3 3.8 %collective-permute-start.1 = (bf16[256,1792]{0,1:T(8,128)(2,1)}, bf16[256,1792]{0,1:T(8,128)(2,1)S(1)}, u32[]{:S(2)}, u32[]{:S(2)}) collective-permute-start(bf16[256,1792]{0,1:T(8,128)(2,1)} %fusion.16), channel_id=1, source_target_pairs={{0,8},{8,16},{16,24},{24,32},{32,40},{40,48},{48,56},{56,64},{64,7... | collective-permute-start | bytes 2752520 | tf_op jit(solution)/shard_map/ppermute | solution.py:34
  18.3 5.7 %collective-permute-start.2 = (bf16[256,1792]{0,1:T(8,128)(2,1)}, bf16[256,1792]{0,1:T(8,128)(2,1)}, u32[]{:S(2)}, u32[]{:S(2)}) collective-permute-start(bf16[256,1792]{0,1:T(8,128)(2,1)} %fusion.16), channel_id=1, source_target_pairs={{8,0},{16,8},{24,16},{32,24},{40,32},{48,40},{56,48},{64,56},{72,6... | collective-permute-start | bytes 2752520 | tf_op jit(solution)/shard_map/ppermute | solution.py:34
  24.1 42.9 %all-gather.3.cloned.1.call-done = bf16[1024,1792]{0,1:T(8,128)(2,1)} async-done(((bf16[256,1792]{0,1:T(8,128)(2,1)}), bf16[1024,1792]{0,1:T(8,128)(2,1)}) %all-gather.3.cloned.1.call-update) | async-done | bytes 3670032 | tf_op jit(solution)/shard_map/all_gather | solution.py:87
  67.0 2.2 %constant_dynamic-slice_fusion.2 = bf16[256,1792]{0,1:T(8,128)(2,1)} fusion(bf16[1024,1792]{0,1:T(8,128)(2,1)} %all-gather.3.cloned.1.call-done, s32[]{:T(128)S(6)} %select_n.122), kind=kLoop, calls=%fused_computation.48 | loop fusion | bytes 1835012 | tf_op jit(solution)/shard_map/dynamic_slice | solution.py:105
  69.2 3.5 %collective-permute-start.3 = (bf16[256,1792]{0,1:T(8,128)(2,1)}, bf16[256,1792]{0,1:T(8,128)(2,1)}, u32[]{:S(2)}, u32[]{:S(2)}) collective-permute-start(bf16[256,1792]{0,1:T(8,128)(2,1)} %constant_dynamic-slice_fusion.2), channel_id=1, source_target_pairs={{0,8},{1,9},{2,10},{3,11},{8,16},{9,17},{10,18},{11,19},{12,4},{13... | collective-permute-start | bytes 2752520 | tf_op jit(solution)/shard_map/ppermute | solution.py:113
  72.6 4.3 %constant_dynamic-update-slice_fusion.5 = bf16[2304,1792]{0,1:T(8,128)(2,1)} fusion(bf16[1024,1792]{0,1:T(8,128)(2,1)} %all-gather.3.cloned.1.call-done), kind=kLoop, calls=%fused_computation.38 | loop fusion | bytes 7340032
  78.1 2.8 %broadcast_select_fusion = (bf16[256,1792]{0,1:T(8,128)(2,1)S(1)}, bf16[256,1792]{0,1:T(8,128)(2,1)}, bf16[2304,1792]{0,1:T(8,128)(2,1)}) fusion(bf16[256,1792]{0,1:T(8,128)(2,1)S(1)} %collective-permute-done.1, bf16[256,1792]{0,1:T(8,128)(2,1)} %collective-permute-done.2, pred[]{:T(512)S(6)} %ge.14, pred[]{:T(512)S(6)} %ge.13, ...), kind=kLoop, calls=%fused_computation.18 | loop fusion | flops 917504 | bytes 4587522 | tf_op jit(solution)/shard_map/jit(_where)/select_n | solution.py:125
  81.7 3.0 %collective-permute-start.4 = (bf16[256,1792]{0,1:T(8,128)(2,1)}, bf16[256,1792]{0,1:T(8,128)(2,1)}, u32[]{:S(2)}, u32[]{:S(2)}) collective-permute-start(bf16[256,1792]{0,1:T(8,128)(2,1)} %get-tuple-element.11), channel_id=1, source_target_pairs={{0,6},{2,0},{4,2},{6,4},{1,7},{3,1},{5,3},{7,5},{8,14},{10,8},{12,... | collective-permute-start | bytes 2752520 | tf_op jit(solution)/shard_map/ppermute | solution.py:39
  86.8 7.9 %collective-permute-done.3 = bf16[256,1792]{0,1:T(8,128)(2,1)} collective-permute-done((bf16[256,1792]{0,1:T(8,128)(2,1)}, bf16[256,1792]{0,1:T(8,128)(2,1)}, u32[]{:S(2)}, u32[]{:S(2)}) %collective-permute-start.3) | collective-permute-done | bytes 917536 | tf_op jit(solution)/shard_map/ppermute | solution.py:113
  94.7 2.3 %constant_dynamic-update-slice_fusion.2 = bf16[2304,1792]{0,1:T(8,128)(2,1)} fusion(bf16[2304,1792]{0,1:T(8,128)(2,1)} %get-tuple-element.14, bf16[256,1792]{0,1:T(8,128)(2,1)} %collective-permute-done.3), kind=kLoop, calls=%fused_computation.35 | loop fusion | bytes 1835008
  97.0 7.6 %collective-permute-done.4 = bf16[256,1792]{0,1:T(8,128)(2,1)} collective-permute-done((bf16[256,1792]{0,1:T(8,128)(2,1)}, bf16[256,1792]{0,1:T(8,128)(2,1)}, u32[]{:S(2)}, u32[]{:S(2)}) %collective-permute-start.4) | collective-permute-done | bytes 917536 | tf_op jit(solution)/shard_map/ppermute | solution.py:39
  104.6 2.2 %constant_dynamic-update-slice_fusion.1 = bf16[2304,1792]{0,1:T(8,128)(2,1)} fusion(bf16[2304,1792]{0,1:T(8,128)(2,1)} %constant_dynamic-update-slice_fusion.2, bf16[256,1792]{0,1:T(8,128)(2,1)} %collective-permute-done.4), kind=kLoop, calls=%fused_computation.34 | loop fusion | bytes 1835008
  107.8 5.7 %fusion.23 = (bf16[2304,896]{0,1:T(8,128)(2,1)}, bf16[2304,896]{0,1:T(8,128)(2,1)}) fusion(bf16[2304,1792]{0,1:T(8,128)(2,1)} %constant_dynamic-update-slice_fusion), kind=kLoop, calls=%fused_computation.101 | loop fusion | bytes 16515072 | tf_op jit(solution)/shard_map/slice | solution.py:141
  113.5 12.6 %fusion.25 = (f32[7,256]{1,0:T(8,128)S(1)}, bf16[7,256,2304]{2,1,0:T(8,128)(2,1)}) fusion(pred[256,2304]{1,0:T(8,128)(4,1)S(1)} %copy-done, bf16[256,7,128]{0,2,1:T(8,128)(2,1)S(1)} %bitcast.112, bf16[2304,7,128]{0,2,1:T(8,128)(2,1)} %bitcast.111), kind=kOutput, calls=%fused_computation.103 | convolution fusion | flops 1081739520 | bytes 13442048 | tf_op jit(solution)/shard_map/sub | solution.py:25
  126.1 7.4 %fusion.13 = bf16[256,7,128]{0,2,1:T(8,128)(2,1)S(1)} fusion(bf16[2304,7,128]{0,2,1:T(8,128)(2,1)} %bitcast.110, bf16[7,256,2304]{2,1,0:T(8,128)(2,1)} %get-tuple-element.40, f32[256,7]{0,1:T(8,128)S(1)} %maximum_bitcast_fusion), kind=kOutput, calls=%fused_computation.14 | convolution fusion | flops 1057423360 | bytes 12852224 | tf_op jit(solution)/shard_map/hrk,khd->rhd/dot_general | solution.py:28
  134.2 1.3 collective-permute-done.6
  137.0 30.5 %all-gather.5.cloned.1.call-done = bf16[256,6656]{1,0:T(8,128)(2,1)} async-done(((bf16[32,6656]{1,0:T(8,128)(2,1)}), bf16[256,6656]{1,0:T(8,128)(2,1)}) %all-gather.5.cloned.1.call-update) | async-done | bytes 3407888 | tf_op jit(solution)/shard_map/all_gather | solution.py:158
  167.5 5.5 %multiply_reduce_fusion = (f32[256]{0:T(256)S(1)}, f32[256]{0:T(256)S(1)}, f32[256,384]{1,0:T(8,128)S(1)}) fusion(bf16[256,6656]{1,0:T(8,128)(2,1)} %all-gather.5.cloned.1.call-done, bf16[6656,384]{1,0:T(8,128)(2,1)} %param.9), kind=kOutput, calls=%fused_computation.27 | convolution fusion | flops 1308917248 | bytes 8914944 | tf_op jit(solution)/shard_map/dot_general | solution.py:157
  174.8 3.2 %collective-permute-done.8 = f32[2,32]{1,0:T(2,128)S(1)} collective-permute-done((f32[2,32]{1,0:T(2,128)S(1)}, f32[2,32]{1,0:T(2,128)S(1)}, u32[]{:S(2)}, u32[]{:S(2)}) %collective-permute-start.8) | collective-permute-done | bytes 288 | tf_op jit(solution)/shard_map/ppermute | solution.py:49
  178.0 1.7 collective-permute-start.9
  179.7 3.5 %collective-permute-done.9 = f32[2,32]{1,0:T(2,128)S(1)} collective-permute-done((f32[2,32]{1,0:T(2,128)S(1)}, f32[2,32]{1,0:T(2,128)S(1)}, u32[]{:S(2)}, u32[]{:S(2)}) %collective-permute-start.9) | collective-permute-done | bytes 288 | tf_op jit(solution)/shard_map/ppermute | solution.py:49
  183.2 1.6 collective-permute-start.10
  184.9 2.0 collective-permute-done.10
  186.9 2.6 %collective-permute-start.11 = (f32[2,32]{1,0:T(2,128)S(1)}, f32[2,32]{1,0:T(2,128)S(1)}, u32[]{:S(2)}, u32[]{:S(2)}) collective-permute-start(f32[2,32]{1,0:T(2,128)S(1)} %pad_maximum_fusion.7), channel_id=1, source_target_pairs={{0,16},{1,17},{2,18},{3,19},{4,20},{5,21},{6,22},{7,23},{8,24},{9,... | collective-permute-start | bytes 776 | tf_op jit(solution)/shard_map/ppermute | solution.py:49
  189.5 1.9 collective-permute-done.11
  191.5 5.8 %collective-permute-start.12 = (f32[2,32]{1,0:T(2,128)S(1)}, f32[2,32]{1,0:T(2,128)S(1)}, u32[]{:S(2)}, u32[]{:S(2)}) collective-permute-start(f32[2,32]{1,0:T(2,128)S(1)} %pad_maximum_fusion.8), channel_id=1, source_target_pairs={{0,32},{1,33},{2,34},{3,35},{4,36},{5,37},{6,38},{7,39},{8,40},{9,... | collective-permute-start | bytes 776 | tf_op jit(solution)/shard_map/ppermute | solution.py:49
  197.3 1.7 collective-permute-done.12
  200.9 1.8 collective-permute-done.13
  202.7 2.2 %collective-permute-start.14 = (f32[2,32]{1,0:T(2,128)S(1)}, f32[2,32]{1,0:T(2,128)S(1)}, u32[]{:S(2)}, u32[]{:S(2)}) collective-permute-start(f32[2,32]{1,0:T(2,128)S(1)} %pad_maximum_fusion.10), channel_id=1, source_target_pairs={{0,128},{1,129},{2,130},{3,131},{4,132},{5,133},{6,134},{7,135},{8... | collective-permute-start | bytes 776 | tf_op jit(solution)/shard_map/ppermute | solution.py:49
  205.2 2.7 %collective-permute-done.14 = f32[2,32]{1,0:T(2,128)S(1)} collective-permute-done((f32[2,32]{1,0:T(2,128)S(1)}, f32[2,32]{1,0:T(2,128)S(1)}, u32[]{:S(2)}, u32[]{:S(2)}) %collective-permute-start.14) | collective-permute-done | bytes 288 | tf_op jit(solution)/shard_map/ppermute | solution.py:49
  (74 shorter events, 16.9 us)
Async XLA Ops:
  7.2 59.8 %all-gather.3.cloned.1.call-start = ((), (), s32[]{:S(2)}) async-start(), calls=%async_computation | async-start | bytes 4587520 | tf_op jit(solution)/shard_map/all_gather | solution.py:87
  9.9 4.1 %copy-start.2 = (s32[32768]{0:T(1024)S(1)}, s32[32768]{0:T(1024)}, u32[]{:S(2)}) copy-start(s32[32768]{0:T(1024)} %param.8) | copy-start | bytes 393220
  10.3 2.2 %collective-permute-start = (bf16[128,2688]{0,1:T(8,128)(2,1)S(1)}, bf16[128,2688]{0,1:T(8,128)(2,1)S(1)}, u32[]{:S(2)}, u32[]{:S(2)}) collective-permute-start(bf16[128,2688]{0,1:T(8,128)(2,1)S(1)} %pad_maximum_fusion.1), channel_id=1, source_target_pairs={{0,1},{1,0},{2,3},{3,2},{4,5},{5,4},{6,7},{7,6},{8,9},{9,8},{10,11... | collective-permute-start | bytes 2064392 | tf_op jit(solution)/shard_map/ppermute | solution.py:39
  13.9 153.6 %all-gather.5.cloned.1.call-start = ((), (), s32[]{:S(2)}) async-start(), calls=%async_computation.1 | async-start | bytes 3833856 | tf_op jit(solution)/shard_map/all_gather | solution.py:158
  14.3 62.7 %collective-permute-start.1 = (bf16[256,1792]{0,1:T(8,128)(2,1)}, bf16[256,1792]{0,1:T(8,128)(2,1)S(1)}, u32[]{:S(2)}, u32[]{:S(2)}) collective-permute-start(bf16[256,1792]{0,1:T(8,128)(2,1)} %fusion.16), channel_id=1, source_target_pairs={{0,8},{8,16},{16,24},{24,32},{32,40},{40,48},{48,56},{56,64},{64,7... | collective-permute-start | bytes 2752520 | tf_op jit(solution)/shard_map/ppermute | solution.py:34
  18.3 59.8 %collective-permute-start.2 = (bf16[256,1792]{0,1:T(8,128)(2,1)}, bf16[256,1792]{0,1:T(8,128)(2,1)}, u32[]{:S(2)}, u32[]{:S(2)}) collective-permute-start(bf16[256,1792]{0,1:T(8,128)(2,1)} %fusion.16), channel_id=1, source_target_pairs={{8,0},{16,8},{24,16},{32,24},{40,32},{48,40},{56,48},{64,56},{72,6... | collective-permute-start | bytes 2752520 | tf_op jit(solution)/shard_map/ppermute | solution.py:34
  69.2 25.5 %collective-permute-start.3 = (bf16[256,1792]{0,1:T(8,128)(2,1)}, bf16[256,1792]{0,1:T(8,128)(2,1)}, u32[]{:S(2)}, u32[]{:S(2)}) collective-permute-start(bf16[256,1792]{0,1:T(8,128)(2,1)} %constant_dynamic-slice_fusion.2), channel_id=1, source_target_pairs={{0,8},{1,9},{2,10},{3,11},{8,16},{9,17},{10,18},{11,19},{12,4},{13... | collective-permute-start | bytes 2752520 | tf_op jit(solution)/shard_map/ppermute | solution.py:113
  80.9 25.9 %collective-permute-start.5 = (bf16[256,1792]{0,1:T(8,128)(2,1)S(1)}, bf16[256,1792]{0,1:T(8,128)(2,1)S(1)}, u32[]{:S(2)}, u32[]{:S(2)}) collective-permute-start(bf16[256,1792]{0,1:T(8,128)(2,1)S(1)} %get-tuple-element.10), channel_id=1, source_target_pairs={{0,2},{2,4},{4,6},{6,0},{1,3},{3,5},{5,7},{7,1},{8,10},{10,12},{12... | collective-permute-start | bytes 2752520 | tf_op jit(solution)/shard_map/ppermute | solution.py:39
  81.7 22.8 %collective-permute-start.4 = (bf16[256,1792]{0,1:T(8,128)(2,1)}, bf16[256,1792]{0,1:T(8,128)(2,1)}, u32[]{:S(2)}, u32[]{:S(2)}) collective-permute-start(bf16[256,1792]{0,1:T(8,128)(2,1)} %get-tuple-element.11), channel_id=1, source_target_pairs={{0,6},{2,0},{4,2},{6,4},{1,7},{3,1},{5,3},{7,5},{8,14},{10,8},{12,... | collective-permute-start | bytes 2752520 | tf_op jit(solution)/shard_map/ppermute | solution.py:39
  107.8 5.7 %copy-start = (pred[256,2304]{1,0:T(8,128)(4,1)S(1)}, pred[256,2304]{1,0:T(8,128)(4,1)}, u32[]{:S(2)}) copy-start(pred[256,2304]{1,0:T(8,128)(4,1)} %compare_and_fusion) | copy-start | bytes 1769476
  107.8 5.7 %copy-start.1 = (bf16[256,896]{0,1:T(8,128)(2,1)S(1)}, bf16[256,896]{0,1:T(8,128)(2,1)}, u32[]{:S(2)}) copy-start(bf16[256,896]{0,1:T(8,128)(2,1)} %pad_maximum_fusion.2) | copy-start | bytes 1376260
  133.7 1.8 collective-permute-start.6
  173.1 1.2 collective-permute-start.7
  174.4 3.7 %collective-permute-start.8 = (f32[2,32]{1,0:T(2,128)S(1)}, f32[2,32]{1,0:T(2,128)S(1)}, u32[]{:S(2)}, u32[]{:S(2)}) collective-permute-start(f32[2,32]{1,0:T(2,128)S(1)} %pad_maximum_fusion.4), channel_id=1, source_target_pairs={{0,2},{1,3},{2,0},{3,1},{4,6},{5,7},{6,4},{7,5},{8,10},{9,11},{10,... | collective-permute-start | bytes 776 | tf_op jit(solution)/shard_map/ppermute | solution.py:49
  178.0 5.2 %collective-permute-start.9 = (f32[2,32]{1,0:T(2,128)S(1)}, f32[2,32]{1,0:T(2,128)S(1)}, u32[]{:S(2)}, u32[]{:S(2)}) collective-permute-start(f32[2,32]{1,0:T(2,128)S(1)} %pad_maximum_fusion.5), channel_id=1, source_target_pairs={{0,4},{1,5},{2,6},{3,7},{4,0},{5,1},{6,2},{7,3},{8,12},{9,13},{10,... | collective-permute-start | bytes 776 | tf_op jit(solution)/shard_map/ppermute | solution.py:49
  183.2 3.7 %collective-permute-start.10 = (f32[2,32]{1,0:T(2,128)S(1)}, f32[2,32]{1,0:T(2,128)S(1)}, u32[]{:S(2)}, u32[]{:S(2)}) collective-permute-start(f32[2,32]{1,0:T(2,128)S(1)} %pad_maximum_fusion.6), channel_id=1, source_target_pairs={{0,8},{1,9},{2,10},{3,11},{4,12},{5,13},{6,14},{7,15},{8,0},{9,1},... | collective-permute-start | bytes 776 | tf_op jit(solution)/shard_map/ppermute | solution.py:49
  186.9 4.6 %collective-permute-start.11 = (f32[2,32]{1,0:T(2,128)S(1)}, f32[2,32]{1,0:T(2,128)S(1)}, u32[]{:S(2)}, u32[]{:S(2)}) collective-permute-start(f32[2,32]{1,0:T(2,128)S(1)} %pad_maximum_fusion.7), channel_id=1, source_target_pairs={{0,16},{1,17},{2,18},{3,19},{4,20},{5,21},{6,22},{7,23},{8,24},{9,... | collective-permute-start | bytes 776 | tf_op jit(solution)/shard_map/ppermute | solution.py:49
  191.5 7.6 %collective-permute-start.12 = (f32[2,32]{1,0:T(2,128)S(1)}, f32[2,32]{1,0:T(2,128)S(1)}, u32[]{:S(2)}, u32[]{:S(2)}) collective-permute-start(f32[2,32]{1,0:T(2,128)S(1)} %pad_maximum_fusion.8), channel_id=1, source_target_pairs={{0,32},{1,33},{2,34},{3,35},{4,36},{5,37},{6,38},{7,39},{8,40},{9,... | collective-permute-start | bytes 776 | tf_op jit(solution)/shard_map/ppermute | solution.py:49
  199.0 3.7 %collective-permute-start.13 = (f32[2,32]{1,0:T(2,128)S(1)}, f32[2,32]{1,0:T(2,128)S(1)}, u32[]{:S(2)}, u32[]{:S(2)}) collective-permute-start(f32[2,32]{1,0:T(2,128)S(1)} %pad_maximum_fusion.9), channel_id=1, source_target_pairs={{0,64},{1,65},{2,66},{3,67},{4,68},{5,69},{6,70},{7,71},{8,72},{9,... | collective-permute-start | bytes 776 | tf_op jit(solution)/shard_map/ppermute | solution.py:49
  202.7 5.2 %collective-permute-start.14 = (f32[2,32]{1,0:T(2,128)S(1)}, f32[2,32]{1,0:T(2,128)S(1)}, u32[]{:S(2)}, u32[]{:S(2)}) collective-permute-start(f32[2,32]{1,0:T(2,128)S(1)} %pad_maximum_fusion.10), channel_id=1, source_target_pairs={{0,128},{1,129},{2,130},{3,131},{4,132},{5,133},{6,134},{7,135},{8... | collective-permute-start | bytes 776 | tf_op jit(solution)/shard_map/ppermute | solution.py:49
Sparse Core Ops, SparseCore 0:
  14.0 52.9 all-gather.2
  136.8 30.5 all-gather.4

commit v4 on v3

--- a/solution.py
+++ b/solution.py
@@ -84,7 +84,11 @@
     q_chip = chip_rows[:, :slot]
     kv_chip = chip_rows[:, slot:]
 
-    kv_block = lax.all_gather(kv_chip, "x", axis=0, tiled=True)
+    from_right = cyclic(kv_chip, "x", -1)
+    from_left = cyclic(kv_chip, "x", 1)
+    relay = jnp.concatenate(
+        [cyclic(from_right[: row_count], "x", -1), cyclic(from_left[row_count:], "x", 1)], axis=0
+    )
     kv_prev = shifted(kv_chip, "blk", 1)
     kv_next = shifted(kv_chip, "blk", -1)
 
@@ -95,14 +99,17 @@
     def segs_at(begin, length):
         return lax.dynamic_slice_in_dim(padded_segs, begin + block_len, length)
 
-    kv_sets = [kv_block, kv_prev, kv_next]
+    kv_sets = [kv_chip, from_right, from_left, relay, kv_prev, kv_next]
     seg_sets = [
-        segs_at(b * block_len, block_len),
+        segs_at(b * block_len + xi * chunk, chunk),
+        segs_at(b * block_len + ((xi + 1) % chips) * chunk, chunk),
+        segs_at(b * block_len + ((xi + chips - 1) % chips) * chunk, chunk),
+        segs_at(b * block_len + ((xi + 2) % chips) * chunk, chunk),
         segs_at((b - 1) * block_len + xi * chunk, chunk),
         segs_at((b + 1) * block_len + xi * chunk, chunk),
     ]
     half = chips // 2
-    far = lax.dynamic_slice_in_dim(kv_block, ((xi + half) % chips) * chunk, chunk)
+    far = relay
     pairs = []
     for bb in range(group_count):
         for xx in range(chips):

time: 217 us -> 198 us (0.912)
  waiting for transfers between devices: 109 us -> 78.7 us
  starting transfers between devices: 32.7 us -> 42.8 us
    all_gather x1 -> x0, waiting for transfers between devices: 42.9 us -> none  [per_device(): kv_block = lax.all_gather(kv_chip, 'x', axis=0, tiled=True)]
    ppermute x4 -> x8, waiting for transfers between devices: 10.5 us -> 22.3 us  [cyclic(): return lax.ppermute(x, axis, [(i, (i + by) % n) for i in range(n)])]
    ppermute x4 -> x8, starting transfers between devices: 4.21 us -> 13.9 us  [cyclic(): return lax.ppermute(x, axis, [(i, (i + by) % n) for i in range(n)])]
    dynamic_slice x1 -> x0, local copies, waits for them, and re-layouts: 2.2 us -> none  [per_device(): far = lax.dynamic_slice_in_dim(kv_block, (xi + half) % chips * chunk, chunk)]
    unnamed x23 -> x27, local copies, waits for them, and re-layouts: 11.6 us -> 11.5 us
  transfers between devices with their start and end apart: 17 -> 20, of which waited for: 14 -> 15; matrix products, arithmetic and copies ran while one was open for 9% -> 10% of each run, Pallas kernels for 0% -> 0%
where the time goes in v4:
time: 198 us; the launch traced here: 197 us
  waiting for transfers between devices  78.7 us (40%)
  starting transfers between devices  42.8 us (22%)
  local copies, waits for them, and re-layouts  26.1 us (13%)
  matrix products  25.5 us (13%)
  between operations  14.3 us (7%)
  other arithmetic  10 us (5%)
    all_gather x1, waiting for transfers between devices, per_device(): lax.all_gather(merged, ('x', 'core'), axis=0, tiled=True)  29.7 us
    ppermute x8, waiting for transfers between devices, cyclic(): return lax.ppermute(x, axis, [(i, (i + by) % n) for i in range(n)])  22.3 us
    ppermute x8, waiting for transfers between devices, butterfly(): other = lax.ppermute(jnp.stack([sums, peaks]), ALL, perm)  16.8 us
    ppermute x8, starting transfers between devices, butterfly(): other = lax.ppermute(jnp.stack([sums, peaks]), ALL, perm)  15.4 us
    ppermute x8, starting transfers between devices, cyclic(): return lax.ppermute(x, axis, [(i, (i + by) % n) for i in range(n)])  13.9 us
    sub x1, matrix products, finish(): exp_terms = jnp.where(allowed[None], jnp.exp(scores - row_top), 0.0)  12.6 us
    unnamed x27, local copies, waits for them, and re-layouts  11.5 us
    ppermute x1, waiting for transfers between devices, per_device(): kv_sets.append(lax.ppermute(far, ALL, pairs))  9.78 us
  transfers between devices with their start and end apart: 20, of which 15 were waited for; matrix products, arithmetic and copies ran while one was open for 10% of the time, Pallas kernels for 0%

profile of v4, /device:TPU:8, one launch (start us, length us, event | category | flops | bytes accessed | tf_op | source)
XLA Modules:
  0.0 197.4 jit_solution(2309595650641006350)
XLA Ops:
  12.8 1.5 constant_dynamic-update-slice_fusion.9
  14.2 1.5 collective-permute-start.2
  15.7 1.7 collective-permute-start.1
  18.9 7.6 %collective-permute-start.6 = (bf16[256,1792]{0,1:T(8,128)(2,1)}, bf16[256,1792]{0,1:T(8,128)(2,1)S(1)}, u32[]{:S(2)}, u32[]{:S(2)}) collective-permute-start(bf16[256,1792]{0,1:T(8,128)(2,1)} %get-tuple-element.9), channel_id=1, source_target_pairs={{8,0},{16,8},{24,16},{32,24},{40,32},{48,40},{56,48},{64,56},{72,6... | collective-permute-start | bytes 2752520 | tf_op jit(solution)/shard_map/ppermute | solution.py:34
  26.5 1.9 collective-permute-start.5
  28.5 9.6 %collective-permute-done.2 = bf16[256,1792]{0,1:T(8,128)(2,1)S(1)} collective-permute-done((bf16[256,1792]{0,1:T(8,128)(2,1)}, bf16[256,1792]{0,1:T(8,128)(2,1)S(1)}, u32[]{:S(2)}, u32[]{:S(2)}) %collective-permute-start.2) | collective-permute-done | bytes 917536 | tf_op jit(solution)/shard_map/ppermute | solution.py:39
  38.5 3.0 %collective-permute-start.3 = (bf16[128,1792]{0,1:T(8,128)(2,1)S(1)}, bf16[128,1792]{0,1:T(8,128)(2,1)S(1)}, u32[]{:S(2)}, u32[]{:S(2)}) collective-permute-start(bf16[128,1792]{0,1:T(8,128)(2,1)S(1)} %slice.106), channel_id=1, source_target_pairs={{0,6},{2,0},{4,2},{6,4},{1,7},{3,1},{5,3},{7,5},{8,14},{10,8},{12,... | collective-permute-start | bytes 1376264 | tf_op jit(solution)/shard_map/ppermute | solution.py:39
  43.7 7.4 %collective-permute-done.4 = bf16[128,1792]{0,1:T(8,128)(2,1)S(1)} collective-permute-done((bf16[128,1792]{0,1:T(8,128)(2,1)S(1)}, bf16[128,1792]{0,1:T(8,128)(2,1)S(1)}, u32[]{:S(2)}, u32[]{:S(2)}) %collective-permute-start.4) | collective-permute-done | bytes 458784 | tf_op jit(solution)/shard_map/ppermute | solution.py:39
  52.1 3.8 %collective-permute-start.7 = (bf16[256,1792]{0,1:T(8,128)(2,1)}, bf16[256,1792]{0,1:T(8,128)(2,1)}, u32[]{:S(2)}, u32[]{:S(2)}) collective-permute-start(bf16[256,1792]{0,1:T(8,128)(2,1)} %pad_maximum_fusion), channel_id=1, source_target_pairs={{0,8},{1,9},{2,10},{3,11},{8,16},{9,17},{10,18},{11,19},{12,4},{13... | collective-permute-start | bytes 2752520 | tf_op jit(solution)/shard_map/ppermute | solution.py:120
  60.6 6.5 %collective-permute-start.8 = (bf16[256,1792]{0,1:T(8,128)(2,1)S(1)}, bf16[256,1792]{0,1:T(8,128)(2,1)}, u32[]{:S(2)}, u32[]{:S(2)}) collective-permute-start(bf16[256,1792]{0,1:T(8,128)(2,1)S(1)} %get-tuple-element.13), channel_id=1, source_target_pairs={{0,6},{2,0},{4,2},{6,4},{1,7},{3,1},{5,3},{7,5},{8,14},{10,8},{12,... | collective-permute-start | bytes 2752520 | tf_op jit(solution)/shard_map/ppermute | solution.py:39
  69.2 9.8 %collective-permute-done.7 = bf16[256,1792]{0,1:T(8,128)(2,1)} collective-permute-done((bf16[256,1792]{0,1:T(8,128)(2,1)}, bf16[256,1792]{0,1:T(8,128)(2,1)}, u32[]{:S(2)}, u32[]{:S(2)}) %collective-permute-start.7) | collective-permute-done | bytes 917536 | tf_op jit(solution)/shard_map/ppermute | solution.py:120
  79.0 2.2 %constant_dynamic-update-slice_fusion.2 = bf16[2304,1792]{0,1:T(8,128)(2,1)} fusion(bf16[2304,1792]{0,1:T(8,128)(2,1)} %get-tuple-element.16, bf16[256,1792]{0,1:T(8,128)(2,1)} %collective-permute-done.7), kind=kLoop, calls=%fused_computation.36 | loop fusion | bytes 1835008
  81.2 3.5 %collective-permute-done.8 = bf16[256,1792]{0,1:T(8,128)(2,1)} collective-permute-done((bf16[256,1792]{0,1:T(8,128)(2,1)S(1)}, bf16[256,1792]{0,1:T(8,128)(2,1)}, u32[]{:S(2)}, u32[]{:S(2)}) %collective-permute-start.8) | collective-permute-done | bytes 917536 | tf_op jit(solution)/shard_map/ppermute | solution.py:39
  84.7 2.3 %constant_dynamic-update-slice_fusion.1 = bf16[2304,1792]{0,1:T(8,128)(2,1)} fusion(bf16[2304,1792]{0,1:T(8,128)(2,1)} %constant_dynamic-update-slice_fusion.2, bf16[256,1792]{0,1:T(8,128)(2,1)} %collective-permute-done.8), kind=kLoop, calls=%fused_computation.35 | loop fusion | bytes 1835008
  87.0 2.2 %constant_dynamic-update-slice_fusion = bf16[2304,1792]{0,1:T(8,128)(2,1)} fusion(bf16[2304,1792]{0,1:T(8,128)(2,1)} %constant_dynamic-update-slice_fusion.1, bf16[256,1792]{0,1:T(8,128)(2,1)} %collective-permute-done.9), kind=kLoop, calls=%fused_computation.34 | loop fusion | bytes 1835008 | tf_op jit(solution)/shard_map/concatenate | solution.py:144
  89.2 5.7 %fusion.24 = (bf16[2304,896]{0,1:T(8,128)(2,1)}, bf16[2304,896]{0,1:T(8,128)(2,1)}) fusion(bf16[2304,1792]{0,1:T(8,128)(2,1)} %constant_dynamic-update-slice_fusion), kind=kLoop, calls=%fused_computation.108 | loop fusion | bytes 16515072 | tf_op jit(solution)/shard_map/slice | solution.py:148
  94.9 12.6 %fusion.26 = (f32[7,256]{1,0:T(8,128)S(1)}, bf16[7,256,2304]{2,1,0:T(8,128)(2,1)}) fusion(pred[256,2304]{1,0:T(8,128)(4,1)S(1)} %copy-done, bf16[256,7,128]{0,2,1:T(8,128)(2,1)S(1)} %bitcast.112, bf16[2304,7,128]{0,2,1:T(8,128)(2,1)} %bitcast.111), kind=kOutput, calls=%fused_computation.110 | convolution fusion | flops 1081739520 | bytes 13442048 | tf_op jit(solution)/shard_map/sub | solution.py:25
  107.5 7.4 %fusion.13 = bf16[256,7,128]{0,2,1:T(8,128)(2,1)S(1)} fusion(bf16[2304,7,128]{0,2,1:T(8,128)(2,1)} %bitcast.110, bf16[7,256,2304]{2,1,0:T(8,128)(2,1)} %get-tuple-element.42, f32[256,7]{0,1:T(8,128)S(1)} %maximum_bitcast_fusion), kind=kOutput, calls=%fused_computation.14 | convolution fusion | flops 1057423360 | bytes 12852224 | tf_op jit(solution)/shard_map/hrk,khd->rhd/dot_general | solution.py:28
  119.0 29.7 %all-gather.2.cloned.1.call-done = bf16[256,6656]{1,0:T(8,128)(2,1)} async-done(((bf16[32,6656]{1,0:T(8,128)(2,1)}), bf16[256,6656]{1,0:T(8,128)(2,1)}) %all-gather.2.cloned.1.call-update) | async-done | bytes 3407888 | tf_op jit(solution)/shard_map/all_gather | solution.py:165
  148.7 5.5 %multiply_reduce_fusion = (f32[256]{0:T(256)S(1)}, f32[256]{0:T(256)S(1)}, f32[256,384]{1,0:T(8,128)S(1)}) fusion(bf16[256,6656]{1,0:T(8,128)(2,1)} %all-gather.2.cloned.1.call-done, bf16[6656,384]{1,0:T(8,128)(2,1)} %param.9), kind=kOutput, calls=%fused_computation.28 | convolution fusion | flops 1308917248 | bytes 8914944 | tf_op jit(solution)/shard_map/dot_general | solution.py:164
  156.1 3.2 %collective-permute-done.12 = f32[2,32]{1,0:T(2,128)S(1)} collective-permute-done((f32[2,32]{1,0:T(2,128)S(1)}, f32[2,32]{1,0:T(2,128)S(1)}, u32[]{:S(2)}, u32[]{:S(2)}) %collective-permute-start.12) | collective-permute-done | bytes 288 | tf_op jit(solution)/shard_map/ppermute | solution.py:49
  159.3 1.7 collective-permute-start.13
  161.0 3.5 %collective-permute-done.13 = f32[2,32]{1,0:T(2,128)S(1)} collective-permute-done((f32[2,32]{1,0:T(2,128)S(1)}, f32[2,32]{1,0:T(2,128)S(1)}, u32[]{:S(2)}, u32[]{:S(2)}) %collective-permute-start.13) | collective-permute-done | bytes 288 | tf_op jit(solution)/shard_map/ppermute | solution.py:49
  164.5 1.6 collective-permute-start.14
  166.1 2.0 %collective-permute-done.14 = f32[2,32]{1,0:T(2,128)S(1)} collective-permute-done((f32[2,32]{1,0:T(2,128)S(1)}, f32[2,32]{1,0:T(2,128)S(1)}, u32[]{:S(2)}, u32[]{:S(2)}) %collective-permute-start.14) | collective-permute-done | bytes 288 | tf_op jit(solution)/shard_map/ppermute | solution.py:49
  168.2 2.6 %collective-permute-start.15 = (f32[2,32]{1,0:T(2,128)S(1)}, f32[2,32]{1,0:T(2,128)S(1)}, u32[]{:S(2)}, u32[]{:S(2)}) collective-permute-start(f32[2,32]{1,0:T(2,128)S(1)} %pad_maximum_fusion.8), channel_id=1, source_target_pairs={{0,16},{1,17},{2,18},{3,19},{4,20},{5,21},{6,22},{7,23},{8,24},{9,... | collective-permute-start | bytes 776 | tf_op jit(solution)/shard_map/ppermute | solution.py:49
  170.8 1.9 collective-permute-done.15
  172.7 5.8 %collective-permute-start.16 = (f32[2,32]{1,0:T(2,128)S(1)}, f32[2,32]{1,0:T(2,128)S(1)}, u32[]{:S(2)}, u32[]{:S(2)}) collective-permute-start(f32[2,32]{1,0:T(2,128)S(1)} %pad_maximum_fusion.9), channel_id=1, source_target_pairs={{0,32},{1,33},{2,34},{3,35},{4,36},{5,37},{6,38},{7,39},{8,40},{9,... | collective-permute-start | bytes 776 | tf_op jit(solution)/shard_map/ppermute | solution.py:49
  178.6 1.7 collective-permute-done.16
  180.9 2.1 %slice.102 = s32[8192]{0:T(1024)S(1)} slice(s32[32768]{0:T(1024)} %param.8), slice={[0:32768:4]} | slice | bytes 65536 | tf_op jit(solution)/shard_map/slice | solution.py:175
  184.0 2.2 %collective-permute-start.18 = (f32[2,32]{1,0:T(2,128)S(1)}, f32[2,32]{1,0:T(2,128)S(1)}, u32[]{:S(2)}, u32[]{:S(2)}) collective-permute-start(f32[2,32]{1,0:T(2,128)S(1)} %pad_maximum_fusion.11), channel_id=1, source_target_pairs={{0,128},{1,129},{2,130},{3,131},{4,132},{5,133},{6,134},{7,135},{8... | collective-permute-start | bytes 776 | tf_op jit(solution)/shard_map/ppermute | solution.py:49
  186.4 2.7 %collective-permute-done.18 = f32[2,32]{1,0:T(2,128)S(1)} collective-permute-done((f32[2,32]{1,0:T(2,128)S(1)}, f32[2,32]{1,0:T(2,128)S(1)}, u32[]{:S(2)}, u32[]{:S(2)}) %collective-permute-start.18) | collective-permute-done | bytes 288 | tf_op jit(solution)/shard_map/ppermute | solution.py:49
  (86 shorter events, 26.6 us)
Async XLA Ops:
  7.2 141.6 %all-gather.2.cloned.1.call-start = ((), (), s32[]{:S(2)}) async-start(), calls=%async_computation | async-start | bytes 3833856 | tf_op jit(solution)/shard_map/all_gather | solution.py:165
  10.3 2.2 %collective-permute-start = (bf16[128,2688]{0,1:T(8,128)(2,1)S(1)}, bf16[128,2688]{0,1:T(8,128)(2,1)S(1)}, u32[]{:S(2)}, u32[]{:S(2)}) collective-permute-start(bf16[128,2688]{0,1:T(8,128)(2,1)S(1)} %pad_maximum_fusion.2), channel_id=1, source_target_pairs={{0,1},{1,0},{2,3},{3,2},{4,5},{5,4},{6,7},{7,6},{8,9},{9,8},{10,11... | collective-permute-start | bytes 2064392 | tf_op jit(solution)/shard_map/ppermute | solution.py:39
  14.2 23.8 %collective-permute-start.2 = (bf16[256,1792]{0,1:T(8,128)(2,1)}, bf16[256,1792]{0,1:T(8,128)(2,1)S(1)}, u32[]{:S(2)}, u32[]{:S(2)}) collective-permute-start(bf16[256,1792]{0,1:T(8,128)(2,1)} %get-tuple-element.9), channel_id=1, source_target_pairs={{0,2},{2,4},{4,6},{6,0},{1,3},{3,5},{5,7},{7,1},{8,10},{10,12},{12... | collective-permute-start | bytes 2752520 | tf_op jit(solution)/shard_map/ppermute | solution.py:39
  15.7 22.7 %collective-permute-start.1 = (bf16[256,1792]{0,1:T(8,128)(2,1)}, bf16[256,1792]{0,1:T(8,128)(2,1)S(1)}, u32[]{:S(2)}, u32[]{:S(2)}) collective-permute-start(bf16[256,1792]{0,1:T(8,128)(2,1)} %get-tuple-element.9), channel_id=1, source_target_pairs={{0,6},{2,0},{4,2},{6,4},{1,7},{3,1},{5,3},{7,5},{8,14},{10,8},{12,... | collective-permute-start | bytes 2752520 | tf_op jit(solution)/shard_map/ppermute | solution.py:39
  18.9 39.9 %collective-permute-start.6 = (bf16[256,1792]{0,1:T(8,128)(2,1)}, bf16[256,1792]{0,1:T(8,128)(2,1)S(1)}, u32[]{:S(2)}, u32[]{:S(2)}) collective-permute-start(bf16[256,1792]{0,1:T(8,128)(2,1)} %get-tuple-element.9), channel_id=1, source_target_pairs={{8,0},{16,8},{24,16},{32,24},{40,32},{48,40},{56,48},{64,56},{72,6... | collective-permute-start | bytes 2752520 | tf_op jit(solution)/shard_map/ppermute | solution.py:34
  26.5 31.2 %collective-permute-start.5 = (bf16[256,1792]{0,1:T(8,128)(2,1)}, bf16[256,1792]{0,1:T(8,128)(2,1)S(1)}, u32[]{:S(2)}, u32[]{:S(2)}) collective-permute-start(bf16[256,1792]{0,1:T(8,128)(2,1)} %get-tuple-element.9), channel_id=1, source_target_pairs={{0,8},{8,16},{16,24},{24,32},{32,40},{40,48},{48,56},{56,64},{64,7... | collective-permute-start | bytes 2752520 | tf_op jit(solution)/shard_map/ppermute | solution.py:34
  38.1 13.0 %collective-permute-start.4 = (bf16[128,1792]{0,1:T(8,128)(2,1)S(1)}, bf16[128,1792]{0,1:T(8,128)(2,1)S(1)}, u32[]{:S(2)}, u32[]{:S(2)}) collective-permute-start(bf16[128,1792]{0,1:T(8,128)(2,1)S(1)} %slice.107), channel_id=1, source_target_pairs={{0,2},{2,4},{4,6},{6,0},{1,3},{3,5},{5,7},{7,1},{8,10},{10,12},{12... | collective-permute-start | bytes 1376264 | tf_op jit(solution)/shard_map/ppermute | solution.py:39
  38.5 12.6 %collective-permute-start.3 = (bf16[128,1792]{0,1:T(8,128)(2,1)S(1)}, bf16[128,1792]{0,1:T(8,128)(2,1)S(1)}, u32[]{:S(2)}, u32[]{:S(2)}) collective-permute-start(bf16[128,1792]{0,1:T(8,128)(2,1)S(1)} %slice.106), channel_id=1, source_target_pairs={{0,6},{2,0},{4,2},{6,4},{1,7},{3,1},{5,3},{7,5},{8,14},{10,8},{12,... | collective-permute-start | bytes 1376264 | tf_op jit(solution)/shard_map/ppermute | solution.py:39
  52.1 26.8 %collective-permute-start.7 = (bf16[256,1792]{0,1:T(8,128)(2,1)}, bf16[256,1792]{0,1:T(8,128)(2,1)}, u32[]{:S(2)}, u32[]{:S(2)}) collective-permute-start(bf16[256,1792]{0,1:T(8,128)(2,1)} %pad_maximum_fusion), channel_id=1, source_target_pairs={{0,8},{1,9},{2,10},{3,11},{8,16},{9,17},{10,18},{11,19},{12,4},{13... | collective-permute-start | bytes 2752520 | tf_op jit(solution)/shard_map/ppermute | solution.py:120
  60.2 26.8 %collective-permute-start.9 = (bf16[256,1792]{0,1:T(8,128)(2,1)S(1)}, bf16[256,1792]{0,1:T(8,128)(2,1)}, u32[]{:S(2)}, u32[]{:S(2)}) collective-permute-start(bf16[256,1792]{0,1:T(8,128)(2,1)S(1)} %get-tuple-element.12), channel_id=1, source_target_pairs={{0,2},{2,4},{4,6},{6,0},{1,3},{3,5},{5,7},{7,1},{8,10},{10,12},{12... | collective-permute-start | bytes 2752520 | tf_op jit(solution)/shard_map/ppermute | solution.py:39
  60.6 24.1 %collective-permute-start.8 = (bf16[256,1792]{0,1:T(8,128)(2,1)S(1)}, bf16[256,1792]{0,1:T(8,128)(2,1)}, u32[]{:S(2)}, u32[]{:S(2)}) collective-permute-start(bf16[256,1792]{0,1:T(8,128)(2,1)S(1)} %get-tuple-element.13), channel_id=1, source_target_pairs={{0,6},{2,0},{4,2},{6,4},{1,7},{3,1},{5,3},{7,5},{8,14},{10,8},{12,... | collective-permute-start | bytes 2752520 | tf_op jit(solution)/shard_map/ppermute | solution.py:39
  89.2 5.7 %copy-start = (pred[256,2304]{1,0:T(8,128)(4,1)S(1)}, pred[256,2304]{1,0:T(8,128)(4,1)}, u32[]{:S(2)}) copy-start(pred[256,2304]{1,0:T(8,128)(4,1)} %compare_and_fusion) | copy-start | bytes 1769476
  89.2 5.7 %copy-start.1 = (bf16[256,896]{0,1:T(8,128)(2,1)S(1)}, bf16[256,896]{0,1:T(8,128)(2,1)}, u32[]{:S(2)}) copy-start(bf16[256,896]{0,1:T(8,128)(2,1)} %pad_maximum_fusion.3) | copy-start | bytes 1376260
  115.1 1.8 collective-permute-start.10
  154.4 1.2 collective-permute-start.11
  155.7 3.7 %collective-permute-start.12 = (f32[2,32]{1,0:T(2,128)S(1)}, f32[2,32]{1,0:T(2,128)S(1)}, u32[]{:S(2)}, u32[]{:S(2)}) collective-permute-start(f32[2,32]{1,0:T(2,128)S(1)} %pad_maximum_fusion.5), channel_id=1, source_target_pairs={{0,2},{1,3},{2,0},{3,1},{4,6},{5,7},{6,4},{7,5},{8,10},{9,11},{10,... | collective-permute-start | bytes 776 | tf_op jit(solution)/shard_map/ppermute | solution.py:49
  159.3 5.2 %collective-permute-start.13 = (f32[2,32]{1,0:T(2,128)S(1)}, f32[2,32]{1,0:T(2,128)S(1)}, u32[]{:S(2)}, u32[]{:S(2)}) collective-permute-start(f32[2,32]{1,0:T(2,128)S(1)} %pad_maximum_fusion.6), channel_id=1, source_target_pairs={{0,4},{1,5},{2,6},{3,7},{4,0},{5,1},{6,2},{7,3},{8,12},{9,13},{10,... | collective-permute-start | bytes 776 | tf_op jit(solution)/shard_map/ppermute | solution.py:49
  164.5 3.7 %collective-permute-start.14 = (f32[2,32]{1,0:T(2,128)S(1)}, f32[2,32]{1,0:T(2,128)S(1)}, u32[]{:S(2)}, u32[]{:S(2)}) collective-permute-start(f32[2,32]{1,0:T(2,128)S(1)} %pad_maximum_fusion.7), channel_id=1, source_target_pairs={{0,8},{1,9},{2,10},{3,11},{4,12},{5,13},{6,14},{7,15},{8,0},{9,1},... | collective-permute-start | bytes 776 | tf_op jit(solution)/shard_map/ppermute | solution.py:49
  168.2 4.6 %collective-permute-start.15 = (f32[2,32]{1,0:T(2,128)S(1)}, f32[2,32]{1,0:T(2,128)S(1)}, u32[]{:S(2)}, u32[]{:S(2)}) collective-permute-start(f32[2,32]{1,0:T(2,128)S(1)} %pad_maximum_fusion.8), channel_id=1, source_target_pairs={{0,16},{1,17},{2,18},{3,19},{4,20},{5,21},{6,22},{7,23},{8,24},{9,... | collective-permute-start | bytes 776 | tf_op jit(solution)/shard_map/ppermute | solution.py:49
  172.7 7.6 %collective-permute-start.16 = (f32[2,32]{1,0:T(2,128)S(1)}, f32[2,32]{1,0:T(2,128)S(1)}, u32[]{:S(2)}, u32[]{:S(2)}) collective-permute-start(f32[2,32]{1,0:T(2,128)S(1)} %pad_maximum_fusion.9), channel_id=1, source_target_pairs={{0,32},{1,33},{2,34},{3,35},{4,36},{5,37},{6,38},{7,39},{8,40},{9,... | collective-permute-start | bytes 776 | tf_op jit(solution)/shard_map/ppermute | solution.py:49
  180.3 3.7 %collective-permute-start.17 = (f32[2,32]{1,0:T(2,128)S(1)}, f32[2,32]{1,0:T(2,128)S(1)}, u32[]{:S(2)}, u32[]{:S(2)}) collective-permute-start(f32[2,32]{1,0:T(2,128)S(1)} %pad_maximum_fusion.10), channel_id=1, source_target_pairs={{0,64},{1,65},{2,66},{3,67},{4,68},{5,69},{6,70},{7,71},{8,72},{9,... | collective-permute-start | bytes 776 | tf_op jit(solution)/shard_map/ppermute | solution.py:49
  184.0 5.2 %collective-permute-start.18 = (f32[2,32]{1,0:T(2,128)S(1)}, f32[2,32]{1,0:T(2,128)S(1)}, u32[]{:S(2)}, u32[]{:S(2)}) collective-permute-start(f32[2,32]{1,0:T(2,128)S(1)} %pad_maximum_fusion.11), channel_id=1, source_target_pairs={{0,128},{1,129},{2,130},{3,131},{4,132},{5,133},{6,134},{7,135},{8... | collective-permute-start | bytes 776 | tf_op jit(solution)/shard_map/ppermute | solution.py:49
Sparse Core Ops, SparseCore 0:
  118.2 30.4 all-gather.1

commit v5 on v4

--- a/solution.py
+++ b/solution.py
@@ -161,11 +161,20 @@
     )
 
     merged = attended.reshape(row_count // 4, 4 * width)
-    projected = jnp.dot(
-        lax.all_gather(merged, ("x", "core"), axis=0, tiled=True),
-        proj_weight,
-        preferred_element_type=jnp.float32,
-    )
+    piece = merged.shape[0]
+    m_right = cyclic(merged, "x", -1)
+    m_left = cyclic(merged, "x", 1)
+    m_far = jnp.concatenate(
+        [cyclic(m_right[: piece // 2], "x", -1), cyclic(m_left[piece // 2 :], "x", 1)], axis=0
+    )
+    mine4 = jnp.stack([merged, m_right, m_left, m_far])
+    sib4 = cyclic(mine4, "core", 1)
+    gathered = jnp.zeros((piece * chips * cores, merged.shape[1]), merged.dtype)
+    for k, dx in enumerate((0, 1, chips - 1, 2)):
+        at = (xi + dx) % chips
+        gathered = lax.dynamic_update_slice_in_dim(gathered, mine4[k], (at * cores + c) * piece, 0)
+        gathered = lax.dynamic_update_slice_in_dim(gathered, sib4[k], (at * cores + 1 - c) * piece, 0)
+    projected = jnp.dot(gathered, proj_weight, preferred_element_type=jnp.float32)
     own_begin = b * block_len
     row_segs = lax.dynamic_slice_in_dim(segment_ids, own_begin, block_len)[::4]
     member = row_segs[:, None] == jnp.arange(group_count, dtype=jnp.int32)[None, :]

time: 198 us -> 183 us (0.924)
  between operations: 14.3 us -> 1.13 us
  waiting for transfers between devices: 78.7 us -> 84.9 us
  starting transfers between devices: 42.8 us -> 36.7 us
    all_gather x1 -> x0, waiting for transfers between devices: 29.7 us -> none  [per_device(): lax.all_gather(merged, ('x', 'core'), axis=0, tiled=True)]
    ppermute x8 -> x13, waiting for transfers between devices: 22.3 us -> 45.5 us  [cyclic(): return lax.ppermute(x, axis, [(i, (i + by) % n) for i in range(n)])]
    ppermute x8, waiting for transfers between devices: 16.8 us -> 26.9 us  [butterfly(): other = lax.ppermute(jnp.stack([sums, peaks]), ALL, perm)]
    ppermute x8, starting transfers between devices: 15.4 us -> 6.12 us  [butterfly(): other = lax.ppermute(jnp.stack([sums, peaks]), ALL, perm)]
    ppermute x8 -> x13, starting transfers between devices: 13.9 us -> 17.2 us  [cyclic(): return lax.ppermute(x, axis, [(i, (i + by) % n) for i in range(n)])]
    ppermute x1, waiting for transfers between devices: 9.78 us -> 12.4 us  [per_device(): kv_sets.append(lax.ppermute(far, ALL, pairs))]
    unnamed x27 -> x30, local copies, waits for them, and re-layouts: 11.5 us -> 11.4 us
  transfers between devices with their start and end apart: 20 -> 24, of which waited for: 15 -> 20; matrix products, arithmetic and copies ran while one was open for 10% -> 10% of each run, Pallas kernels for 0% -> 0%
where the time goes in v5:
time: 183 us; the launch traced here: 182 us
  waiting for transfers between devices  84.9 us (46%)
  starting transfers between devices  36.7 us (20%)
  local copies, waits for them, and re-layouts  24.8 us (14%)
  matrix products  24.5 us (13%)
  other arithmetic  9.94 us (5%)
    ppermute x13, waiting for transfers between devices, cyclic(): return lax.ppermute(x, axis, [(i, (i + by) % n) for i in range(n)])  45.5 us
    ppermute x8, waiting for transfers between devices, butterfly(): other = lax.ppermute(jnp.stack([sums, peaks]), ALL, perm)  26.9 us
    ppermute x13, starting transfers between devices, cyclic(): return lax.ppermute(x, axis, [(i, (i + by) % n) for i in range(n)])  17.2 us
    sub x1, matrix products, finish(): exp_terms = jnp.where(allowed[None], jnp.exp(scores - row_top), 0.0)  12.6 us
    ppermute x1, waiting for transfers between devices, per_device(): kv_sets.append(lax.ppermute(far, ALL, pairs))  12.4 us
    unnamed x30, local copies, waits for them, and re-layouts  11.4 us
    ppermute x2, starting transfers between devices, shifted(): lax.ppermute(x, axis, [(i, i + by) for i in range(n) if 0 <= i + by < n])  9.56 us
    dot_general x1, matrix products, finish(): jnp.einsum('hrk,khd->rhd', weights, value_heads, preferred_element_type=j...  7.37 us
  transfers between devices with their start and end apart: 24, of which 20 were waited for; matrix products, arithmetic and copies ran while one was open for 10% of the time, Pallas kernels for 0%

profile of v5, /device:TPU:8, one launch (start us, length us, event | category | flops | bytes accessed | tf_op | source)
XLA Modules:
  0.0 181.9 jit_solution(12844807868516192964)
XLA Ops:
  7.7 2.8 %collective-permute-start.1 = (bf16[256,1792]{0,1:T(8,128)(2,1)}, bf16[256,1792]{0,1:T(8,128)(2,1)S(1)}, u32[]{:S(2)}, u32[]{:S(2)}) collective-permute-start(bf16[256,1792]{0,1:T(8,128)(2,1)} %get-tuple-element.9), channel_id=1, source_target_pairs={{0,6},{2,0},{4,2},{6,4},{1,7},{3,1},{5,3},{7,5},{8,14},{10,8},{12,... | collective-permute-start | bytes 2752520 | tf_op jit(solution)/shard_map/ppermute | solution.py:39
  11.2 3.8 %collective-permute-start.5 = (bf16[256,1792]{0,1:T(8,128)(2,1)}, bf16[256,1792]{0,1:T(8,128)(2,1)S(1)}, u32[]{:S(2)}, u32[]{:S(2)}) collective-permute-start(bf16[256,1792]{0,1:T(8,128)(2,1)} %get-tuple-element.9), channel_id=1, source_target_pairs={{0,8},{8,16},{16,24},{24,32},{32,40},{40,48},{48,56},{56,64},{64,7... | collective-permute-start | bytes 2752520 | tf_op jit(solution)/shard_map/ppermute | solution.py:34
  15.0 5.7 %collective-permute-start.6 = (bf16[256,1792]{0,1:T(8,128)(2,1)}, bf16[256,1792]{0,1:T(8,128)(2,1)S(1)}, u32[]{:S(2)}, u32[]{:S(2)}) collective-permute-start(bf16[256,1792]{0,1:T(8,128)(2,1)} %get-tuple-element.9), channel_id=1, source_target_pairs={{8,0},{16,8},{24,16},{32,24},{40,32},{48,40},{56,48},{64,56},{72,6... | collective-permute-start | bytes 2752520 | tf_op jit(solution)/shard_map/ppermute | solution.py:34
  20.7 9.9 %collective-permute-done.1 = bf16[256,1792]{0,1:T(8,128)(2,1)S(1)} collective-permute-done((bf16[256,1792]{0,1:T(8,128)(2,1)}, bf16[256,1792]{0,1:T(8,128)(2,1)S(1)}, u32[]{:S(2)}, u32[]{:S(2)}) %collective-permute-start.1) | collective-permute-done | bytes 917536 | tf_op jit(solution)/shard_map/ppermute | solution.py:39
  30.7 3.7 %collective-permute-start.3 = (bf16[128,1792]{0,1:T(8,128)(2,1)S(1)}, bf16[128,1792]{0,1:T(8,128)(2,1)S(1)}, u32[]{:S(2)}, u32[]{:S(2)}) collective-permute-start(bf16[128,1792]{0,1:T(8,128)(2,1)S(1)} %slice.130), channel_id=1, source_target_pairs={{0,6},{2,0},{4,2},{6,4},{1,7},{3,1},{5,3},{7,5},{8,14},{10,8},{12,... | collective-permute-start | bytes 1376264 | tf_op jit(solution)/shard_map/ppermute | solution.py:39
  36.6 7.0 %collective-permute-done.3 = bf16[128,1792]{0,1:T(8,128)(2,1)S(1)} collective-permute-done((bf16[128,1792]{0,1:T(8,128)(2,1)S(1)}, bf16[128,1792]{0,1:T(8,128)(2,1)S(1)}, u32[]{:S(2)}, u32[]{:S(2)}) %collective-permute-start.3) | collective-permute-done | bytes 458784 | tf_op jit(solution)/shard_map/ppermute | solution.py:39
  43.6 3.5 %collective-permute-done.4 = bf16[128,1792]{0,1:T(8,128)(2,1)S(1)} collective-permute-done((bf16[128,1792]{0,1:T(8,128)(2,1)S(1)}, bf16[128,1792]{0,1:T(8,128)(2,1)S(1)}, u32[]{:S(2)}, u32[]{:S(2)}) %collective-permute-start.4) | collective-permute-done | bytes 458784 | tf_op jit(solution)/shard_map/ppermute | solution.py:39
  48.2 3.8 %collective-permute-start.7 = (bf16[256,1792]{0,1:T(8,128)(2,1)}, bf16[256,1792]{0,1:T(8,128)(2,1)}, u32[]{:S(2)}, u32[]{:S(2)}) collective-permute-start(bf16[256,1792]{0,1:T(8,128)(2,1)} %pad_maximum_fusion.1), channel_id=1, source_target_pairs={{0,8},{1,9},{2,10},{3,11},{8,16},{9,17},{10,18},{11,19},{12,4},{13... | collective-permute-start | bytes 2752520 | tf_op jit(solution)/shard_map/ppermute | solution.py:120
  56.2 4.0 %collective-permute-start.8 = (bf16[256,1792]{0,1:T(8,128)(2,1)S(1)}, bf16[256,1792]{0,1:T(8,128)(2,1)}, u32[]{:S(2)}, u32[]{:S(2)}) collective-permute-start(bf16[256,1792]{0,1:T(8,128)(2,1)S(1)} %get-tuple-element.13), channel_id=1, source_target_pairs={{0,6},{2,0},{4,2},{6,4},{1,7},{3,1},{5,3},{7,5},{8,14},{10,8},{12,... | collective-permute-start | bytes 2752520 | tf_op jit(solution)/shard_map/ppermute | solution.py:39
  62.3 12.4 %collective-permute-done.7 = bf16[256,1792]{0,1:T(8,128)(2,1)} collective-permute-done((bf16[256,1792]{0,1:T(8,128)(2,1)}, bf16[256,1792]{0,1:T(8,128)(2,1)}, u32[]{:S(2)}, u32[]{:S(2)}) %collective-permute-start.7) | collective-permute-done | bytes 917536 | tf_op jit(solution)/shard_map/ppermute | solution.py:120
  74.8 2.3 %constant_dynamic-update-slice_fusion.2 = bf16[2304,1792]{0,1:T(8,128)(2,1)} fusion(bf16[2304,1792]{0,1:T(8,128)(2,1)} %get-tuple-element.16, bf16[256,1792]{0,1:T(8,128)(2,1)} %collective-permute-done.7), kind=kLoop, calls=%fused_computation.45 | loop fusion | bytes 1835008
  78.1 2.3 %constant_dynamic-update-slice_fusion.1 = bf16[2304,1792]{0,1:T(8,128)(2,1)} fusion(bf16[2304,1792]{0,1:T(8,128)(2,1)} %constant_dynamic-update-slice_fusion.2, bf16[256,1792]{0,1:T(8,128)(2,1)} %collective-permute-done.8), kind=kLoop, calls=%fused_computation.44 | loop fusion | bytes 1835008
  81.6 2.3 %constant_dynamic-update-slice_fusion = bf16[2304,1792]{0,1:T(8,128)(2,1)} fusion(bf16[2304,1792]{0,1:T(8,128)(2,1)} %constant_dynamic-update-slice_fusion.1, bf16[256,1792]{0,1:T(8,128)(2,1)} %collective-permute-done.9), kind=kLoop, calls=%fused_computation.43 | loop fusion | bytes 1835008 | tf_op jit(solution)/shard_map/concatenate | solution.py:144
  83.9 5.7 %fusion.28 = (bf16[2304,896]{0,1:T(8,128)(2,1)}, bf16[2304,896]{0,1:T(8,128)(2,1)}) fusion(bf16[2304,1792]{0,1:T(8,128)(2,1)} %constant_dynamic-update-slice_fusion), kind=kLoop, calls=%fused_computation.123 | loop fusion | bytes 16515072 | tf_op jit(solution)/shard_map/slice | solution.py:148
  89.6 12.6 %fusion.30 = (f32[7,256]{1,0:T(8,128)S(1)}, bf16[7,256,2304]{2,1,0:T(8,128)(2,1)}) fusion(pred[256,2304]{1,0:T(8,128)(4,1)S(1)} %copy-done, bf16[256,7,128]{0,2,1:T(8,128)(2,1)S(1)} %bitcast.134, bf16[2304,7,128]{0,2,1:T(8,128)(2,1)} %bitcast.130), kind=kOutput, calls=%fused_computation.125 | convolution fusion | flops 1081739520 | bytes 13442048 | tf_op jit(solution)/shard_map/sub | solution.py:25
  102.2 7.4 %fusion.13 = bf16[256,7,128]{0,2,1:T(8,128)(2,1)S(1)} fusion(bf16[2304,7,128]{0,2,1:T(8,128)(2,1)} %bitcast.129, bf16[7,256,2304]{2,1,0:T(8,128)(2,1)} %get-tuple-element.42, f32[256,7]{0,1:T(8,128)S(1)} %maximum_bitcast_fusion), kind=kOutput, calls=%fused_computation.15 | convolution fusion | flops 1057423360 | bytes 12852224 | tf_op jit(solution)/shard_map/hrk,khd->rhd/dot_general | solution.py:28
  111.8 2.7 %collective-permute-start.11 = (bf16[32,6656]{1,0:T(8,128)(2,1)S(1)}, bf16[32,6656]{1,0:T(8,128)(2,1)S(1)}, u32[]{:S(2)}, u32[]{:S(2)}) collective-permute-start(bf16[32,6656]{1,0:T(8,128)(2,1)S(1)} %select_n.204), channel_id=1, source_target_pairs={{0,6},{2,0},{4,2},{6,4},{1,7},{3,1},{5,3},{7,5},{8,14},{10,8},{12,... | collective-permute-start | bytes 1277960 | tf_op jit(solution)/shard_map/ppermute | solution.py:39
  114.5 9.4 %collective-permute-done.11 = bf16[32,6656]{1,0:T(8,128)(2,1)S(1)} collective-permute-done((bf16[32,6656]{1,0:T(8,128)(2,1)S(1)}, bf16[32,6656]{1,0:T(8,128)(2,1)S(1)}, u32[]{:S(2)}, u32[]{:S(2)}) %collective-permute-start.11) | collective-permute-done | bytes 426016 | tf_op jit(solution)/shard_map/ppermute | solution.py:39
  123.9 3.8 %collective-permute-start.13 = (bf16[16,6656]{1,0:T(8,128)(2,1)S(1)}, bf16[16,6656]{1,0:T(8,128)(2,1)S(1)}, u32[]{:S(2)}, u32[]{:S(2)}) collective-permute-start(bf16[16,6656]{1,0:T(8,128)(2,1)S(1)} %slice.136), channel_id=1, source_target_pairs={{0,6},{2,0},{4,2},{6,4},{1,7},{3,1},{5,3},{7,5},{8,14},{10,8},{12,... | collective-permute-start | bytes 638984 | tf_op jit(solution)/shard_map/ppermute | solution.py:39
  128.1 3.6 %collective-permute-done.13 = bf16[16,6656]{1,0:T(8,128)(2,1)S(1)} collective-permute-done((bf16[16,6656]{1,0:T(8,128)(2,1)S(1)}, bf16[16,6656]{1,0:T(8,128)(2,1)S(1)}, u32[]{:S(2)}, u32[]{:S(2)}) %collective-permute-start.13) | collective-permute-done | bytes 213024 | tf_op jit(solution)/shard_map/ppermute | solution.py:39
  131.6 3.8 %collective-permute-done.14 = bf16[16,6656]{1,0:T(8,128)(2,1)S(1)} collective-permute-done((bf16[16,6656]{1,0:T(8,128)(2,1)S(1)}, bf16[16,6656]{1,0:T(8,128)(2,1)S(1)}, u32[]{:S(2)}, u32[]{:S(2)}) %collective-permute-start.14) | collective-permute-done | bytes 213024 | tf_op jit(solution)/shard_map/ppermute | solution.py:39
  137.5 3.3 %collective-permute-done.15 = bf16[4,32,6656]{2,1,0:T(8,128)(2,1)S(1)} collective-permute-done((bf16[4,32,6656]{2,1,0:T(8,128)(2,1)}, bf16[4,32,6656]{2,1,0:T(8,128)(2,1)S(1)}, u32[]{:S(2)}, u32[]{:S(2)}) %collective-permute-start.15) | collective-permute-done | bytes 1703968 | tf_op jit(solution)/shard_map/ppermute | solution.py:39
  141.0 4.6 %multiply_reduce_fusion = (f32[256]{0:T(256)S(1)}, f32[256]{0:T(256)S(1)}, f32[256,384]{1,0:T(8,128)S(1)}) fusion(bf16[256,6656]{1,0:T(8,128)(2,1)S(1)} %fusion.17, bf16[6656,384]{1,0:T(8,128)(2,1)} %param.9), kind=kOutput, calls=%fused_computation.37 | convolution fusion | flops 1308917248 | bytes 8914944 | tf_op jit(solution)/shard_map/dot_general | solution.py:177
  147.1 3.6 %collective-permute-done.17 = f32[2,32]{1,0:T(2,128)S(1)} collective-permute-done((f32[2,32]{1,0:T(2,128)S(1)}, f32[2,32]{1,0:T(2,128)S(1)}, u32[]{:S(2)}, u32[]{:S(2)}) %collective-permute-start.17) | collective-permute-done | bytes 288 | tf_op jit(solution)/shard_map/ppermute | solution.py:49
  150.8 5.1 %collective-permute-done.18 = f32[2,32]{1,0:T(2,128)S(1)} collective-permute-done((f32[2,32]{1,0:T(2,128)S(1)}, f32[2,32]{1,0:T(2,128)S(1)}, u32[]{:S(2)}, u32[]{:S(2)}) %collective-permute-start.18) | collective-permute-done | bytes 288 | tf_op jit(solution)/shard_map/ppermute | solution.py:49
  156.0 3.6 %collective-permute-done.19 = f32[2,32]{1,0:T(2,128)S(1)} collective-permute-done((f32[2,32]{1,0:T(2,128)S(1)}, f32[2,32]{1,0:T(2,128)S(1)}, u32[]{:S(2)}, u32[]{:S(2)}) %collective-permute-start.19) | collective-permute-done | bytes 288 | tf_op jit(solution)/shard_map/ppermute | solution.py:49
  160.0 4.1 %collective-permute-done.20 = f32[2,32]{1,0:T(2,128)S(1)} collective-permute-done((f32[2,32]{1,0:T(2,128)S(1)}, f32[2,32]{1,0:T(2,128)S(1)}, u32[]{:S(2)}, u32[]{:S(2)}) %collective-permute-start.20) | collective-permute-done | bytes 288 | tf_op jit(solution)/shard_map/ppermute | solution.py:49
  164.1 2.4 %collective-permute-start.21 = (f32[2,32]{1,0:T(2,128)S(1)}, f32[2,32]{1,0:T(2,128)S(1)}, u32[]{:S(2)}, u32[]{:S(2)}) collective-permute-start(f32[2,32]{1,0:T(2,128)S(1)} %pad_maximum_fusion.10), channel_id=1, source_target_pairs={{0,32},{1,33},{2,34},{3,35},{4,36},{5,37},{6,38},{7,39},{8,40},{9,... | collective-permute-start | bytes 776 | tf_op jit(solution)/shard_map/ppermute | solution.py:49
  166.5 5.2 %collective-permute-done.21 = f32[2,32]{1,0:T(2,128)S(1)} collective-permute-done((f32[2,32]{1,0:T(2,128)S(1)}, f32[2,32]{1,0:T(2,128)S(1)}, u32[]{:S(2)}, u32[]{:S(2)}) %collective-permute-start.21) | collective-permute-done | bytes 288 | tf_op jit(solution)/shard_map/ppermute | solution.py:49
  173.0 2.3 %collective-permute-done.22 = f32[2,32]{1,0:T(2,128)S(1)} collective-permute-done((f32[2,32]{1,0:T(2,128)S(1)}, f32[2,32]{1,0:T(2,128)S(1)}, u32[]{:S(2)}, u32[]{:S(2)}) %collective-permute-start.22) | collective-permute-done | bytes 288 | tf_op jit(solution)/shard_map/ppermute | solution.py:49
  175.3 2.7 %collective-permute-start.23 = (f32[2,32]{1,0:T(2,128)S(1)}, f32[2,32]{1,0:T(2,128)S(1)}, u32[]{:S(2)}, u32[]{:S(2)}) collective-permute-start(f32[2,32]{1,0:T(2,128)S(1)} %pad_maximum_fusion.12), channel_id=1, source_target_pairs={{0,128},{1,129},{2,130},{3,131},{4,132},{5,133},{6,134},{7,135},{8... | collective-permute-start | bytes 776 | tf_op jit(solution)/shard_map/ppermute | solution.py:49
  178.3 2.2 %collective-permute-done.23 = f32[2,32]{1,0:T(2,128)S(1)} collective-permute-done((f32[2,32]{1,0:T(2,128)S(1)}, f32[2,32]{1,0:T(2,128)S(1)}, u32[]{:S(2)}, u32[]{:S(2)}) %collective-permute-start.23) | collective-permute-done | bytes 288 | tf_op jit(solution)/shard_map/ppermute | solution.py:49
  (110 shorter events, 29.6 us)
Async XLA Ops:
  0.6 3.8 %copy-start.2 = (s32[32768]{0:T(1024)S(1)}, s32[32768]{0:T(1024)}, u32[]{:S(2)}) copy-start(s32[32768]{0:T(1024)} %param.8) | copy-start | bytes 393220
  3.7 2.2 %collective-permute-start = (bf16[128,2688]{0,1:T(8,128)(2,1)S(1)}, bf16[128,2688]{0,1:T(8,128)(2,1)S(1)}, u32[]{:S(2)}, u32[]{:S(2)}) collective-permute-start(bf16[128,2688]{0,1:T(8,128)(2,1)S(1)} %pad_maximum_fusion.3), channel_id=1, source_target_pairs={{0,1},{1,0},{2,3},{3,2},{4,5},{5,4},{6,7},{7,6},{8,9},{9,8},{10,11... | collective-permute-start | bytes 2064392 | tf_op jit(solution)/shard_map/ppermute | solution.py:39
  7.7 23.0 %collective-permute-start.1 = (bf16[256,1792]{0,1:T(8,128)(2,1)}, bf16[256,1792]{0,1:T(8,128)(2,1)S(1)}, u32[]{:S(2)}, u32[]{:S(2)}) collective-permute-start(bf16[256,1792]{0,1:T(8,128)(2,1)} %get-tuple-element.9), channel_id=1, source_target_pairs={{0,6},{2,0},{4,2},{6,4},{1,7},{3,1},{5,3},{7,5},{8,14},{10,8},{12,... | collective-permute-start | bytes 2752520 | tf_op jit(solution)/shard_map/ppermute | solution.py:39
  10.4 23.9 %collective-permute-start.2 = (bf16[256,1792]{0,1:T(8,128)(2,1)}, bf16[256,1792]{0,1:T(8,128)(2,1)S(1)}, u32[]{:S(2)}, u32[]{:S(2)}) collective-permute-start(bf16[256,1792]{0,1:T(8,128)(2,1)} %get-tuple-element.9), channel_id=1, source_target_pairs={{0,2},{2,4},{4,6},{6,0},{1,3},{3,5},{5,7},{7,1},{8,10},{10,12},{12... | collective-permute-start | bytes 2752520 | tf_op jit(solution)/shard_map/ppermute | solution.py:39
  11.2 42.5 %collective-permute-start.5 = (bf16[256,1792]{0,1:T(8,128)(2,1)}, bf16[256,1792]{0,1:T(8,128)(2,1)S(1)}, u32[]{:S(2)}, u32[]{:S(2)}) collective-permute-start(bf16[256,1792]{0,1:T(8,128)(2,1)} %get-tuple-element.9), channel_id=1, source_target_pairs={{0,8},{8,16},{16,24},{24,32},{32,40},{40,48},{48,56},{56,64},{64,7... | collective-permute-start | bytes 2752520 | tf_op jit(solution)/shard_map/ppermute | solution.py:34
  15.0 39.8 %collective-permute-start.6 = (bf16[256,1792]{0,1:T(8,128)(2,1)}, bf16[256,1792]{0,1:T(8,128)(2,1)S(1)}, u32[]{:S(2)}, u32[]{:S(2)}) collective-permute-start(bf16[256,1792]{0,1:T(8,128)(2,1)} %get-tuple-element.9), channel_id=1, source_target_pairs={{8,0},{16,8},{24,16},{32,24},{40,32},{48,40},{56,48},{64,56},{72,6... | collective-permute-start | bytes 2752520 | tf_op jit(solution)/shard_map/ppermute | solution.py:34
  30.7 12.9 %collective-permute-start.3 = (bf16[128,1792]{0,1:T(8,128)(2,1)S(1)}, bf16[128,1792]{0,1:T(8,128)(2,1)S(1)}, u32[]{:S(2)}, u32[]{:S(2)}) collective-permute-start(bf16[128,1792]{0,1:T(8,128)(2,1)S(1)} %slice.130), channel_id=1, source_target_pairs={{0,6},{2,0},{4,2},{6,4},{1,7},{3,1},{5,3},{7,5},{8,14},{10,8},{12,... | collective-permute-start | bytes 1376264 | tf_op jit(solution)/shard_map/ppermute | solution.py:39
  34.4 12.7 %collective-permute-start.4 = (bf16[128,1792]{0,1:T(8,128)(2,1)S(1)}, bf16[128,1792]{0,1:T(8,128)(2,1)S(1)}, u32[]{:S(2)}, u32[]{:S(2)}) collective-permute-start(bf16[128,1792]{0,1:T(8,128)(2,1)S(1)} %slice.131), channel_id=1, source_target_pairs={{0,2},{2,4},{4,6},{6,0},{1,3},{3,5},{5,7},{7,1},{8,10},{10,12},{12... | collective-permute-start | bytes 1376264 | tf_op jit(solution)/shard_map/ppermute | solution.py:39
  48.2 26.6 %collective-permute-start.7 = (bf16[256,1792]{0,1:T(8,128)(2,1)}, bf16[256,1792]{0,1:T(8,128)(2,1)}, u32[]{:S(2)}, u32[]{:S(2)}) collective-permute-start(bf16[256,1792]{0,1:T(8,128)(2,1)} %pad_maximum_fusion.1), channel_id=1, source_target_pairs={{0,8},{1,9},{2,10},{3,11},{8,16},{9,17},{10,18},{11,19},{12,4},{13... | collective-permute-start | bytes 2752520 | tf_op jit(solution)/shard_map/ppermute | solution.py:120
  56.2 21.9 %collective-permute-start.8 = (bf16[256,1792]{0,1:T(8,128)(2,1)S(1)}, bf16[256,1792]{0,1:T(8,128)(2,1)}, u32[]{:S(2)}, u32[]{:S(2)}) collective-permute-start(bf16[256,1792]{0,1:T(8,128)(2,1)S(1)} %get-tuple-element.13), channel_id=1, source_target_pairs={{0,6},{2,0},{4,2},{6,4},{1,7},{3,1},{5,3},{7,5},{8,14},{10,8},{12,... | collective-permute-start | bytes 2752520 | tf_op jit(solution)/shard_map/ppermute | solution.py:39
  60.2 21.4 %collective-permute-start.9 = (bf16[256,1792]{0,1:T(8,128)(2,1)S(1)}, bf16[256,1792]{0,1:T(8,128)(2,1)}, u32[]{:S(2)}, u32[]{:S(2)}) collective-permute-start(bf16[256,1792]{0,1:T(8,128)(2,1)S(1)} %get-tuple-element.12), channel_id=1, source_target_pairs={{0,2},{2,4},{4,6},{6,0},{1,3},{3,5},{5,7},{7,1},{8,10},{10,12},{12... | collective-permute-start | bytes 2752520 | tf_op jit(solution)/shard_map/ppermute | solution.py:39
  83.9 5.7 %copy-start = (pred[256,2304]{1,0:T(8,128)(4,1)S(1)}, pred[256,2304]{1,0:T(8,128)(4,1)}, u32[]{:S(2)}) copy-start(pred[256,2304]{1,0:T(8,128)(4,1)} %compare_and_fusion) | copy-start | bytes 1769476
  83.9 5.7 %copy-start.1 = (bf16[256,896]{0,1:T(8,128)(2,1)S(1)}, bf16[256,896]{0,1:T(8,128)(2,1)}, u32[]{:S(2)}) copy-start(bf16[256,896]{0,1:T(8,128)(2,1)} %pad_maximum_fusion.4) | copy-start | bytes 1376260
  109.8 1.6 collective-permute-start.10
  111.8 12.0 %collective-permute-start.11 = (bf16[32,6656]{1,0:T(8,128)(2,1)S(1)}, bf16[32,6656]{1,0:T(8,128)(2,1)S(1)}, u32[]{:S(2)}, u32[]{:S(2)}) collective-permute-start(bf16[32,6656]{1,0:T(8,128)(2,1)S(1)} %select_n.204), channel_id=1, source_target_pairs={{0,6},{2,0},{4,2},{6,4},{1,7},{3,1},{5,3},{7,5},{8,14},{10,8},{12,... | collective-permute-start | bytes 1277960 | tf_op jit(solution)/shard_map/ppermute | solution.py:39
  114.5 13.5 %collective-permute-start.12 = (bf16[32,6656]{1,0:T(8,128)(2,1)S(1)}, bf16[32,6656]{1,0:T(8,128)(2,1)S(1)}, u32[]{:S(2)}, u32[]{:S(2)}) collective-permute-start(bf16[32,6656]{1,0:T(8,128)(2,1)S(1)} %select_n.204), channel_id=1, source_target_pairs={{0,2},{2,4},{4,6},{6,0},{1,3},{3,5},{5,7},{7,1},{8,10},{10,12},{12... | collective-permute-start | bytes 1277960 | tf_op jit(solution)/shard_map/ppermute | solution.py:39
  123.9 7.8 %collective-permute-start.13 = (bf16[16,6656]{1,0:T(8,128)(2,1)S(1)}, bf16[16,6656]{1,0:T(8,128)(2,1)S(1)}, u32[]{:S(2)}, u32[]{:S(2)}) collective-permute-start(bf16[16,6656]{1,0:T(8,128)(2,1)S(1)} %slice.136), channel_id=1, source_target_pairs={{0,6},{2,0},{4,2},{6,4},{1,7},{3,1},{5,3},{7,5},{8,14},{10,8},{12,... | collective-permute-start | bytes 638984 | tf_op jit(solution)/shard_map/ppermute | solution.py:39
  128.0 7.5 %collective-permute-start.14 = (bf16[16,6656]{1,0:T(8,128)(2,1)S(1)}, bf16[16,6656]{1,0:T(8,128)(2,1)S(1)}, u32[]{:S(2)}, u32[]{:S(2)}) collective-permute-start(bf16[16,6656]{1,0:T(8,128)(2,1)S(1)} %slice.137), channel_id=1, source_target_pairs={{0,2},{2,4},{4,6},{6,0},{1,3},{3,5},{5,7},{7,1},{8,10},{10,12},{12... | collective-permute-start | bytes 638984 | tf_op jit(solution)/shard_map/ppermute | solution.py:39
  136.9 3.8 %collective-permute-start.15 = (bf16[4,32,6656]{2,1,0:T(8,128)(2,1)}, bf16[4,32,6656]{2,1,0:T(8,128)(2,1)S(1)}, u32[]{:S(2)}, u32[]{:S(2)}) collective-permute-start(bf16[4,32,6656]{2,1,0:T(8,128)(2,1)} %pad_maximum_fusion), channel_id=1, source_target_pairs={{0,1},{1,0},{2,3},{3,2},{4,5},{5,4},{6,7},{7,6},{8,9},{9,8},{10,11... | collective-permute-start | bytes 5111816 | tf_op jit(solution)/shard_map/ppermute | solution.py:39
  145.8 1.2 collective-permute-start.16
  147.0 3.7 %collective-permute-start.17 = (f32[2,32]{1,0:T(2,128)S(1)}, f32[2,32]{1,0:T(2,128)S(1)}, u32[]{:S(2)}, u32[]{:S(2)}) collective-permute-start(f32[2,32]{1,0:T(2,128)S(1)} %pad_maximum_fusion.6), channel_id=1, source_target_pairs={{0,2},{1,3},{2,0},{3,1},{4,6},{5,7},{6,4},{7,5},{8,10},{9,11},{10,... | collective-permute-start | bytes 776 | tf_op jit(solution)/shard_map/ppermute | solution.py:49
  150.7 5.2 %collective-permute-start.18 = (f32[2,32]{1,0:T(2,128)S(1)}, f32[2,32]{1,0:T(2,128)S(1)}, u32[]{:S(2)}, u32[]{:S(2)}) collective-permute-start(f32[2,32]{1,0:T(2,128)S(1)} %pad_maximum_fusion.7), channel_id=1, source_target_pairs={{0,4},{1,5},{2,6},{3,7},{4,0},{5,1},{6,2},{7,3},{8,12},{9,13},{10,... | collective-permute-start | bytes 776 | tf_op jit(solution)/shard_map/ppermute | solution.py:49
  155.9 3.7 %collective-permute-start.19 = (f32[2,32]{1,0:T(2,128)S(1)}, f32[2,32]{1,0:T(2,128)S(1)}, u32[]{:S(2)}, u32[]{:S(2)}) collective-permute-start(f32[2,32]{1,0:T(2,128)S(1)} %pad_maximum_fusion.8), channel_id=1, source_target_pairs={{0,8},{1,9},{2,10},{3,11},{4,12},{5,13},{6,14},{7,15},{8,0},{9,1},... | collective-permute-start | bytes 776 | tf_op jit(solution)/shard_map/ppermute | solution.py:49
  159.5 4.6 %collective-permute-start.20 = (f32[2,32]{1,0:T(2,128)S(1)}, f32[2,32]{1,0:T(2,128)S(1)}, u32[]{:S(2)}, u32[]{:S(2)}) collective-permute-start(f32[2,32]{1,0:T(2,128)S(1)} %pad_maximum_fusion.9), channel_id=1, source_target_pairs={{0,16},{1,17},{2,18},{3,19},{4,20},{5,21},{6,22},{7,23},{8,24},{9,... | collective-permute-start | bytes 776 | tf_op jit(solution)/shard_map/ppermute | solution.py:49
  164.1 7.6 %collective-permute-start.21 = (f32[2,32]{1,0:T(2,128)S(1)}, f32[2,32]{1,0:T(2,128)S(1)}, u32[]{:S(2)}, u32[]{:S(2)}) collective-permute-start(f32[2,32]{1,0:T(2,128)S(1)} %pad_maximum_fusion.10), channel_id=1, source_target_pairs={{0,32},{1,33},{2,34},{3,35},{4,36},{5,37},{6,38},{7,39},{8,40},{9,... | collective-permute-start | bytes 776 | tf_op jit(solution)/shard_map/ppermute | solution.py:49
  171.7 3.7 %collective-permute-start.22 = (f32[2,32]{1,0:T(2,128)S(1)}, f32[2,32]{1,0:T(2,128)S(1)}, u32[]{:S(2)}, u32[]{:S(2)}) collective-permute-start(f32[2,32]{1,0:T(2,128)S(1)} %pad_maximum_fusion.11), channel_id=1, source_target_pairs={{0,64},{1,65},{2,66},{3,67},{4,68},{5,69},{6,70},{7,71},{8,72},{9,... | collective-permute-start | bytes 776 | tf_op jit(solution)/shard_map/ppermute | solution.py:49
  175.3 5.2 %collective-permute-start.23 = (f32[2,32]{1,0:T(2,128)S(1)}, f32[2,32]{1,0:T(2,128)S(1)}, u32[]{:S(2)}, u32[]{:S(2)}) collective-permute-start(f32[2,32]{1,0:T(2,128)S(1)} %pad_maximum_fusion.12), channel_id=1, source_target_pairs={{0,128},{1,129},{2,130},{3,131},{4,132},{5,133},{6,134},{7,135},{8... | collective-permute-start | bytes 776 | tf_op jit(solution)/shard_map/ppermute | solution.py:49

commit v6 on v5

--- a/solution.py
+++ b/solution.py
@@ -86,9 +86,9 @@
 
     from_right = cyclic(kv_chip, "x", -1)
     from_left = cyclic(kv_chip, "x", 1)
-    relay = jnp.concatenate(
-        [cyclic(from_right[: row_count], "x", -1), cyclic(from_left[row_count:], "x", 1)], axis=0
-    )
+    relay_a = cyclic(from_right[:row_count], "x", -1)
+    relay_b = cyclic(from_left[row_count:], "x", 1)
+    relay = jnp.concatenate([relay_a, relay_b], axis=0)
     kv_prev = shifted(kv_chip, "blk", 1)
     kv_next = shifted(kv_chip, "blk", -1)
 
@@ -109,7 +109,6 @@
         segs_at((b + 1) * block_len + xi * chunk, chunk),
     ]
     half = chips // 2
-    far = relay
     pairs = []
     for bb in range(group_count):
         for xx in range(chips):
@@ -117,7 +116,9 @@
                 to = bb + 1 if xx < half else bb - 1
                 if 0 <= to < group_count:
                     pairs.append(((bb * chips + xx) * cores + cc, (to * chips + xx) * cores + cc))
-    kv_sets.append(lax.ppermute(far, ALL, pairs))
+    kv_sets.append(
+        jnp.concatenate([lax.ppermute(relay_a, ALL, pairs), lax.ppermute(relay_b, ALL, pairs)], axis=0)
+    )
     seg_sets.append(
         segs_at(
             jnp.where(

time: 183 us -> 185 us (1.011)
  waiting for transfers between devices: 84.9 us -> 80.8 us
  starting transfers between devices: 36.7 us -> 40.7 us
  local copies, waits for them, and re-layouts: 24.8 us -> 28.2 us
    ppermute x1 -> x2, starting transfers between devices: 3.81 us -> 7.82 us  [the longest x1 4.01 us: per_device(): lax.ppermute(relay_b, ALL, pairs)]
    ppermute x13, waiting for transfers between devices: 45.5 us -> 41.6 us  [cyclic(): return lax.ppermute(x, axis, [(i, (i + by) % n) for i in range(n)])]
    unnamed x30 -> x31, local copies, waits for them, and re-layouts: 11.4 us -> 15 us
    ppermute x13, starting transfers between devices: 17.2 us -> 14.6 us  [cyclic(): return lax.ppermute(x, axis, [(i, (i + by) % n) for i in range(n)])]
    ppermute x8, waiting for transfers between devices: 26.9 us -> 24.4 us  [butterfly(): other = lax.ppermute(jnp.stack([sums, peaks]), ALL, perm)]
    ppermute x8, starting transfers between devices: 6.12 us -> 8.68 us  [butterfly(): other = lax.ppermute(jnp.stack([sums, peaks]), ALL, perm)]
    ppermute x1 -> x2, waiting for transfers between devices: 12.4 us -> 14.8 us  [the longest x1 9.44 us: per_device(): lax.ppermute(relay_a, ALL, pairs)]
  transfers between devices with their start and end apart: 24 -> 25, of which waited for: 20 -> 19; matrix products, arithmetic and copies ran while one was open for 10% -> 10% of each run, Pallas kernels for 0% -> 0%
where the time goes in v6:
time: 185 us; the launch traced here: 184 us
  waiting for transfers between devices  80.8 us (44%)
  starting transfers between devices  40.7 us (22%)
  local copies, waits for them, and re-layouts  28.2 us (15%)
  matrix products  24.5 us (13%)
  other arithmetic  8.9 us (5%)
    ppermute x13, waiting for transfers between devices, cyclic(): return lax.ppermute(x, axis, [(i, (i + by) % n) for i in range(n)])  41.6 us
    ppermute x8, waiting for transfers between devices, butterfly(): other = lax.ppermute(jnp.stack([sums, peaks]), ALL, perm)  24.4 us
    unnamed x31, local copies, waits for them, and re-layouts  15 us
    ppermute x13, starting transfers between devices, cyclic(): return lax.ppermute(x, axis, [(i, (i + by) % n) for i in range(n)])  14.6 us
    sub x1, matrix products, finish(): exp_terms = jnp.where(allowed[None], jnp.exp(scores - row_top), 0.0)  12.6 us
    ppermute x2, starting transfers between devices, shifted(): lax.ppermute(x, axis, [(i, i + by) for i in range(n) if 0 <= i + by < n])  9.56 us
    ppermute x1, waiting for transfers between devices, per_device(): lax.ppermute(relay_a, ALL, pairs)  9.44 us
    ppermute x8, starting transfers between devices, butterfly(): other = lax.ppermute(jnp.stack([sums, peaks]), ALL, perm)  8.68 us
  transfers between devices with their start and end apart: 25, of which 19 were waited for; matrix products, arithmetic and copies ran while one was open for 10% of the time, Pallas kernels for 0%

profile of v6, /device:TPU:8, one launch (start us, length us, event | category | flops | bytes accessed | tf_op | source)
XLA Modules:
  0.0 184.3 jit_solution(4555634366502655471)
XLA Ops:
  7.8 2.8 %collective-permute-start.1 = (bf16[256,1792]{0,1:T(8,128)(2,1)}, bf16[256,1792]{0,1:T(8,128)(2,1)S(1)}, u32[]{:S(2)}, u32[]{:S(2)}) collective-permute-start(bf16[256,1792]{0,1:T(8,128)(2,1)} %get-tuple-element.9), channel_id=1, source_target_pairs={{0,6},{2,0},{4,2},{6,4},{1,7},{3,1},{5,3},{7,5},{8,14},{10,8},{12,... | collective-permute-start | bytes 2752520 | tf_op jit(solution)/shard_map/ppermute | solution.py:39
  11.2 3.8 %collective-permute-start.5 = (bf16[256,1792]{0,1:T(8,128)(2,1)}, bf16[256,1792]{0,1:T(8,128)(2,1)S(1)}, u32[]{:S(2)}, u32[]{:S(2)}) collective-permute-start(bf16[256,1792]{0,1:T(8,128)(2,1)} %get-tuple-element.9), channel_id=1, source_target_pairs={{0,8},{8,16},{16,24},{24,32},{32,40},{40,48},{48,56},{56,64},{64,7... | collective-permute-start | bytes 2752520 | tf_op jit(solution)/shard_map/ppermute | solution.py:34
  15.1 5.7 %collective-permute-start.6 = (bf16[256,1792]{0,1:T(8,128)(2,1)}, bf16[256,1792]{0,1:T(8,128)(2,1)S(1)}, u32[]{:S(2)}, u32[]{:S(2)}) collective-permute-start(bf16[256,1792]{0,1:T(8,128)(2,1)} %get-tuple-element.9), channel_id=1, source_target_pairs={{8,0},{16,8},{24,16},{32,24},{40,32},{48,40},{56,48},{64,56},{72,6... | collective-permute-start | bytes 2752520 | tf_op jit(solution)/shard_map/ppermute | solution.py:34
  20.8 9.9 %collective-permute-done.1 = bf16[256,1792]{0,1:T(8,128)(2,1)S(1)} collective-permute-done((bf16[256,1792]{0,1:T(8,128)(2,1)}, bf16[256,1792]{0,1:T(8,128)(2,1)S(1)}, u32[]{:S(2)}, u32[]{:S(2)}) %collective-permute-start.1) | collective-permute-done | bytes 917536 | tf_op jit(solution)/shard_map/ppermute | solution.py:39
  30.8 3.7 %collective-permute-start.3 = (bf16[128,1792]{0,1:T(8,128)(2,1)S(1)}, bf16[128,1792]{0,1:T(8,128)(2,1)}, u32[]{:S(2)}, u32[]{:S(2)}) collective-permute-start(bf16[128,1792]{0,1:T(8,128)(2,1)S(1)} %slice.130), channel_id=1, source_target_pairs={{0,6},{2,0},{4,2},{6,4},{1,7},{3,1},{5,3},{7,5},{8,14},{10,8},{12,... | collective-permute-start | bytes 1376264 | tf_op jit(solution)/shard_map/ppermute | solution.py:39
  36.7 7.0 %collective-permute-done.3 = bf16[128,1792]{0,1:T(8,128)(2,1)} collective-permute-done((bf16[128,1792]{0,1:T(8,128)(2,1)S(1)}, bf16[128,1792]{0,1:T(8,128)(2,1)}, u32[]{:S(2)}, u32[]{:S(2)}) %collective-permute-start.3) | collective-permute-done | bytes 458784 | tf_op jit(solution)/shard_map/ppermute | solution.py:39
  51.7 2.1 %collective-permute-start.9 = (bf16[256,1792]{0,1:T(8,128)(2,1)S(1)}, bf16[256,1792]{0,1:T(8,128)(2,1)}, u32[]{:S(2)}, u32[]{:S(2)}) collective-permute-start(bf16[256,1792]{0,1:T(8,128)(2,1)S(1)} %get-tuple-element.13), channel_id=1, source_target_pairs={{0,6},{2,0},{4,2},{6,4},{1,7},{3,1},{5,3},{7,5},{8,14},{10,8},{12,... | collective-permute-start | bytes 2752520 | tf_op jit(solution)/shard_map/ppermute | solution.py:39
  53.8 3.8 %collective-permute-start.7 = (bf16[128,1792]{0,1:T(8,128)(2,1)}, bf16[128,1792]{0,1:T(8,128)(2,1)}, u32[]{:S(2)}, u32[]{:S(2)}) collective-permute-start(bf16[128,1792]{0,1:T(8,128)(2,1)} %collective-permute-done.3), channel_id=1, source_target_pairs={{0,8},{1,9},{2,10},{3,11},{8,16},{9,17},{10,18},{11,19},{12,4},{13... | collective-permute-start | bytes 1376264 | tf_op jit(solution)/shard_map/ppermute | solution.py:120
  57.6 4.0 %collective-permute-start.8 = (bf16[128,1792]{0,1:T(8,128)(2,1)}, bf16[128,1792]{0,1:T(8,128)(2,1)}, u32[]{:S(2)}, u32[]{:S(2)}) collective-permute-start(bf16[128,1792]{0,1:T(8,128)(2,1)} %collective-permute-done.4), channel_id=1, source_target_pairs={{0,8},{1,9},{2,10},{3,11},{8,16},{9,17},{10,18},{11,19},{12,4},{13... | collective-permute-start | bytes 1376264 | tf_op jit(solution)/shard_map/ppermute | solution.py:120
  63.7 9.4 %collective-permute-done.7 = bf16[128,1792]{0,1:T(8,128)(2,1)} collective-permute-done((bf16[128,1792]{0,1:T(8,128)(2,1)}, bf16[128,1792]{0,1:T(8,128)(2,1)}, u32[]{:S(2)}, u32[]{:S(2)}) %collective-permute-start.7) | collective-permute-done | bytes 458784 | tf_op jit(solution)/shard_map/ppermute | solution.py:120
  75.0 5.4 %collective-permute-done.8 = bf16[128,1792]{0,1:T(8,128)(2,1)} collective-permute-done((bf16[128,1792]{0,1:T(8,128)(2,1)}, bf16[128,1792]{0,1:T(8,128)(2,1)}, u32[]{:S(2)}, u32[]{:S(2)}) %collective-permute-start.8) | collective-permute-done | bytes 458784 | tf_op jit(solution)/shard_map/ppermute | solution.py:120
  82.2 2.2 %constant_dynamic-update-slice_fusion.1 = bf16[2304,1792]{0,1:T(8,128)(2,1)} fusion(bf16[2304,1792]{0,1:T(8,128)(2,1)} %constant_dynamic-update-slice_fusion.2, bf16[256,1792]{0,1:T(8,128)(2,1)} %collective-permute-done.9), kind=kLoop, calls=%fused_computation.43 | loop fusion | bytes 1835008
  84.4 2.2 %constant_dynamic-update-slice_fusion = bf16[2304,1792]{0,1:T(8,128)(2,1)} fusion(bf16[2304,1792]{0,1:T(8,128)(2,1)} %constant_dynamic-update-slice_fusion.1, bf16[256,1792]{0,1:T(8,128)(2,1)} %collective-permute-done.10), kind=kLoop, calls=%fused_computation.42 | loop fusion | bytes 1835008 | tf_op jit(solution)/shard_map/concatenate | solution.py:145
  86.6 5.7 %fusion.28 = (bf16[2304,896]{0,1:T(8,128)(2,1)}, bf16[2304,896]{0,1:T(8,128)(2,1)}) fusion(bf16[2304,1792]{0,1:T(8,128)(2,1)} %constant_dynamic-update-slice_fusion), kind=kLoop, calls=%fused_computation.123 | loop fusion | bytes 16515072 | tf_op jit(solution)/shard_map/slice | solution.py:149
  92.4 12.6 %fusion.30 = (f32[7,256]{1,0:T(8,128)S(1)}, bf16[7,256,2304]{2,1,0:T(8,128)(2,1)}) fusion(pred[256,2304]{1,0:T(8,128)(4,1)S(1)} %copy-done, bf16[256,7,128]{0,2,1:T(8,128)(2,1)S(1)} %bitcast.134, bf16[2304,7,128]{0,2,1:T(8,128)(2,1)} %bitcast.130), kind=kOutput, calls=%fused_computation.125 | convolution fusion | flops 1081739520 | bytes 13442048 | tf_op jit(solution)/shard_map/sub | solution.py:25
  104.9 7.4 %fusion.13 = bf16[256,7,128]{0,2,1:T(8,128)(2,1)S(1)} fusion(bf16[2304,7,128]{0,2,1:T(8,128)(2,1)} %bitcast.129, bf16[7,256,2304]{2,1,0:T(8,128)(2,1)} %get-tuple-element.42, f32[256,7]{0,1:T(8,128)S(1)} %maximum_bitcast_fusion), kind=kOutput, calls=%fused_computation.15 | convolution fusion | flops 1057423360 | bytes 12852224 | tf_op jit(solution)/shard_map/hrk,khd->rhd/dot_general | solution.py:28
  114.6 2.3 %collective-permute-start.12 = (bf16[32,6656]{1,0:T(8,128)(2,1)S(1)}, bf16[32,6656]{1,0:T(8,128)(2,1)S(1)}, u32[]{:S(2)}, u32[]{:S(2)}) collective-permute-start(bf16[32,6656]{1,0:T(8,128)(2,1)S(1)} %select_n.204), channel_id=1, source_target_pairs={{0,6},{2,0},{4,2},{6,4},{1,7},{3,1},{5,3},{7,5},{8,14},{10,8},{12,... | collective-permute-start | bytes 1277960 | tf_op jit(solution)/shard_map/ppermute | solution.py:39
  116.8 9.7 %collective-permute-done.12 = bf16[32,6656]{1,0:T(8,128)(2,1)S(1)} collective-permute-done((bf16[32,6656]{1,0:T(8,128)(2,1)S(1)}, bf16[32,6656]{1,0:T(8,128)(2,1)S(1)}, u32[]{:S(2)}, u32[]{:S(2)}) %collective-permute-start.12) | collective-permute-done | bytes 426016 | tf_op jit(solution)/shard_map/ppermute | solution.py:39
  126.5 3.5 %collective-permute-start.14 = (bf16[16,6656]{1,0:T(8,128)(2,1)S(1)}, bf16[16,6656]{1,0:T(8,128)(2,1)S(1)}, u32[]{:S(2)}, u32[]{:S(2)}) collective-permute-start(bf16[16,6656]{1,0:T(8,128)(2,1)S(1)} %slice.136), channel_id=1, source_target_pairs={{0,6},{2,0},{4,2},{6,4},{1,7},{3,1},{5,3},{7,5},{8,14},{10,8},{12,... | collective-permute-start | bytes 638984 | tf_op jit(solution)/shard_map/ppermute | solution.py:39
  130.4 3.6 %collective-permute-done.14 = bf16[16,6656]{1,0:T(8,128)(2,1)S(1)} collective-permute-done((bf16[16,6656]{1,0:T(8,128)(2,1)S(1)}, bf16[16,6656]{1,0:T(8,128)(2,1)S(1)}, u32[]{:S(2)}, u32[]{:S(2)}) %collective-permute-start.14) | collective-permute-done | bytes 213024 | tf_op jit(solution)/shard_map/ppermute | solution.py:39
  134.0 3.8 %collective-permute-done.15 = bf16[16,6656]{1,0:T(8,128)(2,1)S(1)} collective-permute-done((bf16[16,6656]{1,0:T(8,128)(2,1)S(1)}, bf16[16,6656]{1,0:T(8,128)(2,1)S(1)}, u32[]{:S(2)}, u32[]{:S(2)}) %collective-permute-start.15) | collective-permute-done | bytes 213024 | tf_op jit(solution)/shard_map/ppermute | solution.py:39
  139.8 3.3 %collective-permute-done.16 = bf16[4,32,6656]{2,1,0:T(8,128)(2,1)S(1)} collective-permute-done((bf16[4,32,6656]{2,1,0:T(8,128)(2,1)}, bf16[4,32,6656]{2,1,0:T(8,128)(2,1)S(1)}, u32[]{:S(2)}, u32[]{:S(2)}) %collective-permute-start.16) | collective-permute-done | bytes 1703968 | tf_op jit(solution)/shard_map/ppermute | solution.py:39
  143.4 4.6 %multiply_reduce_fusion = (f32[256]{0:T(256)S(1)}, f32[256]{0:T(256)S(1)}, f32[256,384]{1,0:T(8,128)S(1)}) fusion(bf16[256,6656]{1,0:T(8,128)(2,1)S(1)} %fusion.17, bf16[6656,384]{1,0:T(8,128)(2,1)} %param.9), kind=kOutput, calls=%fused_computation.36 | convolution fusion | flops 1308917248 | bytes 8914944 | tf_op jit(solution)/shard_map/dot_general | solution.py:178
  149.5 3.6 %collective-permute-done.18 = f32[2,32]{1,0:T(2,128)S(1)} collective-permute-done((f32[2,32]{1,0:T(2,128)S(1)}, f32[2,32]{1,0:T(2,128)S(1)}, u32[]{:S(2)}, u32[]{:S(2)}) %collective-permute-start.18) | collective-permute-done | bytes 288 | tf_op jit(solution)/shard_map/ppermute | solution.py:49
  153.1 5.1 %collective-permute-done.19 = f32[2,32]{1,0:T(2,128)S(1)} collective-permute-done((f32[2,32]{1,0:T(2,128)S(1)}, f32[2,32]{1,0:T(2,128)S(1)}, u32[]{:S(2)}, u32[]{:S(2)}) %collective-permute-start.19) | collective-permute-done | bytes 288 | tf_op jit(solution)/shard_map/ppermute | solution.py:49
  158.3 3.6 %collective-permute-done.20 = f32[2,32]{1,0:T(2,128)S(1)} collective-permute-done((f32[2,32]{1,0:T(2,128)S(1)}, f32[2,32]{1,0:T(2,128)S(1)}, u32[]{:S(2)}, u32[]{:S(2)}) %collective-permute-start.20) | collective-permute-done | bytes 288 | tf_op jit(solution)/shard_map/ppermute | solution.py:49
  163.3 3.2 %collective-permute-done.21 = f32[2,32]{1,0:T(2,128)S(1)} collective-permute-done((f32[2,32]{1,0:T(2,128)S(1)}, f32[2,32]{1,0:T(2,128)S(1)}, u32[]{:S(2)}, u32[]{:S(2)}) %collective-permute-start.21) | collective-permute-done | bytes 288 | tf_op jit(solution)/shard_map/ppermute | solution.py:49
  166.4 4.0 %collective-permute-start.22 = (f32[2,32]{1,0:T(2,128)S(1)}, f32[2,32]{1,0:T(2,128)S(1)}, u32[]{:S(2)}, u32[]{:S(2)}) collective-permute-start(f32[2,32]{1,0:T(2,128)S(1)} %pad_maximum_fusion.9), channel_id=1, source_target_pairs={{0,32},{1,33},{2,34},{3,35},{4,36},{5,37},{6,38},{7,39},{8,40},{9,... | collective-permute-start | bytes 776 | tf_op jit(solution)/shard_map/ppermute | solution.py:49
  170.5 3.5 %collective-permute-done.22 = f32[2,32]{1,0:T(2,128)S(1)} collective-permute-done((f32[2,32]{1,0:T(2,128)S(1)}, f32[2,32]{1,0:T(2,128)S(1)}, u32[]{:S(2)}, u32[]{:S(2)}) %collective-permute-start.22) | collective-permute-done | bytes 288 | tf_op jit(solution)/shard_map/ppermute | solution.py:49
  175.4 2.3 %collective-permute-done.23 = f32[2,32]{1,0:T(2,128)S(1)} collective-permute-done((f32[2,32]{1,0:T(2,128)S(1)}, f32[2,32]{1,0:T(2,128)S(1)}, u32[]{:S(2)}, u32[]{:S(2)}) %collective-permute-start.23) | collective-permute-done | bytes 288 | tf_op jit(solution)/shard_map/ppermute | solution.py:49
  177.7 2.7 %collective-permute-start.24 = (f32[2,32]{1,0:T(2,128)S(1)}, f32[2,32]{1,0:T(2,128)S(1)}, u32[]{:S(2)}, u32[]{:S(2)}) collective-permute-start(f32[2,32]{1,0:T(2,128)S(1)} %pad_maximum_fusion.11), channel_id=1, source_target_pairs={{0,128},{1,129},{2,130},{3,131},{4,132},{5,133},{6,134},{7,135},{8... | collective-permute-start | bytes 776 | tf_op jit(solution)/shard_map/ppermute | solution.py:49
  180.6 2.2 %collective-permute-done.24 = f32[2,32]{1,0:T(2,128)S(1)} collective-permute-done((f32[2,32]{1,0:T(2,128)S(1)}, f32[2,32]{1,0:T(2,128)S(1)}, u32[]{:S(2)}, u32[]{:S(2)}) %collective-permute-start.24) | collective-permute-done | bytes 288 | tf_op jit(solution)/shard_map/ppermute | solution.py:49
  (112 shorter events, 34.8 us)
Async XLA Ops:
  0.6 3.8 %copy-start.2 = (s32[32768]{0:T(1024)S(1)}, s32[32768]{0:T(1024)}, u32[]{:S(2)}) copy-start(s32[32768]{0:T(1024)} %param.8) | copy-start | bytes 393220
  3.7 2.2 %collective-permute-start = (bf16[128,2688]{0,1:T(8,128)(2,1)S(1)}, bf16[128,2688]{0,1:T(8,128)(2,1)S(1)}, u32[]{:S(2)}, u32[]{:S(2)}) collective-permute-start(bf16[128,2688]{0,1:T(8,128)(2,1)S(1)} %pad_maximum_fusion.2), channel_id=1, source_target_pairs={{0,1},{1,0},{2,3},{3,2},{4,5},{5,4},{6,7},{7,6},{8,9},{9,8},{10,11... | collective-permute-start | bytes 2064392 | tf_op jit(solution)/shard_map/ppermute | solution.py:39
  7.8 23.0 %collective-permute-start.1 = (bf16[256,1792]{0,1:T(8,128)(2,1)}, bf16[256,1792]{0,1:T(8,128)(2,1)S(1)}, u32[]{:S(2)}, u32[]{:S(2)}) collective-permute-start(bf16[256,1792]{0,1:T(8,128)(2,1)} %get-tuple-element.9), channel_id=1, source_target_pairs={{0,6},{2,0},{4,2},{6,4},{1,7},{3,1},{5,3},{7,5},{8,14},{10,8},{12,... | collective-permute-start | bytes 2752520 | tf_op jit(solution)/shard_map/ppermute | solution.py:39
  10.5 23.9 %collective-permute-start.2 = (bf16[256,1792]{0,1:T(8,128)(2,1)}, bf16[256,1792]{0,1:T(8,128)(2,1)S(1)}, u32[]{:S(2)}, u32[]{:S(2)}) collective-permute-start(bf16[256,1792]{0,1:T(8,128)(2,1)} %get-tuple-element.9), channel_id=1, source_target_pairs={{0,2},{2,4},{4,6},{6,0},{1,3},{3,5},{5,7},{7,1},{8,10},{10,12},{12... | collective-permute-start | bytes 2752520 | tf_op jit(solution)/shard_map/ppermute | solution.py:39
  11.2 38.0 %collective-permute-start.5 = (bf16[256,1792]{0,1:T(8,128)(2,1)}, bf16[256,1792]{0,1:T(8,128)(2,1)S(1)}, u32[]{:S(2)}, u32[]{:S(2)}) collective-permute-start(bf16[256,1792]{0,1:T(8,128)(2,1)} %get-tuple-element.9), channel_id=1, source_target_pairs={{0,8},{8,16},{16,24},{24,32},{32,40},{40,48},{48,56},{56,64},{64,7... | collective-permute-start | bytes 2752520 | tf_op jit(solution)/shard_map/ppermute | solution.py:34
  15.1 35.2 %collective-permute-start.6 = (bf16[256,1792]{0,1:T(8,128)(2,1)}, bf16[256,1792]{0,1:T(8,128)(2,1)S(1)}, u32[]{:S(2)}, u32[]{:S(2)}) collective-permute-start(bf16[256,1792]{0,1:T(8,128)(2,1)} %get-tuple-element.9), channel_id=1, source_target_pairs={{8,0},{16,8},{24,16},{32,24},{40,32},{48,40},{56,48},{64,56},{72,6... | collective-permute-start | bytes 2752520 | tf_op jit(solution)/shard_map/ppermute | solution.py:34
  30.8 12.9 %collective-permute-start.3 = (bf16[128,1792]{0,1:T(8,128)(2,1)S(1)}, bf16[128,1792]{0,1:T(8,128)(2,1)}, u32[]{:S(2)}, u32[]{:S(2)}) collective-permute-start(bf16[128,1792]{0,1:T(8,128)(2,1)S(1)} %slice.130), channel_id=1, source_target_pairs={{0,6},{2,0},{4,2},{6,4},{1,7},{3,1},{5,3},{7,5},{8,14},{10,8},{12,... | collective-permute-start | bytes 1376264 | tf_op jit(solution)/shard_map/ppermute | solution.py:39
  34.5 12.8 %collective-permute-start.4 = (bf16[128,1792]{0,1:T(8,128)(2,1)S(1)}, bf16[128,1792]{0,1:T(8,128)(2,1)}, u32[]{:S(2)}, u32[]{:S(2)}) collective-permute-start(bf16[128,1792]{0,1:T(8,128)(2,1)S(1)} %slice.131), channel_id=1, source_target_pairs={{0,2},{2,4},{4,6},{6,0},{1,3},{3,5},{5,7},{7,1},{8,10},{10,12},{12... | collective-permute-start | bytes 1376264 | tf_op jit(solution)/shard_map/ppermute | solution.py:39
  51.7 30.5 %collective-permute-start.9 = (bf16[256,1792]{0,1:T(8,128)(2,1)S(1)}, bf16[256,1792]{0,1:T(8,128)(2,1)}, u32[]{:S(2)}, u32[]{:S(2)}) collective-permute-start(bf16[256,1792]{0,1:T(8,128)(2,1)S(1)} %get-tuple-element.13), channel_id=1, source_target_pairs={{0,6},{2,0},{4,2},{6,4},{1,7},{3,1},{5,3},{7,5},{8,14},{10,8},{12,... | collective-permute-start | bytes 2752520 | tf_op jit(solution)/shard_map/ppermute | solution.py:39
  53.8 30.7 %collective-permute-start.10 = (bf16[256,1792]{0,1:T(8,128)(2,1)S(1)}, bf16[256,1792]{0,1:T(8,128)(2,1)}, u32[]{:S(2)}, u32[]{:S(2)}) collective-permute-start(bf16[256,1792]{0,1:T(8,128)(2,1)S(1)} %get-tuple-element.12), channel_id=1, source_target_pairs={{0,2},{2,4},{4,6},{6,0},{1,3},{3,5},{5,7},{7,1},{8,10},{10,12},{12... | collective-permute-start | bytes 2752520 | tf_op jit(solution)/shard_map/ppermute | solution.py:39
  53.8 19.4 %collective-permute-start.7 = (bf16[128,1792]{0,1:T(8,128)(2,1)}, bf16[128,1792]{0,1:T(8,128)(2,1)}, u32[]{:S(2)}, u32[]{:S(2)}) collective-permute-start(bf16[128,1792]{0,1:T(8,128)(2,1)} %collective-permute-done.3), channel_id=1, source_target_pairs={{0,8},{1,9},{2,10},{3,11},{8,16},{9,17},{10,18},{11,19},{12,4},{13... | collective-permute-start | bytes 1376264 | tf_op jit(solution)/shard_map/ppermute | solution.py:120
  57.6 22.7 %collective-permute-start.8 = (bf16[128,1792]{0,1:T(8,128)(2,1)}, bf16[128,1792]{0,1:T(8,128)(2,1)}, u32[]{:S(2)}, u32[]{:S(2)}) collective-permute-start(bf16[128,1792]{0,1:T(8,128)(2,1)} %collective-permute-done.4), channel_id=1, source_target_pairs={{0,8},{1,9},{2,10},{3,11},{8,16},{9,17},{10,18},{11,19},{12,4},{13... | collective-permute-start | bytes 1376264 | tf_op jit(solution)/shard_map/ppermute | solution.py:120
  86.6 5.7 %copy-start = (pred[256,2304]{1,0:T(8,128)(4,1)S(1)}, pred[256,2304]{1,0:T(8,128)(4,1)}, u32[]{:S(2)}) copy-start(pred[256,2304]{1,0:T(8,128)(4,1)} %compare_and_fusion) | copy-start | bytes 1769476
  86.6 5.7 %copy-start.1 = (bf16[256,896]{0,1:T(8,128)(2,1)S(1)}, bf16[256,896]{0,1:T(8,128)(2,1)}, u32[]{:S(2)}) copy-start(bf16[256,896]{0,1:T(8,128)(2,1)} %pad_maximum_fusion.3) | copy-start | bytes 1376260
  112.5 1.6 collective-permute-start.11
  114.6 11.9 %collective-permute-start.12 = (bf16[32,6656]{1,0:T(8,128)(2,1)S(1)}, bf16[32,6656]{1,0:T(8,128)(2,1)S(1)}, u32[]{:S(2)}, u32[]{:S(2)}) collective-permute-start(bf16[32,6656]{1,0:T(8,128)(2,1)S(1)} %select_n.204), channel_id=1, source_target_pairs={{0,6},{2,0},{4,2},{6,4},{1,7},{3,1},{5,3},{7,5},{8,14},{10,8},{12,... | collective-permute-start | bytes 1277960 | tf_op jit(solution)/shard_map/ppermute | solution.py:39
  116.8 13.5 %collective-permute-start.13 = (bf16[32,6656]{1,0:T(8,128)(2,1)S(1)}, bf16[32,6656]{1,0:T(8,128)(2,1)S(1)}, u32[]{:S(2)}, u32[]{:S(2)}) collective-permute-start(bf16[32,6656]{1,0:T(8,128)(2,1)S(1)} %select_n.204), channel_id=1, source_target_pairs={{0,2},{2,4},{4,6},{6,0},{1,3},{3,5},{5,7},{7,1},{8,10},{10,12},{12... | collective-permute-start | bytes 1277960 | tf_op jit(solution)/shard_map/ppermute | solution.py:39
  126.5 7.5 %collective-permute-start.14 = (bf16[16,6656]{1,0:T(8,128)(2,1)S(1)}, bf16[16,6656]{1,0:T(8,128)(2,1)S(1)}, u32[]{:S(2)}, u32[]{:S(2)}) collective-permute-start(bf16[16,6656]{1,0:T(8,128)(2,1)S(1)} %slice.136), channel_id=1, source_target_pairs={{0,6},{2,0},{4,2},{6,4},{1,7},{3,1},{5,3},{7,5},{8,14},{10,8},{12,... | collective-permute-start | bytes 638984 | tf_op jit(solution)/shard_map/ppermute | solution.py:39
  130.3 7.5 %collective-permute-start.15 = (bf16[16,6656]{1,0:T(8,128)(2,1)S(1)}, bf16[16,6656]{1,0:T(8,128)(2,1)S(1)}, u32[]{:S(2)}, u32[]{:S(2)}) collective-permute-start(bf16[16,6656]{1,0:T(8,128)(2,1)S(1)} %slice.137), channel_id=1, source_target_pairs={{0,2},{2,4},{4,6},{6,0},{1,3},{3,5},{5,7},{7,1},{8,10},{10,12},{12... | collective-permute-start | bytes 638984 | tf_op jit(solution)/shard_map/ppermute | solution.py:39
  139.3 3.8 %collective-permute-start.16 = (bf16[4,32,6656]{2,1,0:T(8,128)(2,1)}, bf16[4,32,6656]{2,1,0:T(8,128)(2,1)S(1)}, u32[]{:S(2)}, u32[]{:S(2)}) collective-permute-start(bf16[4,32,6656]{2,1,0:T(8,128)(2,1)} %pad_maximum_fusion), channel_id=1, source_target_pairs={{0,1},{1,0},{2,3},{3,2},{4,5},{5,4},{6,7},{7,6},{8,9},{9,8},{10,11... | collective-permute-start | bytes 5111816 | tf_op jit(solution)/shard_map/ppermute | solution.py:39
  148.1 1.2 collective-permute-start.17
  149.4 3.7 %collective-permute-start.18 = (f32[2,32]{1,0:T(2,128)S(1)}, f32[2,32]{1,0:T(2,128)S(1)}, u32[]{:S(2)}, u32[]{:S(2)}) collective-permute-start(f32[2,32]{1,0:T(2,128)S(1)} %pad_maximum_fusion.5), channel_id=1, source_target_pairs={{0,2},{1,3},{2,0},{3,1},{4,6},{5,7},{6,4},{7,5},{8,10},{9,11},{10,... | collective-permute-start | bytes 776 | tf_op jit(solution)/shard_map/ppermute | solution.py:49
  153.0 5.2 %collective-permute-start.19 = (f32[2,32]{1,0:T(2,128)S(1)}, f32[2,32]{1,0:T(2,128)S(1)}, u32[]{:S(2)}, u32[]{:S(2)}) collective-permute-start(f32[2,32]{1,0:T(2,128)S(1)} %pad_maximum_fusion.6), channel_id=1, source_target_pairs={{0,4},{1,5},{2,6},{3,7},{4,0},{5,1},{6,2},{7,3},{8,12},{9,13},{10,... | collective-permute-start | bytes 776 | tf_op jit(solution)/shard_map/ppermute | solution.py:49
  158.2 3.7 %collective-permute-start.20 = (f32[2,32]{1,0:T(2,128)S(1)}, f32[2,32]{1,0:T(2,128)S(1)}, u32[]{:S(2)}, u32[]{:S(2)}) collective-permute-start(f32[2,32]{1,0:T(2,128)S(1)} %pad_maximum_fusion.7), channel_id=1, source_target_pairs={{0,8},{1,9},{2,10},{3,11},{4,12},{5,13},{6,14},{7,15},{8,0},{9,1},... | collective-permute-start | bytes 776 | tf_op jit(solution)/shard_map/ppermute | solution.py:49
  161.9 4.6 %collective-permute-start.21 = (f32[2,32]{1,0:T(2,128)S(1)}, f32[2,32]{1,0:T(2,128)S(1)}, u32[]{:S(2)}, u32[]{:S(2)}) collective-permute-start(f32[2,32]{1,0:T(2,128)S(1)} %pad_maximum_fusion.8), channel_id=1, source_target_pairs={{0,16},{1,17},{2,18},{3,19},{4,20},{5,21},{6,22},{7,23},{8,24},{9,... | collective-permute-start | bytes 776 | tf_op jit(solution)/shard_map/ppermute | solution.py:49
  166.4 7.6 %collective-permute-start.22 = (f32[2,32]{1,0:T(2,128)S(1)}, f32[2,32]{1,0:T(2,128)S(1)}, u32[]{:S(2)}, u32[]{:S(2)}) collective-permute-start(f32[2,32]{1,0:T(2,128)S(1)} %pad_maximum_fusion.9), channel_id=1, source_target_pairs={{0,32},{1,33},{2,34},{3,35},{4,36},{5,37},{6,38},{7,39},{8,40},{9,... | collective-permute-start | bytes 776 | tf_op jit(solution)/shard_map/ppermute | solution.py:49
  174.0 3.7 %collective-permute-start.23 = (f32[2,32]{1,0:T(2,128)S(1)}, f32[2,32]{1,0:T(2,128)S(1)}, u32[]{:S(2)}, u32[]{:S(2)}) collective-permute-start(f32[2,32]{1,0:T(2,128)S(1)} %pad_maximum_fusion.10), channel_id=1, source_target_pairs={{0,64},{1,65},{2,66},{3,67},{4,68},{5,69},{6,70},{7,71},{8,72},{9,... | collective-permute-start | bytes 776 | tf_op jit(solution)/shard_map/ppermute | solution.py:49
  177.7 5.2 %collective-permute-start.24 = (f32[2,32]{1,0:T(2,128)S(1)}, f32[2,32]{1,0:T(2,128)S(1)}, u32[]{:S(2)}, u32[]{:S(2)}) collective-permute-start(f32[2,32]{1,0:T(2,128)S(1)} %pad_maximum_fusion.11), channel_id=1, source_target_pairs={{0,128},{1,129},{2,130},{3,131},{4,132},{5,133},{6,134},{7,135},{8... | collective-permute-start | bytes 776 | tf_op jit(solution)/shard_map/ppermute | solution.py:49

commit v7 on v5

--- a/solution.py
+++ b/solution.py
@@ -140,15 +140,31 @@
         seg_sets.append(segs_at(begin, chunk))
 
     query_segs = lax.dynamic_slice_in_dim(segment_ids, chip_begin, chunk)
-    key_segs = jnp.concatenate(seg_sets)
-    all_kv = jnp.concatenate(kv_sets, axis=0)
-    key_total = all_kv.shape[0]
-    allowed = (query_segs[:, None] == key_segs[None, :]) & (query_segs[:, None] >= 0)
     query_heads = q_chip.reshape(chunk, slot_heads, HEAD)
-    key_heads = all_kv[:, :slot].reshape(key_total, slot_heads, HEAD)
-    value_heads = all_kv[:, slot:].reshape(key_total, slot_heads, HEAD)
-    scores = key_scores(query_heads, key_heads)
-    mixed = finish(scores, allowed, value_heads).reshape(chunk, slot).astype(jnp.bfloat16)
+    live = query_segs[:, None] >= 0
+    blocks = []
+    for kv, key_segs in zip(kv_sets, seg_sets):
+        allowed = (query_segs[:, None] == key_segs[None, :]) & live
+        key_heads = kv[:, :slot].reshape(kv.shape[0], slot_heads, HEAD)
+        value_heads = kv[:, slot:].reshape(kv.shape[0], slot_heads, HEAD)
+        scores = jnp.where(allowed[None], key_scores(query_heads, key_heads), masked_score)
+        blocks.append((scores, allowed, value_heads))
+    row_top = blocks[0][0].max(axis=2, keepdims=True)
+    for scores, _, _ in blocks[1:]:
+        row_top = jnp.maximum(row_top, scores.max(axis=2, keepdims=True))
+    row_total = None
+    mixed_out = None
+    for scores, allowed, value_heads in blocks:
+        exp_terms = jnp.where(allowed[None], jnp.exp(scores - row_top), 0.0)
+        total = jnp.sum(exp_terms, axis=2)
+        part = jnp.einsum(
+            "hrk,khd->rhd", exp_terms.astype(jnp.bfloat16), value_heads,
+            preferred_element_type=jnp.float32,
+        )
+        row_total = total if row_total is None else row_total + total
+        mixed_out = part if mixed_out is None else mixed_out + part
+    row_total = jnp.maximum(row_total, 1.0)
+    mixed = (mixed_out / row_total.T[:, :, None]).reshape(chunk, slot).astype(jnp.bfloat16)
 
     mine = lax.dynamic_slice_in_dim(mixed, c * row_count, row_count)
     theirs = lax.dynamic_slice_in_dim(mixed, (1 - c) * row_count, row_count)

time: 183 us -> 156 us (0.85)
  local copies, waits for them, and re-layouts: 24.8 us -> 10.7 us
  matrix products: 24.5 us -> 14.8 us
  waiting for transfers between devices: 84.9 us -> 82.4 us
    sub x1 -> x0, matrix products: 12.6 us -> none  [finish(): exp_terms = jnp.where(allowed[None], jnp.exp(scores - row_top), 0.0)]
    unnamed x30 -> x14, local copies, waits for them, and re-layouts: 11.4 us -> 1.47 us
    ppermute x1, waiting for transfers between devices: 12.4 us -> 5.32 us  [per_device(): kv_sets.append(lax.ppermute(far, ALL, pairs))]
    reduce_sum x0 -> x1, other arithmetic: none -> 4.89 us  [per_device(): total = jnp.sum(exp_terms, axis=2)]
    ppermute x13, waiting for transfers between devices: 45.5 us -> 49.7 us  [cyclic(): return lax.ppermute(x, axis, [(i, (i + by) % n) for i in range(n)])]
    ppermute x13, starting transfers between devices: 17.2 us -> 13.1 us  [cyclic(): return lax.ppermute(x, axis, [(i, (i + by) % n) for i in range(n)])]
    ppermute x2, waiting for transfers between devices: 0.01 us -> 3.3 us  [shifted(): lax.ppermute(x, axis, [(i, i + by) for i in range(n) if 0 <= i + by < n])]
    slice x1 -> x8, local copies, waits for them, and re-layouts: 5.73 us -> 2.8 us  [the longest x7 2.74 us: per_device(): value_heads = kv[:, slot:].reshape(kv.shape[0], slot_heads, HEAD)]
  transfers between devices with their start and end apart: 24 -> 24, of which waited for: 20 -> 21; matrix products, arithmetic and copies ran while one was open for 10% -> 8% of each run, Pallas kernels for 0% -> 0%
where the time goes in v7:
time: 156 us
  waiting for transfers between devices  82.4 us (53%)
  starting transfers between devices  35.7 us (23%)
  matrix products  14.8 us (9%)
  local copies, waits for them, and re-layouts  10.7 us (7%)
  other arithmetic  10.6 us (7%)
    ppermute x13, waiting for transfers between devices, cyclic(): return lax.ppermute(x, axis, [(i, (i + by) % n) for i in range(n)])  49.7 us
    ppermute x8, waiting for transfers between devices, butterfly(): other = lax.ppermute(jnp.stack([sums, peaks]), ALL, perm)  24.1 us
    ppermute x13, starting transfers between devices, cyclic(): return lax.ppermute(x, axis, [(i, (i + by) % n) for i in range(n)])  13.1 us
    ppermute x2, starting transfers between devices, shifted(): lax.ppermute(x, axis, [(i, i + by) for i in range(n) if 0 <= i + by < n])  9.56 us
    ppermute x8, starting transfers between devices, butterfly(): other = lax.ppermute(jnp.stack([sums, peaks]), ALL, perm)  8.96 us
    dot_general x9, matrix products, per_device(): jnp.einsum('hrk,khd->rhd', exp_terms.astype(jnp.bfloat16), value_heads, p...  5.76 us
    ppermute x1, waiting for transfers between devices, per_device(): kv_sets.append(lax.ppermute(far, ALL, pairs))  5.32 us
    reduce_sum x1, other arithmetic, per_device(): total = jnp.sum(exp_terms, axis=2)  4.89 us
  transfers between devices with their start and end apart: 24, of which 21 were waited for; matrix products, arithmetic and copies ran while one was open for 8% of the time, Pallas kernels for 0%

profile of v7, /device:TPU:8, one launch (start us, length us, event | category | flops | bytes accessed | tf_op | source)
XLA Modules:
  0.0 155.6 jit_solution(7502237665308223907)
XLA Ops:
  3.4 1.6 %collective-permute-done = bf16[128,2688]{0,1:T(8,128)(2,1)S(1)} collective-permute-done((bf16[128,2688]{0,1:T(8,128)(2,1)S(1)}, bf16[128,2688]{0,1:T(8,128)(2,1)S(1)}, u32[]{:S(2)}, u32[]{:S(2)}) %collective-permute-start) | collective-permute-done | bytes 688160 | tf_op jit(solution)/shard_map/ppermute | solution.py:39
  6.3 1.5 collective-permute-start.2
  7.8 1.7 %collective-permute-start.1 = (bf16[256,1792]{0,1:T(8,128)(2,1)}, bf16[256,1792]{0,1:T(8,128)(2,1)}, u32[]{:S(2)}, u32[]{:S(2)}) collective-permute-start(bf16[256,1792]{0,1:T(8,128)(2,1)} %pad_maximum_fusion.1), channel_id=1, source_target_pairs={{0,6},{2,0},{4,2},{6,4},{1,7},{3,1},{5,3},{7,5},{8,14},{10,8},{12,... | collective-permute-start | bytes 2752520 | tf_op jit(solution)/shard_map/ppermute | solution.py:39
  9.5 3.8 %collective-permute-start.5 = (bf16[256,1792]{0,1:T(8,128)(2,1)}, bf16[256,1792]{0,1:T(8,128)(2,1)S(1)}, u32[]{:S(2)}, u32[]{:S(2)}) collective-permute-start(bf16[256,1792]{0,1:T(8,128)(2,1)} %pad_maximum_fusion.1), channel_id=1, source_target_pairs={{0,8},{8,16},{16,24},{24,32},{32,40},{40,48},{48,56},{56,64},{64,7... | collective-permute-start | bytes 2752520 | tf_op jit(solution)/shard_map/ppermute | solution.py:34
  13.3 5.7 %collective-permute-start.6 = (bf16[256,1792]{0,1:T(8,128)(2,1)}, bf16[256,1792]{0,1:T(8,128)(2,1)S(1)}, u32[]{:S(2)}, u32[]{:S(2)}) collective-permute-start(bf16[256,1792]{0,1:T(8,128)(2,1)} %pad_maximum_fusion.1), channel_id=1, source_target_pairs={{8,0},{16,8},{24,16},{32,24},{40,32},{48,40},{56,48},{64,56},{72,6... | collective-permute-start | bytes 2752520 | tf_op jit(solution)/shard_map/ppermute | solution.py:34
  20.7 9.5 %collective-permute-done.1 = bf16[256,1792]{0,1:T(8,128)(2,1)} collective-permute-done((bf16[256,1792]{0,1:T(8,128)(2,1)}, bf16[256,1792]{0,1:T(8,128)(2,1)}, u32[]{:S(2)}, u32[]{:S(2)}) %collective-permute-start.1) | collective-permute-done | bytes 917536 | tf_op jit(solution)/shard_map/ppermute | solution.py:39
  31.2 3.0 %collective-permute-start.3 = (bf16[128,1792]{0,1:T(8,128)(2,1)S(1)}, bf16[128,1792]{0,1:T(8,128)(2,1)S(1)}, u32[]{:S(2)}, u32[]{:S(2)}) collective-permute-start(bf16[128,1792]{0,1:T(8,128)(2,1)S(1)} %slice.202), channel_id=1, source_target_pairs={{0,6},{2,0},{4,2},{6,4},{1,7},{3,1},{5,3},{7,5},{8,14},{10,8},{12,... | collective-permute-start | bytes 1376264 | tf_op jit(solution)/shard_map/ppermute | solution.py:39
  35.4 2.0 %collective-permute-done.5 = bf16[256,1792]{0,1:T(8,128)(2,1)S(1)} collective-permute-done((bf16[256,1792]{0,1:T(8,128)(2,1)}, bf16[256,1792]{0,1:T(8,128)(2,1)S(1)}, u32[]{:S(2)}, u32[]{:S(2)}) %collective-permute-start.5) | collective-permute-done | bytes 917536 | tf_op jit(solution)/shard_map/ppermute | solution.py:34
  38.9 1.6 %collective-permute-start.8 = (bf16[256,1792]{0,1:T(8,128)(2,1)S(1)}, bf16[256,1792]{0,1:T(8,128)(2,1)S(1)}, u32[]{:S(2)}, u32[]{:S(2)}) collective-permute-start(bf16[256,1792]{0,1:T(8,128)(2,1)S(1)} %get-tuple-element.17), channel_id=1, source_target_pairs={{0,6},{2,0},{4,2},{6,4},{1,7},{3,1},{5,3},{7,5},{8,14},{10,8},{12,... | collective-permute-start | bytes 2752520 | tf_op jit(solution)/shard_map/ppermute | solution.py:39
  45.6 4.4 %collective-permute-done.4 = bf16[128,1792]{0,1:T(8,128)(2,1)S(1)} collective-permute-done((bf16[128,1792]{0,1:T(8,128)(2,1)S(1)}, bf16[128,1792]{0,1:T(8,128)(2,1)S(1)}, u32[]{:S(2)}, u32[]{:S(2)}) %collective-permute-start.4) | collective-permute-done | bytes 458784 | tf_op jit(solution)/shard_map/ppermute | solution.py:39
  50.2 4.0 %collective-permute-start.7 = (bf16[256,1792]{0,1:T(8,128)(2,1)S(1)}, bf16[256,1792]{0,1:T(8,128)(2,1)S(1)}, u32[]{:S(2)}, u32[]{:S(2)}) collective-permute-start(bf16[256,1792]{0,1:T(8,128)(2,1)S(1)} %constant_dynamic-update-slice_fusion), channel_id=1, source_target_pairs={{0,8},{1,9},{2,10},{3,11},{8,16},{9,17},{10,18},{11,19},{12,4},{13... | collective-permute-start | bytes 2752520 | tf_op jit(solution)/shard_map/ppermute | solution.py:120
  54.8 8.1 %collective-permute-done.8 = bf16[256,1792]{0,1:T(8,128)(2,1)S(1)} collective-permute-done((bf16[256,1792]{0,1:T(8,128)(2,1)S(1)}, bf16[256,1792]{0,1:T(8,128)(2,1)S(1)}, u32[]{:S(2)}, u32[]{:S(2)}) %collective-permute-start.8) | collective-permute-done | bytes 917536 | tf_op jit(solution)/shard_map/ppermute | solution.py:39
  62.9 4.5 %collective-permute-done.9 = bf16[256,1792]{0,1:T(8,128)(2,1)S(1)} collective-permute-done((bf16[256,1792]{0,1:T(8,128)(2,1)S(1)}, bf16[256,1792]{0,1:T(8,128)(2,1)S(1)}, u32[]{:S(2)}, u32[]{:S(2)}) %collective-permute-start.9) | collective-permute-done | bytes 917536 | tf_op jit(solution)/shard_map/ppermute | solution.py:39
  68.5 5.3 %collective-permute-done.7 = bf16[256,1792]{0,1:T(8,128)(2,1)S(1)} collective-permute-done((bf16[256,1792]{0,1:T(8,128)(2,1)S(1)}, bf16[256,1792]{0,1:T(8,128)(2,1)S(1)}, u32[]{:S(2)}, u32[]{:S(2)}) %collective-permute-start.7) | collective-permute-done | bytes 917536 | tf_op jit(solution)/shard_map/ppermute | solution.py:120
  78.6 4.9 %fusion.19 = (f32[7,256]{1,0:T(8,128)S(1)}, f32[7,256]{1,0:T(8,128)S(1)}, f32[7,256]{1,0:T(8,128)S(1)}, f32[7,256]{1,0:T(8,128)S(1)}, f32[7,256]{1,0:T(8,128)S(1...) fusion(f32[7,256,256]{1,2,0:T(8,128)S(1)} %get-tuple-element.99, ...), kind=kLoop, calls=%fused_computation.45 | loop fusion | flops 20627712 | bytes 17176576 | tf_op jit(solution)/shard_map/reduce_sum | solution.py:159
  87.4 2.0 %collective-permute-start.12 = (bf16[32,6656]{1,0:T(8,128)(2,1)S(1)}, bf16[32,6656]{1,0:T(8,128)(2,1)S(1)}, u32[]{:S(2)}, u32[]{:S(2)}) collective-permute-start(bf16[32,6656]{1,0:T(8,128)(2,1)S(1)} %select_n.268), channel_id=1, source_target_pairs={{0,2},{2,4},{4,6},{6,0},{1,3},{3,5},{5,7},{7,1},{8,10},{10,12},{12... | collective-permute-start | bytes 1277960 | tf_op jit(solution)/shard_map/ppermute | solution.py:39
  89.4 9.8 %collective-permute-done.11 = bf16[32,6656]{1,0:T(8,128)(2,1)S(1)} collective-permute-done((bf16[32,6656]{1,0:T(8,128)(2,1)S(1)}, bf16[32,6656]{1,0:T(8,128)(2,1)S(1)}, u32[]{:S(2)}, u32[]{:S(2)}) %collective-permute-start.11) | collective-permute-done | bytes 426016 | tf_op jit(solution)/shard_map/ppermute | solution.py:39
  99.3 1.8 %collective-permute-start.13 = (bf16[16,6656]{1,0:T(8,128)(2,1)S(1)}, bf16[16,6656]{1,0:T(8,128)(2,1)S(1)}, u32[]{:S(2)}, u32[]{:S(2)}) collective-permute-start(bf16[16,6656]{1,0:T(8,128)(2,1)S(1)} %slice.220), channel_id=1, source_target_pairs={{0,6},{2,0},{4,2},{6,4},{1,7},{3,1},{5,3},{7,5},{8,14},{10,8},{12,... | collective-permute-start | bytes 638984 | tf_op jit(solution)/shard_map/ppermute | solution.py:39
  102.0 4.0 %collective-permute-done.13 = bf16[16,6656]{1,0:T(8,128)(2,1)S(1)} collective-permute-done((bf16[16,6656]{1,0:T(8,128)(2,1)S(1)}, bf16[16,6656]{1,0:T(8,128)(2,1)S(1)}, u32[]{:S(2)}, u32[]{:S(2)}) %collective-permute-start.13) | collective-permute-done | bytes 213024 | tf_op jit(solution)/shard_map/ppermute | solution.py:39
  106.1 3.1 %collective-permute-done.14 = bf16[16,6656]{1,0:T(8,128)(2,1)S(1)} collective-permute-done((bf16[16,6656]{1,0:T(8,128)(2,1)S(1)}, bf16[16,6656]{1,0:T(8,128)(2,1)S(1)}, u32[]{:S(2)}, u32[]{:S(2)}) %collective-permute-start.14) | collective-permute-done | bytes 213024 | tf_op jit(solution)/shard_map/ppermute | solution.py:39
  109.2 1.4 pad_maximum_fusion
  111.2 3.3 %collective-permute-done.15 = bf16[4,32,6656]{2,1,0:T(8,128)(2,1)S(1)} collective-permute-done((bf16[4,32,6656]{2,1,0:T(8,128)(2,1)}, bf16[4,32,6656]{2,1,0:T(8,128)(2,1)S(1)}, u32[]{:S(2)}, u32[]{:S(2)}) %collective-permute-start.15) | collective-permute-done | bytes 1703968 | tf_op jit(solution)/shard_map/ppermute | solution.py:39
  114.7 4.6 %multiply_reduce_fusion = (f32[256]{0:T(256)S(1)}, f32[256]{0:T(256)S(1)}, f32[256,384]{1,0:T(8,128)S(1)}) fusion(bf16[256,6656]{1,0:T(8,128)(2,1)S(1)} %fusion.104, bf16[6656,384]{1,0:T(8,128)(2,1)} %param.9), kind=kOutput, calls=%fused_computation.138 | convolution fusion | flops 1308917248 | bytes 8914944 | tf_op jit(solution)/shard_map/dot_general | solution.py:193
  120.8 3.6 %collective-permute-done.17 = f32[2,32]{1,0:T(2,128)S(1)} collective-permute-done((f32[2,32]{1,0:T(2,128)S(1)}, f32[2,32]{1,0:T(2,128)S(1)}, u32[]{:S(2)}, u32[]{:S(2)}) %collective-permute-start.17) | collective-permute-done | bytes 288 | tf_op jit(solution)/shard_map/ppermute | solution.py:49
  124.5 5.1 %collective-permute-done.18 = f32[2,32]{1,0:T(2,128)S(1)} collective-permute-done((f32[2,32]{1,0:T(2,128)S(1)}, f32[2,32]{1,0:T(2,128)S(1)}, u32[]{:S(2)}, u32[]{:S(2)}) %collective-permute-start.18) | collective-permute-done | bytes 288 | tf_op jit(solution)/shard_map/ppermute | solution.py:49
  129.7 3.6 %collective-permute-done.19 = f32[2,32]{1,0:T(2,128)S(1)} collective-permute-done((f32[2,32]{1,0:T(2,128)S(1)}, f32[2,32]{1,0:T(2,128)S(1)}, u32[]{:S(2)}, u32[]{:S(2)}) %collective-permute-start.19) | collective-permute-done | bytes 288 | tf_op jit(solution)/shard_map/ppermute | solution.py:49
  134.5 3.3 %collective-permute-done.20 = f32[2,32]{1,0:T(2,128)S(1)} collective-permute-done((f32[2,32]{1,0:T(2,128)S(1)}, f32[2,32]{1,0:T(2,128)S(1)}, u32[]{:S(2)}, u32[]{:S(2)}) %collective-permute-start.20) | collective-permute-done | bytes 288 | tf_op jit(solution)/shard_map/ppermute | solution.py:49
  137.8 4.5 %collective-permute-start.21 = (f32[2,32]{1,0:T(2,128)S(1)}, f32[2,32]{1,0:T(2,128)S(1)}, u32[]{:S(2)}, u32[]{:S(2)}) collective-permute-start(f32[2,32]{1,0:T(2,128)S(1)} %pad_maximum_fusion.9), channel_id=1, source_target_pairs={{0,32},{1,33},{2,34},{3,35},{4,36},{5,37},{6,38},{7,39},{8,40},{9,... | collective-permute-start | bytes 776 | tf_op jit(solution)/shard_map/ppermute | solution.py:49
  142.3 3.1 %collective-permute-done.21 = f32[2,32]{1,0:T(2,128)S(1)} collective-permute-done((f32[2,32]{1,0:T(2,128)S(1)}, f32[2,32]{1,0:T(2,128)S(1)}, u32[]{:S(2)}, u32[]{:S(2)}) %collective-permute-start.21) | collective-permute-done | bytes 288 | tf_op jit(solution)/shard_map/ppermute | solution.py:49
  146.8 2.3 %collective-permute-done.22 = f32[2,32]{1,0:T(2,128)S(1)} collective-permute-done((f32[2,32]{1,0:T(2,128)S(1)}, f32[2,32]{1,0:T(2,128)S(1)}, u32[]{:S(2)}, u32[]{:S(2)}) %collective-permute-start.22) | collective-permute-done | bytes 288 | tf_op jit(solution)/shard_map/ppermute | solution.py:49
  149.1 2.7 %collective-permute-start.23 = (f32[2,32]{1,0:T(2,128)S(1)}, f32[2,32]{1,0:T(2,128)S(1)}, u32[]{:S(2)}, u32[]{:S(2)}) collective-permute-start(f32[2,32]{1,0:T(2,128)S(1)} %pad_maximum_fusion.11), channel_id=1, source_target_pairs={{0,128},{1,129},{2,130},{3,131},{4,132},{5,133},{6,134},{7,135},{8... | collective-permute-start | bytes 776 | tf_op jit(solution)/shard_map/ppermute | solution.py:49
  152.0 2.2 %collective-permute-done.23 = f32[2,32]{1,0:T(2,128)S(1)} collective-permute-done((f32[2,32]{1,0:T(2,128)S(1)}, f32[2,32]{1,0:T(2,128)S(1)}, u32[]{:S(2)}, u32[]{:S(2)}) %collective-permute-start.23) | collective-permute-done | bytes 288 | tf_op jit(solution)/shard_map/ppermute | solution.py:49
  (117 shorter events, 32.2 us)
Async XLA Ops:
  0.6 1.8 %copy-start = (bf16[128,1664]{1,0:T(8,128)(2,1)S(1)}, bf16[128,1664]{1,0:T(8,128)(2,1)}, u32[]{:S(2)}) copy-start(bf16[128,1664]{1,0:T(8,128)(2,1)} %param.5) | copy-start | bytes 1277956
  2.7 2.2 %collective-permute-start = (bf16[128,2688]{0,1:T(8,128)(2,1)S(1)}, bf16[128,2688]{0,1:T(8,128)(2,1)S(1)}, u32[]{:S(2)}, u32[]{:S(2)}) collective-permute-start(bf16[128,2688]{0,1:T(8,128)(2,1)S(1)} %pad_maximum_fusion.3), channel_id=1, source_target_pairs={{0,1},{1,0},{2,3},{3,2},{4,5},{5,4},{6,7},{7,6},{8,9},{9,8},{10,11... | collective-permute-start | bytes 2064392 | tf_op jit(solution)/shard_map/ppermute | solution.py:39
  5.2 13.9 %copy-start.1 = (s32[32768]{0:T(1024)S(1)}, s32[32768]{0:T(1024)}, u32[]{:S(2)}) copy-start(s32[32768]{0:T(1024)} %param.8) | copy-start | bytes 393220
  6.3 28.0 %collective-permute-start.2 = (bf16[256,1792]{0,1:T(8,128)(2,1)}, bf16[256,1792]{0,1:T(8,128)(2,1)}, u32[]{:S(2)}, u32[]{:S(2)}) collective-permute-start(bf16[256,1792]{0,1:T(8,128)(2,1)} %pad_maximum_fusion.1), channel_id=1, source_target_pairs={{0,2},{2,4},{4,6},{6,0},{1,3},{3,5},{5,7},{7,1},{8,10},{10,12},{12... | collective-permute-start | bytes 2752520 | tf_op jit(solution)/shard_map/ppermute | solution.py:39
  7.8 22.4 %collective-permute-start.1 = (bf16[256,1792]{0,1:T(8,128)(2,1)}, bf16[256,1792]{0,1:T(8,128)(2,1)}, u32[]{:S(2)}, u32[]{:S(2)}) collective-permute-start(bf16[256,1792]{0,1:T(8,128)(2,1)} %pad_maximum_fusion.1), channel_id=1, source_target_pairs={{0,6},{2,0},{4,2},{6,4},{1,7},{3,1},{5,3},{7,5},{8,14},{10,8},{12,... | collective-permute-start | bytes 2752520 | tf_op jit(solution)/shard_map/ppermute | solution.py:39
  9.5 27.9 %collective-permute-start.5 = (bf16[256,1792]{0,1:T(8,128)(2,1)}, bf16[256,1792]{0,1:T(8,128)(2,1)S(1)}, u32[]{:S(2)}, u32[]{:S(2)}) collective-permute-start(bf16[256,1792]{0,1:T(8,128)(2,1)} %pad_maximum_fusion.1), channel_id=1, source_target_pairs={{0,8},{8,16},{16,24},{24,32},{32,40},{40,48},{48,56},{56,64},{64,7... | collective-permute-start | bytes 2752520 | tf_op jit(solution)/shard_map/ppermute | solution.py:34
  13.3 25.4 %collective-permute-start.6 = (bf16[256,1792]{0,1:T(8,128)(2,1)}, bf16[256,1792]{0,1:T(8,128)(2,1)S(1)}, u32[]{:S(2)}, u32[]{:S(2)}) collective-permute-start(bf16[256,1792]{0,1:T(8,128)(2,1)} %pad_maximum_fusion.1), channel_id=1, source_target_pairs={{8,0},{16,8},{24,16},{32,24},{40,32},{48,40},{56,48},{64,56},{72,6... | collective-permute-start | bytes 2752520 | tf_op jit(solution)/shard_map/ppermute | solution.py:34
  31.2 14.3 %collective-permute-start.3 = (bf16[128,1792]{0,1:T(8,128)(2,1)S(1)}, bf16[128,1792]{0,1:T(8,128)(2,1)S(1)}, u32[]{:S(2)}, u32[]{:S(2)}) collective-permute-start(bf16[128,1792]{0,1:T(8,128)(2,1)S(1)} %slice.202), channel_id=1, source_target_pairs={{0,6},{2,0},{4,2},{6,4},{1,7},{3,1},{5,3},{7,5},{8,14},{10,8},{12,... | collective-permute-start | bytes 1376264 | tf_op jit(solution)/shard_map/ppermute | solution.py:39
  35.3 14.7 %collective-permute-start.4 = (bf16[128,1792]{0,1:T(8,128)(2,1)S(1)}, bf16[128,1792]{0,1:T(8,128)(2,1)S(1)}, u32[]{:S(2)}, u32[]{:S(2)}) collective-permute-start(bf16[128,1792]{0,1:T(8,128)(2,1)S(1)} %slice.203), channel_id=1, source_target_pairs={{0,2},{2,4},{4,6},{6,0},{1,3},{3,5},{5,7},{7,1},{8,10},{10,12},{12... | collective-permute-start | bytes 1376264 | tf_op jit(solution)/shard_map/ppermute | solution.py:39
  38.9 24.0 %collective-permute-start.8 = (bf16[256,1792]{0,1:T(8,128)(2,1)S(1)}, bf16[256,1792]{0,1:T(8,128)(2,1)S(1)}, u32[]{:S(2)}, u32[]{:S(2)}) collective-permute-start(bf16[256,1792]{0,1:T(8,128)(2,1)S(1)} %get-tuple-element.17), channel_id=1, source_target_pairs={{0,6},{2,0},{4,2},{6,4},{1,7},{3,1},{5,3},{7,5},{8,14},{10,8},{12,... | collective-permute-start | bytes 2752520 | tf_op jit(solution)/shard_map/ppermute | solution.py:39
  40.5 26.9 %collective-permute-start.9 = (bf16[256,1792]{0,1:T(8,128)(2,1)S(1)}, bf16[256,1792]{0,1:T(8,128)(2,1)S(1)}, u32[]{:S(2)}, u32[]{:S(2)}) collective-permute-start(bf16[256,1792]{0,1:T(8,128)(2,1)S(1)} %get-tuple-element.18), channel_id=1, source_target_pairs={{0,2},{2,4},{4,6},{6,0},{1,3},{3,5},{5,7},{7,1},{8,10},{10,12},{12... | collective-permute-start | bytes 2752520 | tf_op jit(solution)/shard_map/ppermute | solution.py:39
  50.2 23.6 %collective-permute-start.7 = (bf16[256,1792]{0,1:T(8,128)(2,1)S(1)}, bf16[256,1792]{0,1:T(8,128)(2,1)S(1)}, u32[]{:S(2)}, u32[]{:S(2)}) collective-permute-start(bf16[256,1792]{0,1:T(8,128)(2,1)S(1)} %constant_dynamic-update-slice_fusion), channel_id=1, source_target_pairs={{0,8},{1,9},{2,10},{3,11},{8,16},{9,17},{10,18},{11,19},{12,4},{13... | collective-permute-start | bytes 2752520 | tf_op jit(solution)/shard_map/ppermute | solution.py:120
  85.3 1.6 %collective-permute-start.10 = (bf16[128,896]{1,0:T(8,128)(2,1)S(1)}, bf16[128,896]{1,0:T(8,128)(2,1)S(1)}, u32[]{:S(2)}, u32[]{:S(2)}) collective-permute-start(bf16[128,896]{1,0:T(8,128)(2,1)S(1)} %copy.129), channel_id=1, source_target_pairs={{0,1},{1,0},{2,3},{3,2},{4,5},{5,4},{6,7},{7,6},{8,9},{9,8},{10,11... | collective-permute-start | bytes 688136 | tf_op jit(solution)/shard_map/ppermute | solution.py:39
  87.3 11.9 %collective-permute-start.11 = (bf16[32,6656]{1,0:T(8,128)(2,1)S(1)}, bf16[32,6656]{1,0:T(8,128)(2,1)S(1)}, u32[]{:S(2)}, u32[]{:S(2)}) collective-permute-start(bf16[32,6656]{1,0:T(8,128)(2,1)S(1)} %select_n.268), channel_id=1, source_target_pairs={{0,6},{2,0},{4,2},{6,4},{1,7},{3,1},{5,3},{7,5},{8,14},{10,8},{12,... | collective-permute-start | bytes 1277960 | tf_op jit(solution)/shard_map/ppermute | solution.py:39
  87.4 14.0 %collective-permute-start.12 = (bf16[32,6656]{1,0:T(8,128)(2,1)S(1)}, bf16[32,6656]{1,0:T(8,128)(2,1)S(1)}, u32[]{:S(2)}, u32[]{:S(2)}) collective-permute-start(bf16[32,6656]{1,0:T(8,128)(2,1)S(1)} %select_n.268), channel_id=1, source_target_pairs={{0,2},{2,4},{4,6},{6,0},{1,3},{3,5},{5,7},{7,1},{8,10},{10,12},{12... | collective-permute-start | bytes 1277960 | tf_op jit(solution)/shard_map/ppermute | solution.py:39
  99.3 6.8 %collective-permute-start.13 = (bf16[16,6656]{1,0:T(8,128)(2,1)S(1)}, bf16[16,6656]{1,0:T(8,128)(2,1)S(1)}, u32[]{:S(2)}, u32[]{:S(2)}) collective-permute-start(bf16[16,6656]{1,0:T(8,128)(2,1)S(1)} %slice.220), channel_id=1, source_target_pairs={{0,6},{2,0},{4,2},{6,4},{1,7},{3,1},{5,3},{7,5},{8,14},{10,8},{12,... | collective-permute-start | bytes 638984 | tf_op jit(solution)/shard_map/ppermute | solution.py:39
  101.4 7.8 %collective-permute-start.14 = (bf16[16,6656]{1,0:T(8,128)(2,1)S(1)}, bf16[16,6656]{1,0:T(8,128)(2,1)S(1)}, u32[]{:S(2)}, u32[]{:S(2)}) collective-permute-start(bf16[16,6656]{1,0:T(8,128)(2,1)S(1)} %slice.221), channel_id=1, source_target_pairs={{0,2},{2,4},{4,6},{6,0},{1,3},{3,5},{5,7},{7,1},{8,10},{10,12},{12... | collective-permute-start | bytes 638984 | tf_op jit(solution)/shard_map/ppermute | solution.py:39
  110.6 3.8 %collective-permute-start.15 = (bf16[4,32,6656]{2,1,0:T(8,128)(2,1)}, bf16[4,32,6656]{2,1,0:T(8,128)(2,1)S(1)}, u32[]{:S(2)}, u32[]{:S(2)}) collective-permute-start(bf16[4,32,6656]{2,1,0:T(8,128)(2,1)} %pad_maximum_fusion), channel_id=1, source_target_pairs={{0,1},{1,0},{2,3},{3,2},{4,5},{5,4},{6,7},{7,6},{8,9},{9,8},{10,11... | collective-permute-start | bytes 5111816 | tf_op jit(solution)/shard_map/ppermute | solution.py:39
  119.5 1.2 collective-permute-start.16
  120.7 3.7 %collective-permute-start.17 = (f32[2,32]{1,0:T(2,128)S(1)}, f32[2,32]{1,0:T(2,128)S(1)}, u32[]{:S(2)}, u32[]{:S(2)}) collective-permute-start(f32[2,32]{1,0:T(2,128)S(1)} %pad_maximum_fusion.5), channel_id=1, source_target_pairs={{0,2},{1,3},{2,0},{3,1},{4,6},{5,7},{6,4},{7,5},{8,10},{9,11},{10,... | collective-permute-start | bytes 776 | tf_op jit(solution)/shard_map/ppermute | solution.py:49
  124.4 5.2 %collective-permute-start.18 = (f32[2,32]{1,0:T(2,128)S(1)}, f32[2,32]{1,0:T(2,128)S(1)}, u32[]{:S(2)}, u32[]{:S(2)}) collective-permute-start(f32[2,32]{1,0:T(2,128)S(1)} %pad_maximum_fusion.6), channel_id=1, source_target_pairs={{0,4},{1,5},{2,6},{3,7},{4,0},{5,1},{6,2},{7,3},{8,12},{9,13},{10,... | collective-permute-start | bytes 776 | tf_op jit(solution)/shard_map/ppermute | solution.py:49
  129.6 3.7 %collective-permute-start.19 = (f32[2,32]{1,0:T(2,128)S(1)}, f32[2,32]{1,0:T(2,128)S(1)}, u32[]{:S(2)}, u32[]{:S(2)}) collective-permute-start(f32[2,32]{1,0:T(2,128)S(1)} %pad_maximum_fusion.7), channel_id=1, source_target_pairs={{0,8},{1,9},{2,10},{3,11},{4,12},{5,13},{6,14},{7,15},{8,0},{9,1},... | collective-permute-start | bytes 776 | tf_op jit(solution)/shard_map/ppermute | solution.py:49
  133.2 4.6 %collective-permute-start.20 = (f32[2,32]{1,0:T(2,128)S(1)}, f32[2,32]{1,0:T(2,128)S(1)}, u32[]{:S(2)}, u32[]{:S(2)}) collective-permute-start(f32[2,32]{1,0:T(2,128)S(1)} %pad_maximum_fusion.8), channel_id=1, source_target_pairs={{0,16},{1,17},{2,18},{3,19},{4,20},{5,21},{6,22},{7,23},{8,24},{9,... | collective-permute-start | bytes 776 | tf_op jit(solution)/shard_map/ppermute | solution.py:49
  137.8 7.6 %collective-permute-start.21 = (f32[2,32]{1,0:T(2,128)S(1)}, f32[2,32]{1,0:T(2,128)S(1)}, u32[]{:S(2)}, u32[]{:S(2)}) collective-permute-start(f32[2,32]{1,0:T(2,128)S(1)} %pad_maximum_fusion.9), channel_id=1, source_target_pairs={{0,32},{1,33},{2,34},{3,35},{4,36},{5,37},{6,38},{7,39},{8,40},{9,... | collective-permute-start | bytes 776 | tf_op jit(solution)/shard_map/ppermute | solution.py:49
  145.4 3.7 %collective-permute-start.22 = (f32[2,32]{1,0:T(2,128)S(1)}, f32[2,32]{1,0:T(2,128)S(1)}, u32[]{:S(2)}, u32[]{:S(2)}) collective-permute-start(f32[2,32]{1,0:T(2,128)S(1)} %pad_maximum_fusion.10), channel_id=1, source_target_pairs={{0,64},{1,65},{2,66},{3,67},{4,68},{5,69},{6,70},{7,71},{8,72},{9,... | collective-permute-start | bytes 776 | tf_op jit(solution)/shard_map/ppermute | solution.py:49
  149.1 5.2 %collective-permute-start.23 = (f32[2,32]{1,0:T(2,128)S(1)}, f32[2,32]{1,0:T(2,128)S(1)}, u32[]{:S(2)}, u32[]{:S(2)}) collective-permute-start(f32[2,32]{1,0:T(2,128)S(1)} %pad_maximum_fusion.11), channel_id=1, source_target_pairs={{0,128},{1,129},{2,130},{3,131},{4,132},{5,133},{6,134},{7,135},{8... | collective-permute-start | bytes 776 | tf_op jit(solution)/shard_map/ppermute | solution.py:49

commit v8 on v7

--- a/solution.py
+++ b/solution.py
@@ -84,11 +84,14 @@
     q_chip = chip_rows[:, :slot]
     kv_chip = chip_rows[:, slot:]
 
-    from_right = cyclic(kv_chip, "x", -1)
-    from_left = cyclic(kv_chip, "x", 1)
-    relay = jnp.concatenate(
-        [cyclic(from_right[: row_count], "x", -1), cyclic(from_left[row_count:], "x", 1)], axis=0
-    )
+    right_a = cyclic(kv_chip[:row_count], "x", -1)
+    left_b = cyclic(kv_chip[row_count:], "x", 1)
+    right_a, left_b, rest = lax.optimization_barrier((right_a, left_b, kv_chip))
+    right_b = cyclic(rest[row_count:], "x", -1)
+    left_a = cyclic(rest[:row_count], "x", 1)
+    from_right = jnp.concatenate([right_a, right_b], axis=0)
+    from_left = jnp.concatenate([left_a, left_b], axis=0)
+    relay = jnp.concatenate([cyclic(right_a, "x", -1), cyclic(left_b, "x", 1)], axis=0)
     kv_prev = shifted(kv_chip, "blk", 1)
     kv_next = shifted(kv_chip, "blk", -1)
 

time: 156 us -> 151 us (0.968)
  waiting for transfers between devices: 82.4 us -> 76.2 us
  starting transfers between devices: 35.7 us -> 41.6 us
  local copies, waits for them, and re-layouts: 10.7 us -> 6.93 us
    ppermute x8, starting transfers between devices: 8.96 us -> 15.6 us  [butterfly(): other = lax.ppermute(jnp.stack([sums, peaks]), ALL, perm)]
    ppermute x1, waiting for transfers between devices: 5.32 us -> 10.8 us  [per_device(): kv_sets.append(lax.ppermute(far, ALL, pairs))]
    ppermute x8, waiting for transfers between devices: 24.1 us -> 18.8 us  [butterfly(): other = lax.ppermute(jnp.stack([sums, peaks]), ALL, perm)]
    ppermute x2, waiting for transfers between devices: 3.3 us -> 0.01 us  [shifted(): lax.ppermute(x, axis, [(i, i + by) for i in range(n) if 0 <= i + by < n])]
    ppermute x13 -> x15, waiting for transfers between devices: 49.7 us -> 46.6 us  [cyclic(): return lax.ppermute(x, axis, [(i, (i + by) % n) for i in range(n)])]
    slice x7, local copies, waits for them, and re-layouts: 2.74 us -> 0.43 us  [per_device(): value_heads = kv[:, slot:].reshape(kv.shape[0], slot_heads, HEAD)]
    slice x2 -> x3, local copies, waits for them, and re-layouts: 2.1 us -> 0.12 us  [the longest x1 0.06 us: per_device(): right_b = cyclic(rest[row_count:], 'x', -1)]
    ppermute x13 -> x15, starting transfers between devices: 13.1 us -> 12.6 us  [cyclic(): return lax.ppermute(x, axis, [(i, (i + by) % n) for i in range(n)])]
  transfers between devices with their start and end apart: 24 -> 26, of which waited for: 21 -> 20; matrix products, arithmetic and copies ran while one was open for 8% -> 6% of each run, Pallas kernels for 0% -> 0%
where the time goes in v8:
time: 151 us
  waiting for transfers between devices  76.2 us (50%)
  starting transfers between devices  41.6 us (28%)
  matrix products  14.7 us (10%)
  other arithmetic  9.72 us (6%)
  local copies, waits for them, and re-layouts  6.93 us (5%)
    ppermute x15, waiting for transfers between devices, cyclic(): return lax.ppermute(x, axis, [(i, (i + by) % n) for i in range(n)])  46.6 us
    ppermute x8, waiting for transfers between devices, butterfly(): other = lax.ppermute(jnp.stack([sums, peaks]), ALL, perm)  18.8 us
    ppermute x8, starting transfers between devices, butterfly(): other = lax.ppermute(jnp.stack([sums, peaks]), ALL, perm)  15.6 us
    ppermute x15, starting transfers between devices, cyclic(): return lax.ppermute(x, axis, [(i, (i + by) % n) for i in range(n)])  12.6 us
    ppermute x1, waiting for transfers between devices, per_device(): kv_sets.append(lax.ppermute(far, ALL, pairs))  10.8 us
    ppermute x2, starting transfers between devices, shifted(): lax.ppermute(x, axis, [(i, i + by) for i in range(n) if 0 <= i + by < n])  9.57 us
    dot_general x9, matrix products, per_device(): jnp.einsum('hrk,khd->rhd', exp_terms.astype(jnp.bfloat16), value_heads, p...  5.66 us
    reduce_sum x1, other arithmetic, per_device(): total = jnp.sum(exp_terms, axis=2)  4.9 us
  transfers between devices with their start and end apart: 26, of which 20 were waited for; matrix products, arithmetic and copies ran while one was open for 6% of the time, Pallas kernels for 0%

profile of v8, /device:TPU:8, one launch (start us, length us, event | category | flops | bytes accessed | tf_op | source)
XLA Modules:
  0.0 150.6 jit_solution(1152439122248605265)
XLA Ops:
  5.3 2.8 %collective-permute-start.1 = (bf16[128,1792]{0,1:T(8,128)(2,1)S(1)}, bf16[128,1792]{0,1:T(8,128)(2,1)S(1)}, u32[]{:S(2)}, u32[]{:S(2)}) collective-permute-start(bf16[128,1792]{0,1:T(8,128)(2,1)S(1)} %slice.212), channel_id=1, source_target_pairs={{0,6},{2,0},{4,2},{6,4},{1,7},{3,1},{5,3},{7,5},{8,14},{10,8},{12,... | collective-permute-start | bytes 1376264 | tf_op jit(solution)/shard_map/ppermute | solution.py:39
  8.4 3.8 %collective-permute-start.7 = (bf16[256,1792]{0,1:T(8,128)(2,1)S(1)}, bf16[256,1792]{0,1:T(8,128)(2,1)S(1)}, u32[]{:S(2)}, u32[]{:S(2)}) collective-permute-start(bf16[256,1792]{0,1:T(8,128)(2,1)S(1)} %pad_maximum_fusion.1), channel_id=1, source_target_pairs={{0,8},{8,16},{16,24},{24,32},{32,40},{40,48},{48,56},{56,64},{64,7... | collective-permute-start | bytes 2752520 | tf_op jit(solution)/shard_map/ppermute | solution.py:34
  12.2 5.7 %collective-permute-start.8 = (bf16[256,1792]{0,1:T(8,128)(2,1)S(1)}, bf16[256,1792]{0,1:T(8,128)(2,1)S(1)}, u32[]{:S(2)}, u32[]{:S(2)}) collective-permute-start(bf16[256,1792]{0,1:T(8,128)(2,1)S(1)} %pad_maximum_fusion.1), channel_id=1, source_target_pairs={{8,0},{16,8},{24,16},{32,24},{40,32},{48,40},{56,48},{64,56},{72,6... | collective-permute-start | bytes 2752520 | tf_op jit(solution)/shard_map/ppermute | solution.py:34
  18.6 3.1 %collective-permute-done.2 = bf16[128,1792]{0,1:T(8,128)(2,1)S(1)} collective-permute-done((bf16[128,1792]{0,1:T(8,128)(2,1)S(1)}, bf16[128,1792]{0,1:T(8,128)(2,1)S(1)}, u32[]{:S(2)}, u32[]{:S(2)}) %collective-permute-start.2) | collective-permute-done | bytes 458784 | tf_op jit(solution)/shard_map/ppermute | solution.py:39
  22.1 2.0 %collective-permute-start.6 = (bf16[128,1792]{0,1:T(8,128)(2,1)S(1)}, bf16[128,1792]{0,1:T(8,128)(2,1)S(1)}, u32[]{:S(2)}, u32[]{:S(2)}) collective-permute-start(bf16[128,1792]{0,1:T(8,128)(2,1)S(1)} %collective-permute-done.2), channel_id=1, source_target_pairs={{0,2},{2,4},{4,6},{6,0},{1,3},{3,5},{5,7},{7,1},{8,10},{10,12},{12... | collective-permute-start | bytes 1376264 | tf_op jit(solution)/shard_map/ppermute | solution.py:39
  24.2 11.0 %collective-permute-done.5 = bf16[128,1792]{0,1:T(8,128)(2,1)S(1)} collective-permute-done((bf16[128,1792]{0,1:T(8,128)(2,1)S(1)}, bf16[128,1792]{0,1:T(8,128)(2,1)S(1)}, u32[]{:S(2)}, u32[]{:S(2)}) %collective-permute-start.5) | collective-permute-done | bytes 458784 | tf_op jit(solution)/shard_map/ppermute | solution.py:39
  35.4 3.8 %collective-permute-start.9 = (bf16[256,1792]{0,1:T(8,128)(2,1)S(1)}, bf16[256,1792]{0,1:T(8,128)(2,1)S(1)}, u32[]{:S(2)}, u32[]{:S(2)}) collective-permute-start(bf16[256,1792]{0,1:T(8,128)(2,1)S(1)} %constant_dynamic-update-slice_fusion.4), channel_id=1, source_target_pairs={{0,8},{1,9},{2,10},{3,11},{8,16},{9,17},{10,18},{11,19},{12,4},{13... | collective-permute-start | bytes 2752520 | tf_op jit(solution)/shard_map/ppermute | solution.py:123
  39.2 5.6 %collective-permute-done.4 = bf16[128,1792]{0,1:T(8,128)(2,1)S(1)} collective-permute-done((bf16[128,1792]{0,1:T(8,128)(2,1)S(1)}, bf16[128,1792]{0,1:T(8,128)(2,1)S(1)}, u32[]{:S(2)}, u32[]{:S(2)}) %collective-permute-start.4) | collective-permute-done | bytes 458784 | tf_op jit(solution)/shard_map/ppermute | solution.py:39
  45.6 1.5 %collective-permute-start.10 = (bf16[256,1792]{0,1:T(8,128)(2,1)S(1)}, bf16[256,1792]{0,1:T(8,128)(2,1)S(1)}, u32[]{:S(2)}, u32[]{:S(2)}) collective-permute-start(bf16[256,1792]{0,1:T(8,128)(2,1)S(1)} %get-tuple-element.23), channel_id=1, source_target_pairs={{0,6},{2,0},{4,2},{6,4},{1,7},{3,1},{5,3},{7,5},{8,14},{10,8},{12,... | collective-permute-start | bytes 2752520 | tf_op jit(solution)/shard_map/ppermute | solution.py:39
  50.3 10.8 %collective-permute-done.9 = bf16[256,1792]{0,1:T(8,128)(2,1)S(1)} collective-permute-done((bf16[256,1792]{0,1:T(8,128)(2,1)S(1)}, bf16[256,1792]{0,1:T(8,128)(2,1)S(1)}, u32[]{:S(2)}, u32[]{:S(2)}) %collective-permute-start.9) | collective-permute-done | bytes 917536 | tf_op jit(solution)/shard_map/ppermute | solution.py:123
  61.2 2.6 %collective-permute-done.10 = bf16[256,1792]{0,1:T(8,128)(2,1)S(1)} collective-permute-done((bf16[256,1792]{0,1:T(8,128)(2,1)S(1)}, bf16[256,1792]{0,1:T(8,128)(2,1)S(1)}, u32[]{:S(2)}, u32[]{:S(2)}) %collective-permute-start.10) | collective-permute-done | bytes 917536 | tf_op jit(solution)/shard_map/ppermute | solution.py:39
  64.9 1.9 %collective-permute-done.11 = bf16[256,1792]{0,1:T(8,128)(2,1)S(1)} collective-permute-done((bf16[256,1792]{0,1:T(8,128)(2,1)S(1)}, bf16[256,1792]{0,1:T(8,128)(2,1)S(1)}, u32[]{:S(2)}, u32[]{:S(2)}) %collective-permute-start.11) | collective-permute-done | bytes 917536 | tf_op jit(solution)/shard_map/ppermute | solution.py:39
  71.0 4.9 %fusion.18 = (f32[7,256]{1,0:T(8,128)S(1)}, f32[7,256]{1,0:T(8,128)S(1)}, f32[7,256]{1,0:T(8,128)S(1)}, f32[7,256]{1,0:T(8,128)S(1)}, f32[7,256]{1,0:T(8,128)S(1...) fusion(f32[7,256,256]{1,2,0:T(8,128)S(1)} %get-tuple-element.107, ...), kind=kLoop, calls=%fused_computation.45 | loop fusion | flops 20627712 | bytes 17176576 | tf_op jit(solution)/shard_map/reduce_sum | solution.py:162
  80.2 1.7 %collective-permute-start.13 = (bf16[32,6656]{1,0:T(8,128)(2,1)S(1)}, bf16[32,6656]{1,0:T(8,128)(2,1)S(1)}, u32[]{:S(2)}, u32[]{:S(2)}) collective-permute-start(bf16[32,6656]{1,0:T(8,128)(2,1)S(1)} %select_n.268), channel_id=1, source_target_pairs={{0,6},{2,0},{4,2},{6,4},{1,7},{3,1},{5,3},{7,5},{8,14},{10,8},{12,... | collective-permute-start | bytes 1277960 | tf_op jit(solution)/shard_map/ppermute | solution.py:39
  82.6 9.8 %collective-permute-done.13 = bf16[32,6656]{1,0:T(8,128)(2,1)S(1)} collective-permute-done((bf16[32,6656]{1,0:T(8,128)(2,1)S(1)}, bf16[32,6656]{1,0:T(8,128)(2,1)S(1)}, u32[]{:S(2)}, u32[]{:S(2)}) %collective-permute-start.13) | collective-permute-done | bytes 426016 | tf_op jit(solution)/shard_map/ppermute | solution.py:39
  92.4 2.7 %collective-permute-start.15 = (bf16[16,6656]{1,0:T(8,128)(2,1)S(1)}, bf16[16,6656]{1,0:T(8,128)(2,1)S(1)}, u32[]{:S(2)}, u32[]{:S(2)}) collective-permute-start(bf16[16,6656]{1,0:T(8,128)(2,1)S(1)} %slice.232), channel_id=1, source_target_pairs={{0,6},{2,0},{4,2},{6,4},{1,7},{3,1},{5,3},{7,5},{8,14},{10,8},{12,... | collective-permute-start | bytes 638984 | tf_op jit(solution)/shard_map/ppermute | solution.py:39
  95.5 3.6 %collective-permute-done.15 = bf16[16,6656]{1,0:T(8,128)(2,1)S(1)} collective-permute-done((bf16[16,6656]{1,0:T(8,128)(2,1)S(1)}, bf16[16,6656]{1,0:T(8,128)(2,1)S(1)}, u32[]{:S(2)}, u32[]{:S(2)}) %collective-permute-start.15) | collective-permute-done | bytes 213024 | tf_op jit(solution)/shard_map/ppermute | solution.py:39
  99.1 3.8 %collective-permute-done.16 = bf16[16,6656]{1,0:T(8,128)(2,1)S(1)} collective-permute-done((bf16[16,6656]{1,0:T(8,128)(2,1)S(1)}, bf16[16,6656]{1,0:T(8,128)(2,1)S(1)}, u32[]{:S(2)}, u32[]{:S(2)}) %collective-permute-start.16) | collective-permute-done | bytes 213024 | tf_op jit(solution)/shard_map/ppermute | solution.py:39
  102.9 1.4 pad_maximum_fusion
  104.9 3.3 %collective-permute-done.17 = bf16[4,32,6656]{2,1,0:T(8,128)(2,1)S(1)} collective-permute-done((bf16[4,32,6656]{2,1,0:T(8,128)(2,1)}, bf16[4,32,6656]{2,1,0:T(8,128)(2,1)S(1)}, u32[]{:S(2)}, u32[]{:S(2)}) %collective-permute-start.17) | collective-permute-done | bytes 1703968 | tf_op jit(solution)/shard_map/ppermute | solution.py:39
  108.4 4.6 %multiply_reduce_fusion = (f32[256]{0:T(256)S(1)}, f32[256]{0:T(256)S(1)}, f32[256,384]{1,0:T(8,128)S(1)}) fusion(bf16[256,6656]{1,0:T(8,128)(2,1)S(1)} %fusion.102, bf16[6656,384]{1,0:T(8,128)(2,1)} %param.9), kind=kOutput, calls=%fused_computation.137 | convolution fusion | flops 1308917248 | bytes 8914944 | tf_op jit(solution)/shard_map/dot_general | solution.py:196
  114.5 3.6 %collective-permute-done.19 = f32[2,32]{1,0:T(2,128)S(1)} collective-permute-done((f32[2,32]{1,0:T(2,128)S(1)}, f32[2,32]{1,0:T(2,128)S(1)}, u32[]{:S(2)}, u32[]{:S(2)}) %collective-permute-start.19) | collective-permute-done | bytes 288 | tf_op jit(solution)/shard_map/ppermute | solution.py:49
  118.2 5.1 %collective-permute-done.20 = f32[2,32]{1,0:T(2,128)S(1)} collective-permute-done((f32[2,32]{1,0:T(2,128)S(1)}, f32[2,32]{1,0:T(2,128)S(1)}, u32[]{:S(2)}, u32[]{:S(2)}) %collective-permute-start.20) | collective-permute-done | bytes 288 | tf_op jit(solution)/shard_map/ppermute | solution.py:49
  123.2 2.0 %collective-permute-start.21 = (f32[2,32]{1,0:T(2,128)S(1)}, f32[2,32]{1,0:T(2,128)S(1)}, u32[]{:S(2)}, u32[]{:S(2)}) collective-permute-start(f32[2,32]{1,0:T(2,128)S(1)} %pad_maximum_fusion.7), channel_id=1, source_target_pairs={{0,8},{1,9},{2,10},{3,11},{4,12},{5,13},{6,14},{7,15},{8,0},{9,1},... | collective-permute-start | bytes 776 | tf_op jit(solution)/shard_map/ppermute | solution.py:49
  125.2 1.7 %collective-permute-done.21 = f32[2,32]{1,0:T(2,128)S(1)} collective-permute-done((f32[2,32]{1,0:T(2,128)S(1)}, f32[2,32]{1,0:T(2,128)S(1)}, u32[]{:S(2)}, u32[]{:S(2)}) %collective-permute-start.21) | collective-permute-done | bytes 288 | tf_op jit(solution)/shard_map/ppermute | solution.py:49
  126.9 3.3 %collective-permute-start.22 = (f32[2,32]{1,0:T(2,128)S(1)}, f32[2,32]{1,0:T(2,128)S(1)}, u32[]{:S(2)}, u32[]{:S(2)}) collective-permute-start(f32[2,32]{1,0:T(2,128)S(1)} %pad_maximum_fusion.8), channel_id=1, source_target_pairs={{0,16},{1,17},{2,18},{3,19},{4,20},{5,21},{6,22},{7,23},{8,24},{9,... | collective-permute-start | bytes 776 | tf_op jit(solution)/shard_map/ppermute | solution.py:49
  130.3 1.5 %collective-permute-done.22 = f32[2,32]{1,0:T(2,128)S(1)} collective-permute-done((f32[2,32]{1,0:T(2,128)S(1)}, f32[2,32]{1,0:T(2,128)S(1)}, u32[]{:S(2)}, u32[]{:S(2)}) %collective-permute-start.22) | collective-permute-done | bytes 288 | tf_op jit(solution)/shard_map/ppermute | solution.py:49
  131.8 6.9 %collective-permute-start.23 = (f32[2,32]{1,0:T(2,128)S(1)}, f32[2,32]{1,0:T(2,128)S(1)}, u32[]{:S(2)}, u32[]{:S(2)}) collective-permute-start(f32[2,32]{1,0:T(2,128)S(1)} %pad_maximum_fusion.9), channel_id=1, source_target_pairs={{0,32},{1,33},{2,34},{3,35},{4,36},{5,37},{6,38},{7,39},{8,40},{9,... | collective-permute-start | bytes 776 | tf_op jit(solution)/shard_map/ppermute | solution.py:49
  138.8 1.5 %collective-permute-done.23 = f32[2,32]{1,0:T(2,128)S(1)} collective-permute-done((f32[2,32]{1,0:T(2,128)S(1)}, f32[2,32]{1,0:T(2,128)S(1)}, u32[]{:S(2)}, u32[]{:S(2)}) %collective-permute-start.23) | collective-permute-done | bytes 288 | tf_op jit(solution)/shard_map/ppermute | solution.py:49
  142.1 1.9 %collective-permute-done.24 = f32[2,32]{1,0:T(2,128)S(1)} collective-permute-done((f32[2,32]{1,0:T(2,128)S(1)}, f32[2,32]{1,0:T(2,128)S(1)}, u32[]{:S(2)}, u32[]{:S(2)}) %collective-permute-start.24) | collective-permute-done | bytes 288 | tf_op jit(solution)/shard_map/ppermute | solution.py:49
  144.0 2.4 %collective-permute-start.25 = (f32[2,32]{1,0:T(2,128)S(1)}, f32[2,32]{1,0:T(2,128)S(1)}, u32[]{:S(2)}, u32[]{:S(2)}) collective-permute-start(f32[2,32]{1,0:T(2,128)S(1)} %pad_maximum_fusion.11), channel_id=1, source_target_pairs={{0,128},{1,129},{2,130},{3,131},{4,132},{5,133},{6,134},{7,135},{8... | collective-permute-start | bytes 776 | tf_op jit(solution)/shard_map/ppermute | solution.py:49
  146.6 2.5 %collective-permute-done.25 = f32[2,32]{1,0:T(2,128)S(1)} collective-permute-done((f32[2,32]{1,0:T(2,128)S(1)}, f32[2,32]{1,0:T(2,128)S(1)}, u32[]{:S(2)}, u32[]{:S(2)}) %collective-permute-start.25) | collective-permute-done | bytes 288 | tf_op jit(solution)/shard_map/ppermute | solution.py:49
  (126 shorter events, 26.2 us)
Async XLA Ops:
  0.6 1.8 %copy-start = (bf16[128,1664]{1,0:T(8,128)(2,1)S(1)}, bf16[128,1664]{1,0:T(8,128)(2,1)}, u32[]{:S(2)}) copy-start(bf16[128,1664]{1,0:T(8,128)(2,1)} %param.5) | copy-start | bytes 1277956
  2.0 0.9 copy-start.1
  2.7 2.2 %collective-permute-start = (bf16[128,2688]{0,1:T(8,128)(2,1)S(1)}, bf16[128,2688]{0,1:T(8,128)(2,1)S(1)}, u32[]{:S(2)}, u32[]{:S(2)}) collective-permute-start(bf16[128,2688]{0,1:T(8,128)(2,1)S(1)} %pad_maximum_fusion.3), channel_id=1, source_target_pairs={{0,1},{1,0},{2,3},{3,2},{4,5},{5,4},{6,7},{7,6},{8,9},{9,8},{10,11... | collective-permute-start | bytes 2064392 | tf_op jit(solution)/shard_map/ppermute | solution.py:39
  5.3 13.3 %collective-permute-start.1 = (bf16[128,1792]{0,1:T(8,128)(2,1)S(1)}, bf16[128,1792]{0,1:T(8,128)(2,1)S(1)}, u32[]{:S(2)}, u32[]{:S(2)}) collective-permute-start(bf16[128,1792]{0,1:T(8,128)(2,1)S(1)} %slice.212), channel_id=1, source_target_pairs={{0,6},{2,0},{4,2},{6,4},{1,7},{3,1},{5,3},{7,5},{8,14},{10,8},{12,... | collective-permute-start | bytes 1376264 | tf_op jit(solution)/shard_map/ppermute | solution.py:39
  8.2 13.6 %collective-permute-start.2 = (bf16[128,1792]{0,1:T(8,128)(2,1)S(1)}, bf16[128,1792]{0,1:T(8,128)(2,1)S(1)}, u32[]{:S(2)}, u32[]{:S(2)}) collective-permute-start(bf16[128,1792]{0,1:T(8,128)(2,1)S(1)} %slice.213), channel_id=1, source_target_pairs={{0,2},{2,4},{4,6},{6,0},{1,3},{3,5},{5,7},{7,1},{8,10},{10,12},{12... | collective-permute-start | bytes 1376264 | tf_op jit(solution)/shard_map/ppermute | solution.py:39
  8.4 37.1 %collective-permute-start.7 = (bf16[256,1792]{0,1:T(8,128)(2,1)S(1)}, bf16[256,1792]{0,1:T(8,128)(2,1)S(1)}, u32[]{:S(2)}, u32[]{:S(2)}) collective-permute-start(bf16[256,1792]{0,1:T(8,128)(2,1)S(1)} %pad_maximum_fusion.1), channel_id=1, source_target_pairs={{0,8},{8,16},{16,24},{24,32},{32,40},{40,48},{48,56},{56,64},{64,7... | collective-permute-start | bytes 2752520 | tf_op jit(solution)/shard_map/ppermute | solution.py:34
  12.2 33.2 %collective-permute-start.8 = (bf16[256,1792]{0,1:T(8,128)(2,1)S(1)}, bf16[256,1792]{0,1:T(8,128)(2,1)S(1)}, u32[]{:S(2)}, u32[]{:S(2)}) collective-permute-start(bf16[256,1792]{0,1:T(8,128)(2,1)S(1)} %pad_maximum_fusion.1), channel_id=1, source_target_pairs={{8,0},{16,8},{24,16},{32,24},{40,32},{48,40},{56,48},{64,56},{72,6... | collective-permute-start | bytes 2752520 | tf_op jit(solution)/shard_map/ppermute | solution.py:34
  21.7 13.5 %collective-permute-start.5 = (bf16[128,1792]{0,1:T(8,128)(2,1)S(1)}, bf16[128,1792]{0,1:T(8,128)(2,1)S(1)}, u32[]{:S(2)}, u32[]{:S(2)}) collective-permute-start(bf16[128,1792]{0,1:T(8,128)(2,1)S(1)} %collective-permute-done.1), channel_id=1, source_target_pairs={{0,6},{2,0},{4,2},{6,4},{1,7},{3,1},{5,3},{7,5},{8,14},{10,8},{12,... | collective-permute-start | bytes 1376264 | tf_op jit(solution)/shard_map/ppermute | solution.py:39
  22.0 23.1 %collective-permute-start.3 = (bf16[128,1792]{0,1:T(8,128)(2,1)S(1)}, bf16[128,1792]{0,1:T(8,128)(2,1)S(1)}, u32[]{:S(2)}, u32[]{:S(2)}) collective-permute-start(bf16[128,1792]{0,1:T(8,128)(2,1)S(1)} %get-tuple-element.44), channel_id=1, source_target_pairs={{0,6},{2,0},{4,2},{6,4},{1,7},{3,1},{5,3},{7,5},{8,14},{10,8},{12,... | collective-permute-start | bytes 1376264 | tf_op jit(solution)/shard_map/ppermute | solution.py:39
  22.1 13.2 %collective-permute-start.6 = (bf16[128,1792]{0,1:T(8,128)(2,1)S(1)}, bf16[128,1792]{0,1:T(8,128)(2,1)S(1)}, u32[]{:S(2)}, u32[]{:S(2)}) collective-permute-start(bf16[128,1792]{0,1:T(8,128)(2,1)S(1)} %collective-permute-done.2), channel_id=1, source_target_pairs={{0,2},{2,4},{4,6},{6,0},{1,3},{3,5},{5,7},{7,1},{8,10},{10,12},{12... | collective-permute-start | bytes 1376264 | tf_op jit(solution)/shard_map/ppermute | solution.py:39
  35.2 9.7 %collective-permute-start.4 = (bf16[128,1792]{0,1:T(8,128)(2,1)S(1)}, bf16[128,1792]{0,1:T(8,128)(2,1)S(1)}, u32[]{:S(2)}, u32[]{:S(2)}) collective-permute-start(bf16[128,1792]{0,1:T(8,128)(2,1)S(1)} %get-tuple-element.45), channel_id=1, source_target_pairs={{0,2},{2,4},{4,6},{6,0},{1,3},{3,5},{5,7},{7,1},{8,10},{10,12},{12... | collective-permute-start | bytes 1376264 | tf_op jit(solution)/shard_map/ppermute | solution.py:39
  35.4 25.8 %collective-permute-start.9 = (bf16[256,1792]{0,1:T(8,128)(2,1)S(1)}, bf16[256,1792]{0,1:T(8,128)(2,1)S(1)}, u32[]{:S(2)}, u32[]{:S(2)}) collective-permute-start(bf16[256,1792]{0,1:T(8,128)(2,1)S(1)} %constant_dynamic-update-slice_fusion.4), channel_id=1, source_target_pairs={{0,8},{1,9},{2,10},{3,11},{8,16},{9,17},{10,18},{11,19},{12,4},{13... | collective-permute-start | bytes 2752520 | tf_op jit(solution)/shard_map/ppermute | solution.py:123
  45.6 18.3 %collective-permute-start.10 = (bf16[256,1792]{0,1:T(8,128)(2,1)S(1)}, bf16[256,1792]{0,1:T(8,128)(2,1)S(1)}, u32[]{:S(2)}, u32[]{:S(2)}) collective-permute-start(bf16[256,1792]{0,1:T(8,128)(2,1)S(1)} %get-tuple-element.23), channel_id=1, source_target_pairs={{0,6},{2,0},{4,2},{6,4},{1,7},{3,1},{5,3},{7,5},{8,14},{10,8},{12,... | collective-permute-start | bytes 2752520 | tf_op jit(solution)/shard_map/ppermute | solution.py:39
  47.1 19.7 %collective-permute-start.11 = (bf16[256,1792]{0,1:T(8,128)(2,1)S(1)}, bf16[256,1792]{0,1:T(8,128)(2,1)S(1)}, u32[]{:S(2)}, u32[]{:S(2)}) collective-permute-start(bf16[256,1792]{0,1:T(8,128)(2,1)S(1)} %get-tuple-element.24), channel_id=1, source_target_pairs={{0,2},{2,4},{4,6},{6,0},{1,3},{3,5},{5,7},{7,1},{8,10},{10,12},{12... | collective-permute-start | bytes 2752520 | tf_op jit(solution)/shard_map/ppermute | solution.py:39
  78.2 1.6 %collective-permute-start.12 = (bf16[128,896]{1,0:T(8,128)(2,1)S(1)}, bf16[128,896]{1,0:T(8,128)(2,1)S(1)}, u32[]{:S(2)}, u32[]{:S(2)}) collective-permute-start(bf16[128,896]{1,0:T(8,128)(2,1)S(1)} %copy.129), channel_id=1, source_target_pairs={{0,1},{1,0},{2,3},{3,2},{4,5},{5,4},{6,7},{7,6},{8,9},{9,8},{10,11... | collective-permute-start | bytes 688136 | tf_op jit(solution)/shard_map/ppermute | solution.py:39
  80.2 12.2 %collective-permute-start.13 = (bf16[32,6656]{1,0:T(8,128)(2,1)S(1)}, bf16[32,6656]{1,0:T(8,128)(2,1)S(1)}, u32[]{:S(2)}, u32[]{:S(2)}) collective-permute-start(bf16[32,6656]{1,0:T(8,128)(2,1)S(1)} %select_n.268), channel_id=1, source_target_pairs={{0,6},{2,0},{4,2},{6,4},{1,7},{3,1},{5,3},{7,5},{8,14},{10,8},{12,... | collective-permute-start | bytes 1277960 | tf_op jit(solution)/shard_map/ppermute | solution.py:39
  81.9 13.5 %collective-permute-start.14 = (bf16[32,6656]{1,0:T(8,128)(2,1)S(1)}, bf16[32,6656]{1,0:T(8,128)(2,1)S(1)}, u32[]{:S(2)}, u32[]{:S(2)}) collective-permute-start(bf16[32,6656]{1,0:T(8,128)(2,1)S(1)} %select_n.268), channel_id=1, source_target_pairs={{0,2},{2,4},{4,6},{6,0},{1,3},{3,5},{5,7},{7,1},{8,10},{10,12},{12... | collective-permute-start | bytes 1277960 | tf_op jit(solution)/shard_map/ppermute | solution.py:39
  92.4 6.6 %collective-permute-start.15 = (bf16[16,6656]{1,0:T(8,128)(2,1)S(1)}, bf16[16,6656]{1,0:T(8,128)(2,1)S(1)}, u32[]{:S(2)}, u32[]{:S(2)}) collective-permute-start(bf16[16,6656]{1,0:T(8,128)(2,1)S(1)} %slice.232), channel_id=1, source_target_pairs={{0,6},{2,0},{4,2},{6,4},{1,7},{3,1},{5,3},{7,5},{8,14},{10,8},{12,... | collective-permute-start | bytes 638984 | tf_op jit(solution)/shard_map/ppermute | solution.py:39
  95.4 7.5 %collective-permute-start.16 = (bf16[16,6656]{1,0:T(8,128)(2,1)S(1)}, bf16[16,6656]{1,0:T(8,128)(2,1)S(1)}, u32[]{:S(2)}, u32[]{:S(2)}) collective-permute-start(bf16[16,6656]{1,0:T(8,128)(2,1)S(1)} %slice.233), channel_id=1, source_target_pairs={{0,2},{2,4},{4,6},{6,0},{1,3},{3,5},{5,7},{7,1},{8,10},{10,12},{12... | collective-permute-start | bytes 638984 | tf_op jit(solution)/shard_map/ppermute | solution.py:39
  104.3 3.8 %collective-permute-start.17 = (bf16[4,32,6656]{2,1,0:T(8,128)(2,1)}, bf16[4,32,6656]{2,1,0:T(8,128)(2,1)S(1)}, u32[]{:S(2)}, u32[]{:S(2)}) collective-permute-start(bf16[4,32,6656]{2,1,0:T(8,128)(2,1)} %pad_maximum_fusion), channel_id=1, source_target_pairs={{0,1},{1,0},{2,3},{3,2},{4,5},{5,4},{6,7},{7,6},{8,9},{9,8},{10,11... | collective-permute-start | bytes 5111816 | tf_op jit(solution)/shard_map/ppermute | solution.py:39
  113.2 1.2 collective-permute-start.18
  114.4 3.7 %collective-permute-start.19 = (f32[2,32]{1,0:T(2,128)S(1)}, f32[2,32]{1,0:T(2,128)S(1)}, u32[]{:S(2)}, u32[]{:S(2)}) collective-permute-start(f32[2,32]{1,0:T(2,128)S(1)} %pad_maximum_fusion.5), channel_id=1, source_target_pairs={{0,2},{1,3},{2,0},{3,1},{4,6},{5,7},{6,4},{7,5},{8,10},{9,11},{10,... | collective-permute-start | bytes 776 | tf_op jit(solution)/shard_map/ppermute | solution.py:49
  118.1 5.2 %collective-permute-start.20 = (f32[2,32]{1,0:T(2,128)S(1)}, f32[2,32]{1,0:T(2,128)S(1)}, u32[]{:S(2)}, u32[]{:S(2)}) collective-permute-start(f32[2,32]{1,0:T(2,128)S(1)} %pad_maximum_fusion.6), channel_id=1, source_target_pairs={{0,4},{1,5},{2,6},{3,7},{4,0},{5,1},{6,2},{7,3},{8,12},{9,13},{10,... | collective-permute-start | bytes 776 | tf_op jit(solution)/shard_map/ppermute | solution.py:49
  123.2 3.7 %collective-permute-start.21 = (f32[2,32]{1,0:T(2,128)S(1)}, f32[2,32]{1,0:T(2,128)S(1)}, u32[]{:S(2)}, u32[]{:S(2)}) collective-permute-start(f32[2,32]{1,0:T(2,128)S(1)} %pad_maximum_fusion.7), channel_id=1, source_target_pairs={{0,8},{1,9},{2,10},{3,11},{4,12},{5,13},{6,14},{7,15},{8,0},{9,1},... | collective-permute-start | bytes 776 | tf_op jit(solution)/shard_map/ppermute | solution.py:49
  126.9 4.9 %collective-permute-start.22 = (f32[2,32]{1,0:T(2,128)S(1)}, f32[2,32]{1,0:T(2,128)S(1)}, u32[]{:S(2)}, u32[]{:S(2)}) collective-permute-start(f32[2,32]{1,0:T(2,128)S(1)} %pad_maximum_fusion.8), channel_id=1, source_target_pairs={{0,16},{1,17},{2,18},{3,19},{4,20},{5,21},{6,22},{7,23},{8,24},{9,... | collective-permute-start | bytes 776 | tf_op jit(solution)/shard_map/ppermute | solution.py:49
  131.8 8.5 %collective-permute-start.23 = (f32[2,32]{1,0:T(2,128)S(1)}, f32[2,32]{1,0:T(2,128)S(1)}, u32[]{:S(2)}, u32[]{:S(2)}) collective-permute-start(f32[2,32]{1,0:T(2,128)S(1)} %pad_maximum_fusion.9), channel_id=1, source_target_pairs={{0,32},{1,33},{2,34},{3,35},{4,36},{5,37},{6,38},{7,39},{8,40},{9,... | collective-permute-start | bytes 776 | tf_op jit(solution)/shard_map/ppermute | solution.py:49
  140.3 3.7 %collective-permute-start.24 = (f32[2,32]{1,0:T(2,128)S(1)}, f32[2,32]{1,0:T(2,128)S(1)}, u32[]{:S(2)}, u32[]{:S(2)}) collective-permute-start(f32[2,32]{1,0:T(2,128)S(1)} %pad_maximum_fusion.10), channel_id=1, source_target_pairs={{0,64},{1,65},{2,66},{3,67},{4,68},{5,69},{6,70},{7,71},{8,72},{9,... | collective-permute-start | bytes 776 | tf_op jit(solution)/shard_map/ppermute | solution.py:49
  144.0 5.2 %collective-permute-start.25 = (f32[2,32]{1,0:T(2,128)S(1)}, f32[2,32]{1,0:T(2,128)S(1)}, u32[]{:S(2)}, u32[]{:S(2)}) collective-permute-start(f32[2,32]{1,0:T(2,128)S(1)} %pad_maximum_fusion.11), channel_id=1, source_target_pairs={{0,128},{1,129},{2,130},{3,131},{4,132},{5,133},{6,134},{7,135},{8... | collective-permute-start | bytes 776 | tf_op jit(solution)/shard_map/ppermute | solution.py:49

commit v9 on v8

--- a/solution.py
+++ b/solution.py
@@ -152,21 +152,34 @@
         value_heads = kv[:, slot:].reshape(kv.shape[0], slot_heads, HEAD)
         scores = jnp.where(allowed[None], key_scores(query_heads, key_heads), masked_score)
         blocks.append((scores, allowed, value_heads))
-    row_top = blocks[0][0].max(axis=2, keepdims=True)
-    for scores, _, _ in blocks[1:]:
-        row_top = jnp.maximum(row_top, scores.max(axis=2, keepdims=True))
-    row_total = None
-    mixed_out = None
-    for scores, allowed, value_heads in blocks:
-        exp_terms = jnp.where(allowed[None], jnp.exp(scores - row_top), 0.0)
-        total = jnp.sum(exp_terms, axis=2)
-        part = jnp.einsum(
-            "hrk,khd->rhd", exp_terms.astype(jnp.bfloat16), value_heads,
-            preferred_element_type=jnp.float32,
-        )
-        row_total = total if row_total is None else row_total + total
-        mixed_out = part if mixed_out is None else mixed_out + part
-    row_total = jnp.maximum(row_total, 1.0)
+    def accumulate(group, row_top):
+        row_total = None
+        mixed_out = None
+        for scores, allowed, value_heads in group:
+            exp_terms = jnp.where(allowed[None], jnp.exp(scores - row_top), 0.0)
+            total = jnp.sum(exp_terms, axis=2)
+            part = jnp.einsum(
+                "hrk,khd->rhd", exp_terms.astype(jnp.bfloat16), value_heads,
+                preferred_element_type=jnp.float32,
+            )
+            row_total = total if row_total is None else row_total + total
+            mixed_out = part if mixed_out is None else mixed_out + part
+        return row_total, mixed_out
+
+    def group_top(group):
+        top = group[0][0].max(axis=2, keepdims=True)
+        for scores, _, _ in group[1:]:
+            top = jnp.maximum(top, scores.max(axis=2, keepdims=True))
+        return top
+
+    early, late = blocks[:6], blocks[6:]
+    early_top = group_top(early)
+    early_total, early_out = accumulate(early, early_top)
+    row_top = jnp.maximum(early_top, group_top(late))
+    late_total, late_out = accumulate(late, row_top)
+    rescale = jnp.exp(early_top - row_top)
+    row_total = jnp.maximum(early_total * rescale[:, :, 0] + late_total, 1.0)
+    mixed_out = early_out * rescale[:, :, 0].T[:, :, None] + late_out
     mixed = (mixed_out / row_total.T[:, :, None]).reshape(chunk, slot).astype(jnp.bfloat16)
 
     mine = lax.dynamic_slice_in_dim(mixed, c * row_count, row_count)

time: 151 us -> 150 us (level)
    ppermute x1, waiting for transfers between devices: 10.8 us -> 0.01 us  [per_device(): kv_sets.append(lax.ppermute(far, ALL, pairs))]
    ppermute x15, waiting for transfers between devices: 46.6 us -> 57.4 us  [cyclic(): return lax.ppermute(x, axis, [(i, (i + by) % n) for i in range(n)])]
    reduce_sum x1 -> x2, other arithmetic: 4.9 us -> 4.18 us  [accumulate(): total = jnp.sum(exp_terms, axis=2)]
  transfers between devices with their start and end apart: 26 -> 26, of which waited for: 20 -> 19; matrix products, arithmetic and copies ran while one was open for 6% -> 6% of each run, Pallas kernels for 0% -> 0%
where the time goes in v9:
time: 150 us
  waiting for transfers between devices  76.2 us (51%)
  starting transfers between devices  41.6 us (28%)
  matrix products  14.7 us (10%)
  other arithmetic  9.01 us (6%)
  local copies, waits for them, and re-layouts  6.93 us (5%)
    ppermute x15, waiting for transfers between devices, cyclic(): return lax.ppermute(x, axis, [(i, (i + by) % n) for i in range(n)])  57.4 us
    ppermute x8, waiting for transfers between devices, butterfly(): other = lax.ppermute(jnp.stack([sums, peaks]), ALL, perm)  18.8 us
    ppermute x8, starting transfers between devices, butterfly(): other = lax.ppermute(jnp.stack([sums, peaks]), ALL, perm)  15.6 us
    ppermute x15, starting transfers between devices, cyclic(): return lax.ppermute(x, axis, [(i, (i + by) % n) for i in range(n)])  12.7 us
    ppermute x2, starting transfers between devices, shifted(): lax.ppermute(x, axis, [(i, i + by) for i in range(n) if 0 <= i + by < n])  9.57 us
    dot_general x9, matrix products, accumulate(): jnp.einsum('hrk,khd->rhd', exp_terms.astype(jnp.bfloat16), value_heads, p...  5.67 us
    dot_general x1, matrix products, per_device(): jnp.dot(gathered, proj_weight, preferred_element_type=jnp.float32)  4.6 us
    dot_general x9, matrix products, key_scores(): jnp.einsum('rhd,khd->hrk', query_heads, key_heads, preferred_element_type...  4.46 us
  transfers between devices with their start and end apart: 26, of which 19 were waited for; matrix products, arithmetic and copies ran while one was open for 6% of the time, Pallas kernels for 0%

profile of v9, /device:TPU:8, one launch (start us, length us, event | category | flops | bytes accessed | tf_op | source)
XLA Modules:
  0.0 150.0 jit_solution(13984006515149038314)
XLA Ops:
  0.6 1.4 constant_dynamic-slice_fusion.5
  5.3 2.8 %collective-permute-start.1 = (bf16[128,1792]{0,1:T(8,128)(2,1)S(1)}, bf16[128,1792]{0,1:T(8,128)(2,1)S(1)}, u32[]{:S(2)}, u32[]{:S(2)}) collective-permute-start(bf16[128,1792]{0,1:T(8,128)(2,1)S(1)} %slice.212), channel_id=1, source_target_pairs={{0,6},{2,0},{4,2},{6,4},{1,7},{3,1},{5,3},{7,5},{8,14},{10,8},{12,... | collective-permute-start | bytes 1376264 | tf_op jit(solution)/shard_map/ppermute | solution.py:39
  8.4 3.8 %collective-permute-start.7 = (bf16[256,1792]{0,1:T(8,128)(2,1)S(1)}, bf16[256,1792]{0,1:T(8,128)(2,1)S(1)}, u32[]{:S(2)}, u32[]{:S(2)}) collective-permute-start(bf16[256,1792]{0,1:T(8,128)(2,1)S(1)} %pad_maximum_fusion.1), channel_id=1, source_target_pairs={{0,8},{8,16},{16,24},{24,32},{32,40},{40,48},{48,56},{56,64},{64,7... | collective-permute-start | bytes 2752520 | tf_op jit(solution)/shard_map/ppermute | solution.py:34
  12.2 5.7 %collective-permute-start.8 = (bf16[256,1792]{0,1:T(8,128)(2,1)S(1)}, bf16[256,1792]{0,1:T(8,128)(2,1)S(1)}, u32[]{:S(2)}, u32[]{:S(2)}) collective-permute-start(bf16[256,1792]{0,1:T(8,128)(2,1)S(1)} %pad_maximum_fusion.1), channel_id=1, source_target_pairs={{8,0},{16,8},{24,16},{32,24},{40,32},{48,40},{56,48},{64,56},{72,6... | collective-permute-start | bytes 2752520 | tf_op jit(solution)/shard_map/ppermute | solution.py:34
  18.6 3.1 %collective-permute-done.2 = bf16[128,1792]{0,1:T(8,128)(2,1)S(1)} collective-permute-done((bf16[128,1792]{0,1:T(8,128)(2,1)S(1)}, bf16[128,1792]{0,1:T(8,128)(2,1)S(1)}, u32[]{:S(2)}, u32[]{:S(2)}) %collective-permute-start.2) | collective-permute-done | bytes 458784 | tf_op jit(solution)/shard_map/ppermute | solution.py:39
  22.1 2.0 %collective-permute-start.6 = (bf16[128,1792]{0,1:T(8,128)(2,1)S(1)}, bf16[128,1792]{0,1:T(8,128)(2,1)S(1)}, u32[]{:S(2)}, u32[]{:S(2)}) collective-permute-start(bf16[128,1792]{0,1:T(8,128)(2,1)S(1)} %collective-permute-done.2), channel_id=1, source_target_pairs={{0,2},{2,4},{4,6},{6,0},{1,3},{3,5},{5,7},{7,1},{8,10},{10,12},{12... | collective-permute-start | bytes 1376264 | tf_op jit(solution)/shard_map/ppermute | solution.py:39
  24.2 11.0 %collective-permute-done.5 = bf16[128,1792]{0,1:T(8,128)(2,1)S(1)} collective-permute-done((bf16[128,1792]{0,1:T(8,128)(2,1)S(1)}, bf16[128,1792]{0,1:T(8,128)(2,1)S(1)}, u32[]{:S(2)}, u32[]{:S(2)}) %collective-permute-start.5) | collective-permute-done | bytes 458784 | tf_op jit(solution)/shard_map/ppermute | solution.py:39
  35.4 3.8 %collective-permute-start.9 = (bf16[256,1792]{0,1:T(8,128)(2,1)S(1)}, bf16[256,1792]{0,1:T(8,128)(2,1)S(1)}, u32[]{:S(2)}, u32[]{:S(2)}) collective-permute-start(bf16[256,1792]{0,1:T(8,128)(2,1)S(1)} %constant_dynamic-update-slice_fusion.4), channel_id=1, source_target_pairs={{0,8},{1,9},{2,10},{3,11},{8,16},{9,17},{10,18},{11,19},{12,4},{13... | collective-permute-start | bytes 2752520 | tf_op jit(solution)/shard_map/ppermute | solution.py:123
  39.2 5.6 %collective-permute-done.4 = bf16[128,1792]{0,1:T(8,128)(2,1)S(1)} collective-permute-done((bf16[128,1792]{0,1:T(8,128)(2,1)S(1)}, bf16[128,1792]{0,1:T(8,128)(2,1)S(1)}, u32[]{:S(2)}, u32[]{:S(2)}) %collective-permute-start.4) | collective-permute-done | bytes 458784 | tf_op jit(solution)/shard_map/ppermute | solution.py:39
  45.6 1.5 %collective-permute-start.10 = (bf16[256,1792]{0,1:T(8,128)(2,1)S(1)}, bf16[256,1792]{0,1:T(8,128)(2,1)S(1)}, u32[]{:S(2)}, u32[]{:S(2)}) collective-permute-start(bf16[256,1792]{0,1:T(8,128)(2,1)S(1)} %get-tuple-element.27), channel_id=1, source_target_pairs={{0,6},{2,0},{4,2},{6,4},{1,7},{3,1},{5,3},{7,5},{8,14},{10,8},{12,... | collective-permute-start | bytes 2752520 | tf_op jit(solution)/shard_map/ppermute | solution.py:39
  50.3 13.5 %collective-permute-done.10 = bf16[256,1792]{0,1:T(8,128)(2,1)S(1)} collective-permute-done((bf16[256,1792]{0,1:T(8,128)(2,1)S(1)}, bf16[256,1792]{0,1:T(8,128)(2,1)S(1)}, u32[]{:S(2)}, u32[]{:S(2)}) %collective-permute-start.10) | collective-permute-done | bytes 917536 | tf_op jit(solution)/shard_map/ppermute | solution.py:39
  65.0 1.8 %collective-permute-done.11 = bf16[256,1792]{0,1:T(8,128)(2,1)S(1)} collective-permute-done((bf16[256,1792]{0,1:T(8,128)(2,1)S(1)}, bf16[256,1792]{0,1:T(8,128)(2,1)S(1)}, u32[]{:S(2)}, u32[]{:S(2)}) %collective-permute-start.11) | collective-permute-done | bytes 917536 | tf_op jit(solution)/shard_map/ppermute | solution.py:39
  71.8 2.8 %fusion.19 = (f32[7,256]{1,0:T(8,128)S(1)}, f32[7,256]{1,0:T(8,128)S(1)}, f32[7,256]{1,0:T(8,128)S(1)}, f32[7,256]{1,0:T(8,128)S(1)}, f32[7,256]{1,0:T(8,128)S(1)}, /*index=5*/f32[7,256]{1,0:T(8,128)S(1)}) fusion(f32[7,256,256]{1,2,0:T(8,128)S(1)} %get-tuple-element.111, f32[7,256]{1,0:T(8,128)S(1)} %get-tuple-element.24, ...), kind=kLoop, calls=%fused_computation.47 | loop fusion | flops 13751808 | bytes 11453440 | tf_op jit(solution)/shard_map/reduce_sum | solution.py:160
  79.8 1.5 %collective-permute-start.13 = (bf16[32,6656]{1,0:T(8,128)(2,1)S(1)}, bf16[32,6656]{1,0:T(8,128)(2,1)S(1)}, u32[]{:S(2)}, u32[]{:S(2)}) collective-permute-start(bf16[32,6656]{1,0:T(8,128)(2,1)S(1)} %select_n.268), channel_id=1, source_target_pairs={{0,6},{2,0},{4,2},{6,4},{1,7},{3,1},{5,3},{7,5},{8,14},{10,8},{12,... | collective-permute-start | bytes 1277960 | tf_op jit(solution)/shard_map/ppermute | solution.py:39
  81.9 9.8 %collective-permute-done.13 = bf16[32,6656]{1,0:T(8,128)(2,1)S(1)} collective-permute-done((bf16[32,6656]{1,0:T(8,128)(2,1)S(1)}, bf16[32,6656]{1,0:T(8,128)(2,1)S(1)}, u32[]{:S(2)}, u32[]{:S(2)}) %collective-permute-start.13) | collective-permute-done | bytes 426016 | tf_op jit(solution)/shard_map/ppermute | solution.py:39
  91.7 2.7 %collective-permute-start.15 = (bf16[16,6656]{1,0:T(8,128)(2,1)S(1)}, bf16[16,6656]{1,0:T(8,128)(2,1)S(1)}, u32[]{:S(2)}, u32[]{:S(2)}) collective-permute-start(bf16[16,6656]{1,0:T(8,128)(2,1)S(1)} %slice.232), channel_id=1, source_target_pairs={{0,6},{2,0},{4,2},{6,4},{1,7},{3,1},{5,3},{7,5},{8,14},{10,8},{12,... | collective-permute-start | bytes 638984 | tf_op jit(solution)/shard_map/ppermute | solution.py:39
  94.9 3.6 %collective-permute-done.15 = bf16[16,6656]{1,0:T(8,128)(2,1)S(1)} collective-permute-done((bf16[16,6656]{1,0:T(8,128)(2,1)S(1)}, bf16[16,6656]{1,0:T(8,128)(2,1)S(1)}, u32[]{:S(2)}, u32[]{:S(2)}) %collective-permute-start.15) | collective-permute-done | bytes 213024 | tf_op jit(solution)/shard_map/ppermute | solution.py:39
  98.5 3.8 %collective-permute-done.16 = bf16[16,6656]{1,0:T(8,128)(2,1)S(1)} collective-permute-done((bf16[16,6656]{1,0:T(8,128)(2,1)S(1)}, bf16[16,6656]{1,0:T(8,128)(2,1)S(1)}, u32[]{:S(2)}, u32[]{:S(2)}) %collective-permute-start.16) | collective-permute-done | bytes 213024 | tf_op jit(solution)/shard_map/ppermute | solution.py:39
  102.3 1.4 pad_maximum_fusion
  104.2 3.3 %collective-permute-done.17 = bf16[4,32,6656]{2,1,0:T(8,128)(2,1)S(1)} collective-permute-done((bf16[4,32,6656]{2,1,0:T(8,128)(2,1)}, bf16[4,32,6656]{2,1,0:T(8,128)(2,1)S(1)}, u32[]{:S(2)}, u32[]{:S(2)}) %collective-permute-start.17) | collective-permute-done | bytes 1703968 | tf_op jit(solution)/shard_map/ppermute | solution.py:39
  107.8 4.6 %multiply_reduce_fusion = (f32[256]{0:T(256)S(1)}, f32[256]{0:T(256)S(1)}, f32[256,384]{1,0:T(8,128)S(1)}) fusion(bf16[256,6656]{1,0:T(8,128)(2,1)S(1)} %fusion.102, bf16[6656,384]{1,0:T(8,128)(2,1)} %param.9), kind=kOutput, calls=%fused_computation.138 | convolution fusion | flops 1308917248 | bytes 8914944 | tf_op jit(solution)/shard_map/dot_general | solution.py:209
  113.9 3.6 %collective-permute-done.19 = f32[2,32]{1,0:T(2,128)S(1)} collective-permute-done((f32[2,32]{1,0:T(2,128)S(1)}, f32[2,32]{1,0:T(2,128)S(1)}, u32[]{:S(2)}, u32[]{:S(2)}) %collective-permute-start.19) | collective-permute-done | bytes 288 | tf_op jit(solution)/shard_map/ppermute | solution.py:49
  117.6 5.1 %collective-permute-done.20 = f32[2,32]{1,0:T(2,128)S(1)} collective-permute-done((f32[2,32]{1,0:T(2,128)S(1)}, f32[2,32]{1,0:T(2,128)S(1)}, u32[]{:S(2)}, u32[]{:S(2)}) %collective-permute-start.20) | collective-permute-done | bytes 288 | tf_op jit(solution)/shard_map/ppermute | solution.py:49
  122.6 2.0 %collective-permute-start.21 = (f32[2,32]{1,0:T(2,128)S(1)}, f32[2,32]{1,0:T(2,128)S(1)}, u32[]{:S(2)}, u32[]{:S(2)}) collective-permute-start(f32[2,32]{1,0:T(2,128)S(1)} %pad_maximum_fusion.7), channel_id=1, source_target_pairs={{0,8},{1,9},{2,10},{3,11},{4,12},{5,13},{6,14},{7,15},{8,0},{9,1},... | collective-permute-start | bytes 776 | tf_op jit(solution)/shard_map/ppermute | solution.py:49
  124.6 1.7 %collective-permute-done.21 = f32[2,32]{1,0:T(2,128)S(1)} collective-permute-done((f32[2,32]{1,0:T(2,128)S(1)}, f32[2,32]{1,0:T(2,128)S(1)}, u32[]{:S(2)}, u32[]{:S(2)}) %collective-permute-start.21) | collective-permute-done | bytes 288 | tf_op jit(solution)/shard_map/ppermute | solution.py:49
  126.3 3.3 %collective-permute-start.22 = (f32[2,32]{1,0:T(2,128)S(1)}, f32[2,32]{1,0:T(2,128)S(1)}, u32[]{:S(2)}, u32[]{:S(2)}) collective-permute-start(f32[2,32]{1,0:T(2,128)S(1)} %pad_maximum_fusion.8), channel_id=1, source_target_pairs={{0,16},{1,17},{2,18},{3,19},{4,20},{5,21},{6,22},{7,23},{8,24},{9,... | collective-permute-start | bytes 776 | tf_op jit(solution)/shard_map/ppermute | solution.py:49
  129.7 1.5 %collective-permute-done.22 = f32[2,32]{1,0:T(2,128)S(1)} collective-permute-done((f32[2,32]{1,0:T(2,128)S(1)}, f32[2,32]{1,0:T(2,128)S(1)}, u32[]{:S(2)}, u32[]{:S(2)}) %collective-permute-start.22) | collective-permute-done | bytes 288 | tf_op jit(solution)/shard_map/ppermute | solution.py:49
  131.2 6.9 %collective-permute-start.23 = (f32[2,32]{1,0:T(2,128)S(1)}, f32[2,32]{1,0:T(2,128)S(1)}, u32[]{:S(2)}, u32[]{:S(2)}) collective-permute-start(f32[2,32]{1,0:T(2,128)S(1)} %pad_maximum_fusion.9), channel_id=1, source_target_pairs={{0,32},{1,33},{2,34},{3,35},{4,36},{5,37},{6,38},{7,39},{8,40},{9,... | collective-permute-start | bytes 776 | tf_op jit(solution)/shard_map/ppermute | solution.py:49
  138.2 1.5 %collective-permute-done.23 = f32[2,32]{1,0:T(2,128)S(1)} collective-permute-done((f32[2,32]{1,0:T(2,128)S(1)}, f32[2,32]{1,0:T(2,128)S(1)}, u32[]{:S(2)}, u32[]{:S(2)}) %collective-permute-start.23) | collective-permute-done | bytes 288 | tf_op jit(solution)/shard_map/ppermute | solution.py:49
  141.5 1.9 %collective-permute-done.24 = f32[2,32]{1,0:T(2,128)S(1)} collective-permute-done((f32[2,32]{1,0:T(2,128)S(1)}, f32[2,32]{1,0:T(2,128)S(1)}, u32[]{:S(2)}, u32[]{:S(2)}) %collective-permute-start.24) | collective-permute-done | bytes 288 | tf_op jit(solution)/shard_map/ppermute | solution.py:49
  143.4 2.4 %collective-permute-start.25 = (f32[2,32]{1,0:T(2,128)S(1)}, f32[2,32]{1,0:T(2,128)S(1)}, u32[]{:S(2)}, u32[]{:S(2)}) collective-permute-start(f32[2,32]{1,0:T(2,128)S(1)} %pad_maximum_fusion.11), channel_id=1, source_target_pairs={{0,128},{1,129},{2,130},{3,131},{4,132},{5,133},{6,134},{7,135},{8... | collective-permute-start | bytes 776 | tf_op jit(solution)/shard_map/ppermute | solution.py:49
  146.0 2.5 %collective-permute-done.25 = f32[2,32]{1,0:T(2,128)S(1)} collective-permute-done((f32[2,32]{1,0:T(2,128)S(1)}, f32[2,32]{1,0:T(2,128)S(1)}, u32[]{:S(2)}, u32[]{:S(2)}) %collective-permute-start.25) | collective-permute-done | bytes 288 | tf_op jit(solution)/shard_map/ppermute | solution.py:49
  (127 shorter events, 26.3 us)
Async XLA Ops:
  0.6 1.8 %copy-start = (bf16[128,1664]{1,0:T(8,128)(2,1)S(1)}, bf16[128,1664]{1,0:T(8,128)(2,1)}, u32[]{:S(2)}) copy-start(bf16[128,1664]{1,0:T(8,128)(2,1)} %param.5) | copy-start | bytes 1277956
  2.0 0.9 copy-start.1
  2.7 2.2 %collective-permute-start = (bf16[128,2688]{0,1:T(8,128)(2,1)S(1)}, bf16[128,2688]{0,1:T(8,128)(2,1)S(1)}, u32[]{:S(2)}, u32[]{:S(2)}) collective-permute-start(bf16[128,2688]{0,1:T(8,128)(2,1)S(1)} %pad_maximum_fusion.3), channel_id=1, source_target_pairs={{0,1},{1,0},{2,3},{3,2},{4,5},{5,4},{6,7},{7,6},{8,9},{9,8},{10,11... | collective-permute-start | bytes 2064392 | tf_op jit(solution)/shard_map/ppermute | solution.py:39
  5.3 13.3 %collective-permute-start.1 = (bf16[128,1792]{0,1:T(8,128)(2,1)S(1)}, bf16[128,1792]{0,1:T(8,128)(2,1)S(1)}, u32[]{:S(2)}, u32[]{:S(2)}) collective-permute-start(bf16[128,1792]{0,1:T(8,128)(2,1)S(1)} %slice.212), channel_id=1, source_target_pairs={{0,6},{2,0},{4,2},{6,4},{1,7},{3,1},{5,3},{7,5},{8,14},{10,8},{12,... | collective-permute-start | bytes 1376264 | tf_op jit(solution)/shard_map/ppermute | solution.py:39
  8.2 13.6 %collective-permute-start.2 = (bf16[128,1792]{0,1:T(8,128)(2,1)S(1)}, bf16[128,1792]{0,1:T(8,128)(2,1)S(1)}, u32[]{:S(2)}, u32[]{:S(2)}) collective-permute-start(bf16[128,1792]{0,1:T(8,128)(2,1)S(1)} %slice.213), channel_id=1, source_target_pairs={{0,2},{2,4},{4,6},{6,0},{1,3},{3,5},{5,7},{7,1},{8,10},{10,12},{12... | collective-permute-start | bytes 1376264 | tf_op jit(solution)/shard_map/ppermute | solution.py:39
  8.4 37.1 %collective-permute-start.7 = (bf16[256,1792]{0,1:T(8,128)(2,1)S(1)}, bf16[256,1792]{0,1:T(8,128)(2,1)S(1)}, u32[]{:S(2)}, u32[]{:S(2)}) collective-permute-start(bf16[256,1792]{0,1:T(8,128)(2,1)S(1)} %pad_maximum_fusion.1), channel_id=1, source_target_pairs={{0,8},{8,16},{16,24},{24,32},{32,40},{40,48},{48,56},{56,64},{64,7... | collective-permute-start | bytes 2752520 | tf_op jit(solution)/shard_map/ppermute | solution.py:34
  12.2 33.2 %collective-permute-start.8 = (bf16[256,1792]{0,1:T(8,128)(2,1)S(1)}, bf16[256,1792]{0,1:T(8,128)(2,1)S(1)}, u32[]{:S(2)}, u32[]{:S(2)}) collective-permute-start(bf16[256,1792]{0,1:T(8,128)(2,1)S(1)} %pad_maximum_fusion.1), channel_id=1, source_target_pairs={{8,0},{16,8},{24,16},{32,24},{40,32},{48,40},{56,48},{64,56},{72,6... | collective-permute-start | bytes 2752520 | tf_op jit(solution)/shard_map/ppermute | solution.py:34
  21.7 13.5 %collective-permute-start.5 = (bf16[128,1792]{0,1:T(8,128)(2,1)S(1)}, bf16[128,1792]{0,1:T(8,128)(2,1)S(1)}, u32[]{:S(2)}, u32[]{:S(2)}) collective-permute-start(bf16[128,1792]{0,1:T(8,128)(2,1)S(1)} %collective-permute-done.1), channel_id=1, source_target_pairs={{0,6},{2,0},{4,2},{6,4},{1,7},{3,1},{5,3},{7,5},{8,14},{10,8},{12,... | collective-permute-start | bytes 1376264 | tf_op jit(solution)/shard_map/ppermute | solution.py:39
  22.0 23.1 %collective-permute-start.3 = (bf16[128,1792]{0,1:T(8,128)(2,1)S(1)}, bf16[128,1792]{0,1:T(8,128)(2,1)S(1)}, u32[]{:S(2)}, u32[]{:S(2)}) collective-permute-start(bf16[128,1792]{0,1:T(8,128)(2,1)S(1)} %get-tuple-element.48), channel_id=1, source_target_pairs={{0,6},{2,0},{4,2},{6,4},{1,7},{3,1},{5,3},{7,5},{8,14},{10,8},{12,... | collective-permute-start | bytes 1376264 | tf_op jit(solution)/shard_map/ppermute | solution.py:39
  22.1 13.2 %collective-permute-start.6 = (bf16[128,1792]{0,1:T(8,128)(2,1)S(1)}, bf16[128,1792]{0,1:T(8,128)(2,1)S(1)}, u32[]{:S(2)}, u32[]{:S(2)}) collective-permute-start(bf16[128,1792]{0,1:T(8,128)(2,1)S(1)} %collective-permute-done.2), channel_id=1, source_target_pairs={{0,2},{2,4},{4,6},{6,0},{1,3},{3,5},{5,7},{7,1},{8,10},{10,12},{12... | collective-permute-start | bytes 1376264 | tf_op jit(solution)/shard_map/ppermute | solution.py:39
  35.2 9.7 %collective-permute-start.4 = (bf16[128,1792]{0,1:T(8,128)(2,1)S(1)}, bf16[128,1792]{0,1:T(8,128)(2,1)S(1)}, u32[]{:S(2)}, u32[]{:S(2)}) collective-permute-start(bf16[128,1792]{0,1:T(8,128)(2,1)S(1)} %get-tuple-element.49), channel_id=1, source_target_pairs={{0,2},{2,4},{4,6},{6,0},{1,3},{3,5},{5,7},{7,1},{8,10},{10,12},{12... | collective-permute-start | bytes 1376264 | tf_op jit(solution)/shard_map/ppermute | solution.py:39
  35.4 28.5 %collective-permute-start.9 = (bf16[256,1792]{0,1:T(8,128)(2,1)S(1)}, bf16[256,1792]{0,1:T(8,128)(2,1)S(1)}, u32[]{:S(2)}, u32[]{:S(2)}) collective-permute-start(bf16[256,1792]{0,1:T(8,128)(2,1)S(1)} %constant_dynamic-update-slice_fusion.4), channel_id=1, source_target_pairs={{0,8},{1,9},{2,10},{3,11},{8,16},{9,17},{10,18},{11,19},{12,4},{13... | collective-permute-start | bytes 2752520 | tf_op jit(solution)/shard_map/ppermute | solution.py:123
  45.6 18.3 %collective-permute-start.10 = (bf16[256,1792]{0,1:T(8,128)(2,1)S(1)}, bf16[256,1792]{0,1:T(8,128)(2,1)S(1)}, u32[]{:S(2)}, u32[]{:S(2)}) collective-permute-start(bf16[256,1792]{0,1:T(8,128)(2,1)S(1)} %get-tuple-element.27), channel_id=1, source_target_pairs={{0,6},{2,0},{4,2},{6,4},{1,7},{3,1},{5,3},{7,5},{8,14},{10,8},{12,... | collective-permute-start | bytes 2752520 | tf_op jit(solution)/shard_map/ppermute | solution.py:39
  47.1 19.7 %collective-permute-start.11 = (bf16[256,1792]{0,1:T(8,128)(2,1)S(1)}, bf16[256,1792]{0,1:T(8,128)(2,1)S(1)}, u32[]{:S(2)}, u32[]{:S(2)}) collective-permute-start(bf16[256,1792]{0,1:T(8,128)(2,1)S(1)} %get-tuple-element.28), channel_id=1, source_target_pairs={{0,2},{2,4},{4,6},{6,0},{1,3},{3,5},{5,7},{7,1},{8,10},{10,12},{12... | collective-permute-start | bytes 2752520 | tf_op jit(solution)/shard_map/ppermute | solution.py:39
  77.5 1.8 %collective-permute-start.12 = (bf16[128,896]{1,0:T(8,128)(2,1)S(1)}, bf16[128,896]{1,0:T(8,128)(2,1)S(1)}, u32[]{:S(2)}, u32[]{:S(2)}) collective-permute-start(bf16[128,896]{1,0:T(8,128)(2,1)S(1)} %copy.129), channel_id=1, source_target_pairs={{0,1},{1,0},{2,3},{3,2},{4,5},{5,4},{6,7},{7,6},{8,9},{9,8},{10,11... | collective-permute-start | bytes 688136 | tf_op jit(solution)/shard_map/ppermute | solution.py:39
  79.8 11.9 %collective-permute-start.13 = (bf16[32,6656]{1,0:T(8,128)(2,1)S(1)}, bf16[32,6656]{1,0:T(8,128)(2,1)S(1)}, u32[]{:S(2)}, u32[]{:S(2)}) collective-permute-start(bf16[32,6656]{1,0:T(8,128)(2,1)S(1)} %select_n.268), channel_id=1, source_target_pairs={{0,6},{2,0},{4,2},{6,4},{1,7},{3,1},{5,3},{7,5},{8,14},{10,8},{12,... | collective-permute-start | bytes 1277960 | tf_op jit(solution)/shard_map/ppermute | solution.py:39
  81.3 13.5 %collective-permute-start.14 = (bf16[32,6656]{1,0:T(8,128)(2,1)S(1)}, bf16[32,6656]{1,0:T(8,128)(2,1)S(1)}, u32[]{:S(2)}, u32[]{:S(2)}) collective-permute-start(bf16[32,6656]{1,0:T(8,128)(2,1)S(1)} %select_n.268), channel_id=1, source_target_pairs={{0,2},{2,4},{4,6},{6,0},{1,3},{3,5},{5,7},{7,1},{8,10},{10,12},{12... | collective-permute-start | bytes 1277960 | tf_op jit(solution)/shard_map/ppermute | solution.py:39
  91.7 6.7 %collective-permute-start.15 = (bf16[16,6656]{1,0:T(8,128)(2,1)S(1)}, bf16[16,6656]{1,0:T(8,128)(2,1)S(1)}, u32[]{:S(2)}, u32[]{:S(2)}) collective-permute-start(bf16[16,6656]{1,0:T(8,128)(2,1)S(1)} %slice.232), channel_id=1, source_target_pairs={{0,6},{2,0},{4,2},{6,4},{1,7},{3,1},{5,3},{7,5},{8,14},{10,8},{12,... | collective-permute-start | bytes 638984 | tf_op jit(solution)/shard_map/ppermute | solution.py:39
  94.8 7.5 %collective-permute-start.16 = (bf16[16,6656]{1,0:T(8,128)(2,1)S(1)}, bf16[16,6656]{1,0:T(8,128)(2,1)S(1)}, u32[]{:S(2)}, u32[]{:S(2)}) collective-permute-start(bf16[16,6656]{1,0:T(8,128)(2,1)S(1)} %slice.233), channel_id=1, source_target_pairs={{0,2},{2,4},{4,6},{6,0},{1,3},{3,5},{5,7},{7,1},{8,10},{10,12},{12... | collective-permute-start | bytes 638984 | tf_op jit(solution)/shard_map/ppermute | solution.py:39
  103.7 3.8 %collective-permute-start.17 = (bf16[4,32,6656]{2,1,0:T(8,128)(2,1)}, bf16[4,32,6656]{2,1,0:T(8,128)(2,1)S(1)}, u32[]{:S(2)}, u32[]{:S(2)}) collective-permute-start(bf16[4,32,6656]{2,1,0:T(8,128)(2,1)} %pad_maximum_fusion), channel_id=1, source_target_pairs={{0,1},{1,0},{2,3},{3,2},{4,5},{5,4},{6,7},{7,6},{8,9},{9,8},{10,11... | collective-permute-start | bytes 5111816 | tf_op jit(solution)/shard_map/ppermute | solution.py:39
  112.6 1.2 collective-permute-start.18
  113.8 3.7 %collective-permute-start.19 = (f32[2,32]{1,0:T(2,128)S(1)}, f32[2,32]{1,0:T(2,128)S(1)}, u32[]{:S(2)}, u32[]{:S(2)}) collective-permute-start(f32[2,32]{1,0:T(2,128)S(1)} %pad_maximum_fusion.5), channel_id=1, source_target_pairs={{0,2},{1,3},{2,0},{3,1},{4,6},{5,7},{6,4},{7,5},{8,10},{9,11},{10,... | collective-permute-start | bytes 776 | tf_op jit(solution)/shard_map/ppermute | solution.py:49
  117.5 5.2 %collective-permute-start.20 = (f32[2,32]{1,0:T(2,128)S(1)}, f32[2,32]{1,0:T(2,128)S(1)}, u32[]{:S(2)}, u32[]{:S(2)}) collective-permute-start(f32[2,32]{1,0:T(2,128)S(1)} %pad_maximum_fusion.6), channel_id=1, source_target_pairs={{0,4},{1,5},{2,6},{3,7},{4,0},{5,1},{6,2},{7,3},{8,12},{9,13},{10,... | collective-permute-start | bytes 776 | tf_op jit(solution)/shard_map/ppermute | solution.py:49
  122.6 3.7 %collective-permute-start.21 = (f32[2,32]{1,0:T(2,128)S(1)}, f32[2,32]{1,0:T(2,128)S(1)}, u32[]{:S(2)}, u32[]{:S(2)}) collective-permute-start(f32[2,32]{1,0:T(2,128)S(1)} %pad_maximum_fusion.7), channel_id=1, source_target_pairs={{0,8},{1,9},{2,10},{3,11},{4,12},{5,13},{6,14},{7,15},{8,0},{9,1},... | collective-permute-start | bytes 776 | tf_op jit(solution)/shard_map/ppermute | solution.py:49
  126.3 4.9 %collective-permute-start.22 = (f32[2,32]{1,0:T(2,128)S(1)}, f32[2,32]{1,0:T(2,128)S(1)}, u32[]{:S(2)}, u32[]{:S(2)}) collective-permute-start(f32[2,32]{1,0:T(2,128)S(1)} %pad_maximum_fusion.8), channel_id=1, source_target_pairs={{0,16},{1,17},{2,18},{3,19},{4,20},{5,21},{6,22},{7,23},{8,24},{9,... | collective-permute-start | bytes 776 | tf_op jit(solution)/shard_map/ppermute | solution.py:49
  131.2 8.5 %collective-permute-start.23 = (f32[2,32]{1,0:T(2,128)S(1)}, f32[2,32]{1,0:T(2,128)S(1)}, u32[]{:S(2)}, u32[]{:S(2)}) collective-permute-start(f32[2,32]{1,0:T(2,128)S(1)} %pad_maximum_fusion.9), channel_id=1, source_target_pairs={{0,32},{1,33},{2,34},{3,35},{4,36},{5,37},{6,38},{7,39},{8,40},{9,... | collective-permute-start | bytes 776 | tf_op jit(solution)/shard_map/ppermute | solution.py:49
  139.7 3.7 %collective-permute-start.24 = (f32[2,32]{1,0:T(2,128)S(1)}, f32[2,32]{1,0:T(2,128)S(1)}, u32[]{:S(2)}, u32[]{:S(2)}) collective-permute-start(f32[2,32]{1,0:T(2,128)S(1)} %pad_maximum_fusion.10), channel_id=1, source_target_pairs={{0,64},{1,65},{2,66},{3,67},{4,68},{5,69},{6,70},{7,71},{8,72},{9,... | collective-permute-start | bytes 776 | tf_op jit(solution)/shard_map/ppermute | solution.py:49
  143.4 5.2 %collective-permute-start.25 = (f32[2,32]{1,0:T(2,128)S(1)}, f32[2,32]{1,0:T(2,128)S(1)}, u32[]{:S(2)}, u32[]{:S(2)}) collective-permute-start(f32[2,32]{1,0:T(2,128)S(1)} %pad_maximum_fusion.11), channel_id=1, source_target_pairs={{0,128},{1,129},{2,130},{3,131},{4,132},{5,133},{6,134},{7,135},{8... | collective-permute-start | bytes 776 | tf_op jit(solution)/shard_map/ppermute | solution.py:49

commit v10 on v8

--- a/solution.py
+++ b/solution.py
@@ -82,6 +82,12 @@
         [jnp.where(first, own, got), jnp.where(first, got, own)], axis=0
     )
     q_chip = chip_rows[:, :slot]
+    sib_weight = cyclic(proj_weight, "core", 1)
+    chip_weight = jnp.where(
+        first,
+        jnp.concatenate([proj_weight, sib_weight], axis=1),
+        jnp.concatenate([sib_weight, proj_weight], axis=1),
+    )
     kv_chip = chip_rows[:, slot:]
 
     right_a = cyclic(kv_chip[:row_count], "x", -1)
@@ -186,16 +192,16 @@
     m_far = jnp.concatenate(
         [cyclic(m_right[: piece // 2], "x", -1), cyclic(m_left[piece // 2 :], "x", 1)], axis=0
     )
-    mine4 = jnp.stack([merged, m_right, m_left, m_far])
-    sib4 = cyclic(mine4, "core", 1)
-    gathered = jnp.zeros((piece * chips * cores, merged.shape[1]), merged.dtype)
-    for k, dx in enumerate((0, 1, chips - 1, 2)):
+    gathered = jnp.zeros((piece * chips, merged.shape[1]), merged.dtype)
+    for part, dx in zip((merged, m_right, m_left, m_far), (0, 1, chips - 1, 2)):
         at = (xi + dx) % chips
-        gathered = lax.dynamic_update_slice_in_dim(gathered, mine4[k], (at * cores + c) * piece, 0)
-        gathered = lax.dynamic_update_slice_in_dim(gathered, sib4[k], (at * cores + 1 - c) * piece, 0)
-    projected = jnp.dot(gathered, proj_weight, preferred_element_type=jnp.float32)
+        gathered = lax.dynamic_update_slice_in_dim(gathered, part, at * piece, 0)
+    projected = jnp.dot(gathered, chip_weight, preferred_element_type=jnp.float32)
     own_begin = b * block_len
-    row_segs = lax.dynamic_slice_in_dim(segment_ids, own_begin, block_len)[::4]
+    block_segs = lax.dynamic_slice_in_dim(segment_ids, own_begin, block_len)[::4]
+    row_segs = lax.dynamic_index_in_dim(
+        block_segs.reshape(chips, cores, piece), c, axis=1, keepdims=False
+    ).reshape(chips * piece)
     member = row_segs[:, None] == jnp.arange(group_count, dtype=jnp.int32)[None, :]
     squares = jnp.sum(projected * projected, axis=1)
     seg_sums = jnp.sum(jnp.where(member, squares[:, None], 0.0), axis=0)
@@ -203,12 +209,23 @@
     all_segs = segment_ids[::4]
     all_member = all_segs[:, None] == jnp.arange(group_count, dtype=jnp.int32)[None, :]
     seg_counts = jnp.sum(all_member.astype(jnp.float32), axis=0) * (
-        projected.shape[1] * chips * cores
+        proj_weight.shape[1] * chips * cores
     )
     seg_sums, row_peak = butterfly(seg_sums, row_peak)
     seg_scale = lax.rsqrt(seg_sums / seg_counts + epsilon)
     row_scale = jnp.sum(jnp.where(member, seg_scale[None, :], 0.0), axis=1)
-    normed = (projected * row_scale[:, None]).astype(jnp.bfloat16)
+    normed_pair = (projected * row_scale[:, None]).astype(jnp.bfloat16)
+    cols_out = proj_weight.shape[1]
+    mine_out = lax.dynamic_slice_in_dim(normed_pair, c * cols_out, cols_out, axis=1)
+    theirs_out = lax.dynamic_slice_in_dim(normed_pair, (1 - c) * cols_out, cols_out, axis=1)
+    back_out = cyclic(theirs_out, "core", 1)
+    mine_out = mine_out.reshape(chips, 1, piece, cols_out)
+    back_out = back_out.reshape(chips, 1, piece, cols_out)
+    normed = jnp.where(
+        first,
+        jnp.concatenate([mine_out, back_out], axis=1),
+        jnp.concatenate([back_out, mine_out], axis=1),
+    ).reshape(chips * cores * piece, cols_out)
     return (normed, row_peak * seg_scale)
 
 

time: 151 us -> 160 us (1.060)
  waiting for transfers between devices: 76.2 us -> 85.2 us
  matrix products: 14.7 us -> 21.6 us
  starting transfers between devices: 41.6 us -> 35.8 us
  other arithmetic: 9.72 us -> 7.69 us
    ppermute x8, starting transfers between devices: 15.6 us -> 5.06 us  [butterfly(): other = lax.ppermute(jnp.stack([sums, peaks]), ALL, perm)]
    ppermute x8, waiting for transfers between devices: 18.8 us -> 28 us  [butterfly(): other = lax.ppermute(jnp.stack([sums, peaks]), ALL, perm)]
    dot_general x1, matrix products: 4.6 us -> 11.3 us  [per_device(): jnp.dot(gathered, chip_weight, preferred_element_type=jnp.float32)]
    ppermute x15 -> x16, starting transfers between devices: 12.6 us -> 17.4 us  [cyclic(): return lax.ppermute(x, axis, [(i, (i + by) % n) for i in range(n)])]
    ppermute x15 -> x16, waiting for transfers between devices: 46.6 us -> 43.9 us  [cyclic(): return lax.ppermute(x, axis, [(i, (i + by) % n) for i in range(n)])]
    ppermute x1, waiting for transfers between devices: 10.8 us -> 13.4 us  [per_device(): kv_sets.append(lax.ppermute(far, ALL, pairs))]
  transfers between devices with their start and end apart: 26 -> 27, of which waited for: 20 -> 21; matrix products, arithmetic and copies ran while one was open for 6% -> 14% of each run, Pallas kernels for 0% -> 0%
where the time goes in v10:
time: 160 us; the launch traced here: 159 us
  waiting for transfers between devices  85.2 us (53%)
  starting transfers between devices  35.8 us (22%)
  matrix products  21.6 us (14%)
  other arithmetic  7.69 us (5%)
  local copies, waits for them, and re-layouts  7.15 us (4%)
    ppermute x16, waiting for transfers between devices, cyclic(): return lax.ppermute(x, axis, [(i, (i + by) % n) for i in range(n)])  43.9 us
    ppermute x8, waiting for transfers between devices, butterfly(): other = lax.ppermute(jnp.stack([sums, peaks]), ALL, perm)  28 us
    ppermute x16, starting transfers between devices, cyclic(): return lax.ppermute(x, axis, [(i, (i + by) % n) for i in range(n)])  17.4 us
    ppermute x1, waiting for transfers between devices, per_device(): kv_sets.append(lax.ppermute(far, ALL, pairs))  13.4 us
    dot_general x1, matrix products, per_device(): jnp.dot(gathered, chip_weight, preferred_element_type=jnp.float32)  11.3 us
    ppermute x2, starting transfers between devices, shifted(): lax.ppermute(x, axis, [(i, i + by) for i in range(n) if 0 <= i + by < n])  9.57 us
    dot_general x9, matrix products, per_device(): jnp.einsum('hrk,khd->rhd', exp_terms.astype(jnp.bfloat16), value_heads, p...  5.77 us
    ppermute x8, starting transfers between devices, butterfly(): other = lax.ppermute(jnp.stack([sums, peaks]), ALL, perm)  5.06 us
  transfers between devices with their start and end apart: 27, of which 21 were waited for; matrix products, arithmetic and copies ran while one was open for 14% of the time, Pallas kernels for 0%

profile of v10, /device:TPU:8, one launch (start us, length us, event | category | flops | bytes accessed | tf_op | source)
XLA Modules:
  0.0 159.0 jit_solution(9873303536780692875)
XLA Ops:
  0.6 1.4 constant_dynamic-slice_fusion.8
  5.3 2.8 %collective-permute-start.1 = (bf16[128,1792]{0,1:T(8,128)(2,1)S(1)}, bf16[128,1792]{0,1:T(8,128)(2,1)S(1)}, u32[]{:S(2)}, u32[]{:S(2)}) collective-permute-start(bf16[128,1792]{0,1:T(8,128)(2,1)S(1)} %slice.196), channel_id=1, source_target_pairs={{0,6},{2,0},{4,2},{6,4},{1,7},{3,1},{5,3},{7,5},{8,14},{10,8},{12,... | collective-permute-start | bytes 1376264 | tf_op jit(solution)/shard_map/ppermute | solution.py:39
  8.4 3.8 %collective-permute-start.7 = (bf16[256,1792]{0,1:T(8,128)(2,1)S(1)}, bf16[256,1792]{0,1:T(8,128)(2,1)S(1)}, u32[]{:S(2)}, u32[]{:S(2)}) collective-permute-start(bf16[256,1792]{0,1:T(8,128)(2,1)S(1)} %pad_maximum_fusion), channel_id=1, source_target_pairs={{0,8},{8,16},{16,24},{24,32},{32,40},{40,48},{48,56},{56,64},{64,7... | collective-permute-start | bytes 2752520 | tf_op jit(solution)/shard_map/ppermute | solution.py:34
  12.2 5.7 %collective-permute-start.8 = (bf16[256,1792]{0,1:T(8,128)(2,1)S(1)}, bf16[256,1792]{0,1:T(8,128)(2,1)S(1)}, u32[]{:S(2)}, u32[]{:S(2)}) collective-permute-start(bf16[256,1792]{0,1:T(8,128)(2,1)S(1)} %pad_maximum_fusion), channel_id=1, source_target_pairs={{8,0},{16,8},{24,16},{32,24},{40,32},{48,40},{56,48},{64,56},{72,6... | collective-permute-start | bytes 2752520 | tf_op jit(solution)/shard_map/ppermute | solution.py:34
  18.6 3.1 %collective-permute-done.2 = bf16[128,1792]{0,1:T(8,128)(2,1)S(1)} collective-permute-done((bf16[128,1792]{0,1:T(8,128)(2,1)S(1)}, bf16[128,1792]{0,1:T(8,128)(2,1)S(1)}, u32[]{:S(2)}, u32[]{:S(2)}) %collective-permute-start.2) | collective-permute-done | bytes 458784 | tf_op jit(solution)/shard_map/ppermute | solution.py:39
  22.0 1.9 %collective-permute-start.6 = (bf16[128,1792]{0,1:T(8,128)(2,1)S(1)}, bf16[128,1792]{0,1:T(8,128)(2,1)S(1)}, u32[]{:S(2)}, u32[]{:S(2)}) collective-permute-start(bf16[128,1792]{0,1:T(8,128)(2,1)S(1)} %collective-permute-done.2), channel_id=1, source_target_pairs={{0,2},{2,4},{4,6},{6,0},{1,3},{3,5},{5,7},{7,1},{8,10},{10,12},{12... | collective-permute-start | bytes 1376264 | tf_op jit(solution)/shard_map/ppermute | solution.py:39
  24.0 9.2 %collective-permute-done.5 = bf16[128,1792]{0,1:T(8,128)(2,1)S(1)} collective-permute-done((bf16[128,1792]{0,1:T(8,128)(2,1)S(1)}, bf16[128,1792]{0,1:T(8,128)(2,1)S(1)}, u32[]{:S(2)}, u32[]{:S(2)}) %collective-permute-start.5) | collective-permute-done | bytes 458784 | tf_op jit(solution)/shard_map/ppermute | solution.py:39
  33.2 1.5 collective-permute-done.6
  34.7 1.8 %collective-permute-start.3 = (bf16[128,1792]{0,1:T(8,128)(2,1)S(1)}, bf16[128,1792]{0,1:T(8,128)(2,1)S(1)}, u32[]{:S(2)}, u32[]{:S(2)}) collective-permute-start(bf16[128,1792]{0,1:T(8,128)(2,1)S(1)} %get-tuple-element.44), channel_id=1, source_target_pairs={{0,6},{2,0},{4,2},{6,4},{1,7},{3,1},{5,3},{7,5},{8,14},{10,8},{12,... | collective-permute-start | bytes 1376264 | tf_op jit(solution)/shard_map/ppermute | solution.py:39
  36.6 8.2 %collective-permute-done.4 = bf16[128,1792]{0,1:T(8,128)(2,1)S(1)} collective-permute-done((bf16[128,1792]{0,1:T(8,128)(2,1)S(1)}, bf16[128,1792]{0,1:T(8,128)(2,1)S(1)}, u32[]{:S(2)}, u32[]{:S(2)}) %collective-permute-start.4) | collective-permute-done | bytes 458784 | tf_op jit(solution)/shard_map/ppermute | solution.py:39
  44.8 3.8 %collective-permute-start.9 = (bf16[256,1792]{0,1:T(8,128)(2,1)S(1)}, bf16[256,1792]{0,1:T(8,128)(2,1)S(1)}, u32[]{:S(2)}, u32[]{:S(2)}) collective-permute-start(bf16[256,1792]{0,1:T(8,128)(2,1)S(1)} %constant_dynamic-update-slice_fusion.4), channel_id=1, source_target_pairs={{0,8},{1,9},{2,10},{3,11},{8,16},{9,17},{10,18},{11,19},{12,4},{13... | collective-permute-start | bytes 2752520 | tf_op jit(solution)/shard_map/ppermute | solution.py:129
  49.3 4.7 %collective-permute-start.10 = (bf16[256,1792]{0,1:T(8,128)(2,1)S(1)}, bf16[256,1792]{0,1:T(8,128)(2,1)S(1)}, u32[]{:S(2)}, u32[]{:S(2)}) collective-permute-start(bf16[256,1792]{0,1:T(8,128)(2,1)S(1)} %get-tuple-element.23), channel_id=1, source_target_pairs={{0,6},{2,0},{4,2},{6,4},{1,7},{3,1},{5,3},{7,5},{8,14},{10,8},{12,... | collective-permute-start | bytes 2752520 | tf_op jit(solution)/shard_map/ppermute | solution.py:39
  56.7 13.4 %collective-permute-done.9 = bf16[256,1792]{0,1:T(8,128)(2,1)S(1)} collective-permute-done((bf16[256,1792]{0,1:T(8,128)(2,1)S(1)}, bf16[256,1792]{0,1:T(8,128)(2,1)S(1)}, u32[]{:S(2)}, u32[]{:S(2)}) %collective-permute-start.9) | collective-permute-done | bytes 917536 | tf_op jit(solution)/shard_map/ppermute | solution.py:129
  72.1 2.3 %collective-permute-done.11 = bf16[256,1792]{0,1:T(8,128)(2,1)S(1)} collective-permute-done((bf16[256,1792]{0,1:T(8,128)(2,1)S(1)}, bf16[256,1792]{0,1:T(8,128)(2,1)S(1)}, u32[]{:S(2)}, u32[]{:S(2)}) %collective-permute-start.11) | collective-permute-done | bytes 917536 | tf_op jit(solution)/shard_map/ppermute | solution.py:39
  78.7 4.9 %fusion.25 = (f32[7,256]{1,0:T(8,128)S(1)}, f32[7,256]{1,0:T(8,128)S(1)}, f32[7,256]{1,0:T(8,128)S(1)}, f32[7,256]{1,0:T(8,128)S(1)}, f32[7,256]{1,0:T(8,128)S(1...) fusion(f32[7,256,256]{1,2,0:T(8,128)S(1)} %get-tuple-element.109, ...), kind=kLoop, calls=%fused_computation.52 | loop fusion | flops 20627712 | bytes 17176576 | tf_op jit(solution)/shard_map/reduce_sum | solution.py:168
  88.2 1.4 collective-permute-start.13
  90.5 9.7 %collective-permute-done.13 = bf16[32,6656]{1,0:T(8,128)(2,1)S(1)} collective-permute-done((bf16[32,6656]{1,0:T(8,128)(2,1)S(1)}, bf16[32,6656]{1,0:T(8,128)(2,1)S(1)}, u32[]{:S(2)}, u32[]{:S(2)}) %collective-permute-start.13) | collective-permute-done | bytes 426016 | tf_op jit(solution)/shard_map/ppermute | solution.py:39
  100.2 2.6 %collective-permute-start.15 = (bf16[16,6656]{1,0:T(8,128)(2,1)S(1)}, bf16[16,6656]{1,0:T(8,128)(2,1)S(1)}, u32[]{:S(2)}, u32[]{:S(2)}) collective-permute-start(bf16[16,6656]{1,0:T(8,128)(2,1)S(1)} %slice.216), channel_id=1, source_target_pairs={{0,6},{2,0},{4,2},{6,4},{1,7},{3,1},{5,3},{7,5},{8,14},{10,8},{12,... | collective-permute-start | bytes 638984 | tf_op jit(solution)/shard_map/ppermute | solution.py:39
  103.0 3.8 %collective-permute-done.15 = bf16[16,6656]{1,0:T(8,128)(2,1)S(1)} collective-permute-done((bf16[16,6656]{1,0:T(8,128)(2,1)S(1)}, bf16[16,6656]{1,0:T(8,128)(2,1)S(1)}, u32[]{:S(2)}, u32[]{:S(2)}) %collective-permute-start.15) | collective-permute-done | bytes 213024 | tf_op jit(solution)/shard_map/ppermute | solution.py:39
  106.8 3.5 %collective-permute-done.16 = bf16[16,6656]{1,0:T(8,128)(2,1)S(1)} collective-permute-done((bf16[16,6656]{1,0:T(8,128)(2,1)S(1)}, bf16[16,6656]{1,0:T(8,128)(2,1)S(1)}, u32[]{:S(2)}, u32[]{:S(2)}) %collective-permute-start.16) | collective-permute-done | bytes 213024 | tf_op jit(solution)/shard_map/ppermute | solution.py:39
  110.4 11.3 %multiply_reduce_fusion = (f32[128]{0:T(128)S(1)}, f32[128]{0:T(128)S(1)}, f32[128,768]{1,0:T(8,128)S(1)}) fusion(bf16[128,6656]{1,0:T(8,128)(2,1)S(1)} %maximum_dynamic-update-slice_fusion, bf16[6656,384]{1,0:T(8,128)(2,1)} %collective-permute-done.17, bf16[6656,384]{1,0:T(8,128)(2,1)} %param.9, pred[]{:T(512)S(6)} %eq.176), kind=kOutput, calls=%fused_computation.137 | convolution fusion | flops 1354923776 | bytes 12321793 | tf_op jit(solution)/shard_map/dot_general | solution.py:199
  121.9 1.1 collective-permute-done.18
  123.2 3.6 %collective-permute-done.19 = f32[2,32]{1,0:T(2,128)S(1)} collective-permute-done((f32[2,32]{1,0:T(2,128)S(1)}, f32[2,32]{1,0:T(2,128)S(1)}, u32[]{:S(2)}, u32[]{:S(2)}) %collective-permute-start.19) | collective-permute-done | bytes 288 | tf_op jit(solution)/shard_map/ppermute | solution.py:49
  126.9 5.1 %collective-permute-done.20 = f32[2,32]{1,0:T(2,128)S(1)} collective-permute-done((f32[2,32]{1,0:T(2,128)S(1)}, f32[2,32]{1,0:T(2,128)S(1)}, u32[]{:S(2)}, u32[]{:S(2)}) %collective-permute-start.20) | collective-permute-done | bytes 288 | tf_op jit(solution)/shard_map/ppermute | solution.py:49
  132.0 3.6 %collective-permute-done.21 = f32[2,32]{1,0:T(2,128)S(1)} collective-permute-done((f32[2,32]{1,0:T(2,128)S(1)}, f32[2,32]{1,0:T(2,128)S(1)}, u32[]{:S(2)}, u32[]{:S(2)}) %collective-permute-start.21) | collective-permute-done | bytes 288 | tf_op jit(solution)/shard_map/ppermute | solution.py:49
  135.7 4.5 %collective-permute-done.22 = f32[2,32]{1,0:T(2,128)S(1)} collective-permute-done((f32[2,32]{1,0:T(2,128)S(1)}, f32[2,32]{1,0:T(2,128)S(1)}, u32[]{:S(2)}, u32[]{:S(2)}) %collective-permute-start.22) | collective-permute-done | bytes 288 | tf_op jit(solution)/shard_map/ppermute | solution.py:49
  140.2 1.8 %collective-permute-start.23 = (f32[2,32]{1,0:T(2,128)S(1)}, f32[2,32]{1,0:T(2,128)S(1)}, u32[]{:S(2)}, u32[]{:S(2)}) collective-permute-start(f32[2,32]{1,0:T(2,128)S(1)} %pad_maximum_fusion.8), channel_id=1, source_target_pairs={{0,32},{1,33},{2,34},{3,35},{4,36},{5,37},{6,38},{7,39},{8,40},{9,... | collective-permute-start | bytes 776 | tf_op jit(solution)/shard_map/ppermute | solution.py:49
  142.0 1.2 slice.188
  143.3 4.5 %collective-permute-done.23 = f32[2,32]{1,0:T(2,128)S(1)} collective-permute-done((f32[2,32]{1,0:T(2,128)S(1)}, f32[2,32]{1,0:T(2,128)S(1)}, u32[]{:S(2)}, u32[]{:S(2)}) %collective-permute-start.23) | collective-permute-done | bytes 288 | tf_op jit(solution)/shard_map/ppermute | solution.py:49
  148.1 3.3 %collective-permute-done.24 = f32[2,32]{1,0:T(2,128)S(1)} collective-permute-done((f32[2,32]{1,0:T(2,128)S(1)}, f32[2,32]{1,0:T(2,128)S(1)}, u32[]{:S(2)}, u32[]{:S(2)}) %collective-permute-start.24) | collective-permute-done | bytes 288 | tf_op jit(solution)/shard_map/ppermute | solution.py:49
  151.4 2.7 %collective-permute-start.25 = (f32[2,32]{1,0:T(2,128)S(1)}, f32[2,32]{1,0:T(2,128)S(1)}, u32[]{:S(2)}, u32[]{:S(2)}) collective-permute-start(f32[2,32]{1,0:T(2,128)S(1)} %pad_maximum_fusion.10), channel_id=1, source_target_pairs={{0,128},{1,129},{2,130},{3,131},{4,132},{5,133},{6,134},{7,135},{8... | collective-permute-start | bytes 776 | tf_op jit(solution)/shard_map/ppermute | solution.py:49
  154.1 2.5 %collective-permute-done.25 = f32[2,32]{1,0:T(2,128)S(1)} collective-permute-done((f32[2,32]{1,0:T(2,128)S(1)}, f32[2,32]{1,0:T(2,128)S(1)}, u32[]{:S(2)}, u32[]{:S(2)}) %collective-permute-start.25) | collective-permute-done | bytes 288 | tf_op jit(solution)/shard_map/ppermute | solution.py:49
  (126 shorter events, 22.7 us)
Async XLA Ops:
  0.6 1.8 %copy-start = (bf16[128,1664]{1,0:T(8,128)(2,1)S(1)}, bf16[128,1664]{1,0:T(8,128)(2,1)}, u32[]{:S(2)}) copy-start(bf16[128,1664]{1,0:T(8,128)(2,1)} %param.5) | copy-start | bytes 1277956
  2.0 1.3 copy-start.1
  2.7 2.2 %collective-permute-start = (bf16[128,2688]{0,1:T(8,128)(2,1)S(1)}, bf16[128,2688]{0,1:T(8,128)(2,1)S(1)}, u32[]{:S(2)}, u32[]{:S(2)}) collective-permute-start(bf16[128,2688]{0,1:T(8,128)(2,1)S(1)} %pad_maximum_fusion.2), channel_id=1, source_target_pairs={{0,1},{1,0},{2,3},{3,2},{4,5},{5,4},{6,7},{7,6},{8,9},{9,8},{10,11... | collective-permute-start | bytes 2064392 | tf_op jit(solution)/shard_map/ppermute | solution.py:39
  2.8 107.5 %collective-permute-start.17 = (bf16[6656,384]{1,0:T(8,128)(2,1)}, bf16[6656,384]{1,0:T(8,128)(2,1)}, u32[]{:S(2)}, u32[]{:S(2)}) collective-permute-start(bf16[6656,384]{1,0:T(8,128)(2,1)} %param.9), channel_id=1, source_target_pairs={{0,1},{1,0},{2,3},{3,2},{4,5},{5,4},{6,7},{7,6},{8,9},{9,8},{10,11... | collective-permute-start | bytes 15335432 | tf_op jit(solution)/shard_map/ppermute | solution.py:39
  5.3 13.3 %collective-permute-start.1 = (bf16[128,1792]{0,1:T(8,128)(2,1)S(1)}, bf16[128,1792]{0,1:T(8,128)(2,1)S(1)}, u32[]{:S(2)}, u32[]{:S(2)}) collective-permute-start(bf16[128,1792]{0,1:T(8,128)(2,1)S(1)} %slice.196), channel_id=1, source_target_pairs={{0,6},{2,0},{4,2},{6,4},{1,7},{3,1},{5,3},{7,5},{8,14},{10,8},{12,... | collective-permute-start | bytes 1376264 | tf_op jit(solution)/shard_map/ppermute | solution.py:39
  8.2 13.6 %collective-permute-start.2 = (bf16[128,1792]{0,1:T(8,128)(2,1)S(1)}, bf16[128,1792]{0,1:T(8,128)(2,1)S(1)}, u32[]{:S(2)}, u32[]{:S(2)}) collective-permute-start(bf16[128,1792]{0,1:T(8,128)(2,1)S(1)} %slice.197), channel_id=1, source_target_pairs={{0,2},{2,4},{4,6},{6,0},{1,3},{3,5},{5,7},{7,1},{8,10},{10,12},{12... | collective-permute-start | bytes 1376264 | tf_op jit(solution)/shard_map/ppermute | solution.py:39
  8.4 40.8 %collective-permute-start.7 = (bf16[256,1792]{0,1:T(8,128)(2,1)S(1)}, bf16[256,1792]{0,1:T(8,128)(2,1)S(1)}, u32[]{:S(2)}, u32[]{:S(2)}) collective-permute-start(bf16[256,1792]{0,1:T(8,128)(2,1)S(1)} %pad_maximum_fusion), channel_id=1, source_target_pairs={{0,8},{8,16},{16,24},{24,32},{32,40},{40,48},{48,56},{56,64},{64,7... | collective-permute-start | bytes 2752520 | tf_op jit(solution)/shard_map/ppermute | solution.py:34
  12.2 37.0 %collective-permute-start.8 = (bf16[256,1792]{0,1:T(8,128)(2,1)S(1)}, bf16[256,1792]{0,1:T(8,128)(2,1)S(1)}, u32[]{:S(2)}, u32[]{:S(2)}) collective-permute-start(bf16[256,1792]{0,1:T(8,128)(2,1)S(1)} %pad_maximum_fusion), channel_id=1, source_target_pairs={{8,0},{16,8},{24,16},{32,24},{40,32},{48,40},{56,48},{64,56},{72,6... | collective-permute-start | bytes 2752520 | tf_op jit(solution)/shard_map/ppermute | solution.py:34
  21.7 11.4 %collective-permute-start.5 = (bf16[128,1792]{0,1:T(8,128)(2,1)S(1)}, bf16[128,1792]{0,1:T(8,128)(2,1)S(1)}, u32[]{:S(2)}, u32[]{:S(2)}) collective-permute-start(bf16[128,1792]{0,1:T(8,128)(2,1)S(1)} %collective-permute-done.1), channel_id=1, source_target_pairs={{0,6},{2,0},{4,2},{6,4},{1,7},{3,1},{5,3},{7,5},{8,14},{10,8},{12,... | collective-permute-start | bytes 1376264 | tf_op jit(solution)/shard_map/ppermute | solution.py:39
  22.0 12.7 %collective-permute-start.6 = (bf16[128,1792]{0,1:T(8,128)(2,1)S(1)}, bf16[128,1792]{0,1:T(8,128)(2,1)S(1)}, u32[]{:S(2)}, u32[]{:S(2)}) collective-permute-start(bf16[128,1792]{0,1:T(8,128)(2,1)S(1)} %collective-permute-done.2), channel_id=1, source_target_pairs={{0,2},{2,4},{4,6},{6,0},{1,3},{3,5},{5,7},{7,1},{8,10},{10,12},{12... | collective-permute-start | bytes 1376264 | tf_op jit(solution)/shard_map/ppermute | solution.py:39
  33.1 11.7 %collective-permute-start.4 = (bf16[128,1792]{0,1:T(8,128)(2,1)S(1)}, bf16[128,1792]{0,1:T(8,128)(2,1)S(1)}, u32[]{:S(2)}, u32[]{:S(2)}) collective-permute-start(bf16[128,1792]{0,1:T(8,128)(2,1)S(1)} %get-tuple-element.45), channel_id=1, source_target_pairs={{0,2},{2,4},{4,6},{6,0},{1,3},{3,5},{5,7},{7,1},{8,10},{10,12},{12... | collective-permute-start | bytes 1376264 | tf_op jit(solution)/shard_map/ppermute | solution.py:39
  34.7 14.1 %collective-permute-start.3 = (bf16[128,1792]{0,1:T(8,128)(2,1)S(1)}, bf16[128,1792]{0,1:T(8,128)(2,1)S(1)}, u32[]{:S(2)}, u32[]{:S(2)}) collective-permute-start(bf16[128,1792]{0,1:T(8,128)(2,1)S(1)} %get-tuple-element.44), channel_id=1, source_target_pairs={{0,6},{2,0},{4,2},{6,4},{1,7},{3,1},{5,3},{7,5},{8,14},{10,8},{12,... | collective-permute-start | bytes 1376264 | tf_op jit(solution)/shard_map/ppermute | solution.py:39
  44.8 25.3 %collective-permute-start.9 = (bf16[256,1792]{0,1:T(8,128)(2,1)S(1)}, bf16[256,1792]{0,1:T(8,128)(2,1)S(1)}, u32[]{:S(2)}, u32[]{:S(2)}) collective-permute-start(bf16[256,1792]{0,1:T(8,128)(2,1)S(1)} %constant_dynamic-update-slice_fusion.4), channel_id=1, source_target_pairs={{0,8},{1,9},{2,10},{3,11},{8,16},{9,17},{10,18},{11,19},{12,4},{13... | collective-permute-start | bytes 2752520 | tf_op jit(solution)/shard_map/ppermute | solution.py:129
  49.3 21.7 %collective-permute-start.10 = (bf16[256,1792]{0,1:T(8,128)(2,1)S(1)}, bf16[256,1792]{0,1:T(8,128)(2,1)S(1)}, u32[]{:S(2)}, u32[]{:S(2)}) collective-permute-start(bf16[256,1792]{0,1:T(8,128)(2,1)S(1)} %get-tuple-element.23), channel_id=1, source_target_pairs={{0,6},{2,0},{4,2},{6,4},{1,7},{3,1},{5,3},{7,5},{8,14},{10,8},{12,... | collective-permute-start | bytes 2752520 | tf_op jit(solution)/shard_map/ppermute | solution.py:39
  54.1 20.4 %collective-permute-start.11 = (bf16[256,1792]{0,1:T(8,128)(2,1)S(1)}, bf16[256,1792]{0,1:T(8,128)(2,1)S(1)}, u32[]{:S(2)}, u32[]{:S(2)}) collective-permute-start(bf16[256,1792]{0,1:T(8,128)(2,1)S(1)} %get-tuple-element.24), channel_id=1, source_target_pairs={{0,2},{2,4},{4,6},{6,0},{1,3},{3,5},{5,7},{7,1},{8,10},{10,12},{12... | collective-permute-start | bytes 2752520 | tf_op jit(solution)/shard_map/ppermute | solution.py:39
  86.0 1.8 %collective-permute-start.12 = (bf16[128,896]{1,0:T(8,128)(2,1)S(1)}, bf16[128,896]{1,0:T(8,128)(2,1)S(1)}, u32[]{:S(2)}, u32[]{:S(2)}) collective-permute-start(bf16[128,896]{1,0:T(8,128)(2,1)S(1)} %copy.132), channel_id=1, source_target_pairs={{0,1},{1,0},{2,3},{3,2},{4,5},{5,4},{6,7},{7,6},{8,9},{9,8},{10,11... | collective-permute-start | bytes 688136 | tf_op jit(solution)/shard_map/ppermute | solution.py:39
  88.2 11.9 %collective-permute-start.13 = (bf16[32,6656]{1,0:T(8,128)(2,1)S(1)}, bf16[32,6656]{1,0:T(8,128)(2,1)S(1)}, u32[]{:S(2)}, u32[]{:S(2)}) collective-permute-start(bf16[32,6656]{1,0:T(8,128)(2,1)S(1)} %select_n.277), channel_id=1, source_target_pairs={{0,6},{2,0},{4,2},{6,4},{1,7},{3,1},{5,3},{7,5},{8,14},{10,8},{12,... | collective-permute-start | bytes 1277960 | tf_op jit(solution)/shard_map/ppermute | solution.py:39
  89.7 13.2 %collective-permute-start.14 = (bf16[32,6656]{1,0:T(8,128)(2,1)S(1)}, bf16[32,6656]{1,0:T(8,128)(2,1)S(1)}, u32[]{:S(2)}, u32[]{:S(2)}) collective-permute-start(bf16[32,6656]{1,0:T(8,128)(2,1)S(1)} %select_n.277), channel_id=1, source_target_pairs={{0,2},{2,4},{4,6},{6,0},{1,3},{3,5},{5,7},{7,1},{8,10},{10,12},{12... | collective-permute-start | bytes 1277960 | tf_op jit(solution)/shard_map/ppermute | solution.py:39
  100.2 6.6 %collective-permute-start.15 = (bf16[16,6656]{1,0:T(8,128)(2,1)S(1)}, bf16[16,6656]{1,0:T(8,128)(2,1)S(1)}, u32[]{:S(2)}, u32[]{:S(2)}) collective-permute-start(bf16[16,6656]{1,0:T(8,128)(2,1)S(1)} %slice.216), channel_id=1, source_target_pairs={{0,6},{2,0},{4,2},{6,4},{1,7},{3,1},{5,3},{7,5},{8,14},{10,8},{12,... | collective-permute-start | bytes 638984 | tf_op jit(solution)/shard_map/ppermute | solution.py:39
  102.8 7.5 %collective-permute-start.16 = (bf16[16,6656]{1,0:T(8,128)(2,1)S(1)}, bf16[16,6656]{1,0:T(8,128)(2,1)S(1)}, u32[]{:S(2)}, u32[]{:S(2)}) collective-permute-start(bf16[16,6656]{1,0:T(8,128)(2,1)S(1)} %slice.217), channel_id=1, source_target_pairs={{0,2},{2,4},{4,6},{6,0},{1,3},{3,5},{5,7},{7,1},{8,10},{10,12},{12... | collective-permute-start | bytes 638984 | tf_op jit(solution)/shard_map/ppermute | solution.py:39
  121.8 1.2 collective-permute-start.18
  123.1 3.7 %collective-permute-start.19 = (f32[2,32]{1,0:T(2,128)S(1)}, f32[2,32]{1,0:T(2,128)S(1)}, u32[]{:S(2)}, u32[]{:S(2)}) collective-permute-start(f32[2,32]{1,0:T(2,128)S(1)} %pad_maximum_fusion.4), channel_id=1, source_target_pairs={{0,2},{1,3},{2,0},{3,1},{4,6},{5,7},{6,4},{7,5},{8,10},{9,11},{10,... | collective-permute-start | bytes 776 | tf_op jit(solution)/shard_map/ppermute | solution.py:49
  126.8 5.2 %collective-permute-start.20 = (f32[2,32]{1,0:T(2,128)S(1)}, f32[2,32]{1,0:T(2,128)S(1)}, u32[]{:S(2)}, u32[]{:S(2)}) collective-permute-start(f32[2,32]{1,0:T(2,128)S(1)} %pad_maximum_fusion.5), channel_id=1, source_target_pairs={{0,4},{1,5},{2,6},{3,7},{4,0},{5,1},{6,2},{7,3},{8,12},{9,13},{10,... | collective-permute-start | bytes 776 | tf_op jit(solution)/shard_map/ppermute | solution.py:49
  131.9 3.7 %collective-permute-start.21 = (f32[2,32]{1,0:T(2,128)S(1)}, f32[2,32]{1,0:T(2,128)S(1)}, u32[]{:S(2)}, u32[]{:S(2)}) collective-permute-start(f32[2,32]{1,0:T(2,128)S(1)} %pad_maximum_fusion.6), channel_id=1, source_target_pairs={{0,8},{1,9},{2,10},{3,11},{4,12},{5,13},{6,14},{7,15},{8,0},{9,1},... | collective-permute-start | bytes 776 | tf_op jit(solution)/shard_map/ppermute | solution.py:49
  135.6 4.6 %collective-permute-start.22 = (f32[2,32]{1,0:T(2,128)S(1)}, f32[2,32]{1,0:T(2,128)S(1)}, u32[]{:S(2)}, u32[]{:S(2)}) collective-permute-start(f32[2,32]{1,0:T(2,128)S(1)} %pad_maximum_fusion.7), channel_id=1, source_target_pairs={{0,16},{1,17},{2,18},{3,19},{4,20},{5,21},{6,22},{7,23},{8,24},{9,... | collective-permute-start | bytes 776 | tf_op jit(solution)/shard_map/ppermute | solution.py:49
  140.2 7.6 %collective-permute-start.23 = (f32[2,32]{1,0:T(2,128)S(1)}, f32[2,32]{1,0:T(2,128)S(1)}, u32[]{:S(2)}, u32[]{:S(2)}) collective-permute-start(f32[2,32]{1,0:T(2,128)S(1)} %pad_maximum_fusion.8), channel_id=1, source_target_pairs={{0,32},{1,33},{2,34},{3,35},{4,36},{5,37},{6,38},{7,39},{8,40},{9,... | collective-permute-start | bytes 776 | tf_op jit(solution)/shard_map/ppermute | solution.py:49
  147.8 3.7 %collective-permute-start.24 = (f32[2,32]{1,0:T(2,128)S(1)}, f32[2,32]{1,0:T(2,128)S(1)}, u32[]{:S(2)}, u32[]{:S(2)}) collective-permute-start(f32[2,32]{1,0:T(2,128)S(1)} %pad_maximum_fusion.9), channel_id=1, source_target_pairs={{0,64},{1,65},{2,66},{3,67},{4,68},{5,69},{6,70},{7,71},{8,72},{9,... | collective-permute-start | bytes 776 | tf_op jit(solution)/shard_map/ppermute | solution.py:49
  151.4 5.2 %collective-permute-start.25 = (f32[2,32]{1,0:T(2,128)S(1)}, f32[2,32]{1,0:T(2,128)S(1)}, u32[]{:S(2)}, u32[]{:S(2)}) collective-permute-start(f32[2,32]{1,0:T(2,128)S(1)} %pad_maximum_fusion.10), channel_id=1, source_target_pairs={{0,128},{1,129},{2,130},{3,131},{4,132},{5,133},{6,134},{7,135},{8... | collective-permute-start | bytes 776 | tf_op jit(solution)/shard_map/ppermute | solution.py:49
  156.8 1.4 collective-permute-start.26

commit v11 on v8

--- a/solution.py
+++ b/solution.py
@@ -74,15 +74,14 @@
     def cols(a, at):
         return lax.dynamic_slice_in_dim(a, at, slot, axis=1)
 
-    own = jnp.concatenate([cols(queries, my_col), cols(keys, my_col), cols(values, my_col)], axis=1)
-    give = jnp.concatenate([cols(queries, sib_col), cols(keys, sib_col), cols(values, sib_col)], axis=1)
+    own = jnp.concatenate([cols(keys, my_col), cols(values, my_col)], axis=1)
+    give = jnp.concatenate([cols(keys, sib_col), cols(values, sib_col)], axis=1)
     got = cyclic(give, "core", 1)
     first = c == 0
-    chip_rows = jnp.concatenate(
-        [jnp.where(first, own, got), jnp.where(first, got, own)], axis=0
-    )
-    q_chip = chip_rows[:, :slot]
-    kv_chip = chip_rows[:, slot:]
+    kv_chip = jnp.concatenate([jnp.where(first, own, got), jnp.where(first, got, own)], axis=0)
+    own_q = cols(queries, my_col)
+    got_q = cyclic(cols(queries, sib_col), "core", 1)
+    q_chip = jnp.concatenate([jnp.where(first, own_q, got_q), jnp.where(first, got_q, own_q)], axis=0)
 
     right_a = cyclic(kv_chip[:row_count], "x", -1)
     left_b = cyclic(kv_chip[row_count:], "x", 1)

time: 151 us -> 151 us (level)
    ppermute x15 -> x16, waiting for transfers between devices: 46.6 us -> 45.8 us  [cyclic(): return lax.ppermute(x, axis, [(i, (i + by) % n) for i in range(n)])]
    ppermute x15 -> x16, starting transfers between devices: 12.6 us -> 13.2 us  [cyclic(): return lax.ppermute(x, axis, [(i, (i + by) % n) for i in range(n)])]
  transfers between devices with their start and end apart: 26 -> 27, of which waited for: 20 -> 19; matrix products, arithmetic and copies ran while one was open for 6% -> 6% of each run, Pallas kernels for 0% -> 0%
where the time goes in v11:
time: 151 us; the launch traced here: 150 us
  waiting for transfers between devices  75.8 us (50%)
  starting transfers between devices  42.2 us (28%)
  matrix products  14.7 us (10%)
  other arithmetic  9.61 us (6%)
  local copies, waits for them, and re-layouts  6.76 us (4%)
    ppermute x16, waiting for transfers between devices, cyclic(): return lax.ppermute(x, axis, [(i, (i + by) % n) for i in range(n)])  45.8 us
    ppermute x8, waiting for transfers between devices, butterfly(): other = lax.ppermute(jnp.stack([sums, peaks]), ALL, perm)  18.7 us
    ppermute x8, starting transfers between devices, butterfly(): other = lax.ppermute(jnp.stack([sums, peaks]), ALL, perm)  15.6 us
    ppermute x16, starting transfers between devices, cyclic(): return lax.ppermute(x, axis, [(i, (i + by) % n) for i in range(n)])  13.2 us
    ppermute x1, waiting for transfers between devices, per_device(): kv_sets.append(lax.ppermute(far, ALL, pairs))  11.2 us
    ppermute x2, starting transfers between devices, shifted(): lax.ppermute(x, axis, [(i, i + by) for i in range(n) if 0 <= i + by < n])  9.57 us
    dot_general x9, matrix products, per_device(): jnp.einsum('hrk,khd->rhd', exp_terms.astype(jnp.bfloat16), value_heads, p...  5.63 us
    reduce_sum x1, other arithmetic, per_device(): total = jnp.sum(exp_terms, axis=2)  4.86 us
  transfers between devices with their start and end apart: 27, of which 19 were waited for; matrix products, arithmetic and copies ran while one was open for 6% of the time, Pallas kernels for 0%

profile of v11, /device:TPU:8, one launch (start us, length us, event | category | flops | bytes accessed | tf_op | source)
XLA Modules:
  0.0 150.3 jit_solution(239657107944685535)
XLA Ops:
  5.1 2.8 %collective-permute-start.2 = (bf16[128,1792]{0,1:T(8,128)(2,1)S(1)}, bf16[128,1792]{0,1:T(8,128)(2,1)S(1)}, u32[]{:S(2)}, u32[]{:S(2)}) collective-permute-start(bf16[128,1792]{0,1:T(8,128)(2,1)S(1)} %get-tuple-element.45), channel_id=1, source_target_pairs={{0,6},{2,0},{4,2},{6,4},{1,7},{3,1},{5,3},{7,5},{8,14},{10,8},{12,... | collective-permute-start | bytes 1376264 | tf_op jit(solution)/shard_map/ppermute | solution.py:39
  8.0 7.7 %collective-permute-start.9 = (bf16[256,1792]{0,1:T(8,128)(2,1)S(1)}, bf16[256,1792]{0,1:T(8,128)(2,1)S(1)}, u32[]{:S(2)}, u32[]{:S(2)}) collective-permute-start(bf16[256,1792]{0,1:T(8,128)(2,1)S(1)} %pad_maximum_fusion.1), channel_id=1, source_target_pairs={{8,0},{16,8},{24,16},{32,24},{40,32},{48,40},{56,48},{64,56},{72,6... | collective-permute-start | bytes 2752520 | tf_op jit(solution)/shard_map/ppermute | solution.py:34
  15.7 1.9 %collective-permute-start.8 = (bf16[256,1792]{0,1:T(8,128)(2,1)S(1)}, bf16[256,1792]{0,1:T(8,128)(2,1)S(1)}, u32[]{:S(2)}, u32[]{:S(2)}) collective-permute-start(bf16[256,1792]{0,1:T(8,128)(2,1)S(1)} %pad_maximum_fusion.1), channel_id=1, source_target_pairs={{0,8},{8,16},{16,24},{24,32},{32,40},{40,48},{48,56},{56,64},{64,7... | collective-permute-start | bytes 2752520 | tf_op jit(solution)/shard_map/ppermute | solution.py:34
  18.2 3.2 %collective-permute-done.3 = bf16[128,1792]{0,1:T(8,128)(2,1)S(1)} collective-permute-done((bf16[128,1792]{0,1:T(8,128)(2,1)S(1)}, bf16[128,1792]{0,1:T(8,128)(2,1)S(1)}, u32[]{:S(2)}, u32[]{:S(2)}) %collective-permute-start.3) | collective-permute-done | bytes 458784 | tf_op jit(solution)/shard_map/ppermute | solution.py:39
  21.8 2.0 %collective-permute-start.7 = (bf16[128,1792]{0,1:T(8,128)(2,1)S(1)}, bf16[128,1792]{0,1:T(8,128)(2,1)S(1)}, u32[]{:S(2)}, u32[]{:S(2)}) collective-permute-start(bf16[128,1792]{0,1:T(8,128)(2,1)S(1)} %collective-permute-done.3), channel_id=1, source_target_pairs={{0,2},{2,4},{4,6},{6,0},{1,3},{3,5},{5,7},{7,1},{8,10},{10,12},{12... | collective-permute-start | bytes 1376264 | tf_op jit(solution)/shard_map/ppermute | solution.py:39
  23.9 10.9 %collective-permute-done.6 = bf16[128,1792]{0,1:T(8,128)(2,1)S(1)} collective-permute-done((bf16[128,1792]{0,1:T(8,128)(2,1)S(1)}, bf16[128,1792]{0,1:T(8,128)(2,1)S(1)}, u32[]{:S(2)}, u32[]{:S(2)}) %collective-permute-start.6) | collective-permute-done | bytes 458784 | tf_op jit(solution)/shard_map/ppermute | solution.py:39
  35.1 3.8 %collective-permute-start.10 = (bf16[256,1792]{0,1:T(8,128)(2,1)S(1)}, bf16[256,1792]{0,1:T(8,128)(2,1)S(1)}, u32[]{:S(2)}, u32[]{:S(2)}) collective-permute-start(bf16[256,1792]{0,1:T(8,128)(2,1)S(1)} %constant_dynamic-update-slice_fusion.4), channel_id=1, source_target_pairs={{0,8},{1,9},{2,10},{3,11},{8,16},{9,17},{10,18},{11,19},{12,4},{13... | collective-permute-start | bytes 2752520 | tf_op jit(solution)/shard_map/ppermute | solution.py:122
  38.9 5.6 %collective-permute-done.5 = bf16[128,1792]{0,1:T(8,128)(2,1)S(1)} collective-permute-done((bf16[128,1792]{0,1:T(8,128)(2,1)S(1)}, bf16[128,1792]{0,1:T(8,128)(2,1)S(1)}, u32[]{:S(2)}, u32[]{:S(2)}) %collective-permute-start.5) | collective-permute-done | bytes 458784 | tf_op jit(solution)/shard_map/ppermute | solution.py:39
  45.2 1.5 %collective-permute-start.11 = (bf16[256,1792]{0,1:T(8,128)(2,1)S(1)}, bf16[256,1792]{0,1:T(8,128)(2,1)S(1)}, u32[]{:S(2)}, u32[]{:S(2)}) collective-permute-start(bf16[256,1792]{0,1:T(8,128)(2,1)S(1)} %get-tuple-element.23), channel_id=1, source_target_pairs={{0,6},{2,0},{4,2},{6,4},{1,7},{3,1},{5,3},{7,5},{8,14},{10,8},{12,... | collective-permute-start | bytes 2752520 | tf_op jit(solution)/shard_map/ppermute | solution.py:39
  50.0 11.2 %collective-permute-done.10 = bf16[256,1792]{0,1:T(8,128)(2,1)S(1)} collective-permute-done((bf16[256,1792]{0,1:T(8,128)(2,1)S(1)}, bf16[256,1792]{0,1:T(8,128)(2,1)S(1)}, u32[]{:S(2)}, u32[]{:S(2)}) %collective-permute-start.10) | collective-permute-done | bytes 917536 | tf_op jit(solution)/shard_map/ppermute | solution.py:122
  61.2 2.3 %collective-permute-done.11 = bf16[256,1792]{0,1:T(8,128)(2,1)S(1)} collective-permute-done((bf16[256,1792]{0,1:T(8,128)(2,1)S(1)}, bf16[256,1792]{0,1:T(8,128)(2,1)S(1)}, u32[]{:S(2)}, u32[]{:S(2)}) %collective-permute-start.11) | collective-permute-done | bytes 917536 | tf_op jit(solution)/shard_map/ppermute | solution.py:39
  64.6 2.0 %collective-permute-done.12 = bf16[256,1792]{0,1:T(8,128)(2,1)S(1)} collective-permute-done((bf16[256,1792]{0,1:T(8,128)(2,1)S(1)}, bf16[256,1792]{0,1:T(8,128)(2,1)S(1)}, u32[]{:S(2)}, u32[]{:S(2)}) %collective-permute-start.12) | collective-permute-done | bytes 917536 | tf_op jit(solution)/shard_map/ppermute | solution.py:39
  70.8 4.9 %fusion.18 = (f32[7,256]{1,0:T(8,128)S(1)}, f32[7,256]{1,0:T(8,128)S(1)}, f32[7,256]{1,0:T(8,128)S(1)}, f32[7,256]{1,0:T(8,128)S(1)}, f32[7,256]{1,0:T(8,128)S(1...) fusion(f32[7,256,256]{1,2,0:T(8,128)S(1)} %get-tuple-element.108, ...), kind=kLoop, calls=%fused_computation.40 | loop fusion | flops 20627712 | bytes 17176576 | tf_op jit(solution)/shard_map/reduce_sum | solution.py:161
  80.0 1.7 %collective-permute-start.14 = (bf16[32,6656]{1,0:T(8,128)(2,1)S(1)}, bf16[32,6656]{1,0:T(8,128)(2,1)S(1)}, u32[]{:S(2)}, u32[]{:S(2)}) collective-permute-start(bf16[32,6656]{1,0:T(8,128)(2,1)S(1)} %select_n.283), channel_id=1, source_target_pairs={{0,6},{2,0},{4,2},{6,4},{1,7},{3,1},{5,3},{7,5},{8,14},{10,8},{12,... | collective-permute-start | bytes 1277960 | tf_op jit(solution)/shard_map/ppermute | solution.py:39
  82.3 9.8 %collective-permute-done.14 = bf16[32,6656]{1,0:T(8,128)(2,1)S(1)} collective-permute-done((bf16[32,6656]{1,0:T(8,128)(2,1)S(1)}, bf16[32,6656]{1,0:T(8,128)(2,1)S(1)}, u32[]{:S(2)}, u32[]{:S(2)}) %collective-permute-start.14) | collective-permute-done | bytes 426016 | tf_op jit(solution)/shard_map/ppermute | solution.py:39
  92.2 2.6 %collective-permute-start.16 = (bf16[16,6656]{1,0:T(8,128)(2,1)S(1)}, bf16[16,6656]{1,0:T(8,128)(2,1)S(1)}, u32[]{:S(2)}, u32[]{:S(2)}) collective-permute-start(bf16[16,6656]{1,0:T(8,128)(2,1)S(1)} %slice.206), channel_id=1, source_target_pairs={{0,6},{2,0},{4,2},{6,4},{1,7},{3,1},{5,3},{7,5},{8,14},{10,8},{12,... | collective-permute-start | bytes 638984 | tf_op jit(solution)/shard_map/ppermute | solution.py:39
  95.2 3.6 %collective-permute-done.16 = bf16[16,6656]{1,0:T(8,128)(2,1)S(1)} collective-permute-done((bf16[16,6656]{1,0:T(8,128)(2,1)S(1)}, bf16[16,6656]{1,0:T(8,128)(2,1)S(1)}, u32[]{:S(2)}, u32[]{:S(2)}) %collective-permute-start.16) | collective-permute-done | bytes 213024 | tf_op jit(solution)/shard_map/ppermute | solution.py:39
  98.8 3.8 %collective-permute-done.17 = bf16[16,6656]{1,0:T(8,128)(2,1)S(1)} collective-permute-done((bf16[16,6656]{1,0:T(8,128)(2,1)S(1)}, bf16[16,6656]{1,0:T(8,128)(2,1)S(1)}, u32[]{:S(2)}, u32[]{:S(2)}) %collective-permute-start.17) | collective-permute-done | bytes 213024 | tf_op jit(solution)/shard_map/ppermute | solution.py:39
  102.6 1.4 pad_maximum_fusion
  104.6 3.3 %collective-permute-done.18 = bf16[4,32,6656]{2,1,0:T(8,128)(2,1)S(1)} collective-permute-done((bf16[4,32,6656]{2,1,0:T(8,128)(2,1)}, bf16[4,32,6656]{2,1,0:T(8,128)(2,1)S(1)}, u32[]{:S(2)}, u32[]{:S(2)}) %collective-permute-start.18) | collective-permute-done | bytes 1703968 | tf_op jit(solution)/shard_map/ppermute | solution.py:39
  108.1 4.6 %multiply_reduce_fusion = (f32[256]{0:T(256)S(1)}, f32[256]{0:T(256)S(1)}, f32[256,384]{1,0:T(8,128)S(1)}) fusion(bf16[256,6656]{1,0:T(8,128)(2,1)S(1)} %fusion.97, bf16[6656,384]{1,0:T(8,128)(2,1)} %param.9), kind=kOutput, calls=%fused_computation.134 | convolution fusion | flops 1308917248 | bytes 8914944 | tf_op jit(solution)/shard_map/dot_general | solution.py:195
  114.2 3.6 %collective-permute-done.20 = f32[2,32]{1,0:T(2,128)S(1)} collective-permute-done((f32[2,32]{1,0:T(2,128)S(1)}, f32[2,32]{1,0:T(2,128)S(1)}, u32[]{:S(2)}, u32[]{:S(2)}) %collective-permute-start.20) | collective-permute-done | bytes 288 | tf_op jit(solution)/shard_map/ppermute | solution.py:49
  117.9 5.1 %collective-permute-done.21 = f32[2,32]{1,0:T(2,128)S(1)} collective-permute-done((f32[2,32]{1,0:T(2,128)S(1)}, f32[2,32]{1,0:T(2,128)S(1)}, u32[]{:S(2)}, u32[]{:S(2)}) %collective-permute-start.21) | collective-permute-done | bytes 288 | tf_op jit(solution)/shard_map/ppermute | solution.py:49
  123.0 2.0 %collective-permute-start.22 = (f32[2,32]{1,0:T(2,128)S(1)}, f32[2,32]{1,0:T(2,128)S(1)}, u32[]{:S(2)}, u32[]{:S(2)}) collective-permute-start(f32[2,32]{1,0:T(2,128)S(1)} %pad_maximum_fusion.8), channel_id=1, source_target_pairs={{0,8},{1,9},{2,10},{3,11},{4,12},{5,13},{6,14},{7,15},{8,0},{9,1},... | collective-permute-start | bytes 776 | tf_op jit(solution)/shard_map/ppermute | solution.py:49
  125.0 1.6 %collective-permute-done.22 = f32[2,32]{1,0:T(2,128)S(1)} collective-permute-done((f32[2,32]{1,0:T(2,128)S(1)}, f32[2,32]{1,0:T(2,128)S(1)}, u32[]{:S(2)}, u32[]{:S(2)}) %collective-permute-start.22) | collective-permute-done | bytes 288 | tf_op jit(solution)/shard_map/ppermute | solution.py:49
  126.6 3.3 %collective-permute-start.23 = (f32[2,32]{1,0:T(2,128)S(1)}, f32[2,32]{1,0:T(2,128)S(1)}, u32[]{:S(2)}, u32[]{:S(2)}) collective-permute-start(f32[2,32]{1,0:T(2,128)S(1)} %pad_maximum_fusion.9), channel_id=1, source_target_pairs={{0,16},{1,17},{2,18},{3,19},{4,20},{5,21},{6,22},{7,23},{8,24},{9,... | collective-permute-start | bytes 776 | tf_op jit(solution)/shard_map/ppermute | solution.py:49
  130.0 1.5 %collective-permute-done.23 = f32[2,32]{1,0:T(2,128)S(1)} collective-permute-done((f32[2,32]{1,0:T(2,128)S(1)}, f32[2,32]{1,0:T(2,128)S(1)}, u32[]{:S(2)}, u32[]{:S(2)}) %collective-permute-start.23) | collective-permute-done | bytes 288 | tf_op jit(solution)/shard_map/ppermute | solution.py:49
  131.6 6.9 %collective-permute-start.24 = (f32[2,32]{1,0:T(2,128)S(1)}, f32[2,32]{1,0:T(2,128)S(1)}, u32[]{:S(2)}, u32[]{:S(2)}) collective-permute-start(f32[2,32]{1,0:T(2,128)S(1)} %pad_maximum_fusion.10), channel_id=1, source_target_pairs={{0,32},{1,33},{2,34},{3,35},{4,36},{5,37},{6,38},{7,39},{8,40},{9,... | collective-permute-start | bytes 776 | tf_op jit(solution)/shard_map/ppermute | solution.py:49
  138.5 1.5 %collective-permute-done.24 = f32[2,32]{1,0:T(2,128)S(1)} collective-permute-done((f32[2,32]{1,0:T(2,128)S(1)}, f32[2,32]{1,0:T(2,128)S(1)}, u32[]{:S(2)}, u32[]{:S(2)}) %collective-permute-start.24) | collective-permute-done | bytes 288 | tf_op jit(solution)/shard_map/ppermute | solution.py:49
  141.8 1.9 %collective-permute-done.25 = f32[2,32]{1,0:T(2,128)S(1)} collective-permute-done((f32[2,32]{1,0:T(2,128)S(1)}, f32[2,32]{1,0:T(2,128)S(1)}, u32[]{:S(2)}, u32[]{:S(2)}) %collective-permute-start.25) | collective-permute-done | bytes 288 | tf_op jit(solution)/shard_map/ppermute | solution.py:49
  143.7 2.4 %collective-permute-start.26 = (f32[2,32]{1,0:T(2,128)S(1)}, f32[2,32]{1,0:T(2,128)S(1)}, u32[]{:S(2)}, u32[]{:S(2)}) collective-permute-start(f32[2,32]{1,0:T(2,128)S(1)} %pad_maximum_fusion.12), channel_id=1, source_target_pairs={{0,128},{1,129},{2,130},{3,131},{4,132},{5,133},{6,134},{7,135},{8... | collective-permute-start | bytes 776 | tf_op jit(solution)/shard_map/ppermute | solution.py:49
  146.4 2.5 %collective-permute-done.26 = f32[2,32]{1,0:T(2,128)S(1)} collective-permute-done((f32[2,32]{1,0:T(2,128)S(1)}, f32[2,32]{1,0:T(2,128)S(1)}, u32[]{:S(2)}, u32[]{:S(2)}) %collective-permute-start.26) | collective-permute-done | bytes 288 | tf_op jit(solution)/shard_map/ppermute | solution.py:49
  (128 shorter events, 26.0 us)
Async XLA Ops:
  0.6 1.6 %copy-start = (bf16[128,1664]{1,0:T(8,128)(2,1)S(1)}, bf16[128,1664]{1,0:T(8,128)(2,1)}, u32[]{:S(2)}) copy-start(bf16[128,1664]{1,0:T(8,128)(2,1)} %param.6) | copy-start | bytes 1277956
  2.0 1.4 copy-start.1
  2.5 2.3 %collective-permute-start = (bf16[128,1792]{0,1:T(8,128)(2,1)S(1)}, bf16[128,1792]{0,1:T(8,128)(2,1)S(1)}, u32[]{:S(2)}, u32[]{:S(2)}) collective-permute-start(bf16[128,1792]{0,1:T(8,128)(2,1)S(1)} %pad_maximum_fusion.3), channel_id=1, source_target_pairs={{0,1},{1,0},{2,3},{3,2},{4,5},{5,4},{6,7},{7,6},{8,9},{9,8},{10,11... | collective-permute-start | bytes 1376264 | tf_op jit(solution)/shard_map/ppermute | solution.py:39
  2.8 2.0 %collective-permute-start.1 = (bf16[128,896]{0,1:T(8,128)(2,1)S(1)}, bf16[128,896]{0,1:T(8,128)(2,1)S(1)}, u32[]{:S(2)}, u32[]{:S(2)}) collective-permute-start(bf16[128,896]{0,1:T(8,128)(2,1)S(1)} %copy.127), channel_id=1, source_target_pairs={{0,1},{1,0},{2,3},{3,2},{4,5},{5,4},{6,7},{7,6},{8,9},{9,8},{10,11... | collective-permute-start | bytes 688136 | tf_op jit(solution)/shard_map/ppermute | solution.py:39
  5.1 13.1 %collective-permute-start.2 = (bf16[128,1792]{0,1:T(8,128)(2,1)S(1)}, bf16[128,1792]{0,1:T(8,128)(2,1)S(1)}, u32[]{:S(2)}, u32[]{:S(2)}) collective-permute-start(bf16[128,1792]{0,1:T(8,128)(2,1)S(1)} %get-tuple-element.45), channel_id=1, source_target_pairs={{0,6},{2,0},{4,2},{6,4},{1,7},{3,1},{5,3},{7,5},{8,14},{10,8},{12,... | collective-permute-start | bytes 1376264 | tf_op jit(solution)/shard_map/ppermute | solution.py:39
  7.9 13.5 %collective-permute-start.3 = (bf16[128,1792]{0,1:T(8,128)(2,1)S(1)}, bf16[128,1792]{0,1:T(8,128)(2,1)S(1)}, u32[]{:S(2)}, u32[]{:S(2)}) collective-permute-start(bf16[128,1792]{0,1:T(8,128)(2,1)S(1)} %get-tuple-element.46), channel_id=1, source_target_pairs={{0,2},{2,4},{4,6},{6,0},{1,3},{3,5},{5,7},{7,1},{8,10},{10,12},{12... | collective-permute-start | bytes 1376264 | tf_op jit(solution)/shard_map/ppermute | solution.py:39
  8.0 37.1 %collective-permute-start.9 = (bf16[256,1792]{0,1:T(8,128)(2,1)S(1)}, bf16[256,1792]{0,1:T(8,128)(2,1)S(1)}, u32[]{:S(2)}, u32[]{:S(2)}) collective-permute-start(bf16[256,1792]{0,1:T(8,128)(2,1)S(1)} %pad_maximum_fusion.1), channel_id=1, source_target_pairs={{8,0},{16,8},{24,16},{32,24},{40,32},{48,40},{56,48},{64,56},{72,6... | collective-permute-start | bytes 2752520 | tf_op jit(solution)/shard_map/ppermute | solution.py:34
  15.7 29.4 %collective-permute-start.8 = (bf16[256,1792]{0,1:T(8,128)(2,1)S(1)}, bf16[256,1792]{0,1:T(8,128)(2,1)S(1)}, u32[]{:S(2)}, u32[]{:S(2)}) collective-permute-start(bf16[256,1792]{0,1:T(8,128)(2,1)S(1)} %pad_maximum_fusion.1), channel_id=1, source_target_pairs={{0,8},{8,16},{16,24},{24,32},{32,40},{40,48},{48,56},{56,64},{64,7... | collective-permute-start | bytes 2752520 | tf_op jit(solution)/shard_map/ppermute | solution.py:34
  21.4 13.5 %collective-permute-start.6 = (bf16[128,1792]{0,1:T(8,128)(2,1)S(1)}, bf16[128,1792]{0,1:T(8,128)(2,1)S(1)}, u32[]{:S(2)}, u32[]{:S(2)}) collective-permute-start(bf16[128,1792]{0,1:T(8,128)(2,1)S(1)} %collective-permute-done.2), channel_id=1, source_target_pairs={{0,6},{2,0},{4,2},{6,4},{1,7},{3,1},{5,3},{7,5},{8,14},{10,8},{12,... | collective-permute-start | bytes 1376264 | tf_op jit(solution)/shard_map/ppermute | solution.py:39
  21.8 23.0 %collective-permute-start.4 = (bf16[128,1792]{0,1:T(8,128)(2,1)S(1)}, bf16[128,1792]{0,1:T(8,128)(2,1)S(1)}, u32[]{:S(2)}, u32[]{:S(2)}) collective-permute-start(bf16[128,1792]{0,1:T(8,128)(2,1)S(1)} %get-tuple-element.41), channel_id=1, source_target_pairs={{0,6},{2,0},{4,2},{6,4},{1,7},{3,1},{5,3},{7,5},{8,14},{10,8},{12,... | collective-permute-start | bytes 1376264 | tf_op jit(solution)/shard_map/ppermute | solution.py:39
  21.8 13.1 %collective-permute-start.7 = (bf16[128,1792]{0,1:T(8,128)(2,1)S(1)}, bf16[128,1792]{0,1:T(8,128)(2,1)S(1)}, u32[]{:S(2)}, u32[]{:S(2)}) collective-permute-start(bf16[128,1792]{0,1:T(8,128)(2,1)S(1)} %collective-permute-done.3), channel_id=1, source_target_pairs={{0,2},{2,4},{4,6},{6,0},{1,3},{3,5},{5,7},{7,1},{8,10},{10,12},{12... | collective-permute-start | bytes 1376264 | tf_op jit(solution)/shard_map/ppermute | solution.py:39
  34.9 9.7 %collective-permute-start.5 = (bf16[128,1792]{0,1:T(8,128)(2,1)S(1)}, bf16[128,1792]{0,1:T(8,128)(2,1)S(1)}, u32[]{:S(2)}, u32[]{:S(2)}) collective-permute-start(bf16[128,1792]{0,1:T(8,128)(2,1)S(1)} %get-tuple-element.42), channel_id=1, source_target_pairs={{0,2},{2,4},{4,6},{6,0},{1,3},{3,5},{5,7},{7,1},{8,10},{10,12},{12... | collective-permute-start | bytes 1376264 | tf_op jit(solution)/shard_map/ppermute | solution.py:39
  35.1 26.1 %collective-permute-start.10 = (bf16[256,1792]{0,1:T(8,128)(2,1)S(1)}, bf16[256,1792]{0,1:T(8,128)(2,1)S(1)}, u32[]{:S(2)}, u32[]{:S(2)}) collective-permute-start(bf16[256,1792]{0,1:T(8,128)(2,1)S(1)} %constant_dynamic-update-slice_fusion.4), channel_id=1, source_target_pairs={{0,8},{1,9},{2,10},{3,11},{8,16},{9,17},{10,18},{11,19},{12,4},{13... | collective-permute-start | bytes 2752520 | tf_op jit(solution)/shard_map/ppermute | solution.py:122
  45.2 18.3 %collective-permute-start.11 = (bf16[256,1792]{0,1:T(8,128)(2,1)S(1)}, bf16[256,1792]{0,1:T(8,128)(2,1)S(1)}, u32[]{:S(2)}, u32[]{:S(2)}) collective-permute-start(bf16[256,1792]{0,1:T(8,128)(2,1)S(1)} %get-tuple-element.23), channel_id=1, source_target_pairs={{0,6},{2,0},{4,2},{6,4},{1,7},{3,1},{5,3},{7,5},{8,14},{10,8},{12,... | collective-permute-start | bytes 2752520 | tf_op jit(solution)/shard_map/ppermute | solution.py:39
  46.8 19.8 %collective-permute-start.12 = (bf16[256,1792]{0,1:T(8,128)(2,1)S(1)}, bf16[256,1792]{0,1:T(8,128)(2,1)S(1)}, u32[]{:S(2)}, u32[]{:S(2)}) collective-permute-start(bf16[256,1792]{0,1:T(8,128)(2,1)S(1)} %get-tuple-element.24), channel_id=1, source_target_pairs={{0,2},{2,4},{4,6},{6,0},{1,3},{3,5},{5,7},{7,1},{8,10},{10,12},{12... | collective-permute-start | bytes 2752520 | tf_op jit(solution)/shard_map/ppermute | solution.py:39
  78.0 1.6 %collective-permute-start.13 = (bf16[128,896]{1,0:T(8,128)(2,1)S(1)}, bf16[128,896]{1,0:T(8,128)(2,1)S(1)}, u32[]{:S(2)}, u32[]{:S(2)}) collective-permute-start(bf16[128,896]{1,0:T(8,128)(2,1)S(1)} %copy.129), channel_id=1, source_target_pairs={{0,1},{1,0},{2,3},{3,2},{4,5},{5,4},{6,7},{7,6},{8,9},{9,8},{10,11... | collective-permute-start | bytes 688136 | tf_op jit(solution)/shard_map/ppermute | solution.py:39
  80.0 12.2 %collective-permute-start.14 = (bf16[32,6656]{1,0:T(8,128)(2,1)S(1)}, bf16[32,6656]{1,0:T(8,128)(2,1)S(1)}, u32[]{:S(2)}, u32[]{:S(2)}) collective-permute-start(bf16[32,6656]{1,0:T(8,128)(2,1)S(1)} %select_n.283), channel_id=1, source_target_pairs={{0,6},{2,0},{4,2},{6,4},{1,7},{3,1},{5,3},{7,5},{8,14},{10,8},{12,... | collective-permute-start | bytes 1277960 | tf_op jit(solution)/shard_map/ppermute | solution.py:39
  81.6 13.5 %collective-permute-start.15 = (bf16[32,6656]{1,0:T(8,128)(2,1)S(1)}, bf16[32,6656]{1,0:T(8,128)(2,1)S(1)}, u32[]{:S(2)}, u32[]{:S(2)}) collective-permute-start(bf16[32,6656]{1,0:T(8,128)(2,1)S(1)} %select_n.283), channel_id=1, source_target_pairs={{0,2},{2,4},{4,6},{6,0},{1,3},{3,5},{5,7},{7,1},{8,10},{10,12},{12... | collective-permute-start | bytes 1277960 | tf_op jit(solution)/shard_map/ppermute | solution.py:39
  92.2 6.6 %collective-permute-start.16 = (bf16[16,6656]{1,0:T(8,128)(2,1)S(1)}, bf16[16,6656]{1,0:T(8,128)(2,1)S(1)}, u32[]{:S(2)}, u32[]{:S(2)}) collective-permute-start(bf16[16,6656]{1,0:T(8,128)(2,1)S(1)} %slice.206), channel_id=1, source_target_pairs={{0,6},{2,0},{4,2},{6,4},{1,7},{3,1},{5,3},{7,5},{8,14},{10,8},{12,... | collective-permute-start | bytes 638984 | tf_op jit(solution)/shard_map/ppermute | solution.py:39
  95.1 7.5 %collective-permute-start.17 = (bf16[16,6656]{1,0:T(8,128)(2,1)S(1)}, bf16[16,6656]{1,0:T(8,128)(2,1)S(1)}, u32[]{:S(2)}, u32[]{:S(2)}) collective-permute-start(bf16[16,6656]{1,0:T(8,128)(2,1)S(1)} %slice.207), channel_id=1, source_target_pairs={{0,2},{2,4},{4,6},{6,0},{1,3},{3,5},{5,7},{7,1},{8,10},{10,12},{12... | collective-permute-start | bytes 638984 | tf_op jit(solution)/shard_map/ppermute | solution.py:39
  104.0 3.8 %collective-permute-start.18 = (bf16[4,32,6656]{2,1,0:T(8,128)(2,1)}, bf16[4,32,6656]{2,1,0:T(8,128)(2,1)S(1)}, u32[]{:S(2)}, u32[]{:S(2)}) collective-permute-start(bf16[4,32,6656]{2,1,0:T(8,128)(2,1)} %pad_maximum_fusion), channel_id=1, source_target_pairs={{0,1},{1,0},{2,3},{3,2},{4,5},{5,4},{6,7},{7,6},{8,9},{9,8},{10,11... | collective-permute-start | bytes 5111816 | tf_op jit(solution)/shard_map/ppermute | solution.py:39
  112.9 1.2 collective-permute-start.19
  114.1 3.7 %collective-permute-start.20 = (f32[2,32]{1,0:T(2,128)S(1)}, f32[2,32]{1,0:T(2,128)S(1)}, u32[]{:S(2)}, u32[]{:S(2)}) collective-permute-start(f32[2,32]{1,0:T(2,128)S(1)} %pad_maximum_fusion.6), channel_id=1, source_target_pairs={{0,2},{1,3},{2,0},{3,1},{4,6},{5,7},{6,4},{7,5},{8,10},{9,11},{10,... | collective-permute-start | bytes 776 | tf_op jit(solution)/shard_map/ppermute | solution.py:49
  117.8 5.2 %collective-permute-start.21 = (f32[2,32]{1,0:T(2,128)S(1)}, f32[2,32]{1,0:T(2,128)S(1)}, u32[]{:S(2)}, u32[]{:S(2)}) collective-permute-start(f32[2,32]{1,0:T(2,128)S(1)} %pad_maximum_fusion.7), channel_id=1, source_target_pairs={{0,4},{1,5},{2,6},{3,7},{4,0},{5,1},{6,2},{7,3},{8,12},{9,13},{10,... | collective-permute-start | bytes 776 | tf_op jit(solution)/shard_map/ppermute | solution.py:49
  123.0 3.7 %collective-permute-start.22 = (f32[2,32]{1,0:T(2,128)S(1)}, f32[2,32]{1,0:T(2,128)S(1)}, u32[]{:S(2)}, u32[]{:S(2)}) collective-permute-start(f32[2,32]{1,0:T(2,128)S(1)} %pad_maximum_fusion.8), channel_id=1, source_target_pairs={{0,8},{1,9},{2,10},{3,11},{4,12},{5,13},{6,14},{7,15},{8,0},{9,1},... | collective-permute-start | bytes 776 | tf_op jit(solution)/shard_map/ppermute | solution.py:49
  126.6 4.9 %collective-permute-start.23 = (f32[2,32]{1,0:T(2,128)S(1)}, f32[2,32]{1,0:T(2,128)S(1)}, u32[]{:S(2)}, u32[]{:S(2)}) collective-permute-start(f32[2,32]{1,0:T(2,128)S(1)} %pad_maximum_fusion.9), channel_id=1, source_target_pairs={{0,16},{1,17},{2,18},{3,19},{4,20},{5,21},{6,22},{7,23},{8,24},{9,... | collective-permute-start | bytes 776 | tf_op jit(solution)/shard_map/ppermute | solution.py:49
  131.6 8.5 %collective-permute-start.24 = (f32[2,32]{1,0:T(2,128)S(1)}, f32[2,32]{1,0:T(2,128)S(1)}, u32[]{:S(2)}, u32[]{:S(2)}) collective-permute-start(f32[2,32]{1,0:T(2,128)S(1)} %pad_maximum_fusion.10), channel_id=1, source_target_pairs={{0,32},{1,33},{2,34},{3,35},{4,36},{5,37},{6,38},{7,39},{8,40},{9,... | collective-permute-start | bytes 776 | tf_op jit(solution)/shard_map/ppermute | solution.py:49
  140.1 3.7 %collective-permute-start.25 = (f32[2,32]{1,0:T(2,128)S(1)}, f32[2,32]{1,0:T(2,128)S(1)}, u32[]{:S(2)}, u32[]{:S(2)}) collective-permute-start(f32[2,32]{1,0:T(2,128)S(1)} %pad_maximum_fusion.11), channel_id=1, source_target_pairs={{0,64},{1,65},{2,66},{3,67},{4,68},{5,69},{6,70},{7,71},{8,72},{9,... | collective-permute-start | bytes 776 | tf_op jit(solution)/shard_map/ppermute | solution.py:49
  143.7 5.2 %collective-permute-start.26 = (f32[2,32]{1,0:T(2,128)S(1)}, f32[2,32]{1,0:T(2,128)S(1)}, u32[]{:S(2)}, u32[]{:S(2)}) collective-permute-start(f32[2,32]{1,0:T(2,128)S(1)} %pad_maximum_fusion.12), channel_id=1, source_target_pairs={{0,128},{1,129},{2,130},{3,131},{4,132},{5,133},{6,134},{7,135},{8... | collective-permute-start | bytes 776 | tf_op jit(solution)/shard_map/ppermute | solution.py:49

commit v12 on v11

--- a/solution.py
+++ b/solution.py
@@ -43,13 +43,13 @@
     n = 1
     for name in ALL:
         n *= lax.axis_size(name)
-    bit = 1
-    while bit < n:
+    bit = n // 2
+    while bit >= 1:
         perm = [(i, i ^ bit) for i in range(n)]
         other = lax.ppermute(jnp.stack([sums, peaks]), ALL, perm)
         sums = sums + other[0]
         peaks = jnp.maximum(peaks, other[1])
-        bit *= 2
+        bit //= 2
     return sums, peaks
 
 

time: 151 us -> 152 us (level)
  starting transfers between devices: 42.2 us -> 40.3 us
  waiting for transfers between devices: 75.8 us -> 77.6 us
    ppermute x8, starting transfers between devices: 15.6 us -> 13.8 us  [butterfly(): other = lax.ppermute(jnp.stack([sums, peaks]), ALL, perm)]
    ppermute x8, waiting for transfers between devices: 18.7 us -> 20.6 us  [butterfly(): other = lax.ppermute(jnp.stack([sums, peaks]), ALL, perm)]
where the time goes in v12:
time: 152 us; the launch traced here: 150 us
  waiting for transfers between devices  77.6 us (51%)
  starting transfers between devices  40.3 us (27%)
  matrix products  14.7 us (10%)
  other arithmetic  9.61 us (6%)
  local copies, waits for them, and re-layouts  6.78 us (4%)
    ppermute x16, waiting for transfers between devices, cyclic(): return lax.ppermute(x, axis, [(i, (i + by) % n) for i in range(n)])  45.8 us
    ppermute x8, waiting for transfers between devices, butterfly(): other = lax.ppermute(jnp.stack([sums, peaks]), ALL, perm)  20.6 us
    ppermute x8, starting transfers between devices, butterfly(): other = lax.ppermute(jnp.stack([sums, peaks]), ALL, perm)  13.8 us
    ppermute x16, starting transfers between devices, cyclic(): return lax.ppermute(x, axis, [(i, (i + by) % n) for i in range(n)])  13.2 us
    ppermute x1, waiting for transfers between devices, per_device(): kv_sets.append(lax.ppermute(far, ALL, pairs))  11.2 us
    ppermute x2, starting transfers between devices, shifted(): lax.ppermute(x, axis, [(i, i + by) for i in range(n) if 0 <= i + by < n])  9.57 us
    dot_general x9, matrix products, per_device(): jnp.einsum('hrk,khd->rhd', exp_terms.astype(jnp.bfloat16), value_heads, p...  5.63 us
    reduce_sum x1, other arithmetic, per_device(): total = jnp.sum(exp_terms, axis=2)  4.86 us
  transfers between devices with their start and end apart: 27, of which 19 were waited for; matrix products, arithmetic and copies ran while one was open for 6% of the time, Pallas kernels for 0%

profile of v12, /device:TPU:8, one launch (start us, length us, event | category | flops | bytes accessed | tf_op | source)
XLA Modules:
  0.0 150.3 jit_solution(344121412370055033)
XLA Ops:
  0.6 1.4 constant_dynamic-slice_fusion.3
  5.1 2.8 %collective-permute-start.2 = (bf16[128,1792]{0,1:T(8,128)(2,1)S(1)}, bf16[128,1792]{0,1:T(8,128)(2,1)S(1)}, u32[]{:S(2)}, u32[]{:S(2)}) collective-permute-start(bf16[128,1792]{0,1:T(8,128)(2,1)S(1)} %get-tuple-element.45), channel_id=1, source_target_pairs={{0,6},{2,0},{4,2},{6,4},{1,7},{3,1},{5,3},{7,5},{8,14},{10,8},{12,... | collective-permute-start | bytes 1376264 | tf_op jit(solution)/shard_map/ppermute | solution.py:39
  8.0 7.7 %collective-permute-start.9 = (bf16[256,1792]{0,1:T(8,128)(2,1)S(1)}, bf16[256,1792]{0,1:T(8,128)(2,1)S(1)}, u32[]{:S(2)}, u32[]{:S(2)}) collective-permute-start(bf16[256,1792]{0,1:T(8,128)(2,1)S(1)} %pad_maximum_fusion.1), channel_id=1, source_target_pairs={{8,0},{16,8},{24,16},{32,24},{40,32},{48,40},{56,48},{64,56},{72,6... | collective-permute-start | bytes 2752520 | tf_op jit(solution)/shard_map/ppermute | solution.py:34
  15.7 1.9 %collective-permute-start.8 = (bf16[256,1792]{0,1:T(8,128)(2,1)S(1)}, bf16[256,1792]{0,1:T(8,128)(2,1)S(1)}, u32[]{:S(2)}, u32[]{:S(2)}) collective-permute-start(bf16[256,1792]{0,1:T(8,128)(2,1)S(1)} %pad_maximum_fusion.1), channel_id=1, source_target_pairs={{0,8},{8,16},{16,24},{24,32},{32,40},{40,48},{48,56},{56,64},{64,7... | collective-permute-start | bytes 2752520 | tf_op jit(solution)/shard_map/ppermute | solution.py:34
  18.2 3.2 %collective-permute-done.3 = bf16[128,1792]{0,1:T(8,128)(2,1)S(1)} collective-permute-done((bf16[128,1792]{0,1:T(8,128)(2,1)S(1)}, bf16[128,1792]{0,1:T(8,128)(2,1)S(1)}, u32[]{:S(2)}, u32[]{:S(2)}) %collective-permute-start.3) | collective-permute-done | bytes 458784 | tf_op jit(solution)/shard_map/ppermute | solution.py:39
  21.8 2.0 %collective-permute-start.7 = (bf16[128,1792]{0,1:T(8,128)(2,1)S(1)}, bf16[128,1792]{0,1:T(8,128)(2,1)S(1)}, u32[]{:S(2)}, u32[]{:S(2)}) collective-permute-start(bf16[128,1792]{0,1:T(8,128)(2,1)S(1)} %collective-permute-done.3), channel_id=1, source_target_pairs={{0,2},{2,4},{4,6},{6,0},{1,3},{3,5},{5,7},{7,1},{8,10},{10,12},{12... | collective-permute-start | bytes 1376264 | tf_op jit(solution)/shard_map/ppermute | solution.py:39
  23.9 10.9 %collective-permute-done.6 = bf16[128,1792]{0,1:T(8,128)(2,1)S(1)} collective-permute-done((bf16[128,1792]{0,1:T(8,128)(2,1)S(1)}, bf16[128,1792]{0,1:T(8,128)(2,1)S(1)}, u32[]{:S(2)}, u32[]{:S(2)}) %collective-permute-start.6) | collective-permute-done | bytes 458784 | tf_op jit(solution)/shard_map/ppermute | solution.py:39
  35.1 3.8 %collective-permute-start.10 = (bf16[256,1792]{0,1:T(8,128)(2,1)S(1)}, bf16[256,1792]{0,1:T(8,128)(2,1)S(1)}, u32[]{:S(2)}, u32[]{:S(2)}) collective-permute-start(bf16[256,1792]{0,1:T(8,128)(2,1)S(1)} %constant_dynamic-update-slice_fusion.4), channel_id=1, source_target_pairs={{0,8},{1,9},{2,10},{3,11},{8,16},{9,17},{10,18},{11,19},{12,4},{13... | collective-permute-start | bytes 2752520 | tf_op jit(solution)/shard_map/ppermute | solution.py:122
  38.9 5.6 %collective-permute-done.5 = bf16[128,1792]{0,1:T(8,128)(2,1)S(1)} collective-permute-done((bf16[128,1792]{0,1:T(8,128)(2,1)S(1)}, bf16[128,1792]{0,1:T(8,128)(2,1)S(1)}, u32[]{:S(2)}, u32[]{:S(2)}) %collective-permute-start.5) | collective-permute-done | bytes 458784 | tf_op jit(solution)/shard_map/ppermute | solution.py:39
  45.2 1.5 %collective-permute-start.11 = (bf16[256,1792]{0,1:T(8,128)(2,1)S(1)}, bf16[256,1792]{0,1:T(8,128)(2,1)S(1)}, u32[]{:S(2)}, u32[]{:S(2)}) collective-permute-start(bf16[256,1792]{0,1:T(8,128)(2,1)S(1)} %get-tuple-element.23), channel_id=1, source_target_pairs={{0,6},{2,0},{4,2},{6,4},{1,7},{3,1},{5,3},{7,5},{8,14},{10,8},{12,... | collective-permute-start | bytes 2752520 | tf_op jit(solution)/shard_map/ppermute | solution.py:39
  50.0 11.2 %collective-permute-done.10 = bf16[256,1792]{0,1:T(8,128)(2,1)S(1)} collective-permute-done((bf16[256,1792]{0,1:T(8,128)(2,1)S(1)}, bf16[256,1792]{0,1:T(8,128)(2,1)S(1)}, u32[]{:S(2)}, u32[]{:S(2)}) %collective-permute-start.10) | collective-permute-done | bytes 917536 | tf_op jit(solution)/shard_map/ppermute | solution.py:122
  61.2 2.3 %collective-permute-done.11 = bf16[256,1792]{0,1:T(8,128)(2,1)S(1)} collective-permute-done((bf16[256,1792]{0,1:T(8,128)(2,1)S(1)}, bf16[256,1792]{0,1:T(8,128)(2,1)S(1)}, u32[]{:S(2)}, u32[]{:S(2)}) %collective-permute-start.11) | collective-permute-done | bytes 917536 | tf_op jit(solution)/shard_map/ppermute | solution.py:39
  64.6 2.0 %collective-permute-done.12 = bf16[256,1792]{0,1:T(8,128)(2,1)S(1)} collective-permute-done((bf16[256,1792]{0,1:T(8,128)(2,1)S(1)}, bf16[256,1792]{0,1:T(8,128)(2,1)S(1)}, u32[]{:S(2)}, u32[]{:S(2)}) %collective-permute-start.12) | collective-permute-done | bytes 917536 | tf_op jit(solution)/shard_map/ppermute | solution.py:39
  70.8 4.9 %fusion.18 = (f32[7,256]{1,0:T(8,128)S(1)}, f32[7,256]{1,0:T(8,128)S(1)}, f32[7,256]{1,0:T(8,128)S(1)}, f32[7,256]{1,0:T(8,128)S(1)}, f32[7,256]{1,0:T(8,128)S(1...) fusion(f32[7,256,256]{1,2,0:T(8,128)S(1)} %get-tuple-element.108, ...), kind=kLoop, calls=%fused_computation.40 | loop fusion | flops 20627712 | bytes 17176576 | tf_op jit(solution)/shard_map/reduce_sum | solution.py:161
  80.0 1.7 %collective-permute-start.14 = (bf16[32,6656]{1,0:T(8,128)(2,1)S(1)}, bf16[32,6656]{1,0:T(8,128)(2,1)S(1)}, u32[]{:S(2)}, u32[]{:S(2)}) collective-permute-start(bf16[32,6656]{1,0:T(8,128)(2,1)S(1)} %select_n.283), channel_id=1, source_target_pairs={{0,6},{2,0},{4,2},{6,4},{1,7},{3,1},{5,3},{7,5},{8,14},{10,8},{12,... | collective-permute-start | bytes 1277960 | tf_op jit(solution)/shard_map/ppermute | solution.py:39
  82.3 9.8 %collective-permute-done.14 = bf16[32,6656]{1,0:T(8,128)(2,1)S(1)} collective-permute-done((bf16[32,6656]{1,0:T(8,128)(2,1)S(1)}, bf16[32,6656]{1,0:T(8,128)(2,1)S(1)}, u32[]{:S(2)}, u32[]{:S(2)}) %collective-permute-start.14) | collective-permute-done | bytes 426016 | tf_op jit(solution)/shard_map/ppermute | solution.py:39
  92.2 2.6 %collective-permute-start.16 = (bf16[16,6656]{1,0:T(8,128)(2,1)S(1)}, bf16[16,6656]{1,0:T(8,128)(2,1)S(1)}, u32[]{:S(2)}, u32[]{:S(2)}) collective-permute-start(bf16[16,6656]{1,0:T(8,128)(2,1)S(1)} %slice.206), channel_id=1, source_target_pairs={{0,6},{2,0},{4,2},{6,4},{1,7},{3,1},{5,3},{7,5},{8,14},{10,8},{12,... | collective-permute-start | bytes 638984 | tf_op jit(solution)/shard_map/ppermute | solution.py:39
  95.2 3.6 %collective-permute-done.16 = bf16[16,6656]{1,0:T(8,128)(2,1)S(1)} collective-permute-done((bf16[16,6656]{1,0:T(8,128)(2,1)S(1)}, bf16[16,6656]{1,0:T(8,128)(2,1)S(1)}, u32[]{:S(2)}, u32[]{:S(2)}) %collective-permute-start.16) | collective-permute-done | bytes 213024 | tf_op jit(solution)/shard_map/ppermute | solution.py:39
  98.8 3.8 %collective-permute-done.17 = bf16[16,6656]{1,0:T(8,128)(2,1)S(1)} collective-permute-done((bf16[16,6656]{1,0:T(8,128)(2,1)S(1)}, bf16[16,6656]{1,0:T(8,128)(2,1)S(1)}, u32[]{:S(2)}, u32[]{:S(2)}) %collective-permute-start.17) | collective-permute-done | bytes 213024 | tf_op jit(solution)/shard_map/ppermute | solution.py:39
  102.6 1.4 pad_maximum_fusion
  104.6 3.3 %collective-permute-done.18 = bf16[4,32,6656]{2,1,0:T(8,128)(2,1)S(1)} collective-permute-done((bf16[4,32,6656]{2,1,0:T(8,128)(2,1)}, bf16[4,32,6656]{2,1,0:T(8,128)(2,1)S(1)}, u32[]{:S(2)}, u32[]{:S(2)}) %collective-permute-start.18) | collective-permute-done | bytes 1703968 | tf_op jit(solution)/shard_map/ppermute | solution.py:39
  108.1 4.6 %multiply_reduce_fusion = (f32[256]{0:T(256)S(1)}, f32[256]{0:T(256)S(1)}, f32[256,384]{1,0:T(8,128)S(1)}) fusion(bf16[256,6656]{1,0:T(8,128)(2,1)S(1)} %fusion.97, bf16[6656,384]{1,0:T(8,128)(2,1)} %param.9), kind=kOutput, calls=%fused_computation.134 | convolution fusion | flops 1308917248 | bytes 8914944 | tf_op jit(solution)/shard_map/dot_general | solution.py:195
  112.9 2.5 %collective-permute-start.19 = (f32[2,32]{1,0:T(2,128)S(1)}, f32[2,32]{1,0:T(2,128)S(1)}, u32[]{:S(2)}, u32[]{:S(2)}) collective-permute-start(f32[2,32]{1,0:T(2,128)S(1)} %pad_maximum_fusion.5), channel_id=1, source_target_pairs={{0,128},{1,129},{2,130},{3,131},{4,132},{5,133},{6,134},{7,135},{8... | collective-permute-start | bytes 776 | tf_op jit(solution)/shard_map/ppermute | solution.py:49
  115.4 2.6 %collective-permute-done.19 = f32[2,32]{1,0:T(2,128)S(1)} collective-permute-done((f32[2,32]{1,0:T(2,128)S(1)}, f32[2,32]{1,0:T(2,128)S(1)}, u32[]{:S(2)}, u32[]{:S(2)}) %collective-permute-start.19) | collective-permute-done | bytes 288 | tf_op jit(solution)/shard_map/ppermute | solution.py:49
  118.6 3.1 %collective-permute-done.20 = f32[2,32]{1,0:T(2,128)S(1)} collective-permute-done((f32[2,32]{1,0:T(2,128)S(1)}, f32[2,32]{1,0:T(2,128)S(1)}, u32[]{:S(2)}, u32[]{:S(2)}) %collective-permute-start.20) | collective-permute-done | bytes 288 | tf_op jit(solution)/shard_map/ppermute | solution.py:49
  121.7 7.3 %collective-permute-start.21 = (f32[2,32]{1,0:T(2,128)S(1)}, f32[2,32]{1,0:T(2,128)S(1)}, u32[]{:S(2)}, u32[]{:S(2)}) collective-permute-start(f32[2,32]{1,0:T(2,128)S(1)} %pad_maximum_fusion.7), channel_id=1, source_target_pairs={{0,32},{1,33},{2,34},{3,35},{4,36},{5,37},{6,38},{7,39},{8,40},{9,... | collective-permute-start | bytes 776 | tf_op jit(solution)/shard_map/ppermute | solution.py:49
  129.0 1.5 %collective-permute-done.21 = f32[2,32]{1,0:T(2,128)S(1)} collective-permute-done((f32[2,32]{1,0:T(2,128)S(1)}, f32[2,32]{1,0:T(2,128)S(1)}, u32[]{:S(2)}, u32[]{:S(2)}) %collective-permute-start.21) | collective-permute-done | bytes 288 | tf_op jit(solution)/shard_map/ppermute | solution.py:49
  130.6 2.1 %collective-permute-start.22 = (f32[2,32]{1,0:T(2,128)S(1)}, f32[2,32]{1,0:T(2,128)S(1)}, u32[]{:S(2)}, u32[]{:S(2)}) collective-permute-start(f32[2,32]{1,0:T(2,128)S(1)} %pad_maximum_fusion.8), channel_id=1, source_target_pairs={{0,16},{1,17},{2,18},{3,19},{4,20},{5,21},{6,22},{7,23},{8,24},{9,... | collective-permute-start | bytes 776 | tf_op jit(solution)/shard_map/ppermute | solution.py:49
  132.7 2.5 %collective-permute-done.22 = f32[2,32]{1,0:T(2,128)S(1)} collective-permute-done((f32[2,32]{1,0:T(2,128)S(1)}, f32[2,32]{1,0:T(2,128)S(1)}, u32[]{:S(2)}, u32[]{:S(2)}) %collective-permute-start.22) | collective-permute-done | bytes 288 | tf_op jit(solution)/shard_map/ppermute | solution.py:49
  136.2 2.6 %collective-permute-done.23 = f32[2,32]{1,0:T(2,128)S(1)} collective-permute-done((f32[2,32]{1,0:T(2,128)S(1)}, f32[2,32]{1,0:T(2,128)S(1)}, u32[]{:S(2)}, u32[]{:S(2)}) %collective-permute-start.23) | collective-permute-done | bytes 288 | tf_op jit(solution)/shard_map/ppermute | solution.py:49
  138.9 5.1 %collective-permute-done.24 = f32[2,32]{1,0:T(2,128)S(1)} collective-permute-done((f32[2,32]{1,0:T(2,128)S(1)}, f32[2,32]{1,0:T(2,128)S(1)}, u32[]{:S(2)}, u32[]{:S(2)}) %collective-permute-start.24) | collective-permute-done | bytes 288 | tf_op jit(solution)/shard_map/ppermute | solution.py:49
  145.4 2.3 %collective-permute-done.25 = f32[2,32]{1,0:T(2,128)S(1)} collective-permute-done((f32[2,32]{1,0:T(2,128)S(1)}, f32[2,32]{1,0:T(2,128)S(1)}, u32[]{:S(2)}, u32[]{:S(2)}) %collective-permute-start.25) | collective-permute-done | bytes 288 | tf_op jit(solution)/shard_map/ppermute | solution.py:49
  (128 shorter events, 25.4 us)
Async XLA Ops:
  0.6 1.6 %copy-start = (bf16[128,1664]{1,0:T(8,128)(2,1)S(1)}, bf16[128,1664]{1,0:T(8,128)(2,1)}, u32[]{:S(2)}) copy-start(bf16[128,1664]{1,0:T(8,128)(2,1)} %param.6) | copy-start | bytes 1277956
  2.0 1.4 copy-start.1
  2.5 2.3 %collective-permute-start = (bf16[128,1792]{0,1:T(8,128)(2,1)S(1)}, bf16[128,1792]{0,1:T(8,128)(2,1)S(1)}, u32[]{:S(2)}, u32[]{:S(2)}) collective-permute-start(bf16[128,1792]{0,1:T(8,128)(2,1)S(1)} %pad_maximum_fusion.3), channel_id=1, source_target_pairs={{0,1},{1,0},{2,3},{3,2},{4,5},{5,4},{6,7},{7,6},{8,9},{9,8},{10,11... | collective-permute-start | bytes 1376264 | tf_op jit(solution)/shard_map/ppermute | solution.py:39
  2.8 2.0 %collective-permute-start.1 = (bf16[128,896]{0,1:T(8,128)(2,1)S(1)}, bf16[128,896]{0,1:T(8,128)(2,1)S(1)}, u32[]{:S(2)}, u32[]{:S(2)}) collective-permute-start(bf16[128,896]{0,1:T(8,128)(2,1)S(1)} %copy.127), channel_id=1, source_target_pairs={{0,1},{1,0},{2,3},{3,2},{4,5},{5,4},{6,7},{7,6},{8,9},{9,8},{10,11... | collective-permute-start | bytes 688136 | tf_op jit(solution)/shard_map/ppermute | solution.py:39
  5.1 13.1 %collective-permute-start.2 = (bf16[128,1792]{0,1:T(8,128)(2,1)S(1)}, bf16[128,1792]{0,1:T(8,128)(2,1)S(1)}, u32[]{:S(2)}, u32[]{:S(2)}) collective-permute-start(bf16[128,1792]{0,1:T(8,128)(2,1)S(1)} %get-tuple-element.45), channel_id=1, source_target_pairs={{0,6},{2,0},{4,2},{6,4},{1,7},{3,1},{5,3},{7,5},{8,14},{10,8},{12,... | collective-permute-start | bytes 1376264 | tf_op jit(solution)/shard_map/ppermute | solution.py:39
  7.9 13.5 %collective-permute-start.3 = (bf16[128,1792]{0,1:T(8,128)(2,1)S(1)}, bf16[128,1792]{0,1:T(8,128)(2,1)S(1)}, u32[]{:S(2)}, u32[]{:S(2)}) collective-permute-start(bf16[128,1792]{0,1:T(8,128)(2,1)S(1)} %get-tuple-element.46), channel_id=1, source_target_pairs={{0,2},{2,4},{4,6},{6,0},{1,3},{3,5},{5,7},{7,1},{8,10},{10,12},{12... | collective-permute-start | bytes 1376264 | tf_op jit(solution)/shard_map/ppermute | solution.py:39
  8.0 37.1 %collective-permute-start.9 = (bf16[256,1792]{0,1:T(8,128)(2,1)S(1)}, bf16[256,1792]{0,1:T(8,128)(2,1)S(1)}, u32[]{:S(2)}, u32[]{:S(2)}) collective-permute-start(bf16[256,1792]{0,1:T(8,128)(2,1)S(1)} %pad_maximum_fusion.1), channel_id=1, source_target_pairs={{8,0},{16,8},{24,16},{32,24},{40,32},{48,40},{56,48},{64,56},{72,6... | collective-permute-start | bytes 2752520 | tf_op jit(solution)/shard_map/ppermute | solution.py:34
  15.7 29.4 %collective-permute-start.8 = (bf16[256,1792]{0,1:T(8,128)(2,1)S(1)}, bf16[256,1792]{0,1:T(8,128)(2,1)S(1)}, u32[]{:S(2)}, u32[]{:S(2)}) collective-permute-start(bf16[256,1792]{0,1:T(8,128)(2,1)S(1)} %pad_maximum_fusion.1), channel_id=1, source_target_pairs={{0,8},{8,16},{16,24},{24,32},{32,40},{40,48},{48,56},{56,64},{64,7... | collective-permute-start | bytes 2752520 | tf_op jit(solution)/shard_map/ppermute | solution.py:34
  21.4 13.5 %collective-permute-start.6 = (bf16[128,1792]{0,1:T(8,128)(2,1)S(1)}, bf16[128,1792]{0,1:T(8,128)(2,1)S(1)}, u32[]{:S(2)}, u32[]{:S(2)}) collective-permute-start(bf16[128,1792]{0,1:T(8,128)(2,1)S(1)} %collective-permute-done.2), channel_id=1, source_target_pairs={{0,6},{2,0},{4,2},{6,4},{1,7},{3,1},{5,3},{7,5},{8,14},{10,8},{12,... | collective-permute-start | bytes 1376264 | tf_op jit(solution)/shard_map/ppermute | solution.py:39
  21.8 23.0 %collective-permute-start.4 = (bf16[128,1792]{0,1:T(8,128)(2,1)S(1)}, bf16[128,1792]{0,1:T(8,128)(2,1)S(1)}, u32[]{:S(2)}, u32[]{:S(2)}) collective-permute-start(bf16[128,1792]{0,1:T(8,128)(2,1)S(1)} %get-tuple-element.41), channel_id=1, source_target_pairs={{0,6},{2,0},{4,2},{6,4},{1,7},{3,1},{5,3},{7,5},{8,14},{10,8},{12,... | collective-permute-start | bytes 1376264 | tf_op jit(solution)/shard_map/ppermute | solution.py:39
  21.8 13.1 %collective-permute-start.7 = (bf16[128,1792]{0,1:T(8,128)(2,1)S(1)}, bf16[128,1792]{0,1:T(8,128)(2,1)S(1)}, u32[]{:S(2)}, u32[]{:S(2)}) collective-permute-start(bf16[128,1792]{0,1:T(8,128)(2,1)S(1)} %collective-permute-done.3), channel_id=1, source_target_pairs={{0,2},{2,4},{4,6},{6,0},{1,3},{3,5},{5,7},{7,1},{8,10},{10,12},{12... | collective-permute-start | bytes 1376264 | tf_op jit(solution)/shard_map/ppermute | solution.py:39
  34.9 9.7 %collective-permute-start.5 = (bf16[128,1792]{0,1:T(8,128)(2,1)S(1)}, bf16[128,1792]{0,1:T(8,128)(2,1)S(1)}, u32[]{:S(2)}, u32[]{:S(2)}) collective-permute-start(bf16[128,1792]{0,1:T(8,128)(2,1)S(1)} %get-tuple-element.42), channel_id=1, source_target_pairs={{0,2},{2,4},{4,6},{6,0},{1,3},{3,5},{5,7},{7,1},{8,10},{10,12},{12... | collective-permute-start | bytes 1376264 | tf_op jit(solution)/shard_map/ppermute | solution.py:39
  35.1 26.1 %collective-permute-start.10 = (bf16[256,1792]{0,1:T(8,128)(2,1)S(1)}, bf16[256,1792]{0,1:T(8,128)(2,1)S(1)}, u32[]{:S(2)}, u32[]{:S(2)}) collective-permute-start(bf16[256,1792]{0,1:T(8,128)(2,1)S(1)} %constant_dynamic-update-slice_fusion.4), channel_id=1, source_target_pairs={{0,8},{1,9},{2,10},{3,11},{8,16},{9,17},{10,18},{11,19},{12,4},{13... | collective-permute-start | bytes 2752520 | tf_op jit(solution)/shard_map/ppermute | solution.py:122
  45.2 18.3 %collective-permute-start.11 = (bf16[256,1792]{0,1:T(8,128)(2,1)S(1)}, bf16[256,1792]{0,1:T(8,128)(2,1)S(1)}, u32[]{:S(2)}, u32[]{:S(2)}) collective-permute-start(bf16[256,1792]{0,1:T(8,128)(2,1)S(1)} %get-tuple-element.23), channel_id=1, source_target_pairs={{0,6},{2,0},{4,2},{6,4},{1,7},{3,1},{5,3},{7,5},{8,14},{10,8},{12,... | collective-permute-start | bytes 2752520 | tf_op jit(solution)/shard_map/ppermute | solution.py:39
  46.8 19.8 %collective-permute-start.12 = (bf16[256,1792]{0,1:T(8,128)(2,1)S(1)}, bf16[256,1792]{0,1:T(8,128)(2,1)S(1)}, u32[]{:S(2)}, u32[]{:S(2)}) collective-permute-start(bf16[256,1792]{0,1:T(8,128)(2,1)S(1)} %get-tuple-element.24), channel_id=1, source_target_pairs={{0,2},{2,4},{4,6},{6,0},{1,3},{3,5},{5,7},{7,1},{8,10},{10,12},{12... | collective-permute-start | bytes 2752520 | tf_op jit(solution)/shard_map/ppermute | solution.py:39
  78.0 1.6 %collective-permute-start.13 = (bf16[128,896]{1,0:T(8,128)(2,1)S(1)}, bf16[128,896]{1,0:T(8,128)(2,1)S(1)}, u32[]{:S(2)}, u32[]{:S(2)}) collective-permute-start(bf16[128,896]{1,0:T(8,128)(2,1)S(1)} %copy.129), channel_id=1, source_target_pairs={{0,1},{1,0},{2,3},{3,2},{4,5},{5,4},{6,7},{7,6},{8,9},{9,8},{10,11... | collective-permute-start | bytes 688136 | tf_op jit(solution)/shard_map/ppermute | solution.py:39
  80.0 12.2 %collective-permute-start.14 = (bf16[32,6656]{1,0:T(8,128)(2,1)S(1)}, bf16[32,6656]{1,0:T(8,128)(2,1)S(1)}, u32[]{:S(2)}, u32[]{:S(2)}) collective-permute-start(bf16[32,6656]{1,0:T(8,128)(2,1)S(1)} %select_n.283), channel_id=1, source_target_pairs={{0,6},{2,0},{4,2},{6,4},{1,7},{3,1},{5,3},{7,5},{8,14},{10,8},{12,... | collective-permute-start | bytes 1277960 | tf_op jit(solution)/shard_map/ppermute | solution.py:39
  81.6 13.5 %collective-permute-start.15 = (bf16[32,6656]{1,0:T(8,128)(2,1)S(1)}, bf16[32,6656]{1,0:T(8,128)(2,1)S(1)}, u32[]{:S(2)}, u32[]{:S(2)}) collective-permute-start(bf16[32,6656]{1,0:T(8,128)(2,1)S(1)} %select_n.283), channel_id=1, source_target_pairs={{0,2},{2,4},{4,6},{6,0},{1,3},{3,5},{5,7},{7,1},{8,10},{10,12},{12... | collective-permute-start | bytes 1277960 | tf_op jit(solution)/shard_map/ppermute | solution.py:39
  92.2 6.6 %collective-permute-start.16 = (bf16[16,6656]{1,0:T(8,128)(2,1)S(1)}, bf16[16,6656]{1,0:T(8,128)(2,1)S(1)}, u32[]{:S(2)}, u32[]{:S(2)}) collective-permute-start(bf16[16,6656]{1,0:T(8,128)(2,1)S(1)} %slice.206), channel_id=1, source_target_pairs={{0,6},{2,0},{4,2},{6,4},{1,7},{3,1},{5,3},{7,5},{8,14},{10,8},{12,... | collective-permute-start | bytes 638984 | tf_op jit(solution)/shard_map/ppermute | solution.py:39
  95.1 7.5 %collective-permute-start.17 = (bf16[16,6656]{1,0:T(8,128)(2,1)S(1)}, bf16[16,6656]{1,0:T(8,128)(2,1)S(1)}, u32[]{:S(2)}, u32[]{:S(2)}) collective-permute-start(bf16[16,6656]{1,0:T(8,128)(2,1)S(1)} %slice.207), channel_id=1, source_target_pairs={{0,2},{2,4},{4,6},{6,0},{1,3},{3,5},{5,7},{7,1},{8,10},{10,12},{12... | collective-permute-start | bytes 638984 | tf_op jit(solution)/shard_map/ppermute | solution.py:39
  104.0 3.8 %collective-permute-start.18 = (bf16[4,32,6656]{2,1,0:T(8,128)(2,1)}, bf16[4,32,6656]{2,1,0:T(8,128)(2,1)S(1)}, u32[]{:S(2)}, u32[]{:S(2)}) collective-permute-start(bf16[4,32,6656]{2,1,0:T(8,128)(2,1)} %pad_maximum_fusion), channel_id=1, source_target_pairs={{0,1},{1,0},{2,3},{3,2},{4,5},{5,4},{6,7},{7,6},{8,9},{9,8},{10,11... | collective-permute-start | bytes 5111816 | tf_op jit(solution)/shard_map/ppermute | solution.py:39
  112.9 5.2 %collective-permute-start.19 = (f32[2,32]{1,0:T(2,128)S(1)}, f32[2,32]{1,0:T(2,128)S(1)}, u32[]{:S(2)}, u32[]{:S(2)}) collective-permute-start(f32[2,32]{1,0:T(2,128)S(1)} %pad_maximum_fusion.5), channel_id=1, source_target_pairs={{0,128},{1,129},{2,130},{3,131},{4,132},{5,133},{6,134},{7,135},{8... | collective-permute-start | bytes 776 | tf_op jit(solution)/shard_map/ppermute | solution.py:49
  118.1 3.7 %collective-permute-start.20 = (f32[2,32]{1,0:T(2,128)S(1)}, f32[2,32]{1,0:T(2,128)S(1)}, u32[]{:S(2)}, u32[]{:S(2)}) collective-permute-start(f32[2,32]{1,0:T(2,128)S(1)} %pad_maximum_fusion.6), channel_id=1, source_target_pairs={{0,64},{1,65},{2,66},{3,67},{4,68},{5,69},{6,70},{7,71},{8,72},{9,... | collective-permute-start | bytes 776 | tf_op jit(solution)/shard_map/ppermute | solution.py:49
  121.7 8.8 %collective-permute-start.21 = (f32[2,32]{1,0:T(2,128)S(1)}, f32[2,32]{1,0:T(2,128)S(1)}, u32[]{:S(2)}, u32[]{:S(2)}) collective-permute-start(f32[2,32]{1,0:T(2,128)S(1)} %pad_maximum_fusion.7), channel_id=1, source_target_pairs={{0,32},{1,33},{2,34},{3,35},{4,36},{5,37},{6,38},{7,39},{8,40},{9,... | collective-permute-start | bytes 776 | tf_op jit(solution)/shard_map/ppermute | solution.py:49
  130.6 4.6 %collective-permute-start.22 = (f32[2,32]{1,0:T(2,128)S(1)}, f32[2,32]{1,0:T(2,128)S(1)}, u32[]{:S(2)}, u32[]{:S(2)}) collective-permute-start(f32[2,32]{1,0:T(2,128)S(1)} %pad_maximum_fusion.8), channel_id=1, source_target_pairs={{0,16},{1,17},{2,18},{3,19},{4,20},{5,21},{6,22},{7,23},{8,24},{9,... | collective-permute-start | bytes 776 | tf_op jit(solution)/shard_map/ppermute | solution.py:49
  135.1 3.7 %collective-permute-start.23 = (f32[2,32]{1,0:T(2,128)S(1)}, f32[2,32]{1,0:T(2,128)S(1)}, u32[]{:S(2)}, u32[]{:S(2)}) collective-permute-start(f32[2,32]{1,0:T(2,128)S(1)} %pad_maximum_fusion.9), channel_id=1, source_target_pairs={{0,8},{1,9},{2,10},{3,11},{4,12},{5,13},{6,14},{7,15},{8,0},{9,1},... | collective-permute-start | bytes 776 | tf_op jit(solution)/shard_map/ppermute | solution.py:49
  138.8 5.2 %collective-permute-start.24 = (f32[2,32]{1,0:T(2,128)S(1)}, f32[2,32]{1,0:T(2,128)S(1)}, u32[]{:S(2)}, u32[]{:S(2)}) collective-permute-start(f32[2,32]{1,0:T(2,128)S(1)} %pad_maximum_fusion.10), channel_id=1, source_target_pairs={{0,4},{1,5},{2,6},{3,7},{4,0},{5,1},{6,2},{7,3},{8,12},{9,13},{10,... | collective-permute-start | bytes 776 | tf_op jit(solution)/shard_map/ppermute | solution.py:49
  144.0 3.7 %collective-permute-start.25 = (f32[2,32]{1,0:T(2,128)S(1)}, f32[2,32]{1,0:T(2,128)S(1)}, u32[]{:S(2)}, u32[]{:S(2)}) collective-permute-start(f32[2,32]{1,0:T(2,128)S(1)} %pad_maximum_fusion.11), channel_id=1, source_target_pairs={{0,2},{1,3},{2,0},{3,1},{4,6},{5,7},{6,4},{7,5},{8,10},{9,11},{10,... | collective-permute-start | bytes 776 | tf_op jit(solution)/shard_map/ppermute | solution.py:49
  147.7 1.2 collective-permute-start.26
